TPU v7x, 32 devices: a whole 2x2x4 slice. The times are simulated.
32 devices in a mesh: groups: 2 (over y), ctx: 4 (over x, core), head: 4 (over z).
Axes of the slice: x: 2, y: 2, z: 4, core: 2. Of those that a mesh axis runs over, the one named last changes fastest.
Arguments:
- span_query: bfloat16 [4, 128, 64, 128], P('groups', 'ctx', 'head'), parts along dimension 0, may hold values from -5 to 5
- span_key: bfloat16 [4, 128, 8, 128], P('groups', 'ctx', 'head'), parts along dimension 0, may hold values from -15 to 15
- span_value: bfloat16 [4, 128, 8, 128], P('groups', 'ctx', 'head'), parts along dimension 0, may hold values from -6 to 6
- prefix_key: bfloat16 [64, 128, 8, 128], P(('groups', 'ctx'), None, 'head'), parts along dimension 0, may hold values from -15 to 15
- prefix_value: bfloat16 [64, 128, 8, 128], P(('groups', 'ctx'), None, 'head'), parts along dimension 0, may hold values from -6 to 6
- page_table: int32 [4, 16], P('groups', 'ctx'), parts along dimension 0, may hold values from 0 to 7, as said below
- decode_query: bfloat16 [8, 32, 64, 128], P('groups', 'ctx', 'head'), parts along dimension 0, may hold values from -5 to 5
- decode_key: bfloat16 [8, 32, 8, 128], P('groups', 'ctx', 'head'), parts along dimension 0, may hold values from -15 to 15
- decode_value: bfloat16 [8, 32, 8, 128], P('groups', 'ctx', 'head'), parts along dimension 0, may hold values from -6 to 6
- sample_prompt: int32 [64], P('groups'), parts along dimension 0, may hold values from 0 to 1, as said below
- out_weight: bfloat16 [8192, 8192], P('head', 'ctx'), may hold values from -0.25 to 0.25
Outputs:
- span_out: bfloat16 [4, 128, 8192], P('groups', None, 'ctx'), parts along dimension 0
- decode_out: bfloat16 [8, 32, 8192], P('groups', None, 'ctx'), parts along dimension 0
There are 2 independent parts, one for each index of `groups`. A program takes and returns all parts, laid end to end along the dimension named above; an argument that names none is the same for every part. Nothing has to cross between parts.
Inputs may be any that keep to these rules, and one draw needn't show every extreme that they name: `page_table`: within each block of 4 columns (one index of ctx) the entries of both prompts together are a permutation of 0 to 7. `sample_prompt`: every prompt has exactly 16 samples.
All inputs are finite; a program needn't handle non-finite values.
Results may differ from a plain program's by a relative error of at most 0.0075.
Values may be sent and summed in bfloat16 or wider, within the bound.
No kernel may reach another device: no remote copies, remote signals or barrier semaphores. Data moves between devices by JAX's collectives and lax.ppermute only.
A program may use at most 64 MiB of HBM per device.

v0:
```python
import math

import jax
import jax.numpy as jnp
from jax import lax
from jax.sharding import PartitionSpec as P

negative_floor = -1e30


def absorb(softmax_state, queries, key_rows, value_rows, allowed):
    running_max, running_sum, weighted = softmax_state
    scores = jnp.einsum("brd,bnd->brn", queries, key_rows, preferred_element_type=jnp.float32) * (
        1.0 / math.sqrt(queries.shape[-1])
    )
    if allowed is not None:
        scores = jnp.where(allowed, scores, negative_floor)
    new_max = jnp.maximum(running_max, jnp.max(scores, axis=-1))
    factor = jnp.exp(running_max - new_max)
    weights = jnp.exp(scores - new_max[..., None])
    running_sum = running_sum * factor + jnp.sum(weights, axis=-1)
    weighted = weighted * factor[..., None] + jnp.einsum(
        "brn,bnd->brd", weights.astype(jnp.bfloat16), value_rows, preferred_element_type=jnp.float32
    )
    return (new_max, running_sum, weighted)


def sweep(softmax_state, queries, key_rows, value_rows, block_width):
    total_keys = key_rows.shape[1]
    block_width = math.gcd(total_keys, block_width)

    def one_block(state_in, block_start):
        key_block = lax.dynamic_slice_in_dim(key_rows, block_start, block_width, 1)
        value_block = lax.dynamic_slice_in_dim(value_rows, block_start, block_width, 1)
        return (absorb(state_in, queries, key_block, value_block, None), None)

    starts = jnp.arange(total_keys // block_width, dtype=jnp.int32) * block_width
    softmax_state, unused = lax.scan(one_block, softmax_state, starts)
    return softmax_state


def empty_state(head_batch, row_count, head_depth):
    return (
        jnp.full((head_batch, row_count), negative_floor, jnp.float32),
        jnp.zeros((head_batch, row_count), jnp.float32),
        jnp.zeros((head_batch, row_count, head_depth), jnp.float32),
    )


def own_steps(softmax_state, queries_five, own_key, own_value):
    running_max, running_sum, weighted = softmax_state
    key_rows = own_key.transpose(2, 1, 0, 3)
    value_rows = own_value.transpose(2, 1, 0, 3)
    scores = jnp.einsum(
        "ktsgd,ksud->ktsgu", queries_five, key_rows, preferred_element_type=jnp.float32
    ) * (1.0 / math.sqrt(queries_five.shape[-1]))
    step_total = queries_five.shape[1]
    step_ids = jnp.arange(step_total, dtype=jnp.int32)
    allowed = (step_ids[None, :] <= step_ids[:, None])[None, :, None, None, :]
    scores = jnp.where(allowed, scores, negative_floor)
    new_max = jnp.maximum(running_max, jnp.max(scores, axis=-1))
    factor = jnp.exp(running_max - new_max)
    weights = jnp.exp(scores - new_max[..., None])
    running_sum = running_sum * factor + jnp.sum(weights, axis=-1)
    weighted = weighted * factor[..., None] + jnp.einsum(
        "ktsgu,ksud->ktsgd",
        weights.astype(jnp.bfloat16),
        value_rows,
        preferred_element_type=jnp.float32,
    )
    return (weighted / running_sum[..., None]).astype(jnp.bfloat16)


def shards(
    span_query,
    span_key,
    span_value,
    prefix_key,
    prefix_value,
    page_table,
    decode_query,
    decode_key,
    decode_value,
    sample_prompt,
    out_weight,
):
    prompts, span_dev, heads_dev, head_depth = span_query.shape
    kv_heads = span_key.shape[2]
    group_size = heads_dev // kv_heads
    steps_count = decode_query.shape[0]
    samples_dev = decode_query.shape[1]
    head_batch = prompts * kv_heads
    ctx_index = lax.axis_index("ctx")
    slot_rows = page_table.reshape(-1)
    local_keys = (
        jnp.take(prefix_key, slot_rows, axis=0)
        .reshape(prompts, -1, kv_heads, head_depth)
        .transpose(0, 2, 1, 3)
    )
    local_values = (
        jnp.take(prefix_value, slot_rows, axis=0)
        .reshape(prompts, -1, kv_heads, head_depth)
        .transpose(0, 2, 1, 3)
    )
    span_rows = (
        span_query.reshape(prompts, span_dev, kv_heads, group_size, head_depth)
        .transpose(0, 2, 1, 3, 4)
        .reshape(head_batch, span_dev * group_size, head_depth)
    )
    span_keys_all, span_values_all = (
        lax.all_gather(span_key, "ctx", axis=1, tiled=True),
        lax.all_gather(span_value, "ctx", axis=1, tiled=True),
    )
    span_total = span_keys_all.shape[1]
    span_key_rows = span_keys_all.transpose(0, 2, 1, 3).reshape(head_batch, span_total, head_depth)
    span_value_rows = span_values_all.transpose(0, 2, 1, 3).reshape(
        head_batch, span_total, head_depth
    )
    query_pos = (
        ctx_index * span_dev + jnp.arange(span_dev * group_size, dtype=jnp.int32) // group_size
    )
    causal = (jnp.arange(span_total, dtype=jnp.int32)[None, :] <= query_pos[:, None])[None]
    decode_five = decode_query.reshape(
        steps_count, samples_dev, kv_heads, group_size, head_depth
    ).transpose(2, 0, 1, 3, 4)
    prefill_state = empty_state(head_batch, span_dev * group_size, head_depth)
    prompt_keys_all, prompt_values_all = (
        lax.all_gather(local_keys, "ctx", axis=2, tiled=True),
        lax.all_gather(local_values, "ctx", axis=2, tiled=True),
    )
    prefix_len = prompt_keys_all.shape[2]
    key_rows = prompt_keys_all.reshape(head_batch, prefix_len, head_depth)
    value_rows = prompt_values_all.reshape(head_batch, prefix_len, head_depth)
    prefill_state = sweep(prefill_state, span_rows, key_rows, value_rows, 2048)
    decode_flat = decode_five.reshape(kv_heads, -1, head_depth)
    decode_batch = jnp.broadcast_to(decode_flat[None], (prompts,) + decode_flat.shape).reshape(
        head_batch, -1, head_depth
    )
    decode_state = empty_state(head_batch, decode_flat.shape[1], head_depth)
    decode_state = sweep(decode_state, decode_batch, key_rows, value_rows, 2048)
    decode_state = sweep(decode_state, decode_batch, span_key_rows, span_value_rows, span_total)
    own_prompts = lax.dynamic_slice_in_dim(sample_prompt, ctx_index * samples_dev, samples_dev)
    chosen = (
        own_prompts[None, None, None, :, None]
        == jnp.arange(prompts, dtype=jnp.int32)[:, None, None, None, None]
    )

    def select_prompt(member):
        shaped = member.reshape(
            (prompts, kv_heads, steps_count, samples_dev, group_size) + member.shape[2:]
        )
        select_mask = chosen.reshape(chosen.shape + (1,) * (shaped.ndim - 5))
        return jnp.sum(jnp.where(select_mask, shaped, 0.0), axis=0)

    decode_state = tuple((select_prompt(member) for member in decode_state))
    prefill_state = absorb(prefill_state, span_rows, span_key_rows, span_value_rows, causal)
    span_mixed = (prefill_state[2] / prefill_state[1][..., None]).astype(jnp.bfloat16)
    span_attn = (
        span_mixed.reshape(prompts, kv_heads, span_dev, group_size, head_depth)
        .transpose(0, 2, 1, 3, 4)
        .reshape(prompts * span_dev, heads_dev * head_depth)
    )
    decode_mixed = own_steps(decode_state, decode_five, decode_key, decode_value)
    decode_attn = decode_mixed.transpose(1, 2, 0, 3, 4).reshape(
        steps_count * samples_dev, heads_dev * head_depth
    )
    rows_local = jnp.concatenate([span_attn, decode_attn], axis=0)
    projected = jnp.dot(
        lax.all_gather(rows_local, "ctx", axis=0, tiled=True),
        out_weight,
        preferred_element_type=jnp.float32,
    )
    share = lax.psum_scatter(projected, "head", scatter_dimension=0, tiled=True).astype(
        jnp.bfloat16
    )
    summed = lax.all_gather(share, "head", axis=0, tiled=True)
    rows_dev = rows_local.shape[0]
    blocks_by_ctx = summed.reshape(-1, rows_dev, summed.shape[-1])
    ctx_count = blocks_by_ctx.shape[0]
    span_out = (
        blocks_by_ctx[:, : prompts * span_dev]
        .reshape(ctx_count, prompts, span_dev, -1)
        .transpose(1, 0, 2, 3)
        .reshape(prompts, ctx_count * span_dev, -1)
    )
    decode_out = (
        blocks_by_ctx[:, prompts * span_dev :]
        .reshape(ctx_count, steps_count, samples_dev, -1)
        .transpose(1, 0, 2, 3)
        .reshape(steps_count, ctx_count * samples_dev, -1)
    )
    return (span_out, decode_out)


def solution(mesh):
    return jax.shard_map(
        shards,
        mesh=mesh,
        in_specs=(
            P("groups", "ctx", "head", None),
            P("groups", "ctx", "head", None),
            P("groups", "ctx", "head", None),
            P(("groups", "ctx"), None, "head", None),
            P(("groups", "ctx"), None, "head", None),
            P("groups", "ctx"),
            P("groups", "ctx", "head", None),
            P("groups", "ctx", "head", None),
            P("groups", "ctx", "head", None),
            P("groups"),
            P("head", "ctx"),
        ),
        out_specs=(P("groups", None, "ctx"), P("groups", None, "ctx")),
        check_vma=False,
    )
```

profile of v0, /device:TPU:0, one launch (start us, length us, event | category | flops | bytes accessed | tf_op | source)
XLA Modules:
  0.0 230.2 jit_solution(950019936043663763)
XLA Ops:
  8.3 1.6 gather_fusion
  9.9 2.6 %gather_fusion.1 = bf16[8,128,2,128]{3,2,1,0:T(2,128)(2,1)S(1)} fusion(bf16[8,128,2,128]{3,2,1,0:T(2,128)(2,1)} %param.17, s32[1024]{0:T(1024)S(1)} %pad_clamp_fusion), kind=kCustom, calls=%fused_computation.1.clone | custom fusion | bytes 1048608 | tf_op jit(solution)/shard_map/jit(_take)/gather | solution.py:101
  15.5 6.7 %all_gather.20 = bf16[2,128,2,128]{3,2,1,0:T(2,128)(2,1)S(1)} all-gather(bf16[2,32,2,128]{3,2,1,0:T(2,128)(2,1)} %param.14), channel_id=1, replica_groups=mesh['groups'=2,'ctx'=4,'head'=4] {'ctx'}, dimensions={1}, use_global_device_ids=true | all-gather | bytes 163840 | tf_op jit(solution)/shard_map/all_gather | solution.py:111
  23.4 6.2 %all_gather.21 = bf16[2,128,2,128]{3,2,1,0:T(2,128)(2,1)S(1)} all-gather(bf16[2,32,2,128]{3,2,1,0:T(2,128)(2,1)S(1)} %copy-done.9), channel_id=1, replica_groups=mesh['groups'=2,'ctx'=4,'head'=4] {'ctx'}, dimensions={1}, use_global_device_ids=true | all-gather | bytes 163840 | tf_op jit(solution)/shard_map/all_gather | solution.py:112
  31.1 2.0 fusion.57
  33.3 7.3 %all-gather.5.cloned.1.call-done = bf16[2,2,2048,128]{3,2,1,0:T(8,128)(2,1)} async-done(((bf16[2,2,512,128]{3,2,1,0:T(8,128)(2,1)}), bf16[2,2,2048,128]{3,2,1,0:T(8,128)(2,1)}) %all-gather.5.cloned.1.call-update) | async-done | bytes 2097168 | tf_op jit(solution)/shard_map/all_gather | solution.py:128
  40.6 2.9 %bitcast_reduce_fusion.1 = (f32[4,256]{1,0:T(4,128)S(1)}, f32[4,2048,256]{2,1,0:T(8,128)S(1)}) fusion(bf16[4,2048,128]{2,1,0:T(8,128)(2,1)} %bitcast.123, bf16[4,256,128]{2,1,0:T(8,128)(2,1)S(1)} %bitcast.131), kind=kOutput, calls=%fused_computation.6 | convolution fusion | flops 541064192 | bytes 10752000 | tf_op jit(solution)/shard_map/while/body/eval_jaxpr/brd,bnd->brn/dot_general | solution.py:13
  43.6 3.4 %copy-done.1 = f32[4,2048,256]{2,1,0:T(8,128)} copy-done((f32[4,2048,256]{2,1,0:T(8,128)}, f32[4,2048,256]{2,1,0:T(8,128)S(1)}, u32[]{:S(2)}) %copy-start.1) | copy-done | bytes 8388632
  47.0 1.4 fusion.2
  49.0 5.1 %bitcast_reduce_fusion = (f32[4,256]{1,0:T(4,128)}, f32[4,2048,256]{2,1,0:T(8,128)}) fusion(bf16[4,2048,128]{2,1,0:T(8,128)(2,1)S(1)} %bitcast.124, bf16[4,256,128]{2,1,0:T(8,128)(2,1)S(1)} %bitcast.129), kind=kOutput, calls=%fused_computation.3 | convolution fusion | flops 541064192 | bytes 10752000 | tf_op jit(solution)/shard_map/while/body/eval_jaxpr/brd,bnd->brn/dot_general | solution.py:13
  54.1 11.3 %all-gather.7.cloned.1.call-done = bf16[2,2,2048,128]{3,2,1,0:T(8,128)(2,1)} async-done(((bf16[2,2,512,128]{3,2,1,0:T(8,128)(2,1)}), bf16[2,2,2048,128]{3,2,1,0:T(8,128)(2,1)}) %all-gather.7.cloned.1.call-update) | async-done | bytes 2097168 | tf_op jit(solution)/shard_map/all_gather | solution.py:129
  65.4 5.2 %fusion.25 = f32[4,256,128]{2,1,0:T(8,128)S(1)} fusion(bf16[4,2048,128]{2,1,0:T(8,128)(2,1)} %bitcast.125, f32[4,2048,256]{2,1,0:T(8,128)} %copy-done.1, f32[4,256]{1,0:T(4,128)S(1)} %get-tuple-element.62, f32[4,256]{1,0:T(4,128)S(1)} %get-tuple-element.48, f32[4,256]{1,0:T(4,128)S(1)} %get-tuple-element.60), kind=kOutput, calls=%fused_computation.27 | convolution fusion | flops 543424512 | bytes 11022336 | tf_op jit(solution)/shard_map/while/body/eval_jaxpr/brn,bnd->brd/dot_general | solution.py:22
  71.7 1.1 reshape.239
  72.8 1.3 fusion.54
  74.8 4.8 %fusion.4 = f32[4,256]{1,0:T(4,128)S(1)} fusion(f32[4,2048,256]{2,1,0:T(8,128)} %get-tuple-element.84, f32[4,256]{1,0:T(4,128)S(1)} %get-tuple-element.71), kind=kLoop, calls=%fused_computation.10 | loop fusion | flops 6290432 | bytes 8396800 | tf_op jit(solution)/shard_map/while/body/eval_jaxpr/reduce_sum | solution.py:21
  81.1 1.1 select_reduce_fusion.1
  84.8 4.6 %fusion.22 = f32[4,256,128]{2,1,0:T(8,128)S(1)} fusion(bf16[4,2048,128]{2,1,0:T(8,128)(2,1)S(1)} %bitcast.126, f32[4,2048,256]{2,1,0:T(8,128)} %get-tuple-element.84, f32[4,256]{1,0:T(4,128)S(1)} %get-tuple-element.71, f32[4,256]{1,0:T(4,128)S(1)} %get-tuple-element.59, f32[4,256]{1,0:T(4,128)} %get-tuple-element.70), kind=kOutput, calls=%fused_computation.26 | convolution fusion | flops 543424512 | bytes 11022336 | tf_op jit(solution)/shard_map/while/body/eval_jaxpr/brn,bnd->brd/dot_general | solution.py:22
  91.3 19.5 %all-gather.9.cloned.1.call-done = bf16[384,2048]{1,0:T(8,128)(2,1)} async-done(((bf16[96,2048]{1,0:T(8,128)(2,1)}), bf16[384,2048]{1,0:T(8,128)(2,1)}) %all-gather.9.cloned.1.call-update) | async-done | bytes 1572880 | tf_op jit(solution)/shard_map/all_gather | solution.py:169
  110.8 8.9 %fusion.59 = f32[384,2048]{1,0:T(8,128)} fusion(bf16[384,2048]{1,0:T(8,128)(2,1)} %all-gather.9.cloned.1.call-done, bf16[2048,2048]{1,0:T(8,128)(2,1)} %param.23), kind=kOutput, calls=%fused_computation.93 | convolution fusion | flops 3221225472 | bytes 13107200 | tf_op jit(solution)/shard_map/dot_general | solution.py:168
  119.8 60.4 %reduce-scatter.2.cloned.1.call-done = f32[96,2048]{1,0:T(8,128)} async-done(((f32[384,2048]{1,0:T(8,128)}), f32[96,2048]{1,0:T(8,128)}) %reduce-scatter.2.cloned.1.call-update) | async-done | bytes 786448 | tf_op jit(solution)/shard_map/reduce_scatter | solution.py:173
  180.2 1.9 convert_element_type.35
  182.1 37.3 %all-gather.11.cloned.1.call-done = bf16[384,2048]{1,0:T(8,128)(2,1)} async-done(((bf16[96,2048]{1,0:T(8,128)(2,1)}), bf16[384,2048]{1,0:T(8,128)(2,1)}) %all-gather.11.cloned.1.call-update) | async-done | bytes 1572880 | tf_op jit(solution)/shard_map/all_gather | solution.py:176
  219.4 1.3 slice.12
  220.7 1.9 copy_bitcast_fusion
  (81 shorter events, 16.4 us)
Async XLA Ops:
  7.2 1.2 copy-start
  7.2 23.9 %copy-start.8 = (bf16[4,8,16,128]{3,2,1,0:T(8,128)(2,1)S(1)}, bf16[4,8,16,128]{3,2,1,0:T(8,128)(2,1)}, u32[]{:S(2)}) copy-start(bf16[4,8,16,128]{3,2,1,0:T(8,128)(2,1)} %param.19) | copy-start | bytes 393220
  7.2 16.2 %copy-start.9 = (bf16[2,32,2,128]{3,2,1,0:T(2,128)(2,1)S(1)}, bf16[2,32,2,128]{3,2,1,0:T(2,128)(2,1)}, u32[]{:S(2)}) copy-start(bf16[2,32,2,128]{3,2,1,0:T(2,128)(2,1)} %param.15) | copy-start | bytes 98308
  7.2 22.5 %copy-start.6 = (bf16[2,32,16,128]{3,2,1,0:T(8,128)(2,1)S(1)}, bf16[2,32,16,128]{3,2,1,0:T(8,128)(2,1)}, u32[]{:S(2)}) copy-start(bf16[2,32,16,128]{3,2,1,0:T(8,128)(2,1)} %param.13) | copy-start | bytes 786436
  7.2 23.3 %copy-start.14 = (s32[32]{0:T(128)S(1)}, s32[32]{0:T(128)}, u32[]{:S(2)}) copy-start(s32[32]{0:T(128)} %param.22) | copy-start | bytes 388
  7.2 23.9 %copy-start.12 = (bf16[4,8,2,128]{3,2,1,0:T(2,128)(2,1)S(1)}, bf16[4,8,2,128]{3,2,1,0:T(2,128)(2,1)}, u32[]{:S(2)}) copy-start(bf16[4,8,2,128]{3,2,1,0:T(2,128)(2,1)} %param.20) | copy-start | bytes 49156
  7.2 33.4 %all-gather.5.cloned.1.call-start = ((), (), s32[]{:S(2)}) async-start(), calls=%async_computation.1 | async-start | bytes 2621440 | tf_op jit(solution)/shard_map/all_gather | solution.py:128
  14.5 50.9 %all-gather.7.cloned.1.call-start = ((), (), s32[]{:S(2)}) async-start(), calls=%async_computation.2 | async-start | bytes 2621440 | tf_op jit(solution)/shard_map/all_gather | solution.py:129
  15.4 95.4 %all-gather.9.cloned.1.call-start = ((), (), s32[]{:S(2)}) async-start(), calls=%async_computation.3 | async-start | bytes 1966080 | tf_op jit(solution)/shard_map/all_gather | solution.py:169
  33.3 15.1 %copy-start.4 = (f32[4,256,128]{1,2,0:T(8,128)}, f32[4,256,128]{1,2,0:T(8,128)S(1)}, u32[]{:S(2)}) copy-start(f32[4,256,128]{1,2,0:T(8,128)S(1)} %get-tuple-element.90) | copy-start | bytes 1572868
  43.5 3.5 %copy-start.1 = (f32[4,2048,256]{2,1,0:T(8,128)}, f32[4,2048,256]{2,1,0:T(8,128)S(1)}, u32[]{:S(2)}) copy-start(f32[4,2048,256]{2,1,0:T(8,128)S(1)} %get-tuple-element.88) | copy-start | bytes 25165828
  43.5 5.5 %copy-start.2 = (bf16[2,2,2048,128]{3,2,1,0:T(8,128)(2,1)S(1)}, bf16[2,2,2048,128]{3,2,1,0:T(8,128)(2,1)}, u32[]{:S(2)}) copy-start(bf16[2,2,2048,128]{3,2,1,0:T(8,128)(2,1)} %all-gather.5.cloned.1.call-done) | copy-start | bytes 6291460
  54.1 16.6 %copy-start.10 = (f32[4,256]{1,0:T(4,128)S(1)}, f32[4,256]{1,0:T(4,128)}, u32[]{:S(2)}) copy-start(f32[4,256]{1,0:T(4,128)} %get-tuple-element.47) | copy-start | bytes 12292
  65.4 5.3 %copy-start.5 = (f32[4,256,128]{1,2,0:T(8,128)S(1)}, f32[4,256,128]{1,2,0:T(8,128)}, u32[]{:S(2)}) copy-start(f32[4,256,128]{1,2,0:T(8,128)} %copy-done.4) | copy-start | bytes 1572868
  70.6 14.2 %copy-start.3 = (bf16[2,2,2048,128]{3,2,1,0:T(8,128)(2,1)S(1)}, bf16[2,2,2048,128]{3,2,1,0:T(8,128)(2,1)}, u32[]{:S(2)}) copy-start(bf16[2,2,2048,128]{3,2,1,0:T(8,128)(2,1)} %all-gather.7.cloned.1.call-done) | copy-start | bytes 6291460
  81.1 8.6 %copy-start.11 = (pred[2,8]{1,0:T(4,128)(4,1)S(1)}, pred[2,8]{1,0:T(4,128)(4,1)}, u32[]{:S(2)}) copy-start(pred[2,8]{1,0:T(4,128)(4,1)} %iota_compare_fusion.2) | copy-start | bytes 52
  81.1 8.7 %copy-start.7 = (f32[2,4,8,8,4]{3,4,1,2,0:T(4,128)S(1)}, f32[2,4,8,8,4]{3,4,1,2,0:T(4,128)}, u32[]{:S(2)}) copy-start(f32[2,4,8,8,4]{3,4,1,2,0:T(4,128)} %get-tuple-element.86) | copy-start | bytes 24580
  81.1 8.7 %copy-start.13 = (bf16[4,8,2,128]{3,2,1,0:T(2,128)(2,1)S(1)}, bf16[4,8,2,128]{3,2,1,0:T(2,128)(2,1)}, u32[]{:S(2)}) copy-start(bf16[4,8,2,128]{3,2,1,0:T(2,128)(2,1)} %param.21) | copy-start | bytes 49156
  91.0 89.2 %reduce-scatter.2.cloned.1.call-start = ((), (), s32[]{:S(2)}) async-start(), calls=%async_computation.4 | async-start | bytes 3932160 | tf_op jit(solution)/shard_map/reduce_scatter | solution.py:173
  119.8 99.6 %all-gather.11.cloned.1.call-start = ((), (), s32[]{:S(2)}) async-start(), calls=%async_computation.5 | async-start | bytes 1966080 | tf_op jit(solution)/shard_map/all_gather | solution.py:176
Sparse Core Ops, SparseCore 0:
  14.6 25.9 all-gather.4
  42.7 22.5 all-gather.6
  91.1 19.6 all-gather.8
  119.9 60.2 reduce-scatter.1
  182.2 37.1 all-gather.10
where the time goes:
time: 231 us; the launch traced here: 230 us
  waiting for transfers between devices  136 us (59%)
  matrix products  30 us (13%)
  local copies, waits for them, and re-layouts  20.6 us (9%)
  other arithmetic  16.2 us (7%)
  between operations  14.1 us (6%)
  blocking collectives  12.9 us (6%)
    reduce_scatter x1, waiting for transfers between devices, shards(): lax.psum_scatter(projected, 'head', scatter_dimension=0, tiled=True)  60.4 us
    all_gather x1, waiting for transfers between devices, shards(): summed = lax.all_gather(share, 'head', axis=0, tiled=True)  37.3 us
    all_gather x1, waiting for transfers between devices, shards(): lax.all_gather(rows_local, 'ctx', axis=0, tiled=True)  19.5 us
    all_gather x1, waiting for transfers between devices, shards(): lax.all_gather(local_values, 'ctx', axis=2, tiled=True)  11.3 us
    dot_general x4, matrix products, absorb(): jnp.einsum('brn,bnd->brd', weights.astype(jnp.bfloat16), value_rows, pref...  10.4 us
    dot_general x1, matrix products, shards(): jnp.dot(lax.all_gather(rows_local, 'ctx', axis=0, tiled=True), out_weight...  8.94 us
    dot_general x4, matrix products, absorb(): jnp.einsum('brd,bnd->brn', queries, key_rows, preferred_element_type=jnp....  8.4 us
    all_gather x1, waiting for transfers between devices, shards(): lax.all_gather(local_keys, 'ctx', axis=2, tiled=True)  7.31 us
  transfers between devices with their start and end apart: 5, of which 5 were waited for; matrix products, arithmetic and copies ran while one was open for 7% of the time, Pallas kernels for 0%

commit v1 on v0

--- a/solution.py
+++ b/solution.py
@@ -170,8 +170,8 @@
         out_weight,
         preferred_element_type=jnp.float32,
     )
-    share = lax.psum_scatter(projected, "head", scatter_dimension=0, tiled=True).astype(
-        jnp.bfloat16
+    share = lax.psum_scatter(
+        projected.astype(jnp.bfloat16), "head", scatter_dimension=0, tiled=True
     )
     summed = lax.all_gather(share, "head", axis=0, tiled=True)
     rows_dev = rows_local.shape[0]

time: 231 us -> 204 us (0.88)
  waiting for transfers between devices: 136 us -> 112 us
  other arithmetic: 16.2 us -> 13.7 us
    reduce_scatter x1, waiting for transfers between devices: 60.4 us -> 35.4 us  [shards(): lax.psum_scatter(projected.astype(jnp.bfloat16), 'head', scatter_dimensio...]
where the time goes in v1:
time: 204 us; the launch traced here: 203 us
  waiting for transfers between devices  112 us (55%)
  matrix products  29.5 us (14%)
  local copies, waits for them, and re-layouts  20.6 us (10%)
  between operations  14.1 us (7%)
  other arithmetic  13.7 us (7%)
  blocking collectives  12.9 us (6%)
    all_gather x1, waiting for transfers between devices, shards(): summed = lax.all_gather(share, 'head', axis=0, tiled=True)  37.5 us
    reduce_scatter x1, waiting for transfers between devices, shards(): lax.psum_scatter(projected.astype(jnp.bfloat16), 'head', scatter_dimensio...  35.4 us
    all_gather x1, waiting for transfers between devices, shards(): lax.all_gather(rows_local, 'ctx', axis=0, tiled=True)  19.5 us
    all_gather x1, waiting for transfers between devices, shards(): lax.all_gather(local_values, 'ctx', axis=2, tiled=True)  11.9 us
    dot_general x4, matrix products, absorb(): jnp.einsum('brn,bnd->brd', weights.astype(jnp.bfloat16), value_rows, pref...  10.4 us
    dot_general x1, matrix products, shards(): jnp.dot(lax.all_gather(rows_local, 'ctx', axis=0, tiled=True), out_weight...  8.43 us
    dot_general x4, matrix products, absorb(): jnp.einsum('brd,bnd->brn', queries, key_rows, preferred_element_type=jnp....  8.4 us
    all_gather x1, waiting for transfers between devices, shards(): lax.all_gather(local_keys, 'ctx', axis=2, tiled=True)  7.27 us
  transfers between devices with their start and end apart: 5, of which 5 were waited for; matrix products, arithmetic and copies ran while one was open for 7% of the time, Pallas kernels for 0%

profile of v1, /device:TPU:0, one launch (start us, length us, event | category | flops | bytes accessed | tf_op | source)
XLA Modules:
  0.0 203.0 jit_solution(14247377753341367889)
XLA Ops:
  8.3 1.6 gather_fusion
  9.9 2.6 %gather_fusion.1 = bf16[8,128,2,128]{3,2,1,0:T(2,128)(2,1)S(1)} fusion(bf16[8,128,2,128]{3,2,1,0:T(2,128)(2,1)} %param.17, s32[1024]{0:T(1024)S(1)} %pad_clamp_fusion), kind=kCustom, calls=%fused_computation.1.clone | custom fusion | bytes 1048608 | tf_op jit(solution)/shard_map/jit(_take)/gather | solution.py:101
  15.5 6.7 %all_gather.20 = bf16[2,128,2,128]{3,2,1,0:T(2,128)(2,1)S(1)} all-gather(bf16[2,32,2,128]{3,2,1,0:T(2,128)(2,1)} %param.14), channel_id=1, replica_groups=mesh['groups'=2,'ctx'=4,'head'=4] {'ctx'}, dimensions={1}, use_global_device_ids=true | all-gather | bytes 163840 | tf_op jit(solution)/shard_map/all_gather | solution.py:111
  23.4 6.2 %all_gather.21 = bf16[2,128,2,128]{3,2,1,0:T(2,128)(2,1)S(1)} all-gather(bf16[2,32,2,128]{3,2,1,0:T(2,128)(2,1)S(1)} %copy-done.9), channel_id=1, replica_groups=mesh['groups'=2,'ctx'=4,'head'=4] {'ctx'}, dimensions={1}, use_global_device_ids=true | all-gather | bytes 163840 | tf_op jit(solution)/shard_map/all_gather | solution.py:112
  31.1 2.0 fusion.57
  33.3 7.3 %all-gather.5.cloned.1.call-done = bf16[2,2,2048,128]{3,2,1,0:T(8,128)(2,1)} async-done(((bf16[2,2,512,128]{3,2,1,0:T(8,128)(2,1)}), bf16[2,2,2048,128]{3,2,1,0:T(8,128)(2,1)}) %all-gather.5.cloned.1.call-update) | async-done | bytes 2097168 | tf_op jit(solution)/shard_map/all_gather | solution.py:128
  40.6 2.9 %bitcast_reduce_fusion.1 = (f32[4,256]{1,0:T(4,128)S(1)}, f32[4,2048,256]{2,1,0:T(8,128)S(1)}) fusion(bf16[4,2048,128]{2,1,0:T(8,128)(2,1)} %bitcast.123, bf16[4,256,128]{2,1,0:T(8,128)(2,1)S(1)} %bitcast.131), kind=kOutput, calls=%fused_computation.6 | convolution fusion | flops 541064192 | bytes 10752000 | tf_op jit(solution)/shard_map/while/body/eval_jaxpr/brd,bnd->brn/dot_general | solution.py:13
  43.6 3.4 %copy-done.1 = f32[4,2048,256]{2,1,0:T(8,128)} copy-done((f32[4,2048,256]{2,1,0:T(8,128)}, f32[4,2048,256]{2,1,0:T(8,128)S(1)}, u32[]{:S(2)}) %copy-start.1) | copy-done | bytes 8388632
  47.0 1.4 fusion.2
  48.4 5.1 %bitcast_reduce_fusion = (f32[4,256]{1,0:T(4,128)}, f32[4,2048,256]{2,1,0:T(8,128)}) fusion(bf16[4,2048,128]{2,1,0:T(8,128)(2,1)S(1)} %bitcast.124, bf16[4,256,128]{2,1,0:T(8,128)(2,1)S(1)} %bitcast.129), kind=kOutput, calls=%fused_computation.3 | convolution fusion | flops 541064192 | bytes 10752000 | tf_op jit(solution)/shard_map/while/body/eval_jaxpr/brd,bnd->brn/dot_general | solution.py:13
  53.5 11.9 %all-gather.7.cloned.1.call-done = bf16[2,2,2048,128]{3,2,1,0:T(8,128)(2,1)} async-done(((bf16[2,2,512,128]{3,2,1,0:T(8,128)(2,1)}), bf16[2,2,2048,128]{3,2,1,0:T(8,128)(2,1)}) %all-gather.7.cloned.1.call-update) | async-done | bytes 2097168 | tf_op jit(solution)/shard_map/all_gather | solution.py:129
  65.4 5.2 %fusion.25 = f32[4,256,128]{2,1,0:T(8,128)S(1)} fusion(bf16[4,2048,128]{2,1,0:T(8,128)(2,1)} %bitcast.125, f32[4,2048,256]{2,1,0:T(8,128)} %copy-done.1, f32[4,256]{1,0:T(4,128)S(1)} %get-tuple-element.62, f32[4,256]{1,0:T(4,128)S(1)} %get-tuple-element.48, f32[4,256]{1,0:T(4,128)S(1)} %get-tuple-element.60), kind=kOutput, calls=%fused_computation.28 | convolution fusion | flops 543424512 | bytes 11022336 | tf_op jit(solution)/shard_map/while/body/eval_jaxpr/brn,bnd->brd/dot_general | solution.py:22
  71.7 1.1 reshape.239
  72.8 1.3 fusion.54
  74.8 4.8 %fusion.4 = f32[4,256]{1,0:T(4,128)S(1)} fusion(f32[4,2048,256]{2,1,0:T(8,128)} %get-tuple-element.84, f32[4,256]{1,0:T(4,128)S(1)} %get-tuple-element.71), kind=kLoop, calls=%fused_computation.10 | loop fusion | flops 6290432 | bytes 8396800 | tf_op jit(solution)/shard_map/while/body/eval_jaxpr/reduce_sum | solution.py:21
  81.1 1.1 select_reduce_fusion.1
  84.8 4.6 %fusion.22 = f32[4,256,128]{2,1,0:T(8,128)S(1)} fusion(bf16[4,2048,128]{2,1,0:T(8,128)(2,1)S(1)} %bitcast.126, f32[4,2048,256]{2,1,0:T(8,128)} %get-tuple-element.84, f32[4,256]{1,0:T(4,128)S(1)} %get-tuple-element.71, f32[4,256]{1,0:T(4,128)S(1)} %get-tuple-element.59, f32[4,256]{1,0:T(4,128)} %get-tuple-element.70), kind=kOutput, calls=%fused_computation.27 | convolution fusion | flops 543424512 | bytes 11022336 | tf_op jit(solution)/shard_map/while/body/eval_jaxpr/brn,bnd->brd/dot_general | solution.py:22
  91.2 19.5 %all-gather.9.cloned.1.call-done = bf16[384,2048]{1,0:T(8,128)(2,1)} async-done(((bf16[96,2048]{1,0:T(8,128)(2,1)}), bf16[384,2048]{1,0:T(8,128)(2,1)}) %all-gather.9.cloned.1.call-update) | async-done | bytes 1572880 | tf_op jit(solution)/shard_map/all_gather | solution.py:169
  110.8 8.4 %convolution_convert_fusion = bf16[384,2048]{1,0:T(8,128)(2,1)} fusion(bf16[384,2048]{1,0:T(8,128)(2,1)} %all-gather.9.cloned.1.call-done, bf16[2048,2048]{1,0:T(8,128)(2,1)} %param.23), kind=kOutput, calls=%fused_computation.18 | convolution fusion | flops 3222011904 | bytes 11534336 | tf_op jit(solution)/shard_map/dot_general | solution.py:168
  119.3 35.4 %reduce-scatter.2.cloned.1.call-done = bf16[96,2048]{1,0:T(8,128)(2,1)} async-done(((bf16[384,2048]{1,0:T(8,128)(2,1)}), bf16[96,2048]{1,0:T(8,128)(2,1)}) %reduce-scatter.2.cloned.1.call-update) | async-done | bytes 393232 | tf_op jit(solution)/shard_map/reduce_scatter | solution.py:173
  154.7 37.5 %all-gather.11.cloned.1.call-done = bf16[384,2048]{1,0:T(8,128)(2,1)} async-done(((bf16[96,2048]{1,0:T(8,128)(2,1)}), bf16[384,2048]{1,0:T(8,128)(2,1)}) %all-gather.11.cloned.1.call-update) | async-done | bytes 1572880 | tf_op jit(solution)/shard_map/all_gather | solution.py:176
  192.2 1.3 slice.12
  193.5 1.9 copy_bitcast_fusion
  195.4 1.0 copy.103
  (78 shorter events, 14.8 us)
Async XLA Ops:
  7.2 1.2 copy-start
  7.2 23.9 %copy-start.8 = (bf16[4,8,16,128]{3,2,1,0:T(8,128)(2,1)S(1)}, bf16[4,8,16,128]{3,2,1,0:T(8,128)(2,1)}, u32[]{:S(2)}) copy-start(bf16[4,8,16,128]{3,2,1,0:T(8,128)(2,1)} %param.19) | copy-start | bytes 393220
  7.2 16.2 %copy-start.9 = (bf16[2,32,2,128]{3,2,1,0:T(2,128)(2,1)S(1)}, bf16[2,32,2,128]{3,2,1,0:T(2,128)(2,1)}, u32[]{:S(2)}) copy-start(bf16[2,32,2,128]{3,2,1,0:T(2,128)(2,1)} %param.15) | copy-start | bytes 98308
  7.2 22.5 %copy-start.6 = (bf16[2,32,16,128]{3,2,1,0:T(8,128)(2,1)S(1)}, bf16[2,32,16,128]{3,2,1,0:T(8,128)(2,1)}, u32[]{:S(2)}) copy-start(bf16[2,32,16,128]{3,2,1,0:T(8,128)(2,1)} %param.13) | copy-start | bytes 786436
  7.2 23.3 %copy-start.13 = (s32[32]{0:T(128)S(1)}, s32[32]{0:T(128)}, u32[]{:S(2)}) copy-start(s32[32]{0:T(128)} %param.22) | copy-start | bytes 388
  7.2 23.9 %copy-start.11 = (bf16[4,8,2,128]{3,2,1,0:T(2,128)(2,1)S(1)}, bf16[4,8,2,128]{3,2,1,0:T(2,128)(2,1)}, u32[]{:S(2)}) copy-start(bf16[4,8,2,128]{3,2,1,0:T(2,128)(2,1)} %param.20) | copy-start | bytes 49156
  7.2 33.4 %all-gather.5.cloned.1.call-start = ((), (), s32[]{:S(2)}) async-start(), calls=%async_computation.1 | async-start | bytes 2621440 | tf_op jit(solution)/shard_map/all_gather | solution.py:128
  14.5 50.9 %all-gather.7.cloned.1.call-start = ((), (), s32[]{:S(2)}) async-start(), calls=%async_computation.2 | async-start | bytes 2621440 | tf_op jit(solution)/shard_map/all_gather | solution.py:129
  15.4 95.4 %all-gather.9.cloned.1.call-start = ((), (), s32[]{:S(2)}) async-start(), calls=%async_computation.3 | async-start | bytes 1966080 | tf_op jit(solution)/shard_map/all_gather | solution.py:169
  33.3 15.1 %copy-start.4 = (f32[4,256,128]{1,2,0:T(8,128)}, f32[4,256,128]{1,2,0:T(8,128)S(1)}, u32[]{:S(2)}) copy-start(f32[4,256,128]{1,2,0:T(8,128)S(1)} %get-tuple-element.90) | copy-start | bytes 1572868
  43.5 3.5 %copy-start.1 = (f32[4,2048,256]{2,1,0:T(8,128)}, f32[4,2048,256]{2,1,0:T(8,128)S(1)}, u32[]{:S(2)}) copy-start(f32[4,2048,256]{2,1,0:T(8,128)S(1)} %get-tuple-element.88) | copy-start | bytes 25165828
  43.5 4.9 %copy-start.2 = (bf16[2,2,2048,128]{3,2,1,0:T(8,128)(2,1)S(1)}, bf16[2,2,2048,128]{3,2,1,0:T(8,128)(2,1)}, u32[]{:S(2)}) copy-start(bf16[2,2,2048,128]{3,2,1,0:T(8,128)(2,1)} %all-gather.5.cloned.1.call-done) | copy-start | bytes 6291460
  65.4 5.2 %copy-start.5 = (f32[4,256,128]{1,2,0:T(8,128)S(1)}, f32[4,256,128]{1,2,0:T(8,128)}, u32[]{:S(2)}) copy-start(f32[4,256,128]{1,2,0:T(8,128)} %copy-done.4) | copy-start | bytes 1572868
  70.6 14.2 %copy-start.3 = (bf16[2,2,2048,128]{3,2,1,0:T(8,128)(2,1)S(1)}, bf16[2,2,2048,128]{3,2,1,0:T(8,128)(2,1)}, u32[]{:S(2)}) copy-start(bf16[2,2,2048,128]{3,2,1,0:T(8,128)(2,1)} %all-gather.7.cloned.1.call-done) | copy-start | bytes 6291460
  81.1 8.6 %copy-start.10 = (pred[2,8]{1,0:T(4,128)(4,1)S(1)}, pred[2,8]{1,0:T(4,128)(4,1)}, u32[]{:S(2)}) copy-start(pred[2,8]{1,0:T(4,128)(4,1)} %iota_compare_fusion.2) | copy-start | bytes 52
  81.1 8.7 %copy-start.7 = (f32[2,4,8,8,4]{3,4,1,2,0:T(4,128)S(1)}, f32[2,4,8,8,4]{3,4,1,2,0:T(4,128)}, u32[]{:S(2)}) copy-start(f32[2,4,8,8,4]{3,4,1,2,0:T(4,128)} %get-tuple-element.86) | copy-start | bytes 24580
  81.1 8.7 %copy-start.12 = (bf16[4,8,2,128]{3,2,1,0:T(2,128)(2,1)S(1)}, bf16[4,8,2,128]{3,2,1,0:T(2,128)(2,1)}, u32[]{:S(2)}) copy-start(bf16[4,8,2,128]{3,2,1,0:T(2,128)(2,1)} %param.21) | copy-start | bytes 49156
  91.0 63.7 %reduce-scatter.2.cloned.1.call-start = ((), (), s32[]{:S(2)}) async-start(), calls=%async_computation.4 | async-start | bytes 1966080 | tf_op jit(solution)/shard_map/reduce_scatter | solution.py:173
  119.2 73.0 %all-gather.11.cloned.1.call-start = ((), (), s32[]{:S(2)}) async-start(), calls=%async_computation.5 | async-start | bytes 1966080 | tf_op jit(solution)/shard_map/all_gather | solution.py:176
Sparse Core Ops, SparseCore 0:
  14.6 25.9 all-gather.4
  42.7 22.5 all-gather.6
  91.1 19.6 all-gather.8
  119.4 35.2 reduce-scatter.1
  156.1 36.0 all-gather.10

commit v2 on v1

--- a/solution.py
+++ b/solution.py
@@ -69,6 +69,28 @@
         preferred_element_type=jnp.float32,
     )
     return (weighted / running_sum[..., None]).astype(jnp.bfloat16)
+
+
+def ctx_shards(block, ctx_count):
+    chips = ctx_count // 2
+    received = [block]
+    for shift in range(1, chips):
+        pairs = [(dev, (dev - 2 * shift) % ctx_count) for dev in range(ctx_count)]
+        received.append(lax.ppermute(block, "ctx", pairs))
+    along_x = jnp.stack(received)
+    other_core = lax.ppermute(along_x, "ctx", [(dev, dev ^ 1) for dev in range(ctx_count)])
+    return along_x, other_core
+
+
+def ctx_gather(block, ctx_count):
+    ctx_index = lax.axis_index("ctx")
+    chip, core = ctx_index // 2, ctx_index % 2
+    along_x, other_core = ctx_shards(block, ctx_count)
+    along_x = jnp.roll(along_x, chip, axis=0)
+    other_core = jnp.roll(other_core, chip, axis=0)
+    core_zero = jnp.where(core == 0, along_x, other_core)
+    core_one = jnp.where(core == 0, other_core, along_x)
+    return jnp.stack([core_zero, core_one], axis=1).reshape((ctx_count,) + block.shape)
 
 
 def shards(
@@ -107,9 +129,13 @@
         .transpose(0, 2, 1, 3, 4)
         .reshape(head_batch, span_dev * group_size, head_depth)
     )
+    ctx_count = sample_prompt.shape[0] // samples_dev
+    span_pair = ctx_gather(jnp.stack([span_key, span_value]), ctx_count)
     span_keys_all, span_values_all = (
-        lax.all_gather(span_key, "ctx", axis=1, tiled=True),
-        lax.all_gather(span_value, "ctx", axis=1, tiled=True),
+        span_pair[:, member].transpose(1, 0, 2, 3, 4).reshape(
+            (prompts, ctx_count * span_dev) + span_key.shape[2:]
+        )
+        for member in range(2)
     )
     span_total = span_keys_all.shape[1]
     span_key_rows = span_keys_all.transpose(0, 2, 1, 3).reshape(head_batch, span_total, head_depth)
@@ -124,9 +150,11 @@
         steps_count, samples_dev, kv_heads, group_size, head_depth
     ).transpose(2, 0, 1, 3, 4)
     prefill_state = empty_state(head_batch, span_dev * group_size, head_depth)
+    along_x, other_core = ctx_shards(jnp.stack([local_keys, local_values]), ctx_count)
+    arrived = jnp.concatenate([along_x, other_core], axis=0)
     prompt_keys_all, prompt_values_all = (
-        lax.all_gather(local_keys, "ctx", axis=2, tiled=True),
-        lax.all_gather(local_values, "ctx", axis=2, tiled=True),
+        jnp.concatenate([arrived[shard, member] for shard in range(ctx_count)], axis=2)
+        for member in range(2)
     )
     prefix_len = prompt_keys_all.shape[2]
     key_rows = prompt_keys_all.reshape(head_batch, prefix_len, head_depth)
@@ -166,7 +194,7 @@
     )
     rows_local = jnp.concatenate([span_attn, decode_attn], axis=0)
     projected = jnp.dot(
-        lax.all_gather(rows_local, "ctx", axis=0, tiled=True),
+        ctx_gather(rows_local, ctx_count).reshape(-1, rows_local.shape[-1]),
         out_weight,
         preferred_element_type=jnp.float32,
     )
@@ -176,7 +204,6 @@
     summed = lax.all_gather(share, "head", axis=0, tiled=True)
     rows_dev = rows_local.shape[0]
     blocks_by_ctx = summed.reshape(-1, rows_dev, summed.shape[-1])
-    ctx_count = blocks_by_ctx.shape[0]
     span_out = (
         blocks_by_ctx[:, : prompts * span_dev]
         .reshape(ctx_count, prompts, span_dev, -1)

time: 204 us -> 181 us (0.89)
  blocking collectives: 12.9 us -> 0 us
  local copies, waits for them, and re-layouts: 20.6 us -> 14.5 us
  matrix products: 29.5 us -> 24 us
  starting transfers between devices: 0.43 us -> 5.49 us
  waiting for transfers between devices: 112 us -> 109 us
    all_gather x3 -> x0, waiting for transfers between devices: 38.7 us -> none  [the longest x1 19.5 us: shards(): lax.all_gather(rows_local, 'ctx', axis=0, tiled=True)]
    ppermute x0 -> x6, waiting for transfers between devices: none -> 34.8 us  [the longest x3 30 us: ctx_shards(): received.append(lax.ppermute(block, 'ctx', pairs))]
    all_gather x2 -> x0, blocking collectives: 12.9 us -> none  [the longest x1 6.69 us: shards(): lax.all_gather(span_key, 'ctx', axis=1, tiled=True)]
    ppermute x0 -> x6, starting transfers between devices: none -> 5.41 us  [the longest x3 4.76 us: ctx_shards(): received.append(lax.ppermute(block, 'ctx', pairs))]
    another operation x0 -> x11, other arithmetic: none -> 5.05 us  [the longest x5 3.35 us: ctx_shards(): along_x = jnp.stack(received)]
    unnamed x28 -> x35, local copies, waits for them, and re-layouts: 3.68 us -> 0.28 us
    slice x0 -> x3, local copies, waits for them, and re-layouts: none -> 2.78 us  [shards(): arrived[shard, member]]
    dot_general x4, matrix products: 10.4 us -> 7.74 us  [absorb(): jnp.einsum('brn,bnd->brd', weights.astype(jnp.bfloat16), value_rows, pref...]
  transfers between devices with their start and end apart: 5 -> 8, of which waited for: 5 -> 6; matrix products, arithmetic and copies ran while one was open for 7% -> 4% of each run, Pallas kernels for 0% -> 0%
where the time goes in v2:
time: 181 us
  waiting for transfers between devices  109 us (60%)
  matrix products  24 us (13%)
  between operations  14.7 us (8%)
  local copies, waits for them, and re-layouts  14.5 us (8%)
  other arithmetic  12.9 us (7%)
  starting transfers between devices  5.49 us (3%)
    all_gather x1, waiting for transfers between devices, shards(): summed = lax.all_gather(share, 'head', axis=0, tiled=True)  37.6 us
    reduce_scatter x1, waiting for transfers between devices, shards(): lax.psum_scatter(projected.astype(jnp.bfloat16), 'head', scatter_dimensio...  36.9 us
    ppermute x3, waiting for transfers between devices, ctx_shards(): received.append(lax.ppermute(block, 'ctx', pairs))  30 us
    dot_general x1, matrix products, shards(): jnp.dot(ctx_gather(rows_local, ctx_count).reshape(-1, rows_local.shape[-1...  7.92 us
    dot_general x4, matrix products, absorb(): jnp.einsum('brn,bnd->brd', weights.astype(jnp.bfloat16), value_rows, pref...  7.74 us
    reduce_sum x4, other arithmetic, absorb(): running_sum = running_sum * factor + jnp.sum(weights, axis=-1)  6.44 us
    dot_general x4, matrix products, absorb(): jnp.einsum('brd,bnd->brn', queries, key_rows, preferred_element_type=jnp....  6.09 us
    ppermute x3, waiting for transfers between devices, ctx_shards(): lax.ppermute(along_x, 'ctx', [(dev, dev ^ 1) for dev in range(ctx_count)])  4.85 us
  transfers between devices with their start and end apart: 8, of which 6 were waited for; matrix products, arithmetic and copies ran while one was open for 4% of the time, Pallas kernels for 0%

profile of v2, /device:TPU:0, one launch (start us, length us, event | category | flops | bytes accessed | tf_op | source)
XLA Modules:
  0.0 181.0 jit_solution(12741833400638235368)
XLA Ops:
  8.2 1.6 gather_fusion
  9.9 2.7 %gather_fusion.1 = bf16[8,128,2,128]{3,2,1,0:T(2,128)(2,1)S(1)} fusion(bf16[8,128,2,128]{3,2,1,0:T(2,128)(2,1)} %param.21, s32[1024]{0:T(1024)S(1)} %pad_clamp_fusion), kind=kCustom, calls=%fused_computation.1.clone | custom fusion | bytes 1048608 | tf_op jit(solution)/shard_map/jit(_take)/gather | solution.py:123
  13.7 1.1 fusion.72
  14.8 2.9 %collective-permute-start = (bf16[2,2,2,512,128]{4,3,2,1,0:T(8,128)(2,1)}, bf16[2,2,2,512,128]{4,3,2,1,0:T(8,128)(2,1)S(1)}, u32[]{:S(2)}, u32[]{:S(2)}) collective-permute-start(bf16[2,2,2,512,128]{4,3,2,1,0:T(8,128)(2,1)} %get-tuple-element.87), channel_id=1, source_target_pairs={{0,8},{4,12},{8,0},{12,4},{1,9},{5,13},{9,1},{13,5},{2,10},{6,14},... | collective-permute-start | bytes 3145736 | tf_op jit(solution)/shard_map/ppermute | solution.py:79
  18.4 2.0 %fusion.81 = (f32[2,4,8,8]{3,1,2,0:T(4,128)}, f32[2,4,8,8,4]{3,4,1,2,0:T(4,128)}) fusion(bf16[2,8,4,128,1]{3,0,1,2,4:T(2,128)(2,1)S(1)} %bitcast.217, pred[4,4]{1,0:T(4,128)(4,1)S(1)} %iota_compare_fusion.1, bf16[4,8,16,128]{3,2,1,0:T(8,128)(2,1)S(1)} %copy-done.10), kind=kOutput, calls=%fused_computation.144 | convolution fusion | flops 529920 | bytes 157712 | tf_op jit(solution)/shard_map/ktsgd,ksud->ktsgu/dot_general | solution.py:54
  21.3 20.5 %collective-permute-done = bf16[2,2,2,512,128]{4,3,2,1,0:T(8,128)(2,1)S(1)} collective-permute-done((bf16[2,2,2,512,128]{4,3,2,1,0:T(8,128)(2,1)}, bf16[2,2,2,512,128]{4,3,2,1,0:T(8,128)(2,1)S(1)}, u32[]{:S(2)}, u32[]{:S(2)}) %collective-permute-start) | collective-permute-done | bytes 1048608 | tf_op jit(solution)/shard_map/ppermute | solution.py:79
  41.8 1.5 pad_maximum_fusion
  45.1 2.6 %collective-permute-done.3 = bf16[2,2,2,32,2,128]{5,3,4,2,1,0:T(8,128)(2,1)S(1)} collective-permute-done((bf16[2,2,2,32,2,128]{5,3,4,2,1,0:T(8,128)(2,1)S(1)}, bf16[2,2,2,32,2,128]{5,3,4,2,1,0:T(8,128)(2,1)S(1)}, u32[]{:S(2)}, u32[]{:S(2)}) %collective-permute-start.3) | collective-permute-done | bytes 131104 | tf_op jit(solution)/shard_map/ppermute | solution.py:81
  48.8 1.9 %fusion.76 = (bf16[1,1,2,2,512,128]{5,4,3,2,1,0:T(8,128)(2,1)S(1)}, bf16[1,1,2,2,512,128]{5,4,3,2,1,0:T(8,128)(2,1)S(1)}, bf16[1,1,2,2,512,128]{5,4,3,2,1,0:T(8,128)(2,1)S(1)}, bf16[1,1,2,2,512,128]{5,4,3,2,1,0:T(8,128)(2,1)S(1)}) fusion(bf16[2,2,2,2,512,128]{5,4,3,2,1,0:T(8,128)(2,1)} %collective-permute-done.1), kind=kLoop, calls=%fused_computation.139 | loop fusion | bytes 4194304 | tf_op jit(solution)/shard_map/slice | solution.py:156
  50.7 1.6 bitcast_reduce_fusion.1
  52.3 4.0 %bitcast_reduce_fusion = (f32[4,256]{1,0:T(4,128)S(1)}, f32[4,2048,256]{2,1,0:T(8,128)}) fusion(bf16[4,256,128]{2,1,0:T(8,128)(2,1)S(1)} %bitcast.187, bf16[4,512,128]{2,1,0:T(8,128)(2,1)S(1)} %bitcast.209, bf16[4,512,128]{2,1,0:T(8,128)(2,1)S(1)} %bitcast.211, bf16[4,512,128]{2,1,0:T(8,128)(2,1)S(1)} %bitcast.201, bf16[4,512,128]{2,1,0:T(8,128)(2,1)S(1)} %bitcast.197), kind=kOutput, calls=%fused_computation.3 | convolution fusion | flops 549452800 | bytes 10752000 | tf_op jit(solution)/shard_map/while/body/eval_jaxpr/brd,bnd->brn/dot_general | solution.py:13
  56.4 1.4 fusion.2
  57.8 2.5 %fusion.27 = f32[4,256,128]{2,1,0:T(8,128)S(1)} fusion(f32[4,2048,256]{2,1,0:T(8,128)S(1)} %get-tuple-element.102, f32[4,256]{1,0:T(4,128)S(1)} %get-tuple-element.98, bf16[4,512,128]{2,1,0:T(8,128)(2,1)S(1)} %bitcast.206, bf16[4,512,128]{2,1,0:T(8,128)(2,1)S(1)} %bitcast.204, bf16[4,512,128]{2,1,0:T(8,128)(2,1)S(1)} %bitcast.198, ...), kind=kOutput, calls=%fused_computation.40 | convolution fusion | flops 551813120 | bytes 11022336 | tf_op jit(solution)/shard_map/while/body/eval_jaxpr/brn,bnd->brd/dot_general | solution.py:22
  61.0 4.9 %fusion.4 = f32[4,256]{1,0:T(4,128)S(1)} fusion(f32[4,2048,256]{2,1,0:T(8,128)} %get-tuple-element.108, f32[4,256]{1,0:T(4,128)S(1)} %get-tuple-element.95), kind=kLoop, calls=%fused_computation.10 | loop fusion | flops 6290432 | bytes 8396800 | tf_op jit(solution)/shard_map/while/body/eval_jaxpr/reduce_sum | solution.py:21
  65.9 4.6 %fusion.24 = f32[4,256,128]{2,1,0:T(8,128)S(1)} fusion(f32[4,2048,256]{2,1,0:T(8,128)} %get-tuple-element.108, f32[4,256]{1,0:T(4,128)S(1)} %get-tuple-element.95, bf16[4,512,128]{2,1,0:T(8,128)(2,1)S(1)} %bitcast.207, bf16[4,512,128]{2,1,0:T(8,128)(2,1)S(1)} %bitcast.205, bf16[4,512,128]{2,1,0:T(8,128)(2,1)S(1)} %bitcast.199, ...), kind=kOutput, calls=%fused_computation.39 | convolution fusion | flops 551813120 | bytes 11022336 | tf_op jit(solution)/shard_map/while/body/eval_jaxpr/brn,bnd->brd/dot_general | solution.py:22
  72.0 1.8 collective-permute-start.4
  73.8 9.4 %collective-permute-done.4 = bf16[96,2048]{1,0:T(8,128)(2,1)S(1)} collective-permute-done((bf16[96,2048]{1,0:T(8,128)(2,1)S(1)}, bf16[96,2048]{1,0:T(8,128)(2,1)S(1)}, u32[]{:S(2)}, u32[]{:S(2)}) %collective-permute-start.4) | collective-permute-done | bytes 393248 | tf_op jit(solution)/shard_map/ppermute | solution.py:79
  83.4 2.3 %collective-permute-done.5 = bf16[2,96,2048]{2,1,0:T(8,128)(2,1)S(1)} collective-permute-done((bf16[2,96,2048]{2,1,0:T(8,128)(2,1)S(1)}, bf16[2,96,2048]{2,1,0:T(8,128)(2,1)S(1)}, u32[]{:S(2)}, u32[]{:S(2)}) %collective-permute-start.5) | collective-permute-done | bytes 786464 | tf_op jit(solution)/shard_map/ppermute | solution.py:81
  87.3 7.9 %convolution_convert_fusion = bf16[384,2048]{1,0:T(8,128)(2,1)} fusion(bf16[384,2048]{1,0:T(8,128)(2,1)S(1)} %bitcast.179, bf16[2048,2048]{1,0:T(8,128)(2,1)} %param.27), kind=kOutput, calls=%fused_computation.18 | convolution fusion | flops 3222011904 | bytes 11534336 | tf_op jit(solution)/shard_map/dot_general | solution.py:196
  95.3 36.9 %reduce-scatter.2.cloned.1.call-done = bf16[96,2048]{1,0:T(8,128)(2,1)} async-done(((bf16[384,2048]{1,0:T(8,128)(2,1)}), bf16[96,2048]{1,0:T(8,128)(2,1)}) %reduce-scatter.2.cloned.1.call-update) | async-done | bytes 393232 | tf_op jit(solution)/shard_map/reduce_scatter | solution.py:201
  132.3 37.6 %all-gather.2.cloned.1.call-done = bf16[384,2048]{1,0:T(8,128)(2,1)} async-done(((bf16[96,2048]{1,0:T(8,128)(2,1)}), bf16[384,2048]{1,0:T(8,128)(2,1)}) %all-gather.2.cloned.1.call-update) | async-done | bytes 1572880 | tf_op jit(solution)/shard_map/all_gather | solution.py:204
  169.9 1.3 slice.62
  171.2 1.9 %copy_bitcast_fusion = bf16[4,32,2048]{2,1,0:T(8,128)(2,1)} fusion(bf16[4,96,2048]{2,1,0:T(8,128)(2,1)} %bitcast.181), kind=kLoop, calls=%fused_computation.60 | loop fusion | bytes 1048576 | tf_op jit(solution)/shard_map/reshape | solution.py:217
  173.1 1.0 copy.115
  (102 shorter events, 10.3 us)
Async XLA Ops:
  7.2 1.1 copy-start
  7.2 125.0 %reduce-scatter.2.cloned.1.call-start = ((), (), s32[]{:S(2)}) async-start(), calls=%async_computation.1 | async-start | bytes 1966080 | tf_op jit(solution)/shard_map/reduce_scatter | solution.py:201
  9.8 7.9 %copy-start.12 = (bf16[2,32,2,128]{3,2,1,0:T(2,128)(2,1)S(1)}, bf16[2,32,2,128]{3,2,1,0:T(2,128)(2,1)}, u32[]{:S(2)}) copy-start(bf16[2,32,2,128]{3,2,1,0:T(2,128)(2,1)} %param.19) | copy-start | bytes 98308
  9.8 7.9 %copy-start.13 = (bf16[2,32,2,128]{3,2,1,0:T(2,128)(2,1)S(1)}, bf16[2,32,2,128]{3,2,1,0:T(2,128)(2,1)}, u32[]{:S(2)}) copy-start(bf16[2,32,2,128]{3,2,1,0:T(2,128)(2,1)} %param.18) | copy-start | bytes 98308
  9.9 8.6 %copy-start.10 = (bf16[4,8,16,128]{3,2,1,0:T(8,128)(2,1)S(1)}, bf16[4,8,16,128]{3,2,1,0:T(8,128)(2,1)}, u32[]{:S(2)}) copy-start(bf16[4,8,16,128]{3,2,1,0:T(8,128)(2,1)} %param.23) | copy-start | bytes 393220
  9.9 8.6 %copy-start.14 = (bf16[4,8,2,128]{3,2,1,0:T(2,128)(2,1)S(1)}, bf16[4,8,2,128]{3,2,1,0:T(2,128)(2,1)}, u32[]{:S(2)}) copy-start(bf16[4,8,2,128]{3,2,1,0:T(2,128)(2,1)} %param.24) | copy-start | bytes 49156
  14.8 28.6 %copy-start.8 = (bf16[2,32,16,128]{3,2,1,0:T(8,128)(2,1)S(1)}, bf16[2,32,16,128]{3,2,1,0:T(8,128)(2,1)}, u32[]{:S(2)}) copy-start(bf16[2,32,16,128]{3,2,1,0:T(8,128)(2,1)} %param.17) | copy-start | bytes 786436
  14.8 29.6 %copy-start.16 = (s32[32]{0:T(128)S(1)}, s32[32]{0:T(128)}, u32[]{:S(2)}) copy-start(s32[32]{0:T(128)} %param.26) | copy-start | bytes 388
  14.8 27.0 %collective-permute-start = (bf16[2,2,2,512,128]{4,3,2,1,0:T(8,128)(2,1)}, bf16[2,2,2,512,128]{4,3,2,1,0:T(8,128)(2,1)S(1)}, u32[]{:S(2)}, u32[]{:S(2)}) collective-permute-start(bf16[2,2,2,512,128]{4,3,2,1,0:T(8,128)(2,1)} %get-tuple-element.87), channel_id=1, source_target_pairs={{0,8},{4,12},{8,0},{12,4},{1,9},{5,13},{9,1},{13,5},{2,10},{6,14},... | collective-permute-start | bytes 3145736 | tf_op jit(solution)/shard_map/ppermute | solution.py:79
  18.4 26.1 %collective-permute-start.2 = (bf16[2,2,32,2,128]{4,2,3,1,0:T(8,128)(2,1)}, bf16[2,2,32,2,128]{4,2,3,1,0:T(8,128)(2,1)S(1)}, u32[]{:S(2)}, u32[]{:S(2)}) collective-permute-start(bf16[2,2,32,2,128]{4,2,3,1,0:T(8,128)(2,1)} %get-tuple-element.91), channel_id=1, source_target_pairs={{0,8},{4,12},{8,0},{12,4},{1,9},{5,13},{9,1},{13,5},{2,10},{6,14},... | collective-permute-start | bytes 196616 | tf_op jit(solution)/shard_map/ppermute | solution.py:79
  43.4 5.4 %collective-permute-start.1 = (bf16[2,2,2,2,512,128]{5,4,3,2,1,0:T(8,128)(2,1)}, bf16[2,2,2,2,512,128]{5,4,3,2,1,0:T(8,128)(2,1)}, u32[]{:S(2)}, u32[]{:S(2)}) collective-permute-start(bf16[2,2,2,2,512,128]{5,4,3,2,1,0:T(8,128)(2,1)} %pad_maximum_fusion), channel_id=1, source_target_pairs={{0,4},{4,0},{8,12},{12,8},{1,5},{5,1},{9,13},{13,9},{2,6},{6,2},{1... | collective-permute-start | bytes 6291464 | tf_op jit(solution)/shard_map/ppermute | solution.py:81
  44.5 3.2 %collective-permute-start.3 = (bf16[2,2,2,32,2,128]{5,3,4,2,1,0:T(8,128)(2,1)S(1)}, bf16[2,2,2,32,2,128]{5,3,4,2,1,0:T(8,128)(2,1)S(1)}, u32[]{:S(2)}, u32[]{:S(2)}) collective-permute-start(bf16[2,2,2,32,2,128]{5,3,4,2,1,0:T(8,128)(2,1)S(1)} %pad_maximum_fusion.11), channel_id=1, source_target_pairs={{0,4},{4,0},{8,12},{12,8},{1,5},{5,1},{9,13},{13,9},{2,6},{6,2},{1... | collective-permute-start | bytes 393224 | tf_op jit(solution)/shard_map/ppermute | solution.py:81
  48.8 9.0 %copy-start.2 = (bf16[1,1,2,2,512,128]{5,4,3,2,1,0:T(8,128)(2,1)}, bf16[1,1,2,2,512,128]{5,4,3,2,1,0:T(8,128)(2,1)S(1)}, u32[]{:S(2)}) copy-start(bf16[1,1,2,2,512,128]{5,4,3,2,1,0:T(8,128)(2,1)S(1)} %get-tuple-element.84) | copy-start | bytes 1572868
  50.6 7.2 %copy-start.4 = (bf16[1,1,2,2,512,128]{5,4,3,2,1,0:T(8,128)(2,1)}, bf16[1,1,2,2,512,128]{5,4,3,2,1,0:T(8,128)(2,1)S(1)}, u32[]{:S(2)}) copy-start(bf16[1,1,2,2,512,128]{5,4,3,2,1,0:T(8,128)(2,1)S(1)} %get-tuple-element.71) | copy-start | bytes 1572868
  50.6 7.2 %copy-start.6 = (bf16[1,1,2,2,512,128]{5,4,3,2,1,0:T(8,128)(2,1)}, bf16[1,1,2,2,512,128]{5,4,3,2,1,0:T(8,128)(2,1)S(1)}, u32[]{:S(2)}) copy-start(bf16[1,1,2,2,512,128]{5,4,3,2,1,0:T(8,128)(2,1)S(1)} %get-tuple-element.72) | copy-start | bytes 1572868
  56.4 1.4 copy-start.1
  61.0 4.9 %copy-start.3 = (bf16[1,1,2,2,512,128]{5,4,3,2,1,0:T(8,128)(2,1)S(1)}, bf16[1,1,2,2,512,128]{5,4,3,2,1,0:T(8,128)(2,1)}, u32[]{:S(2)}) copy-start(bf16[1,1,2,2,512,128]{5,4,3,2,1,0:T(8,128)(2,1)} %copy-done.2) | copy-start | bytes 1572868
  61.0 4.9 %copy-start.5 = (bf16[1,1,2,2,512,128]{5,4,3,2,1,0:T(8,128)(2,1)S(1)}, bf16[1,1,2,2,512,128]{5,4,3,2,1,0:T(8,128)(2,1)}, u32[]{:S(2)}) copy-start(bf16[1,1,2,2,512,128]{5,4,3,2,1,0:T(8,128)(2,1)} %copy-done.4) | copy-start | bytes 1572868
  61.0 4.9 %copy-start.7 = (bf16[1,1,2,2,512,128]{5,4,3,2,1,0:T(8,128)(2,1)S(1)}, bf16[1,1,2,2,512,128]{5,4,3,2,1,0:T(8,128)(2,1)}, u32[]{:S(2)}) copy-start(bf16[1,1,2,2,512,128]{5,4,3,2,1,0:T(8,128)(2,1)} %copy-done.6) | copy-start | bytes 1572868
  65.9 5.4 %copy-start.11 = (f32[2,4,8,8]{3,1,2,0:T(4,128)S(1)}, f32[2,4,8,8]{3,1,2,0:T(4,128)}, u32[]{:S(2)}) copy-start(f32[2,4,8,8]{3,1,2,0:T(4,128)} %get-tuple-element.109) | copy-start | bytes 6148
  65.9 5.5 %copy-start.9 = (f32[2,4,8,8,4]{3,4,1,2,0:T(4,128)S(1)}, f32[2,4,8,8,4]{3,4,1,2,0:T(4,128)}, u32[]{:S(2)}) copy-start(f32[2,4,8,8,4]{3,4,1,2,0:T(4,128)} %get-tuple-element.110) | copy-start | bytes 24580
  72.0 11.2 %collective-permute-start.4 = (bf16[96,2048]{1,0:T(8,128)(2,1)S(1)}, bf16[96,2048]{1,0:T(8,128)(2,1)S(1)}, u32[]{:S(2)}, u32[]{:S(2)}) collective-permute-start(bf16[96,2048]{1,0:T(8,128)(2,1)S(1)} %constant_dynamic-update-slice_fusion), channel_id=1, source_target_pairs={{0,8},{4,12},{8,0},{12,4},{1,9},{5,13},{9,1},{13,5},{2,10},{6,14},... | collective-permute-start | bytes 1179656 | tf_op jit(solution)/shard_map/ppermute | solution.py:79
  83.3 2.4 %collective-permute-start.5 = (bf16[2,96,2048]{2,1,0:T(8,128)(2,1)S(1)}, bf16[2,96,2048]{2,1,0:T(8,128)(2,1)S(1)}, u32[]{:S(2)}, u32[]{:S(2)}) collective-permute-start(bf16[2,96,2048]{2,1,0:T(8,128)(2,1)S(1)} %pad_maximum_fusion.5), channel_id=1, source_target_pairs={{0,4},{4,0},{8,12},{12,8},{1,5},{5,1},{9,13},{13,9},{2,6},{6,2},{1... | collective-permute-start | bytes 2359304 | tf_op jit(solution)/shard_map/ppermute | solution.py:81
  95.3 74.6 %all-gather.2.cloned.1.call-start = ((), (), s32[]{:S(2)}) async-start(), calls=%async_computation.2 | async-start | bytes 1966080 | tf_op jit(solution)/shard_map/all_gather | solution.py:204
  (1 other events, 1.0 us)
Sparse Core Ops, SparseCore 0:
  95.4 36.7 reduce-scatter.1
  133.8 36.0 all-gather.1

commit v3 on v2

--- a/solution.py
+++ b/solution.py
@@ -1,3 +1,4 @@
+import functools
 import math
 
 import jax
@@ -82,7 +83,7 @@
     return along_x, other_core
 
 
-def ctx_gather(block, ctx_count):
+def ctx_gather(block, ctx_count, axis=0):
     ctx_index = lax.axis_index("ctx")
     chip, core = ctx_index // 2, ctx_index % 2
     along_x, other_core = ctx_shards(block, ctx_count)
@@ -90,7 +91,36 @@
     other_core = jnp.roll(other_core, chip, axis=0)
     core_zero = jnp.where(core == 0, along_x, other_core)
     core_one = jnp.where(core == 0, other_core, along_x)
-    return jnp.stack([core_zero, core_one], axis=1).reshape((ctx_count,) + block.shape)
+    joined = jnp.moveaxis(jnp.stack([core_zero, core_one], axis=1), (0, 1), (axis, axis + 1))
+    return joined.reshape(block.shape[:axis] + (-1,) + block.shape[axis + 1 :])
+
+
+def project(rows, out_weight):
+    flat = rows.reshape(-1, rows.shape[-1])
+    return jnp.dot(flat, out_weight, preferred_element_type=jnp.float32).astype(jnp.bfloat16)
+
+
+def head_sum_direct(partial, lead_shape, head_count):
+    head_index = lax.axis_index("head")
+    blocks = partial.reshape((head_count, -1) + partial.shape[1:])
+    total = lax.dynamic_index_in_dim(blocks, head_index, 0, keepdims=False).astype(jnp.float32)
+    for shift in range(1, head_count):
+        outgoing = lax.dynamic_index_in_dim(blocks, (head_index + shift) % head_count, 0, False)
+        pairs = [(dev, (dev + shift) % head_count) for dev in range(head_count)]
+        total = total + lax.ppermute(outgoing, "head", pairs).astype(jnp.float32)
+    mine = total.astype(jnp.bfloat16)
+    received = [mine]
+    for shift in range(1, head_count):
+        pairs = [(dev, (dev - shift) % head_count) for dev in range(head_count)]
+        received.append(lax.ppermute(mine, "head", pairs))
+    ordered = jnp.roll(jnp.stack(received), head_index, axis=0)
+    return ordered.reshape(lead_shape + (partial.shape[-1],))
+
+
+def head_sum(partial, lead_shape):
+    share = lax.psum_scatter(partial, "head", scatter_dimension=0, tiled=True)
+    summed = lax.all_gather(share, "head", axis=0, tiled=True)
+    return summed.reshape(lead_shape + (partial.shape[-1],))
 
 
 def shards(
@@ -105,6 +135,7 @@
     decode_value,
     sample_prompt,
     out_weight,
+    head_count,
 ):
     prompts, span_dev, heads_dev, head_depth = span_query.shape
     kv_heads = span_key.shape[2]
@@ -130,13 +161,8 @@
         .reshape(head_batch, span_dev * group_size, head_depth)
     )
     ctx_count = sample_prompt.shape[0] // samples_dev
-    span_pair = ctx_gather(jnp.stack([span_key, span_value]), ctx_count)
-    span_keys_all, span_values_all = (
-        span_pair[:, member].transpose(1, 0, 2, 3, 4).reshape(
-            (prompts, ctx_count * span_dev) + span_key.shape[2:]
-        )
-        for member in range(2)
-    )
+    span_pair = ctx_gather(jnp.stack([span_key, span_value]), ctx_count, axis=2)
+    span_keys_all, span_values_all = span_pair[0], span_pair[1]
     span_total = span_keys_all.shape[1]
     span_key_rows = span_keys_all.transpose(0, 2, 1, 3).reshape(head_batch, span_total, head_depth)
     span_value_rows = span_values_all.transpose(0, 2, 1, 3).reshape(
@@ -159,7 +185,6 @@
     prefix_len = prompt_keys_all.shape[2]
     key_rows = prompt_keys_all.reshape(head_batch, prefix_len, head_depth)
     value_rows = prompt_values_all.reshape(head_batch, prefix_len, head_depth)
-    prefill_state = sweep(prefill_state, span_rows, key_rows, value_rows, 2048)
     decode_flat = decode_five.reshape(kv_heads, -1, head_depth)
     decode_batch = jnp.broadcast_to(decode_flat[None], (prompts,) + decode_flat.shape).reshape(
         head_batch, -1, head_depth
@@ -181,47 +206,34 @@
         return jnp.sum(jnp.where(select_mask, shaped, 0.0), axis=0)
 
     decode_state = tuple((select_prompt(member) for member in decode_state))
+    decode_mixed = own_steps(decode_state, decode_five, decode_key, decode_value)
+    decode_attn = decode_mixed.transpose(1, 2, 0, 3, 4).reshape(
+        steps_count, samples_dev, heads_dev * head_depth
+    )
+    decode_rows = ctx_gather(decode_attn, ctx_count, axis=1)
+    decode_partial = project(decode_rows, out_weight)
+    decode_partial, span_rows, key_rows, value_rows, span_key_rows, span_value_rows = (
+        lax.optimization_barrier(
+            (decode_partial, span_rows, key_rows, value_rows, span_key_rows, span_value_rows)
+        )
+    )
+    decode_out = head_sum_direct(decode_partial, decode_rows.shape[:-1], head_count)
+    prefill_state = sweep(prefill_state, span_rows, key_rows, value_rows, 2048)
     prefill_state = absorb(prefill_state, span_rows, span_key_rows, span_value_rows, causal)
     span_mixed = (prefill_state[2] / prefill_state[1][..., None]).astype(jnp.bfloat16)
     span_attn = (
         span_mixed.reshape(prompts, kv_heads, span_dev, group_size, head_depth)
         .transpose(0, 2, 1, 3, 4)
-        .reshape(prompts * span_dev, heads_dev * head_depth)
-    )
-    decode_mixed = own_steps(decode_state, decode_five, decode_key, decode_value)
-    decode_attn = decode_mixed.transpose(1, 2, 0, 3, 4).reshape(
-        steps_count * samples_dev, heads_dev * head_depth
-    )
-    rows_local = jnp.concatenate([span_attn, decode_attn], axis=0)
-    projected = jnp.dot(
-        ctx_gather(rows_local, ctx_count).reshape(-1, rows_local.shape[-1]),
-        out_weight,
-        preferred_element_type=jnp.float32,
-    )
-    share = lax.psum_scatter(
-        projected.astype(jnp.bfloat16), "head", scatter_dimension=0, tiled=True
-    )
-    summed = lax.all_gather(share, "head", axis=0, tiled=True)
-    rows_dev = rows_local.shape[0]
-    blocks_by_ctx = summed.reshape(-1, rows_dev, summed.shape[-1])
-    span_out = (
-        blocks_by_ctx[:, : prompts * span_dev]
-        .reshape(ctx_count, prompts, span_dev, -1)
-        .transpose(1, 0, 2, 3)
-        .reshape(prompts, ctx_count * span_dev, -1)
-    )
-    decode_out = (
-        blocks_by_ctx[:, prompts * span_dev :]
-        .reshape(ctx_count, steps_count, samples_dev, -1)
-        .transpose(1, 0, 2, 3)
-        .reshape(steps_count, ctx_count * samples_dev, -1)
-    )
+        .reshape(prompts, span_dev, heads_dev * head_depth)
+    )
+    span_rows_all = ctx_gather(span_attn, ctx_count, axis=1)
+    span_out = head_sum(project(span_rows_all, out_weight), span_rows_all.shape[:-1])
     return (span_out, decode_out)
 
 
 def solution(mesh):
     return jax.shard_map(
-        shards,
+        functools.partial(shards, head_count=mesh.shape["head"]),
         mesh=mesh,
         in_specs=(
             P("groups", "ctx", "head", None),

time: 181 us -> 186 us (1.028)
  waiting for transfers between devices: 109 us -> 92.8 us
  starting transfers between devices: 5.49 us -> 15.4 us
  other arithmetic: 12.9 us -> 19.4 us
  matrix products: 24 us -> 26.9 us
    reduce_scatter x1, waiting for transfers between devices: 36.9 us -> 8.91 us  [head_sum(): share = lax.psum_scatter(partial, 'head', scatter_dimension=0, tiled=True)]
    ppermute x0 -> x6, waiting for transfers between devices: none -> 21 us  [the longest x3 17.8 us: head_sum_direct(): received.append(lax.ppermute(mine, 'head', pairs))]
    ppermute x0 -> x6, starting transfers between devices: none -> 7.98 us  [the longest x3 4.91 us: head_sum_direct(): total = total + lax.ppermute(outgoing, 'head', pairs).astype(jnp.float32)]
    all_gather x1, waiting for transfers between devices: 37.6 us -> 30.1 us  [head_sum(): summed = lax.all_gather(share, 'head', axis=0, tiled=True)]
    dot_general x1 -> x2, matrix products: 7.92 us -> 11.4 us  [project(): jnp.dot(flat, out_weight, preferred_element_type=jnp.float32)]
    ppermute x3 -> x4, waiting for transfers between devices: 4.85 us -> 1.44 us  [ctx_shards(): lax.ppermute(along_x, 'ctx', [(dev, dev ^ 1) for dev in range(ctx_count)])]
    concatenate x0 -> x2, other arithmetic: none -> 3.01 us  [shards(): jnp.concatenate([arrived[shard, member] for shard in range(ctx_count)], a...]
    reshape x2 -> x0, local copies, waits for them, and re-layouts: 2.92 us -> none  [the longest x1 1.89 us: shards(): decode_out = blocks_by_ctx[:, prompts * span_dev:].reshape(ctx_count, ste...]
  transfers between devices with their start and end apart: 8 -> 16, of which waited for: 6 -> 9; matrix products, arithmetic and copies ran while one was open for 4% -> 11% of each run, Pallas kernels for 0% -> 0%
where the time goes in v3:
time: 186 us; the launch traced here: 185 us
  waiting for transfers between devices  92.8 us (50%)
  matrix products  26.9 us (14%)
  other arithmetic  19.4 us (10%)
  local copies, waits for them, and re-layouts  16.1 us (9%)
  starting transfers between devices  15.4 us (8%)
  between operations  14.9 us (8%)
    ppermute x4, waiting for transfers between devices, ctx_shards(): received.append(lax.ppermute(block, 'ctx', pairs))  31.3 us
    all_gather x1, waiting for transfers between devices, head_sum(): summed = lax.all_gather(share, 'head', axis=0, tiled=True)  30.1 us
    ppermute x3, waiting for transfers between devices, head_sum_direct(): received.append(lax.ppermute(mine, 'head', pairs))  17.8 us
    dot_general x2, matrix products, project(): jnp.dot(flat, out_weight, preferred_element_type=jnp.float32)  11.4 us
    reduce_scatter x1, waiting for transfers between devices, head_sum(): share = lax.psum_scatter(partial, 'head', scatter_dimension=0, tiled=True)  8.91 us
    dot_general x4, matrix products, absorb(): jnp.einsum('brn,bnd->brd', weights.astype(jnp.bfloat16), value_rows, pref...  7.27 us
    reduce_sum x4, other arithmetic, absorb(): running_sum = running_sum * factor + jnp.sum(weights, axis=-1)  6.74 us
    ppermute x4, starting transfers between devices, ctx_shards(): received.append(lax.ppermute(block, 'ctx', pairs))  6.58 us
  transfers between devices with their start and end apart: 16, of which 9 were waited for; matrix products, arithmetic and copies ran while one was open for 11% of the time, Pallas kernels for 0%

profile of v3, /device:TPU:0, one launch (start us, length us, event | category | flops | bytes accessed | tf_op | source)
XLA Modules:
  0.0 185.4 jit_solution(2273941046279042836)
XLA Ops:
  9.9 2.7 %gather_fusion.1 = bf16[8,128,2,128]{3,2,1,0:T(2,128)(2,1)S(1)} fusion(bf16[8,128,2,128]{3,2,1,0:T(2,128)(2,1)} %param.23, s32[1024]{0:T(1024)S(1)} %pad_clamp_fusion), kind=kCustom, calls=%fused_computation.1.clone | custom fusion | bytes 1048608 | tf_op jit(solution)/shard_map/jit(_take)/gather | solution.py:154
  14.8 2.9 %collective-permute-start = (bf16[2,2,2,512,128]{4,3,2,1,0:T(8,128)(2,1)}, bf16[2,2,2,512,128]{4,3,2,1,0:T(8,128)(2,1)S(1)}, u32[]{:S(2)}, u32[]{:S(2)}) collective-permute-start(bf16[2,2,2,512,128]{4,3,2,1,0:T(8,128)(2,1)} %get-tuple-element.104), channel_id=1, source_target_pairs={{0,8},{4,12},{8,0},{12,4},{1,9},{5,13},{9,1},{13,5},{2,10},{6,14},... | collective-permute-start | bytes 3145736 | tf_op jit(solution)/shard_map/ppermute | solution.py:80
  17.9 1.9 %fusion.83 = (f32[2,4,8,8]{3,1,2,0:T(4,128)}, f32[2,4,8,8,4]{3,4,1,2,0:T(4,128)}) fusion(bf16[2,8,4,128,1]{3,0,1,2,4:T(2,128)(2,1)S(1)} %bitcast.221, pred[4,4]{1,0:T(4,128)(4,1)S(1)} %iota_compare_fusion.1, bf16[4,8,16,128]{3,2,1,0:T(8,128)(2,1)S(1)} %copy-done.18), kind=kOutput, calls=%fused_computation.162 | convolution fusion | flops 529920 | bytes 157712 | tf_op jit(solution)/shard_map/ktsgd,ksud->ktsgu/dot_general | solution.py:55
  19.9 22.0 %collective-permute-done = bf16[2,2,2,512,128]{4,3,2,1,0:T(8,128)(2,1)S(1)} collective-permute-done((bf16[2,2,2,512,128]{4,3,2,1,0:T(8,128)(2,1)}, bf16[2,2,2,512,128]{4,3,2,1,0:T(8,128)(2,1)S(1)}, u32[]{:S(2)}, u32[]{:S(2)}) %collective-permute-start) | collective-permute-done | bytes 1048608 | tf_op jit(solution)/shard_map/ppermute | solution.py:80
  50.2 2.8 %fusion.78 = (bf16[1,1,2,2,512,128]{5,4,3,2,1,0:T(8,128)(2,1)}, bf16[1,1,2,2,512,128]{5,4,3,2,1,0:T(8,128)(2,1)}, bf16[1,1,2,2,512,128]{5,4,3,2,1,0:T(8,128)(2,1)S(1)}, bf16[1,1,2,2,512,128]{5,4,3,2,1,0:T(8,128)(2,1)S(1)}) fusion(bf16[2,2,2,2,512,128]{5,4,3,2,1,0:T(8,128)(2,1)} %collective-permute-done.1), kind=kLoop, calls=%fused_computation.157 | loop fusion | bytes 4194304 | tf_op jit(solution)/shard_map/slice | solution.py:182
  53.1 4.2 %bitcast_reduce_fusion = (f32[4,256]{1,0:T(4,128)S(1)}, f32[4,2048,256]{2,1,0:T(8,128)}) fusion(bf16[4,256,128]{2,1,0:T(8,128)(2,1)S(1)} %bitcast.208, bf16[4,512,128]{2,1,0:T(8,128)(2,1)S(1)} %bitcast.197, bf16[4,512,128]{2,1,0:T(8,128)(2,1)S(1)} %bitcast.199, bf16[4,512,128]{2,1,0:T(8,128)(2,1)S(1)} %bitcast.193, bf16[4,512,128]{2,1,0:T(8,128)(2,1)S(1)} %bitcast.189), kind=kOutput, calls=%fused_computation.3 | convolution fusion | flops 549452800 | bytes 10752000 | tf_op jit(solution)/shard_map/while/body/eval_jaxpr/brd,bnd->brn/dot_general | solution.py:14
  58.1 4.9 %fusion.3 = f32[4,256]{1,0:T(4,128)S(1)} fusion(f32[4,2048,256]{2,1,0:T(8,128)} %get-tuple-element.124, f32[4,256]{1,0:T(4,128)S(1)} %get-tuple-element.118), kind=kLoop, calls=%fused_computation.9 | loop fusion | flops 6290432 | bytes 8396800 | tf_op jit(solution)/shard_map/while/body/eval_jaxpr/reduce_sum | solution.py:22
  63.7 4.6 %fusion.22 = f32[4,256,128]{2,1,0:T(8,128)S(1)} fusion(f32[4,2048,256]{2,1,0:T(8,128)} %get-tuple-element.124, f32[4,256]{1,0:T(4,128)S(1)} %get-tuple-element.118, f32[4,256]{1,0:T(4,128)S(1)} %get-tuple-element.113, f32[4,256]{1,0:T(4,128)S(1)} %copy-done.23, bf16[4,512,128]{2,1,0:T(8,128)(2,1)S(1)} %bitcast.204, bf16[4,512,128]{2,1,0:T(8,128)(2,1)S(1)} %bitcast.202, ...), kind=kOutput, calls=%fused_computation.31 | convolution fusion | flops 551813120 | bytes 11022336 | tf_op jit(solution)/shard_map/while/body/eval_jaxpr/brn,bnd->brd/dot_general | solution.py:23
  69.8 1.8 collective-permute-start.4
  73.1 2.5 %collective-permute-done.4 = bf16[4,8,2048]{2,1,0:T(8,128)(2,1)} collective-permute-done((bf16[4,8,2048]{2,1,0:T(8,128)(2,1)}, bf16[4,8,2048]{2,1,0:T(8,128)(2,1)}, u32[]{:S(2)}, u32[]{:S(2)}) %collective-permute-start.4) | collective-permute-done | bytes 131104 | tf_op jit(solution)/shard_map/ppermute | solution.py:80
  79.7 4.6 %convolution_convert_fusion.1 = bf16[128,2048]{1,0:T(8,128)(2,1)S(1)} fusion(bf16[128,2048]{1,0:T(8,128)(2,1)S(1)} %bitcast.179, bf16[2048,2048]{1,0:T(8,128)(2,1)} %param.29), kind=kOutput, calls=%fused_computation.18 | convolution fusion | flops 1074003968 | bytes 9437184 | tf_op jit(solution)/shard_map/dot_general | solution.py:100
  86.0 1.6 fusion.1
  87.7 2.1 %fusion.25 = f32[4,256,128]{2,1,0:T(8,128)S(1)} fusion(bf16[4,2048,128]{2,1,0:T(8,128)(2,1)S(1)} %pad_maximum_fusion.2, f32[4,256,2048]{2,1,0:T(8,128)S(1)} %get-tuple-element.128, f32[4,256]{1,0:T(4,128)S(1)} %get-tuple-element.116, f32[4,256]{1,0:T(4,128)S(1)} %get-tuple-element.88, f32[4,256]{1,0:T(4,128)S(1)} %get-tuple-element.114), kind=kOutput, calls=%fused_computation.32 | convolution fusion | flops 543424512 | bytes 11022336 | tf_op jit(solution)/shard_map/while/body/eval_jaxpr/brn,bnd->brd/dot_general | solution.py:23
  90.4 1.8 collective-permute-start.6
  92.3 6.8 %collective-permute-done.6 = bf16[2,32,2048]{2,1,0:T(8,128)(2,1)S(1)} collective-permute-done((bf16[2,32,2048]{2,1,0:T(8,128)(2,1)S(1)}, bf16[2,32,2048]{2,1,0:T(8,128)(2,1)S(1)}, u32[]{:S(2)}, u32[]{:S(2)}) %collective-permute-start.6) | collective-permute-done | bytes 262176 | tf_op jit(solution)/shard_map/ppermute | solution.py:80
  99.3 3.9 %collective-permute-start.10 = (bf16[32,2048]{1,0:T(8,128)(2,1)S(1)}, bf16[32,2048]{1,0:T(8,128)(2,1)S(1)}, u32[]{:S(2)}, u32[]{:S(2)}) collective-permute-start(bf16[32,2048]{1,0:T(8,128)(2,1)S(1)} %get-tuple-element.106), channel_id=1, source_target_pairs={{0,3},{1,0},{2,1},{3,2},{4,7},{5,4},{6,5},{7,6},{8,11},{9,8},{10,9... | collective-permute-start | bytes 393224 | tf_op jit(solution)/shard_map/ppermute | solution.py:110
  105.3 6.8 %convolution_convert_fusion = bf16[256,2048]{1,0:T(8,128)(2,1)} fusion(bf16[256,2048]{1,0:T(8,128)(2,1)S(1)} %bitcast.210, bf16[2048,2048]{1,0:T(8,128)(2,1)} %param.29), kind=kOutput, calls=%fused_computation.17 | convolution fusion | flops 2148007936 | bytes 10485760 | tf_op jit(solution)/shard_map/dot_general | solution.py:100
  112.2 3.1 %collective-permute-done.9 = bf16[32,2048]{1,0:T(8,128)(2,1)S(1)} collective-permute-done((bf16[32,2048]{1,0:T(8,128)(2,1)S(1)}, bf16[32,2048]{1,0:T(8,128)(2,1)S(1)}, u32[]{:S(2)}, u32[]{:S(2)}) %collective-permute-start.9) | collective-permute-done | bytes 131104 | tf_op jit(solution)/shard_map/ppermute | solution.py:110
  115.4 2.4 %collective-permute-start.11 = (bf16[32,2048]{1,0:T(8,128)(2,1)S(1)}, bf16[32,2048]{1,0:T(8,128)(2,1)S(1)}, u32[]{:S(2)}, u32[]{:S(2)}) collective-permute-start(bf16[32,2048]{1,0:T(8,128)(2,1)S(1)} %get-tuple-element.84), channel_id=1, source_target_pairs={{0,3},{1,0},{2,1},{3,2},{4,7},{5,4},{6,5},{7,6},{8,11},{9,8},{10,9... | collective-permute-start | bytes 393224 | tf_op jit(solution)/shard_map/ppermute | solution.py:115
  118.5 6.0 %collective-permute-done.11 = bf16[32,2048]{1,0:T(8,128)(2,1)S(1)} collective-permute-done((bf16[32,2048]{1,0:T(8,128)(2,1)S(1)}, bf16[32,2048]{1,0:T(8,128)(2,1)S(1)}, u32[]{:S(2)}, u32[]{:S(2)}) %collective-permute-start.11) | collective-permute-done | bytes 131104 | tf_op jit(solution)/shard_map/ppermute | solution.py:115
  124.4 11.9 %collective-permute-done.12 = bf16[32,2048]{1,0:T(8,128)(2,1)S(1)} collective-permute-done((bf16[32,2048]{1,0:T(8,128)(2,1)S(1)}, bf16[32,2048]{1,0:T(8,128)(2,1)S(1)}, u32[]{:S(2)}, u32[]{:S(2)}) %collective-permute-start.12) | collective-permute-done | bytes 131104 | tf_op jit(solution)/shard_map/ppermute | solution.py:115
  136.4 8.9 %reduce-scatter.2.cloned.1.call-done = bf16[64,2048]{1,0:T(8,128)(2,1)} async-done(((bf16[256,2048]{1,0:T(8,128)(2,1)}), bf16[64,2048]{1,0:T(8,128)(2,1)}) %reduce-scatter.2.cloned.1.call-update) | async-done | bytes 262160 | tf_op jit(solution)/shard_map/reduce_scatter | solution.py:121
  146.2 30.1 %all-gather.2.cloned.1.call-done = bf16[256,2048]{1,0:T(8,128)(2,1)} async-done(((bf16[64,2048]{1,0:T(8,128)(2,1)}), bf16[256,2048]{1,0:T(8,128)(2,1)}) %all-gather.2.cloned.1.call-update) | async-done | bytes 1048592 | tf_op jit(solution)/shard_map/all_gather | solution.py:122
  176.3 2.3 %copy.146 = bf16[2,128,2048]{2,1,0:T(8,128)(2,1)} copy(bf16[2,128,2048]{2,1,0:T(8,128)(2,1)} %bitcast.209) | data formatting | bytes 2097152
  (156 shorter events, 27.9 us)
Async XLA Ops:
  7.2 138.1 %reduce-scatter.2.cloned.1.call-start = ((), (), s32[]{:S(2)}) async-start(), calls=%async_computation.1 | async-start | bytes 1310720 | tf_op jit(solution)/shard_map/reduce_scatter | solution.py:121
  9.9 8.0 %copy-start.18 = (bf16[4,8,16,128]{3,2,1,0:T(8,128)(2,1)S(1)}, bf16[4,8,16,128]{3,2,1,0:T(8,128)(2,1)}, u32[]{:S(2)}) copy-start(bf16[4,8,16,128]{3,2,1,0:T(8,128)(2,1)} %param.25) | copy-start | bytes 393220
  9.9 8.0 %copy-start.26 = (bf16[4,8,2,128]{3,2,1,0:T(2,128)(2,1)S(1)}, bf16[4,8,2,128]{3,2,1,0:T(2,128)(2,1)}, u32[]{:S(2)}) copy-start(bf16[4,8,2,128]{3,2,1,0:T(2,128)(2,1)} %param.26) | copy-start | bytes 49156
  14.8 30.1 %copy-start.16 = (bf16[2,32,16,128]{3,2,1,0:T(8,128)(2,1)S(1)}, bf16[2,32,16,128]{3,2,1,0:T(8,128)(2,1)}, u32[]{:S(2)}) copy-start(bf16[2,32,16,128]{3,2,1,0:T(8,128)(2,1)} %param.19) | copy-start | bytes 786436
  14.8 30.2 %copy-start.28 = (s32[32]{0:T(128)S(1)}, s32[32]{0:T(128)}, u32[]{:S(2)}) copy-start(s32[32]{0:T(128)} %param.28) | copy-start | bytes 388
  14.8 27.0 %collective-permute-start = (bf16[2,2,2,512,128]{4,3,2,1,0:T(8,128)(2,1)}, bf16[2,2,2,512,128]{4,3,2,1,0:T(8,128)(2,1)S(1)}, u32[]{:S(2)}, u32[]{:S(2)}) collective-permute-start(bf16[2,2,2,512,128]{4,3,2,1,0:T(8,128)(2,1)} %get-tuple-element.104), channel_id=1, source_target_pairs={{0,8},{4,12},{8,0},{12,4},{1,9},{5,13},{9,1},{13,5},{2,10},{6,14},... | collective-permute-start | bytes 3145736 | tf_op jit(solution)/shard_map/ppermute | solution.py:80
  17.8 27.3 %collective-permute-start.2 = (bf16[2,2,32,2,128]{4,2,3,1,0:T(8,128)(2,1)S(1)}, bf16[2,2,32,2,128]{4,2,3,1,0:T(8,128)(2,1)S(1)}, u32[]{:S(2)}, u32[]{:S(2)}) collective-permute-start(bf16[2,2,32,2,128]{4,2,3,1,0:T(8,128)(2,1)S(1)} %get-tuple-element.111), channel_id=1, source_target_pairs={{0,8},{4,12},{8,0},{12,4},{1,9},{5,13},{9,1},{13,5},{2,10},{6,14},... | collective-permute-start | bytes 196616 | tf_op jit(solution)/shard_map/ppermute | solution.py:80
  43.4 6.9 %collective-permute-start.1 = (bf16[2,2,2,2,512,128]{5,4,3,2,1,0:T(8,128)(2,1)}, bf16[2,2,2,2,512,128]{5,4,3,2,1,0:T(8,128)(2,1)}, u32[]{:S(2)}, u32[]{:S(2)}) collective-permute-start(bf16[2,2,2,2,512,128]{5,4,3,2,1,0:T(8,128)(2,1)} %pad_maximum_fusion), channel_id=1, source_target_pairs={{0,4},{4,0},{8,12},{12,8},{1,5},{5,1},{9,13},{13,9},{2,6},{6,2},{1... | collective-permute-start | bytes 6291464 | tf_op jit(solution)/shard_map/ppermute | solution.py:82
  44.2 8.9 %copy-start.2 = (bf16[1,1,2,2,512,128]{5,4,3,2,1,0:T(8,128)(2,1)}, bf16[1,1,2,2,512,128]{5,4,3,2,1,0:T(8,128)(2,1)S(1)}, u32[]{:S(2)}) copy-start(bf16[1,1,2,2,512,128]{5,4,3,2,1,0:T(8,128)(2,1)S(1)} %get-tuple-element.100) | copy-start | bytes 1572868
  45.1 2.6 %collective-permute-start.3 = (bf16[2,2,2,32,2,128]{5,3,0,4,2,1:T(8,128)(2,1)S(1)}, bf16[2,2,2,32,2,128]{5,3,0,4,2,1:T(8,128)(2,1)S(1)}, u32[]{:S(2)}, u32[]{:S(2)}) collective-permute-start(bf16[2,2,2,32,2,128]{5,3,0,4,2,1:T(8,128)(2,1)S(1)} %pad_maximum_fusion.6), channel_id=1, source_target_pairs={{0,4},{4,0},{8,12},{12,8},{1,5},{5,1},{9,13},{13,9},{2,6},{6,2},{1... | collective-permute-start | bytes 393224 | tf_op jit(solution)/shard_map/ppermute | solution.py:82
  48.0 20.3 %copy-start.13 = (bf16[1,2,2,2,32,2,128]{6,4,3,2,5,1,0:T(8,128)(2,1)}, bf16[1,2,2,2,32,2,128]{6,4,3,2,5,1,0:T(8,128)(2,1)S(1)}, u32[]{:S(2)}) copy-start(bf16[1,2,2,2,32,2,128]{6,4,3,2,5,1,0:T(8,128)(2,1)S(1)} %get-tuple-element.108) | copy-start | bytes 393220
  68.6 8.1 %copy-start.3 = (bf16[1,1,2,2,512,128]{5,4,3,2,1,0:T(8,128)(2,1)S(1)}, bf16[1,1,2,2,512,128]{5,4,3,2,1,0:T(8,128)(2,1)}, u32[]{:S(2)}) copy-start(bf16[1,1,2,2,512,128]{5,4,3,2,1,0:T(8,128)(2,1)} %copy-done.2) | copy-start | bytes 1572868
  69.8 5.9 %collective-permute-start.4 = (bf16[4,8,2048]{2,1,0:T(8,128)(2,1)}, bf16[4,8,2048]{2,1,0:T(8,128)(2,1)}, u32[]{:S(2)}, u32[]{:S(2)}) collective-permute-start(bf16[4,8,2048]{2,1,0:T(8,128)(2,1)} %reshape.247), channel_id=1, source_target_pairs={{0,8},{4,12},{8,0},{12,4},{1,9},{5,13},{9,1},{13,5},{2,10},{6,14},... | collective-permute-start | bytes 393224 | tf_op jit(solution)/shard_map/ppermute | solution.py:80
  76.6 1.6 collective-permute-start.5
  90.4 8.8 %collective-permute-start.6 = (bf16[2,32,2048]{2,1,0:T(8,128)(2,1)S(1)}, bf16[2,32,2048]{2,1,0:T(8,128)(2,1)S(1)}, u32[]{:S(2)}, u32[]{:S(2)}) collective-permute-start(bf16[2,32,2048]{2,1,0:T(8,128)(2,1)S(1)} %reshape.251), channel_id=1, source_target_pairs={{0,8},{4,12},{8,0},{12,4},{1,9},{5,13},{9,1},{13,5},{2,10},{6,14},... | collective-permute-start | bytes 786440 | tf_op jit(solution)/shard_map/ppermute | solution.py:80
  99.2 5.1 %collective-permute-start.7 = (bf16[2,2,32,2048]{3,2,1,0:T(8,128)(2,1)S(1)}, bf16[2,2,32,2048]{3,2,1,0:T(8,128)(2,1)S(1)}, u32[]{:S(2)}, u32[]{:S(2)}) collective-permute-start(bf16[2,2,32,2048]{3,2,1,0:T(8,128)(2,1)S(1)} %pad_maximum_fusion.4), channel_id=1, source_target_pairs={{0,4},{4,0},{8,12},{12,8},{1,5},{5,1},{9,13},{13,9},{2,6},{6,2},{1... | collective-permute-start | bytes 1572872 | tf_op jit(solution)/shard_map/ppermute | solution.py:82
  99.3 12.8 %collective-permute-start.10 = (bf16[32,2048]{1,0:T(8,128)(2,1)S(1)}, bf16[32,2048]{1,0:T(8,128)(2,1)S(1)}, u32[]{:S(2)}, u32[]{:S(2)}) collective-permute-start(bf16[32,2048]{1,0:T(8,128)(2,1)S(1)} %get-tuple-element.106), channel_id=1, source_target_pairs={{0,3},{1,0},{2,1},{3,2},{4,7},{5,4},{6,5},{7,6},{8,11},{9,8},{10,9... | collective-permute-start | bytes 393224 | tf_op jit(solution)/shard_map/ppermute | solution.py:110
  103.2 8.9 %collective-permute-start.8 = (bf16[32,2048]{1,0:T(8,128)(2,1)S(1)}, bf16[32,2048]{1,0:T(8,128)(2,1)S(1)}, u32[]{:S(2)}, u32[]{:S(2)}) collective-permute-start(bf16[32,2048]{1,0:T(8,128)(2,1)S(1)} %get-tuple-element.105), channel_id=1, source_target_pairs={{0,1},{1,2},{2,3},{3,0},{4,5},{5,6},{6,7},{7,4},{8,9},{9,10},{10,1... | collective-permute-start | bytes 393224 | tf_op jit(solution)/shard_map/ppermute | solution.py:110
  103.2 12.1 %collective-permute-start.9 = (bf16[32,2048]{1,0:T(8,128)(2,1)S(1)}, bf16[32,2048]{1,0:T(8,128)(2,1)S(1)}, u32[]{:S(2)}, u32[]{:S(2)}) collective-permute-start(bf16[32,2048]{1,0:T(8,128)(2,1)S(1)} %get-tuple-element.107), channel_id=1, source_target_pairs={{0,2},{1,3},{2,0},{3,1},{4,6},{5,7},{6,4},{7,5},{8,10},{9,11},{10,... | collective-permute-start | bytes 393224 | tf_op jit(solution)/shard_map/ppermute | solution.py:110
  105.3 73.3 %copy-start.1 = (bf16[8,128,2,128]{3,2,1,0:T(2,128)(2,1)S(1)}, bf16[8,128,2,128]{3,2,1,0:T(2,128)(2,1)}, u32[]{:S(2)}) copy-start(bf16[8,128,2,128]{3,2,1,0:T(2,128)(2,1)} %param.22) | copy-start | bytes 1572868
  112.1 64.1 %all-gather.2.cloned.1.call-start = ((), (), s32[]{:S(2)}) async-start(), calls=%async_computation.2 | async-start | bytes 1310720 | tf_op jit(solution)/shard_map/all_gather | solution.py:122
  115.4 9.0 %collective-permute-start.11 = (bf16[32,2048]{1,0:T(8,128)(2,1)S(1)}, bf16[32,2048]{1,0:T(8,128)(2,1)S(1)}, u32[]{:S(2)}, u32[]{:S(2)}) collective-permute-start(bf16[32,2048]{1,0:T(8,128)(2,1)S(1)} %get-tuple-element.84), channel_id=1, source_target_pairs={{0,3},{1,0},{2,1},{3,2},{4,7},{5,4},{6,5},{7,6},{8,11},{9,8},{10,9... | collective-permute-start | bytes 393224 | tf_op jit(solution)/shard_map/ppermute | solution.py:115
  117.8 18.5 %collective-permute-start.12 = (bf16[32,2048]{1,0:T(8,128)(2,1)S(1)}, bf16[32,2048]{1,0:T(8,128)(2,1)S(1)}, u32[]{:S(2)}, u32[]{:S(2)}) collective-permute-start(bf16[32,2048]{1,0:T(8,128)(2,1)S(1)} %get-tuple-element.84), channel_id=1, source_target_pairs={{0,2},{1,3},{2,0},{3,1},{4,6},{5,7},{6,4},{7,5},{8,10},{9,11},{10,... | collective-permute-start | bytes 393224 | tf_op jit(solution)/shard_map/ppermute | solution.py:115
  117.8 18.5 %collective-permute-start.13 = (bf16[32,2048]{1,0:T(8,128)(2,1)S(1)}, bf16[32,2048]{1,0:T(8,128)(2,1)S(1)}, u32[]{:S(2)}, u32[]{:S(2)}) collective-permute-start(bf16[32,2048]{1,0:T(8,128)(2,1)S(1)} %get-tuple-element.84), channel_id=1, source_target_pairs={{0,1},{1,2},{2,3},{3,0},{4,5},{5,6},{6,7},{7,4},{8,9},{9,10},{10,1... | collective-permute-start | bytes 393224 | tf_op jit(solution)/shard_map/ppermute | solution.py:115
  (21 other events, 97.8 us)
Sparse Core Ops, SparseCore 0:
  112.2 32.9 reduce-scatter.1
  146.9 29.3 all-gather.1

commit v4 on v2

--- a/solution.py
+++ b/solution.py
@@ -82,7 +82,7 @@
     return along_x, other_core
 
 
-def ctx_gather(block, ctx_count):
+def ctx_gather(block, ctx_count, axis=0):
     ctx_index = lax.axis_index("ctx")
     chip, core = ctx_index // 2, ctx_index % 2
     along_x, other_core = ctx_shards(block, ctx_count)
@@ -90,7 +90,8 @@
     other_core = jnp.roll(other_core, chip, axis=0)
     core_zero = jnp.where(core == 0, along_x, other_core)
     core_one = jnp.where(core == 0, other_core, along_x)
-    return jnp.stack([core_zero, core_one], axis=1).reshape((ctx_count,) + block.shape)
+    joined = jnp.moveaxis(jnp.stack([core_zero, core_one], axis=1), (0, 1), (axis, axis + 1))
+    return joined.reshape(block.shape[:axis] + (-1,) + block.shape[axis + 1 :])
 
 
 def shards(
@@ -130,13 +131,8 @@
         .reshape(head_batch, span_dev * group_size, head_depth)
     )
     ctx_count = sample_prompt.shape[0] // samples_dev
-    span_pair = ctx_gather(jnp.stack([span_key, span_value]), ctx_count)
-    span_keys_all, span_values_all = (
-        span_pair[:, member].transpose(1, 0, 2, 3, 4).reshape(
-            (prompts, ctx_count * span_dev) + span_key.shape[2:]
-        )
-        for member in range(2)
-    )
+    span_pair = ctx_gather(jnp.stack([span_key, span_value]), ctx_count, axis=2)
+    span_keys_all, span_values_all = span_pair[0], span_pair[1]
     span_total = span_keys_all.shape[1]
     span_key_rows = span_keys_all.transpose(0, 2, 1, 3).reshape(head_batch, span_total, head_depth)
     span_value_rows = span_values_all.transpose(0, 2, 1, 3).reshape(
@@ -186,35 +182,20 @@
     span_attn = (
         span_mixed.reshape(prompts, kv_heads, span_dev, group_size, head_depth)
         .transpose(0, 2, 1, 3, 4)
-        .reshape(prompts * span_dev, heads_dev * head_depth)
+        .reshape(prompts, span_dev, heads_dev * head_depth)
     )
     decode_mixed = own_steps(decode_state, decode_five, decode_key, decode_value)
     decode_attn = decode_mixed.transpose(1, 2, 0, 3, 4).reshape(
-        steps_count * samples_dev, heads_dev * head_depth
-    )
-    rows_local = jnp.concatenate([span_attn, decode_attn], axis=0)
-    projected = jnp.dot(
-        ctx_gather(rows_local, ctx_count).reshape(-1, rows_local.shape[-1]),
-        out_weight,
-        preferred_element_type=jnp.float32,
-    )
-    share = lax.psum_scatter(
-        projected.astype(jnp.bfloat16), "head", scatter_dimension=0, tiled=True
-    )
-    summed = lax.all_gather(share, "head", axis=0, tiled=True)
-    rows_dev = rows_local.shape[0]
-    blocks_by_ctx = summed.reshape(-1, rows_dev, summed.shape[-1])
-    span_out = (
-        blocks_by_ctx[:, : prompts * span_dev]
-        .reshape(ctx_count, prompts, span_dev, -1)
-        .transpose(1, 0, 2, 3)
-        .reshape(prompts, ctx_count * span_dev, -1)
-    )
-    decode_out = (
-        blocks_by_ctx[:, prompts * span_dev :]
-        .reshape(ctx_count, steps_count, samples_dev, -1)
-        .transpose(1, 0, 2, 3)
-        .reshape(steps_count, ctx_count * samples_dev, -1)
+        steps_count, samples_dev, heads_dev * head_depth
+    )
+    span_rows_all = ctx_gather(span_attn, ctx_count, axis=1)
+    decode_rows_all = ctx_gather(decode_attn, ctx_count, axis=1)
+    span_out, decode_out = lax.psum(
+        tuple(
+            jnp.dot(rows, out_weight, preferred_element_type=jnp.float32).astype(jnp.bfloat16)
+            for rows in (span_rows_all, decode_rows_all)
+        ),
+        "head",
     )
     return (span_out, decode_out)
 

time: 181 us -> 186 us (1.028)
  matrix products: 24 us -> 31.7 us
  waiting for transfers between devices: 109 us -> 103 us
  other arithmetic: 12.9 us -> 15.7 us
    psum x0 -> x1, waiting for transfers between devices: none -> 70.1 us  [shards(): lax.psum(tuple((jnp.dot(rows, out_weight, preferred_element_type=jnp.floa...]
    all_gather x1 -> x0, waiting for transfers between devices: 37.6 us -> none  [shards(): summed = lax.all_gather(share, 'head', axis=0, tiled=True)]
    reduce_scatter x1 -> x0, waiting for transfers between devices: 36.9 us -> none  [shards(): lax.psum_scatter(projected.astype(jnp.bfloat16), 'head', scatter_dimensio...]
    unnamed x35 -> x36, local copies, waits for them, and re-layouts: 0.28 us -> 4.44 us
    dot_general x4, matrix products: 6.09 us -> 10 us  [absorb(): jnp.einsum('brd,bnd->brn', queries, key_rows, preferred_element_type=jnp....]
    reduce_sum x4, other arithmetic: 6.44 us -> 9.87 us  [absorb(): running_sum = running_sum * factor + jnp.sum(weights, axis=-1)]
    dot_general x4, matrix products: 7.74 us -> 11 us  [absorb(): jnp.einsum('brn,bnd->brd', weights.astype(jnp.bfloat16), value_rows, pref...]
    reshape x2 -> x0, local copies, waits for them, and re-layouts: 2.92 us -> none  [the longest x1 1.89 us: shards(): decode_out = blocks_by_ctx[:, prompts * span_dev:].reshape(ctx_count, ste...]
  transfers between devices with their start and end apart: 8 -> 9, of which waited for: 6 -> 4; matrix products, arithmetic and copies ran while one was open for 4% -> 12% of each run, Pallas kernels for 0% -> 0%
where the time goes in v4:
time: 186 us
  waiting for transfers between devices  103 us (55%)
  matrix products  31.7 us (17%)
  other arithmetic  15.7 us (8%)
  local copies, waits for them, and re-layouts  15.4 us (8%)
  between operations  14.7 us (8%)
  starting transfers between devices  5.93 us (3%)
    psum x1, waiting for transfers between devices, shards(): lax.psum(tuple((jnp.dot(rows, out_weight, preferred_element_type=jnp.floa...  70.1 us
    ppermute x4, waiting for transfers between devices, ctx_shards(): received.append(lax.ppermute(block, 'ctx', pairs))  29 us
    dot_general x4, matrix products, absorb(): jnp.einsum('brn,bnd->brd', weights.astype(jnp.bfloat16), value_rows, pref...  11 us
    dot_general x4, matrix products, absorb(): jnp.einsum('brd,bnd->brn', queries, key_rows, preferred_element_type=jnp....  10 us
    reduce_sum x4, other arithmetic, absorb(): running_sum = running_sum * factor + jnp.sum(weights, axis=-1)  9.87 us
    dot_general x2, matrix products, shards(): jnp.dot(rows, out_weight, preferred_element_type=jnp.float32)  8.99 us
    ppermute x4, starting transfers between devices, ctx_shards(): received.append(lax.ppermute(block, 'ctx', pairs))  5.18 us
    slice x3, local copies, waits for them, and re-layouts, shards(): arrived[shard, member]  4.55 us
  transfers between devices with their start and end apart: 9, of which 4 were waited for; matrix products, arithmetic and copies ran while one was open for 12% of the time, Pallas kernels for 0%

profile of v4, /device:TPU:0, one launch (start us, length us, event | category | flops | bytes accessed | tf_op | source)
XLA Modules:
  0.0 186.0 jit_solution(12920115150365041624)
XLA Ops:
  8.2 1.6 gather_fusion
  9.9 2.7 %gather_fusion.1 = bf16[8,128,2,128]{3,2,1,0:T(2,128)(2,1)S(1)} fusion(bf16[8,128,2,128]{3,2,1,0:T(2,128)(2,1)} %param.23, s32[1024]{0:T(1024)S(1)} %pad_clamp_fusion), kind=kCustom, calls=%fused_computation.1.clone | custom fusion | bytes 1048608 | tf_op jit(solution)/shard_map/jit(_take)/gather | solution.py:124
  12.6 1.0 broadcast_select_fusion.1
  13.7 1.1 fusion.86
  14.8 2.9 %collective-permute-start = (bf16[2,2,2,512,128]{4,3,2,1,0:T(8,128)(2,1)}, bf16[2,2,2,512,128]{4,3,2,1,0:T(8,128)(2,1)S(1)}, u32[]{:S(2)}, u32[]{:S(2)}) collective-permute-start(bf16[2,2,2,512,128]{4,3,2,1,0:T(8,128)(2,1)} %get-tuple-element.92), channel_id=1, source_target_pairs={{0,8},{4,12},{8,0},{12,4},{1,9},{5,13},{9,1},{13,5},{2,10},{6,14},... | collective-permute-start | bytes 3145736 | tf_op jit(solution)/shard_map/ppermute | solution.py:79
  17.9 1.4 fusion.97
  19.3 1.0 fusion.92
  20.3 21.5 %collective-permute-done = bf16[2,2,2,512,128]{4,3,2,1,0:T(8,128)(2,1)S(1)} collective-permute-done((bf16[2,2,2,512,128]{4,3,2,1,0:T(8,128)(2,1)}, bf16[2,2,2,512,128]{4,3,2,1,0:T(8,128)(2,1)S(1)}, u32[]{:S(2)}, u32[]{:S(2)}) %collective-permute-start) | collective-permute-done | bytes 1048608 | tf_op jit(solution)/shard_map/ppermute | solution.py:79
  41.8 1.5 pad_maximum_fusion
  44.2 3.5 %collective-permute-done.3 = bf16[2,2,2,32,2,128]{5,3,0,4,2,1:T(8,128)(2,1)S(1)} collective-permute-done((bf16[2,2,2,32,2,128]{5,3,0,4,2,1:T(8,128)(2,1)S(1)}, bf16[2,2,2,32,2,128]{5,3,0,4,2,1:T(8,128)(2,1)S(1)}, u32[]{:S(2)}, u32[]{:S(2)}) %collective-permute-start.3) | collective-permute-done | bytes 131104 | tf_op jit(solution)/shard_map/ppermute | solution.py:81
  49.5 2.7 %fusion.91 = (bf16[1,1,2,2,512,128]{5,4,3,2,1,0:T(8,128)(2,1)}, bf16[1,1,2,2,512,128]{5,4,3,2,1,0:T(8,128)(2,1)}, bf16[1,1,2,2,512,128]{5,4,3,2,1,0:T(8,128)(2,1)S(1)}, bf16[1,1,2,2,512,128]{5,4,3,2,1,0:T(8,128)(2,1)S(1)}) fusion(bf16[2,2,2,2,512,128]{5,4,3,2,1,0:T(8,128)(2,1)} %collective-permute-done.1), kind=kLoop, calls=%fused_computation.152 | loop fusion | bytes 4194304 | tf_op jit(solution)/shard_map/slice | solution.py:152
  52.1 5.6 %bitcast_reduce_fusion = (f32[4,256]{1,0:T(4,128)S(1)}, f32[4,2048,256]{2,1,0:T(8,128)}) fusion(bf16[4,256,128]{2,1,0:T(8,128)(2,1)S(1)} %bitcast.189, bf16[4,512,128]{2,1,0:T(8,128)(2,1)S(1)} %bitcast.212, bf16[4,512,128]{2,1,0:T(8,128)(2,1)S(1)} %bitcast.214, bf16[4,512,128]{2,1,0:T(8,128)(2,1)S(1)} %bitcast.204, bf16[4,512,128]{2,1,0:T(8,128)(2,1)} %bitcast.200), kind=kOutput, calls=%fused_computation.3 | convolution fusion | flops 549452800 | bytes 10752000 | tf_op jit(solution)/shard_map/while/body/eval_jaxpr/brd,bnd->brn/dot_general | solution.py:13
  57.7 3.9 %bitcast_reduce_fusion.1 = (f32[4,256]{1,0:T(4,128)S(1)}, f32[4,2048,256]{2,1,0:T(8,128)}) fusion(bf16[4,256,128]{2,1,0:T(8,128)(2,1)S(1)} %bitcast.192, bf16[4,512,128]{2,1,0:T(8,128)(2,1)S(1)} %bitcast.213, bf16[4,512,128]{2,1,0:T(8,128)(2,1)S(1)} %bitcast.215, bf16[4,512,128]{2,1,0:T(8,128)(2,1)S(1)} %bitcast.205, bf16[4,512,128]{2,1,0:T(8,128)(2,1)S(1)} %bitcast.201), kind=kOutput, calls=%fused_computation.10 | convolution fusion | flops 549452800 | bytes 10752000 | tf_op jit(solution)/shard_map/while/body/eval_jaxpr/brd,bnd->brn/dot_general | solution.py:13
  61.8 4.8 %fusion.8 = f32[4,256]{1,0:T(4,128)S(1)} fusion(f32[4,2048,256]{2,1,0:T(8,128)} %get-tuple-element.113, f32[4,256]{1,0:T(4,128)S(1)} %get-tuple-element.100), kind=kLoop, calls=%fused_computation.14 | loop fusion | flops 6290432 | bytes 8396800 | tf_op jit(solution)/shard_map/while/body/eval_jaxpr/reduce_sum | solution.py:21
  67.3 5.6 %fusion.34 = f32[4,256,128]{2,1,0:T(8,128)S(1)} fusion(f32[4,2048,256]{2,1,0:T(8,128)} %get-tuple-element.113, f32[4,256]{1,0:T(4,128)S(1)} %get-tuple-element.100, bf16[4,512,128]{2,1,0:T(8,128)(2,1)} %bitcast.210, bf16[4,512,128]{2,1,0:T(8,128)(2,1)} %bitcast.208, bf16[4,512,128]{2,1,0:T(8,128)(2,1)S(1)} %bitcast.202, ...), kind=kOutput, calls=%fused_computation.37 | convolution fusion | flops 551813120 | bytes 11022336 | tf_op jit(solution)/shard_map/while/body/eval_jaxpr/brn,bnd->brd/dot_general | solution.py:22
  73.8 1.8 collective-permute-start.6
  75.6 4.8 %fusion.6 = f32[4,256]{1,0:T(4,128)S(1)} fusion(f32[4,2048,256]{2,1,0:T(8,128)} %get-tuple-element.107, f32[4,256]{1,0:T(4,128)S(1)} %get-tuple-element.103), kind=kLoop, calls=%fused_computation.12 | loop fusion | flops 6290432 | bytes 8396800 | tf_op jit(solution)/shard_map/while/body/eval_jaxpr/reduce_sum | solution.py:21
  80.6 4.8 %fusion.37 = f32[4,256,128]{2,1,0:T(8,128)S(1)} fusion(f32[4,2048,256]{2,1,0:T(8,128)} %get-tuple-element.107, f32[4,256]{1,0:T(4,128)S(1)} %get-tuple-element.103, bf16[4,512,128]{2,1,0:T(8,128)(2,1)S(1)} %bitcast.211, bf16[4,512,128]{2,1,0:T(8,128)(2,1)S(1)} %bitcast.209, bf16[4,512,128]{2,1,0:T(8,128)(2,1)S(1)} %bitcast.203, ...), kind=kOutput, calls=%fused_computation.38 | convolution fusion | flops 551813120 | bytes 11022336 | tf_op jit(solution)/shard_map/while/body/eval_jaxpr/brn,bnd->brd/dot_general | solution.py:22
  86.6 7.5 %collective-permute-done.4 = bf16[2,32,2048]{2,1,0:T(8,128)(2,1)S(1)} collective-permute-done((bf16[2,32,2048]{2,1,0:T(8,128)(2,1)S(1)}, bf16[2,32,2048]{2,1,0:T(8,128)(2,1)S(1)}, u32[]{:S(2)}, u32[]{:S(2)}) %collective-permute-start.4) | collective-permute-done | bytes 262176 | tf_op jit(solution)/shard_map/ppermute | solution.py:79
  94.8 5.6 %fusion.21 = bf16[4,32,2048]{2,1,0:T(8,128)(2,1)} fusion(bf16[4,32,2048]{2,1,0:T(8,128)(2,1)S(1)} %bitcast.180, bf16[2048,2048]{1,0:T(8,128)(2,1)} %param.29), kind=kOutput, calls=%fused_computation.23 | convolution fusion | flops 1074003968 | bytes 9437184 | tf_op jit(solution)/shard_map/dot_general | solution.py:195
  101.5 3.4 %fusion.18 = bf16[2,128,2048]{2,1,0:T(8,128)(2,1)} fusion(bf16[2,128,2048]{2,1,0:T(8,128)(2,1)S(1)} %bitcast.190, bf16[2048,2048]{1,0:T(8,128)(2,1)S(1)} %bitcast.177), kind=kOutput, calls=%fused_computation.22 | convolution fusion | flops 2148007936 | bytes 10485760 | tf_op jit(solution)/shard_map/dot_general | solution.py:195
  104.9 70.1 %all-reduce.3.cloned.1.call-done = (bf16[2,128,2048]{2,1,0:T(8,128)(2,1)}, bf16[4,32,2048]{2,1,0:T(8,128)(2,1)}) async-done(((bf16[2,128,2048]{2,1,0:T(8,128)(2,1)}, bf16[4,32,2048]{2,1,0:T(8,128)(2,1)}), (bf16[2,128,2048]{2,1,0:T(8,128)(2,1)}, bf16[4,32,2048]{2,1,0:T(8,128)(2,1)})) %all-reduce.3.cloned.1.call-update) | async-done | bytes 1572880 | tf_op jit(solution)/shard_map/psum | solution.py:193
  175.0 2.3 %copy.148 = bf16[2,128,2048]{2,1,0:T(8,128)(2,1)} copy(bf16[2,128,2048]{2,1,0:T(8,128)(2,1)} %get-tuple-element.120) | data formatting | bytes 2097152
  177.3 1.9 %copy.149 = bf16[4,32,2048]{2,1,0:T(8,128)(2,1)} copy(bf16[4,32,2048]{2,1,0:T(8,128)(2,1)} %get-tuple-element.121) | data formatting | bytes 1048576
  (107 shorter events, 8.3 us)
Async XLA Ops:
  7.2 167.8 %all-reduce.3.cloned.1.call-start = ((), (), s32[]{:S(2)}) async-start(), calls=%async_computation | async-start | bytes 3145728 | tf_op jit(solution)/shard_map/psum | solution.py:193
  9.8 7.9 %copy-start.10 = (bf16[2,32,2,128]{3,2,1,0:T(2,128)(2,1)S(1)}, bf16[2,32,2,128]{3,2,1,0:T(2,128)(2,1)}, u32[]{:S(2)}) copy-start(bf16[2,32,2,128]{3,2,1,0:T(2,128)(2,1)} %param.21) | copy-start | bytes 98308
  9.8 7.9 %copy-start.11 = (bf16[2,32,2,128]{3,2,1,0:T(2,128)(2,1)S(1)}, bf16[2,32,2,128]{3,2,1,0:T(2,128)(2,1)}, u32[]{:S(2)}) copy-start(bf16[2,32,2,128]{3,2,1,0:T(2,128)(2,1)} %param.20) | copy-start | bytes 98308
  9.9 8.0 %copy-start.9 = (bf16[4,8,16,128]{3,2,1,0:T(8,128)(2,1)S(1)}, bf16[4,8,16,128]{3,2,1,0:T(8,128)(2,1)}, u32[]{:S(2)}) copy-start(bf16[4,8,16,128]{3,2,1,0:T(8,128)(2,1)} %param.25) | copy-start | bytes 393220
  9.9 8.0 %copy-start.12 = (bf16[4,8,2,128]{3,2,1,0:T(2,128)(2,1)S(1)}, bf16[4,8,2,128]{3,2,1,0:T(2,128)(2,1)}, u32[]{:S(2)}) copy-start(bf16[4,8,2,128]{3,2,1,0:T(2,128)(2,1)} %param.26) | copy-start | bytes 49156
  14.8 28.6 %copy-start.6 = (bf16[2,32,16,128]{3,2,1,0:T(8,128)(2,1)S(1)}, bf16[2,32,16,128]{3,2,1,0:T(8,128)(2,1)}, u32[]{:S(2)}) copy-start(bf16[2,32,16,128]{3,2,1,0:T(8,128)(2,1)} %param.19) | copy-start | bytes 786436
  14.8 28.7 %copy-start.14 = (s32[32]{0:T(128)S(1)}, s32[32]{0:T(128)}, u32[]{:S(2)}) copy-start(s32[32]{0:T(128)} %param.28) | copy-start | bytes 388
  14.8 27.0 %collective-permute-start = (bf16[2,2,2,512,128]{4,3,2,1,0:T(8,128)(2,1)}, bf16[2,2,2,512,128]{4,3,2,1,0:T(8,128)(2,1)S(1)}, u32[]{:S(2)}, u32[]{:S(2)}) collective-permute-start(bf16[2,2,2,512,128]{4,3,2,1,0:T(8,128)(2,1)} %get-tuple-element.92), channel_id=1, source_target_pairs={{0,8},{4,12},{8,0},{12,4},{1,9},{5,13},{9,1},{13,5},{2,10},{6,14},... | collective-permute-start | bytes 3145736 | tf_op jit(solution)/shard_map/ppermute | solution.py:79
  17.8 25.8 %collective-permute-start.2 = (bf16[2,2,32,2,128]{4,2,3,1,0:T(8,128)(2,1)S(1)}, bf16[2,2,32,2,128]{4,2,3,1,0:T(8,128)(2,1)S(1)}, u32[]{:S(2)}, u32[]{:S(2)}) collective-permute-start(bf16[2,2,32,2,128]{4,2,3,1,0:T(8,128)(2,1)S(1)} %get-tuple-element.96), channel_id=1, source_target_pairs={{0,8},{4,12},{8,0},{12,4},{1,9},{5,13},{9,1},{13,5},{2,10},{6,14},... | collective-permute-start | bytes 196616 | tf_op jit(solution)/shard_map/ppermute | solution.py:79
  43.3 6.1 %collective-permute-start.1 = (bf16[2,2,2,2,512,128]{5,4,3,2,1,0:T(8,128)(2,1)}, bf16[2,2,2,2,512,128]{5,4,3,2,1,0:T(8,128)(2,1)}, u32[]{:S(2)}, u32[]{:S(2)}) collective-permute-start(bf16[2,2,2,2,512,128]{5,4,3,2,1,0:T(8,128)(2,1)} %pad_maximum_fusion), channel_id=1, source_target_pairs={{0,4},{4,0},{8,12},{12,8},{1,5},{5,1},{9,13},{13,9},{2,6},{6,2},{1... | collective-permute-start | bytes 6291464 | tf_op jit(solution)/shard_map/ppermute | solution.py:81
  43.6 4.1 %collective-permute-start.3 = (bf16[2,2,2,32,2,128]{5,3,0,4,2,1:T(8,128)(2,1)S(1)}, bf16[2,2,2,32,2,128]{5,3,0,4,2,1:T(8,128)(2,1)S(1)}, u32[]{:S(2)}, u32[]{:S(2)}) collective-permute-start(bf16[2,2,2,32,2,128]{5,3,0,4,2,1:T(8,128)(2,1)S(1)} %pad_maximum_fusion.10), channel_id=1, source_target_pairs={{0,4},{4,0},{8,12},{12,8},{1,5},{5,1},{9,13},{13,9},{2,6},{6,2},{1... | collective-permute-start | bytes 393224 | tf_op jit(solution)/shard_map/ppermute | solution.py:81
  52.1 5.6 %copy-start.2 = (bf16[1,1,2,2,512,128]{5,4,3,2,1,0:T(8,128)(2,1)S(1)}, bf16[1,1,2,2,512,128]{5,4,3,2,1,0:T(8,128)(2,1)}, u32[]{:S(2)}) copy-start(bf16[1,1,2,2,512,128]{5,4,3,2,1,0:T(8,128)(2,1)} %get-tuple-element.88) | copy-start | bytes 1572868
  61.8 5.3 %copy-start.7 = (f32[2,4,8,8,4]{3,4,1,2,0:T(4,128)S(1)}, f32[2,4,8,8,4]{3,4,1,2,0:T(4,128)}, u32[]{:S(2)}) copy-start(f32[2,4,8,8,4]{3,4,1,2,0:T(4,128)} %get-tuple-element.115) | copy-start | bytes 24580
  61.8 5.5 %copy-start.1 = (bf16[1,1,2,2,512,128]{5,4,3,2,1,0:T(8,128)(2,1)S(1)}, bf16[1,1,2,2,512,128]{5,4,3,2,1,0:T(8,128)(2,1)}, u32[]{:S(2)}) copy-start(bf16[1,1,2,2,512,128]{5,4,3,2,1,0:T(8,128)(2,1)} %get-tuple-element.87) | copy-start | bytes 1572868
  61.8 5.5 %copy-start.3 = (bf16[1,1,2,2,512,128]{5,4,3,2,1,0:T(8,128)(2,1)S(1)}, bf16[1,1,2,2,512,128]{5,4,3,2,1,0:T(8,128)(2,1)}, u32[]{:S(2)}) copy-start(bf16[1,1,2,2,512,128]{5,4,3,2,1,0:T(8,128)(2,1)} %get-tuple-element.89) | copy-start | bytes 1572868
  67.3 6.1 %copy-start.8 = (f32[2,4,8,8,4]{3,4,1,2,0:T(4,128)S(1)}, f32[2,4,8,8,4]{3,4,1,2,0:T(4,128)}, u32[]{:S(2)}) copy-start(f32[2,4,8,8,4]{3,4,1,2,0:T(4,128)} %get-tuple-element.115) | copy-start | bytes 24580
  67.3 6.1 %copy-start.13 = (bf16[4,8,2,128]{3,2,1,0:T(2,128)(2,1)S(1)}, bf16[4,8,2,128]{3,2,1,0:T(2,128)(2,1)}, u32[]{:S(2)}) copy-start(bf16[4,8,2,128]{3,2,1,0:T(2,128)(2,1)} %param.27) | copy-start | bytes 49156
  73.8 12.5 %collective-permute-start.6 = (bf16[4,8,2048]{2,1,0:T(8,128)(2,1)S(1)}, bf16[4,8,2048]{2,1,0:T(8,128)(2,1)S(1)}, u32[]{:S(2)}, u32[]{:S(2)}) collective-permute-start(bf16[4,8,2048]{2,1,0:T(8,128)(2,1)S(1)} %reshape.250), channel_id=1, source_target_pairs={{0,8},{4,12},{8,0},{12,4},{1,9},{5,13},{9,1},{13,5},{2,10},{6,14},... | collective-permute-start | bytes 393224 | tf_op jit(solution)/shard_map/ppermute | solution.py:79
  75.6 5.0 %copy-start.4 = (bf16[1,1,2,2,512,128]{5,4,3,2,1,0:T(8,128)(2,1)S(1)}, bf16[1,1,2,2,512,128]{5,4,3,2,1,0:T(8,128)(2,1)}, u32[]{:S(2)}) copy-start(bf16[1,1,2,2,512,128]{5,4,3,2,1,0:T(8,128)(2,1)} %get-tuple-element.76) | copy-start | bytes 1572868
  85.9 8.1 %collective-permute-start.4 = (bf16[2,32,2048]{2,1,0:T(8,128)(2,1)S(1)}, bf16[2,32,2048]{2,1,0:T(8,128)(2,1)S(1)}, u32[]{:S(2)}, u32[]{:S(2)}) collective-permute-start(bf16[2,32,2048]{2,1,0:T(8,128)(2,1)S(1)} %reshape.245), channel_id=1, source_target_pairs={{0,8},{4,12},{8,0},{12,4},{1,9},{5,13},{9,1},{13,5},{2,10},{6,14},... | collective-permute-start | bytes 786440 | tf_op jit(solution)/shard_map/ppermute | solution.py:79
  86.4 7.8 %collective-permute-start.7 = (bf16[2,4,8,2048]{3,2,1,0:T(8,128)(2,1)S(1)}, bf16[2,4,8,2048]{3,2,1,0:T(8,128)(2,1)S(1)}, u32[]{:S(2)}, u32[]{:S(2)}) collective-permute-start(bf16[2,4,8,2048]{3,2,1,0:T(8,128)(2,1)S(1)} %pad_maximum_fusion.9), channel_id=1, source_target_pairs={{0,4},{4,0},{8,12},{12,8},{1,5},{5,1},{9,13},{13,9},{2,6},{6,2},{1... | collective-permute-start | bytes 786440 | tf_op jit(solution)/shard_map/ppermute | solution.py:81
  94.1 6.3 %collective-permute-start.5 = (bf16[2,2,32,2048]{3,2,1,0:T(8,128)(2,1)S(1)}, bf16[2,2,32,2048]{3,2,1,0:T(8,128)(2,1)S(1)}, u32[]{:S(2)}, u32[]{:S(2)}) collective-permute-start(bf16[2,2,32,2048]{3,2,1,0:T(8,128)(2,1)S(1)} %pad_maximum_fusion.4), channel_id=1, source_target_pairs={{0,4},{4,0},{8,12},{12,8},{1,5},{5,1},{9,13},{13,9},{2,6},{6,2},{1... | collective-permute-start | bytes 1572872 | tf_op jit(solution)/shard_map/ppermute | solution.py:81
  94.8 6.7 %slice-start = ((s8[8388608]{0:T(1024)(128)(4,1)}), s8[4194304]{0:T(1024)(128)(4,1)S(1)}, s32[]{:S(2)}) async-start(s8[8388608]{0:T(1024)(128)(4,1)} %bitcast.176), calls=%async_computation.1 | async-start | bytes 8388608
  94.8 6.7 %slice-start.1 = ((s8[8388608]{0:T(1024)(128)(4,1)}), s8[4194304]{0:T(1024)(128)(4,1)S(1)}, s32[]{:S(2)}) async-start(s8[8388608]{0:T(1024)(128)(4,1)} %bitcast.176), calls=%async_computation.2 | async-start | bytes 8388608
  (2 other events, 6.0 us)
Sparse Core Ops, SparseCore 0:
  105.0 69.9 all-reduce.2

commit v5 on v2

--- a/solution.py
+++ b/solution.py
@@ -1,50 +1,63 @@
+import functools
 import math
 
 import jax
 import jax.numpy as jnp
 from jax import lax
+from jax.experimental import pallas as pl
 from jax.sharding import PartitionSpec as P
 
 negative_floor = -1e30
 
 
-def absorb(softmax_state, queries, key_rows, value_rows, allowed):
-    running_max, running_sum, weighted = softmax_state
-    scores = jnp.einsum("brd,bnd->brn", queries, key_rows, preferred_element_type=jnp.float32) * (
-        1.0 / math.sqrt(queries.shape[-1])
-    )
-    if allowed is not None:
-        scores = jnp.where(allowed, scores, negative_floor)
-    new_max = jnp.maximum(running_max, jnp.max(scores, axis=-1))
-    factor = jnp.exp(running_max - new_max)
-    weights = jnp.exp(scores - new_max[..., None])
-    running_sum = running_sum * factor + jnp.sum(weights, axis=-1)
-    weighted = weighted * factor[..., None] + jnp.einsum(
-        "brn,bnd->brd", weights.astype(jnp.bfloat16), value_rows, preferred_element_type=jnp.float32
-    )
-    return (new_max, running_sum, weighted)
-
-
-def sweep(softmax_state, queries, key_rows, value_rows, block_width):
-    total_keys = key_rows.shape[1]
-    block_width = math.gcd(total_keys, block_width)
-
-    def one_block(state_in, block_start):
-        key_block = lax.dynamic_slice_in_dim(key_rows, block_start, block_width, 1)
-        value_block = lax.dynamic_slice_in_dim(value_rows, block_start, block_width, 1)
-        return (absorb(state_in, queries, key_block, value_block, None), None)
-
-    starts = jnp.arange(total_keys // block_width, dtype=jnp.int32) * block_width
-    softmax_state, unused = lax.scan(one_block, softmax_state, starts)
-    return softmax_state
-
-
-def empty_state(head_batch, row_count, head_depth):
-    return (
-        jnp.full((head_batch, row_count), negative_floor, jnp.float32),
-        jnp.zeros((head_batch, row_count), jnp.float32),
-        jnp.zeros((head_batch, row_count, head_depth), jnp.float32),
-    )
+def attend_kernel(prompt_ref, limit_ref, q_ref, kp_ref, vp_ref, ks_ref, vs_ref, max_ref, sum_ref, acc_ref):
+    queries = q_ref[0]
+    row_prompt = prompt_ref[0]
+    row_limit = limit_ref[0]
+    scale = 1.0 / math.sqrt(queries.shape[-1])
+    span_pos = lax.broadcasted_iota(jnp.int32, (1, ks_ref.shape[2]), 1)
+    scores, values = [], []
+    for member in range(kp_ref.shape[0]):
+        mine = row_prompt == member
+        for key_ref, value_ref, allowed in (
+            (kp_ref, vp_ref, mine),
+            (ks_ref, vs_ref, mine & (span_pos <= row_limit)),
+        ):
+            raw = lax.dot_general(
+                queries, key_ref[member, 0], (((1,), (1,)), ((), ())),
+                preferred_element_type=jnp.float32,
+            ) * scale
+            scores.append(jnp.where(allowed, raw, negative_floor))
+            values.append(value_ref[member, 0])
+    row_max = functools.reduce(jnp.maximum, [s.max(axis=-1, keepdims=True) for s in scores])
+    weights = [jnp.exp(s - row_max) for s in scores]
+    max_ref[0] = row_max
+    sum_ref[0] = functools.reduce(jnp.add, [w.sum(axis=-1, keepdims=True) for w in weights])
+    acc_ref[0] = functools.reduce(jnp.add, [
+        jnp.dot(w.astype(jnp.bfloat16), v, preferred_element_type=jnp.float32)
+        for w, v in zip(weights, values)
+    ])
+
+
+def attend(queries, prefix_keys, prefix_values, span_keys, span_values, row_prompt, row_limit, per_prompt):
+    grid_count, rows, depth = queries.shape
+    prompts, kv_heads = prefix_keys.shape[:2]
+    if per_prompt:
+        kv_block, kv_map = 1, lambda g: (g // kv_heads, g % kv_heads, 0, 0)
+    else:
+        kv_block, kv_map = prompts, lambda g: (0, g, 0, 0)
+    row_spec = pl.BlockSpec((1, rows, 1), lambda g: (g, 0, 0))
+    def kv_spec(arr):
+        return pl.BlockSpec((kv_block, 1) + arr.shape[2:], kv_map)
+    return pl.pallas_call(
+        attend_kernel,
+        grid=(grid_count,),
+        in_specs=[row_spec, row_spec, pl.BlockSpec((1, rows, depth), lambda g: (g, 0, 0)),
+                  kv_spec(prefix_keys), kv_spec(prefix_values), kv_spec(span_keys), kv_spec(span_values)],
+        out_specs=[row_spec, row_spec, pl.BlockSpec((1, rows, depth), lambda g: (g, 0, 0))],
+        out_shape=[jax.ShapeDtypeStruct((grid_count, rows, 1), jnp.float32)] * 2
+        + [jax.ShapeDtypeStruct((grid_count, rows, depth), jnp.float32)],
+    )(row_prompt, row_limit, queries, prefix_keys, prefix_values, span_keys, span_values)
 
 
 def own_steps(softmax_state, queries_five, own_key, own_value):
@@ -137,52 +150,53 @@
         )
         for member in range(2)
     )
-    span_total = span_keys_all.shape[1]
-    span_key_rows = span_keys_all.transpose(0, 2, 1, 3).reshape(head_batch, span_total, head_depth)
-    span_value_rows = span_values_all.transpose(0, 2, 1, 3).reshape(
-        head_batch, span_total, head_depth
-    )
+    span_key_rows = span_keys_all.transpose(0, 2, 1, 3)
+    span_value_rows = span_values_all.transpose(0, 2, 1, 3)
     query_pos = (
         ctx_index * span_dev + jnp.arange(span_dev * group_size, dtype=jnp.int32) // group_size
     )
-    causal = (jnp.arange(span_total, dtype=jnp.int32)[None, :] <= query_pos[:, None])[None]
     decode_five = decode_query.reshape(
         steps_count, samples_dev, kv_heads, group_size, head_depth
     ).transpose(2, 0, 1, 3, 4)
-    prefill_state = empty_state(head_batch, span_dev * group_size, head_depth)
     along_x, other_core = ctx_shards(jnp.stack([local_keys, local_values]), ctx_count)
     arrived = jnp.concatenate([along_x, other_core], axis=0)
     prompt_keys_all, prompt_values_all = (
         jnp.concatenate([arrived[shard, member] for shard in range(ctx_count)], axis=2)
         for member in range(2)
     )
-    prefix_len = prompt_keys_all.shape[2]
-    key_rows = prompt_keys_all.reshape(head_batch, prefix_len, head_depth)
-    value_rows = prompt_values_all.reshape(head_batch, prefix_len, head_depth)
-    prefill_state = sweep(prefill_state, span_rows, key_rows, value_rows, 2048)
-    decode_flat = decode_five.reshape(kv_heads, -1, head_depth)
-    decode_batch = jnp.broadcast_to(decode_flat[None], (prompts,) + decode_flat.shape).reshape(
-        head_batch, -1, head_depth
-    )
-    decode_state = empty_state(head_batch, decode_flat.shape[1], head_depth)
-    decode_state = sweep(decode_state, decode_batch, key_rows, value_rows, 2048)
-    decode_state = sweep(decode_state, decode_batch, span_key_rows, span_value_rows, span_total)
+    span_rows_count = span_dev * group_size
+    span_limit = jnp.broadcast_to(query_pos[None, :, None], (head_batch, span_rows_count, 1))
+    unused, span_sum, span_acc = attend(
+        span_rows,
+        prompt_keys_all,
+        prompt_values_all,
+        span_key_rows,
+        span_value_rows,
+        jnp.zeros_like(span_limit),
+        span_limit,
+        True,
+    )
+    span_mixed = (span_acc / span_sum).astype(jnp.bfloat16)
     own_prompts = lax.dynamic_slice_in_dim(sample_prompt, ctx_index * samples_dev, samples_dev)
-    chosen = (
-        own_prompts[None, None, None, :, None]
-        == jnp.arange(prompts, dtype=jnp.int32)[:, None, None, None, None]
-    )
-
-    def select_prompt(member):
-        shaped = member.reshape(
-            (prompts, kv_heads, steps_count, samples_dev, group_size) + member.shape[2:]
-        )
-        select_mask = chosen.reshape(chosen.shape + (1,) * (shaped.ndim - 5))
-        return jnp.sum(jnp.where(select_mask, shaped, 0.0), axis=0)
-
-    decode_state = tuple((select_prompt(member) for member in decode_state))
-    prefill_state = absorb(prefill_state, span_rows, span_key_rows, span_value_rows, causal)
-    span_mixed = (prefill_state[2] / prefill_state[1][..., None]).astype(jnp.bfloat16)
+    decode_rows_count = steps_count * samples_dev * group_size
+    decode_prompt = jnp.broadcast_to(
+        own_prompts[None, None, :, None], (kv_heads, steps_count, samples_dev, group_size)
+    ).reshape(kv_heads, decode_rows_count, 1)
+    decode_max, decode_sum, decode_acc = attend(
+        decode_five.reshape(kv_heads, decode_rows_count, head_depth),
+        prompt_keys_all,
+        prompt_values_all,
+        span_key_rows,
+        span_value_rows,
+        decode_prompt,
+        jnp.full_like(decode_prompt, span_keys_all.shape[1]),
+        False,
+    )
+    decode_state = (
+        decode_max.reshape(decode_five.shape[:4]),
+        decode_sum.reshape(decode_five.shape[:4]),
+        decode_acc.reshape(decode_five.shape),
+    )
     span_attn = (
         span_mixed.reshape(prompts, kv_heads, span_dev, group_size, head_depth)
         .transpose(0, 2, 1, 3, 4)

time: 181 us -> 191 us (1.055)
  Pallas kernels: 0 us -> 14.9 us
  matrix products: 24 us -> 10.5 us
  local copies, waits for them, and re-layouts: 14.5 us -> 18.9 us
  waiting for transfers between devices: 109 us -> 112 us
    pallas_call x0 -> x2, Pallas kernels: none -> 14.9 us  [attend(): pl.pallas_call(attend_kernel, grid=(grid_count,), in_specs=[row_spec, row...]
    dot_general x8 -> x0, matrix products: 13.8 us -> none  [the longest x4 7.74 us: absorb(): jnp.einsum('brn,bnd->brd', weights.astype(jnp.bfloat16), value_rows, pref...]
    reduce_sum x6 -> x0, other arithmetic: 6.62 us -> none  [the longest x4 6.44 us: absorb(): running_sum = running_sum * factor + jnp.sum(weights, axis=-1)]
    ppermute x3, waiting for transfers between devices: 30 us -> 35.6 us  [ctx_shards(): received.append(lax.ppermute(block, 'ctx', pairs))]
    broadcast_in_dim x1 -> x6, local copies, waits for them, and re-layouts: 0.04 us -> 3.97 us  [the longest x3 1.53 us: shards(): jnp.broadcast_to(own_prompts[None, None, :, None], (kv_heads, steps_count...]
    pallas_call x0 -> x3, other arithmetic: none -> 3.43 us  [attend(): pl.pallas_call(attend_kernel, grid=(grid_count,), in_specs=[row_spec, row...]
    concatenate x0 -> x2, other arithmetic: none -> 2.93 us  [shards(): jnp.concatenate([arrived[shard, member] for shard in range(ctx_count)], a...]
    slice x3 -> x0, local copies, waits for them, and re-layouts: 2.78 us -> none  [shards(): arrived[shard, member]]
  transfers between devices with their start and end apart: 8 -> 8, of which waited for: 6 -> 6; matrix products, arithmetic and copies ran while one was open for 4% -> 3% of each run, Pallas kernels for 0% -> 0%
where the time goes in v5:
time: 191 us; the launch traced here: 190 us
  waiting for transfers between devices  112 us (59%)
  local copies, waits for them, and re-layouts  18.9 us (10%)
  Pallas kernels  14.9 us (8%)
  between operations  14.4 us (8%)
  other arithmetic  12.3 us (6%)
  matrix products  10.5 us (5%)
  starting transfers between devices  6.92 us (4%)
    all_gather x1, waiting for transfers between devices, shards(): summed = lax.all_gather(share, 'head', axis=0, tiled=True)  37.6 us
    reduce_scatter x1, waiting for transfers between devices, shards(): lax.psum_scatter(projected.astype(jnp.bfloat16), 'head', scatter_dimensio...  36.9 us
    ppermute x3, waiting for transfers between devices, ctx_shards(): received.append(lax.ppermute(block, 'ctx', pairs))  35.6 us
    pallas_call x2, Pallas kernels, attend(): pl.pallas_call(attend_kernel, grid=(grid_count,), in_specs=[row_spec, row...  14.9 us
    dot_general x1, matrix products, shards(): jnp.dot(ctx_gather(rows_local, ctx_count).reshape(-1, rows_local.shape[-1...  7.92 us
    ppermute x3, starting transfers between devices, ctx_shards(): received.append(lax.ppermute(block, 'ctx', pairs))  6.62 us
  transfers between devices with their start and end apart: 8, of which 6 were waited for; matrix products, arithmetic and copies ran while one was open for 3% of the time, Pallas kernels for 0%

profile of v5, /device:TPU:0, one launch (start us, length us, event | category | flops | bytes accessed | tf_op | source)
XLA Modules:
  0.0 190.3 jit_solution(9240083928941167168)
XLA Ops:
  8.2 1.6 gather_fusion
  9.8 2.6 %gather_fusion.1 = bf16[8,128,2,128]{3,2,1,0:T(2,128)(2,1)S(1)} fusion(bf16[8,128,2,128]{3,2,1,0:T(2,128)(2,1)} %param.21, s32[1024]{0:T(1024)S(1)} %pad_clamp_fusion), kind=kCustom, calls=%fused_computation.1.clone | custom fusion | bytes 1048608 | tf_op jit(solution)/shard_map/jit(_take)/gather | solution.py:136
  13.8 3.0 %collective-permute-start = (bf16[2,2,2,512,128]{4,3,2,1,0:T(8,128)(2,1)S(1)}, bf16[2,2,2,512,128]{4,3,2,1,0:T(8,128)(2,1)S(1)}, u32[]{:S(2)}, u32[]{:S(2)}) collective-permute-start(bf16[2,2,2,512,128]{4,3,2,1,0:T(8,128)(2,1)S(1)} %get-tuple-element.30), channel_id=1, source_target_pairs={{0,8},{4,12},{8,0},{12,4},{1,9},{5,13},{9,1},{13,5},{2,10},{6,14},... | collective-permute-start | bytes 3145736 | tf_op jit(solution)/shard_map/ppermute | solution.py:92
  16.8 23.2 %collective-permute-done = bf16[2,2,2,512,128]{4,3,2,1,0:T(8,128)(2,1)S(1)} collective-permute-done((bf16[2,2,2,512,128]{4,3,2,1,0:T(8,128)(2,1)S(1)}, bf16[2,2,2,512,128]{4,3,2,1,0:T(8,128)(2,1)S(1)}, u32[]{:S(2)}, u32[]{:S(2)}) %collective-permute-start) | collective-permute-done | bytes 1048608 | tf_op jit(solution)/shard_map/ppermute | solution.py:92
  39.9 1.5 pad_maximum_fusion
  41.6 1.8 collective-permute-start.2
  43.5 2.6 %collective-permute-done.2 = bf16[2,2,32,2,128]{4,2,3,1,0:T(8,128)(2,1)S(1)} collective-permute-done((bf16[2,2,32,2,128]{4,2,3,1,0:T(8,128)(2,1)S(1)}, bf16[2,2,32,2,128]{4,2,3,1,0:T(8,128)(2,1)S(1)}, u32[]{:S(2)}, u32[]{:S(2)}) %collective-permute-start.2) | collective-permute-done | bytes 65568 | tf_op jit(solution)/shard_map/ppermute | solution.py:92
  46.3 1.3 fusion.28
  51.5 1.7 slice_bitcast_fusion.2
  53.2 1.5 pad_maximum_fusion.2.vp_ref
  54.6 1.5 pad_maximum_fusion.1.kp_ref
  57.7 7.4 %shard_map.123 = (f32[2,256,1]{2,1,0:T(8,128)}, f32[2,256,1]{2,1,0:T(8,128)}, f32[2,256,128]{2,1,0:T(8,128)}) custom-call(s32[2,256,1]{2,1,0:T(8,128)} %broadcast_in_dim.53.prompt_ref, s32[2,256,1]{2,1,0:T(8,128)} %broadcast_in_dim.54.limit_ref, bf16[2,256,128]{2,1,0:T(8,128)(2,1)} %bitcast.146, bf16[2,2,2048,128]{3,2,1,0:T(8,128)(2,1)} %pad_maximum_fusion.1.kp_ref, ...), custom_call_target="tpu_custom_call" | custom-call | tf_op jit(solution)/shard_map/pallas_call | solution.py:52
  67.7 1.3 fusion.3
  70.8 7.5 %shard_map.122 = (f32[4,256,1]{2,1,0:T(8,128)}, f32[4,256,1]{2,1,0:T(8,128)}, f32[4,256,128]{2,1,0:T(8,128)}) custom-call(s32[4,256,1]{2,1,0:T(8,128)} %broadcast_in_dim.49.prompt_ref, s32[4,256,1]{2,1,0:T(8,128)} %broadcast_in_dim.50.limit_ref, bf16[4,256,128]{2,1,0:T(8,128)(2,1)} %bitcast.141, bf16[2,2,2048,128]{3,2,1,0:T(8,128)(2,1)} %pad_maximum_fusion.1.kp_ref, ...), custom_call_target="tpu_custom_call" | custom-call | tf_op jit(solution)/shard_map/pallas_call | solution.py:52
  78.3 1.2 reduce
  79.5 1.3 divide_convert_fusion
  81.0 1.8 collective-permute-start.4
  82.8 9.8 %collective-permute-done.4 = bf16[96,2048]{1,0:T(8,128)(2,1)S(1)} collective-permute-done((bf16[96,2048]{1,0:T(8,128)(2,1)S(1)}, bf16[96,2048]{1,0:T(8,128)(2,1)S(1)}, u32[]{:S(2)}, u32[]{:S(2)}) %collective-permute-start.4) | collective-permute-done | bytes 393248 | tf_op jit(solution)/shard_map/ppermute | solution.py:92
  92.7 2.3 %collective-permute-done.5 = bf16[2,96,2048]{2,1,0:T(8,128)(2,1)S(1)} collective-permute-done((bf16[2,96,2048]{2,1,0:T(8,128)(2,1)S(1)}, bf16[2,96,2048]{2,1,0:T(8,128)(2,1)S(1)}, u32[]{:S(2)}, u32[]{:S(2)}) %collective-permute-start.5) | collective-permute-done | bytes 786464 | tf_op jit(solution)/shard_map/ppermute | solution.py:94
  96.6 7.9 %convolution_convert_fusion = bf16[384,2048]{1,0:T(8,128)(2,1)} fusion(bf16[384,2048]{1,0:T(8,128)(2,1)S(1)} %bitcast.132, bf16[2048,2048]{1,0:T(8,128)(2,1)} %param.27), kind=kOutput, calls=%fused_computation.2 | convolution fusion | flops 3222011904 | bytes 11534336 | tf_op jit(solution)/shard_map/dot_general | solution.py:210
  104.6 36.9 %reduce-scatter.2.cloned.1.call-done = bf16[96,2048]{1,0:T(8,128)(2,1)} async-done(((bf16[384,2048]{1,0:T(8,128)(2,1)}), bf16[96,2048]{1,0:T(8,128)(2,1)}) %reduce-scatter.2.cloned.1.call-update) | async-done | bytes 393232 | tf_op jit(solution)/shard_map/reduce_scatter | solution.py:215
  141.5 37.6 %all-gather.2.cloned.1.call-done = bf16[384,2048]{1,0:T(8,128)(2,1)} async-done(((bf16[96,2048]{1,0:T(8,128)(2,1)}), bf16[384,2048]{1,0:T(8,128)(2,1)}) %all-gather.2.cloned.1.call-update) | async-done | bytes 1572880 | tf_op jit(solution)/shard_map/all_gather | solution.py:218
  179.2 1.3 slice.62
  180.5 1.9 copy_bitcast_fusion.2
  (77 shorter events, 15.4 us)
Async XLA Ops:
  7.2 1.1 copy-start
  7.2 134.3 %reduce-scatter.2.cloned.1.call-start = ((), (), s32[]{:S(2)}) async-start(), calls=%async_computation.1 | async-start | bytes 1966080 | tf_op jit(solution)/shard_map/reduce_scatter | solution.py:215
  13.8 26.2 %collective-permute-start = (bf16[2,2,2,512,128]{4,3,2,1,0:T(8,128)(2,1)S(1)}, bf16[2,2,2,512,128]{4,3,2,1,0:T(8,128)(2,1)S(1)}, u32[]{:S(2)}, u32[]{:S(2)}) collective-permute-start(bf16[2,2,2,512,128]{4,3,2,1,0:T(8,128)(2,1)S(1)} %get-tuple-element.30), channel_id=1, source_target_pairs={{0,8},{4,12},{8,0},{12,4},{1,9},{5,13},{9,1},{13,5},{2,10},{6,14},... | collective-permute-start | bytes 3145736 | tf_op jit(solution)/shard_map/ppermute | solution.py:92
  39.9 1.6 copy-start.4
  39.9 1.6 copy-start.5
  41.5 4.8 %copy-start.2 = (bf16[4,8,16,128]{3,2,1,0:T(8,128)(2,1)S(1)}, bf16[4,8,16,128]{3,2,1,0:T(8,128)(2,1)}, u32[]{:S(2)}) copy-start(bf16[4,8,16,128]{3,2,1,0:T(8,128)(2,1)} %param.23) | copy-start | bytes 393220
  41.5 4.8 %copy-start.7 = (bf16[4,8,2,128]{3,2,1,0:T(2,128)(2,1)S(1)}, bf16[4,8,2,128]{3,2,1,0:T(2,128)(2,1)}, u32[]{:S(2)}) copy-start(bf16[4,8,2,128]{3,2,1,0:T(2,128)(2,1)} %param.24) | copy-start | bytes 49156
  41.5 6.1 %copy-start.9 = (s32[32]{0:T(128)S(1)}, s32[32]{0:T(128)}, u32[]{:S(2)}) copy-start(s32[32]{0:T(128)} %param.26) | copy-start | bytes 388
  41.5 7.6 %copy-start.1 = (bf16[2,32,16,128]{3,2,1,0:T(8,128)(2,1)S(1)}, bf16[2,32,16,128]{3,2,1,0:T(8,128)(2,1)}, u32[]{:S(2)}) copy-start(bf16[2,32,16,128]{3,2,1,0:T(8,128)(2,1)} %param.17) | copy-start | bytes 786436
  41.5 10.0 %collective-permute-start.1 = (bf16[2,2,2,2,512,128]{5,4,3,2,1,0:T(8,128)(2,1)}, bf16[2,2,2,2,512,128]{5,4,3,2,1,0:T(8,128)(2,1)}, u32[]{:S(2)}, u32[]{:S(2)}) collective-permute-start(bf16[2,2,2,2,512,128]{5,4,3,2,1,0:T(8,128)(2,1)} %pad_maximum_fusion), channel_id=1, source_target_pairs={{0,4},{4,0},{8,12},{12,8},{1,5},{5,1},{9,13},{13,9},{2,6},{6,2},{1... | collective-permute-start | bytes 6291464 | tf_op jit(solution)/shard_map/ppermute | solution.py:94
  41.6 4.5 %collective-permute-start.2 = (bf16[2,2,32,2,128]{4,2,3,1,0:T(8,128)(2,1)S(1)}, bf16[2,2,32,2,128]{4,2,3,1,0:T(8,128)(2,1)S(1)}, u32[]{:S(2)}, u32[]{:S(2)}) collective-permute-start(bf16[2,2,32,2,128]{4,2,3,1,0:T(8,128)(2,1)S(1)} %get-tuple-element.34), channel_id=1, source_target_pairs={{0,8},{4,12},{8,0},{12,4},{1,9},{5,13},{9,1},{13,5},{2,10},{6,14},... | collective-permute-start | bytes 196616 | tf_op jit(solution)/shard_map/ppermute | solution.py:92
  46.2 3.6 %collective-permute-start.3 = (bf16[2,2,2,32,2,128]{5,3,4,2,1,0:T(8,128)(2,1)S(1)}, bf16[2,2,2,32,2,128]{5,3,4,2,1,0:T(8,128)(2,1)S(1)}, u32[]{:S(2)}, u32[]{:S(2)}) collective-permute-start(bf16[2,2,2,32,2,128]{5,3,4,2,1,0:T(8,128)(2,1)S(1)} %pad_maximum_fusion.7), channel_id=1, source_target_pairs={{0,4},{4,0},{8,12},{12,8},{1,5},{5,1},{9,13},{13,9},{2,6},{6,2},{1... | collective-permute-start | bytes 393224 | tf_op jit(solution)/shard_map/ppermute | solution.py:94
  54.6 1.5 copy-start.6
  57.7 9.8 %copy-start.3 = (f32[2,4,8,8]{3,1,2,0:T(4,128)S(1)}, f32[2,4,8,8]{3,1,2,0:T(4,128)}, u32[]{:S(2)}) copy-start(f32[2,4,8,8]{3,1,2,0:T(4,128)} %get-tuple-element.37) | copy-start | bytes 6148
  57.7 10.0 %copy-start.8 = (bf16[4,8,2,128]{3,2,1,0:T(2,128)(2,1)S(1)}, bf16[4,8,2,128]{3,2,1,0:T(2,128)(2,1)}, u32[]{:S(2)}) copy-start(bf16[4,8,2,128]{3,2,1,0:T(2,128)(2,1)} %param.25) | copy-start | bytes 49156
  81.0 11.6 %collective-permute-start.4 = (bf16[96,2048]{1,0:T(8,128)(2,1)S(1)}, bf16[96,2048]{1,0:T(8,128)(2,1)S(1)}, u32[]{:S(2)}, u32[]{:S(2)}) collective-permute-start(bf16[96,2048]{1,0:T(8,128)(2,1)S(1)} %constant_dynamic-update-slice_fusion), channel_id=1, source_target_pairs={{0,8},{4,12},{8,0},{12,4},{1,9},{5,13},{9,1},{13,5},{2,10},{6,14},... | collective-permute-start | bytes 1179656 | tf_op jit(solution)/shard_map/ppermute | solution.py:92
  92.6 2.4 %collective-permute-start.5 = (bf16[2,96,2048]{2,1,0:T(8,128)(2,1)S(1)}, bf16[2,96,2048]{2,1,0:T(8,128)(2,1)S(1)}, u32[]{:S(2)}, u32[]{:S(2)}) collective-permute-start(bf16[2,96,2048]{2,1,0:T(8,128)(2,1)S(1)} %pad_maximum_fusion.5), channel_id=1, source_target_pairs={{0,4},{4,0},{8,12},{12,8},{1,5},{5,1},{9,13},{13,9},{2,6},{6,2},{1... | collective-permute-start | bytes 2359304 | tf_op jit(solution)/shard_map/ppermute | solution.py:94
  104.6 74.6 %all-gather.2.cloned.1.call-start = ((), (), s32[]{:S(2)}) async-start(), calls=%async_computation.2 | async-start | bytes 1966080 | tf_op jit(solution)/shard_map/all_gather | solution.py:218
Sparse Core Ops, SparseCore 0:
  104.7 36.7 reduce-scatter.1
  143.1 36.0 all-gather.1

commit v6 on v2

--- a/solution.py
+++ b/solution.py
@@ -1,3 +1,4 @@
+import functools
 import math
 
 import jax
@@ -93,6 +94,42 @@
     return jnp.stack([core_zero, core_one], axis=1).reshape((ctx_count,) + block.shape)
 
 
+def head_sum_line(partial, head_count):
+    last = head_count - 1
+    head_index = lax.axis_index("head")
+    blocks = partial.reshape((head_count, -1) + partial.shape[1:])
+    rightward = [(dev, dev + 1) for dev in range(last)]
+    leftward = [(dev + 1, dev) for dev in range(last)]
+    from_left = from_right = None
+    for step in range(1, head_count):
+        right_block = jnp.clip(head_index + head_count - step, 0, last)
+        left_block = jnp.clip(head_index - head_count + step, 0, last)
+        going_right = lax.dynamic_index_in_dim(blocks, right_block, 0, False)
+        going_left = lax.dynamic_index_in_dim(blocks, left_block, 0, False)
+        if from_left is not None:
+            going_right = going_right + from_left.astype(jnp.float32)
+            going_left = going_left + from_right.astype(jnp.float32)
+        from_left = lax.ppermute(going_right.astype(jnp.bfloat16), "head", rightward)
+        from_right = lax.ppermute(going_left.astype(jnp.bfloat16), "head", leftward)
+    own = lax.dynamic_index_in_dim(blocks, head_index, 0, False)
+    mine = (own + from_left.astype(jnp.float32) + from_right.astype(jnp.float32)).astype(jnp.bfloat16)
+    lefts, rights = [], []
+    send_right = send_left = mine
+    for step in range(1, head_count):
+        send_right = lax.ppermute(send_right, "head", rightward)
+        send_left = lax.ppermute(send_left, "head", leftward)
+        lefts.append(send_right)
+        rights.append(send_left)
+    candidates = jnp.stack([mine] + lefts + rights)
+    wanted = jnp.arange(head_count, dtype=jnp.int32)
+    pick = jnp.where(
+        wanted == head_index,
+        0,
+        jnp.where(wanted < head_index, head_index - wanted, last + wanted - head_index),
+    )
+    return jnp.take(candidates, pick, axis=0).reshape(partial.shape)
+
+
 def shards(
     span_query,
     span_key,
@@ -105,6 +142,7 @@
     decode_value,
     sample_prompt,
     out_weight,
+    head_count,
 ):
     prompts, span_dev, heads_dev, head_depth = span_query.shape
     kv_heads = span_key.shape[2]
@@ -198,10 +236,7 @@
         out_weight,
         preferred_element_type=jnp.float32,
     )
-    share = lax.psum_scatter(
-        projected.astype(jnp.bfloat16), "head", scatter_dimension=0, tiled=True
-    )
-    summed = lax.all_gather(share, "head", axis=0, tiled=True)
+    summed = head_sum_line(projected, head_count)
     rows_dev = rows_local.shape[0]
     blocks_by_ctx = summed.reshape(-1, rows_dev, summed.shape[-1])
     span_out = (
@@ -221,7 +256,7 @@
 
 def solution(mesh):
     return jax.shard_map(
-        shards,
+        functools.partial(shards, head_count=mesh.shape["head"]),
         mesh=mesh,
         in_specs=(
             P("groups", "ctx", "head", None),

time: 181 us -> 182 us (level)
  starting transfers between devices: 5.49 us -> 38.6 us
  waiting for transfers between devices: 109 us -> 81.3 us
  between operations: 14.7 us -> 1.53 us
  other arithmetic: 12.9 us -> 18.6 us
  local copies, waits for them, and re-layouts: 14.5 us -> 20.2 us
  matrix products: 24 us -> 20.6 us
    ppermute x0 -> x12, waiting for transfers between devices: none -> 43.9 us  [the longest x3 15.1 us: head_sum_line(): lax.ppermute(going_right.astype(jnp.bfloat16), 'head', rightward)]
    all_gather x1 -> x0, waiting for transfers between devices: 37.6 us -> none  [shards(): summed = lax.all_gather(share, 'head', axis=0, tiled=True)]
    reduce_scatter x1 -> x0, waiting for transfers between devices: 36.9 us -> none  [shards(): lax.psum_scatter(projected.astype(jnp.bfloat16), 'head', scatter_dimensio...]
    ppermute x0 -> x12, starting transfers between devices: none -> 33.2 us  [the longest x3 13.2 us: head_sum_line(): lax.ppermute(going_right.astype(jnp.bfloat16), 'head', rightward)]
    unnamed x35 -> x40, local copies, waits for them, and re-layouts: 0.28 us -> 5.87 us
    convert_element_type x0 -> x3, other arithmetic: none -> 3.95 us  [the longest x2 2.75 us: head_sum_line(): going_right.astype(jnp.bfloat16)]
    gather x0 -> x1, local copies, waits for them, and re-layouts: none -> 2.42 us  [head_sum_line(): return jnp.take(candidates, pick, axis=0).reshape(partial.shape)]
    dot_general x1, matrix products: 7.92 us -> 5.85 us  [shards(): jnp.dot(ctx_gather(rows_local, ctx_count).reshape(-1, rows_local.shape[-1...]
  transfers between devices with their start and end apart: 8 -> 18, of which waited for: 6 -> 14; matrix products, arithmetic and copies ran while one was open for 4% -> 6% of each run, Pallas kernels for 0% -> 0%
where the time goes in v6:
time: 182 us; the launch traced here: 181 us
  waiting for transfers between devices  81.3 us (45%)
  starting transfers between devices  38.6 us (21%)
  matrix products  20.6 us (11%)
  local copies, waits for them, and re-layouts  20.2 us (11%)
  other arithmetic  18.6 us (10%)
    ppermute x3, waiting for transfers between devices, ctx_shards(): received.append(lax.ppermute(block, 'ctx', pairs))  31.7 us
    ppermute x3, waiting for transfers between devices, head_sum_line(): lax.ppermute(going_right.astype(jnp.bfloat16), 'head', rightward)  15.1 us
    ppermute x3, waiting for transfers between devices, head_sum_line(): from_right = lax.ppermute(going_left.astype(jnp.bfloat16), 'head', leftward)  15 us
    ppermute x3, starting transfers between devices, head_sum_line(): lax.ppermute(going_right.astype(jnp.bfloat16), 'head', rightward)  13.2 us
    ppermute x3, starting transfers between devices, head_sum_line(): send_right = lax.ppermute(send_right, 'head', rightward)  12.2 us
    ppermute x3, waiting for transfers between devices, head_sum_line(): send_right = lax.ppermute(send_right, 'head', rightward)  11 us
    dot_general x4, matrix products, absorb(): jnp.einsum('brn,bnd->brd', weights.astype(jnp.bfloat16), value_rows, pref...  7.69 us
    reduce_sum x4, other arithmetic, absorb(): running_sum = running_sum * factor + jnp.sum(weights, axis=-1)  6.44 us
  transfers between devices with their start and end apart: 18, of which 14 were waited for; matrix products, arithmetic and copies ran while one was open for 6% of the time, Pallas kernels for 0%

profile of v6, /device:TPU:0, one launch (start us, length us, event | category | flops | bytes accessed | tf_op | source)
XLA Modules:
  0.0 180.9 jit_solution(6491003722510733711)
XLA Ops:
  3.3 2.6 %gather_fusion.2 = bf16[8,128,2,128]{3,2,1,0:T(2,128)(2,1)S(1)} fusion(bf16[8,128,2,128]{3,2,1,0:T(2,128)(2,1)} %param.21, s32[1024]{0:T(1024)S(1)} %pad_clamp_fusion.1), kind=kCustom, calls=%fused_computation.1.clone | custom fusion | bytes 1048608 | tf_op jit(solution)/shard_map/jit(_take)/gather | solution.py:161
  8.2 2.9 %collective-permute-start = (bf16[2,2,2,512,128]{4,3,2,1,0:T(8,128)(2,1)}, bf16[2,2,2,512,128]{4,3,2,1,0:T(8,128)(2,1)S(1)}, u32[]{:S(2)}, u32[]{:S(2)}) collective-permute-start(bf16[2,2,2,512,128]{4,3,2,1,0:T(8,128)(2,1)} %get-tuple-element.93), channel_id=1, source_target_pairs={{0,8},{4,12},{8,0},{12,4},{1,9},{5,13},{9,1},{13,5},{2,10},{6,14},... | collective-permute-start | bytes 3145736 | tf_op jit(solution)/shard_map/ppermute | solution.py:80
  12.9 22.3 %collective-permute-done = bf16[2,2,2,512,128]{4,3,2,1,0:T(8,128)(2,1)S(1)} collective-permute-done((bf16[2,2,2,512,128]{4,3,2,1,0:T(8,128)(2,1)}, bf16[2,2,2,512,128]{4,3,2,1,0:T(8,128)(2,1)S(1)}, u32[]{:S(2)}, u32[]{:S(2)}) %collective-permute-start) | collective-permute-done | bytes 1048608 | tf_op jit(solution)/shard_map/ppermute | solution.py:80
  37.6 3.5 %collective-permute-done.3 = bf16[2,2,2,32,2,128]{5,3,4,2,1,0:T(8,128)(2,1)S(1)} collective-permute-done((bf16[2,2,2,32,2,128]{5,3,4,2,1,0:T(8,128)(2,1)S(1)}, bf16[2,2,2,32,2,128]{5,3,4,2,1,0:T(8,128)(2,1)S(1)}, u32[]{:S(2)}, u32[]{:S(2)}) %collective-permute-start.3) | collective-permute-done | bytes 131104 | tf_op jit(solution)/shard_map/ppermute | solution.py:82
  45.8 4.0 %bitcast_reduce_fusion = (f32[4,256]{1,0:T(4,128)S(1)}, f32[4,2048,256]{2,1,0:T(8,128)}) fusion(bf16[4,256,128]{2,1,0:T(8,128)(2,1)S(1)} %bitcast.229, bf16[4,512,128]{2,1,0:T(8,128)(2,1)S(1)} %bitcast.251, bf16[4,512,128]{2,1,0:T(8,128)(2,1)S(1)} %bitcast.253, bf16[4,512,128]{2,1,0:T(8,128)(2,1)S(1)} %bitcast.243, bf16[4,512,128]{2,1,0:T(8,128)(2,1)S(1)} %bitcast.239), kind=kOutput, calls=%fused_computation.6 | convolution fusion | flops 549452800 | bytes 10752000 | tf_op jit(solution)/shard_map/while/body/eval_jaxpr/brd,bnd->brn/dot_general | solution.py:14
  51.3 2.5 %fusion.29 = f32[4,256,128]{2,1,0:T(8,128)S(1)} fusion(f32[4,2048,256]{2,1,0:T(8,128)S(1)} %get-tuple-element.108, f32[4,256]{1,0:T(4,128)S(1)} %get-tuple-element.104, bf16[4,512,128]{2,1,0:T(8,128)(2,1)S(1)} %bitcast.248, bf16[4,512,128]{2,1,0:T(8,128)(2,1)S(1)} %bitcast.246, bf16[4,512,128]{2,1,0:T(8,128)(2,1)S(1)} %bitcast.240, ...), kind=kOutput, calls=%fused_computation.43 | convolution fusion | flops 551813120 | bytes 11022336 | tf_op jit(solution)/shard_map/while/body/eval_jaxpr/brn,bnd->brd/dot_general | solution.py:23
  54.5 4.9 %fusion.6 = f32[4,256]{1,0:T(4,128)S(1)} fusion(f32[4,2048,256]{2,1,0:T(8,128)} %get-tuple-element.114, f32[4,256]{1,0:T(4,128)S(1)} %get-tuple-element.101), kind=kLoop, calls=%fused_computation.13 | loop fusion | flops 6290432 | bytes 8396800 | tf_op jit(solution)/shard_map/while/body/eval_jaxpr/reduce_sum | solution.py:22
  59.4 4.6 %fusion.26 = f32[4,256,128]{2,1,0:T(8,128)S(1)} fusion(f32[4,2048,256]{2,1,0:T(8,128)} %get-tuple-element.114, f32[4,256]{1,0:T(4,128)S(1)} %get-tuple-element.101, bf16[4,512,128]{2,1,0:T(8,128)(2,1)S(1)} %bitcast.249, bf16[4,512,128]{2,1,0:T(8,128)(2,1)S(1)} %bitcast.247, bf16[4,512,128]{2,1,0:T(8,128)(2,1)S(1)} %bitcast.241, ...), kind=kOutput, calls=%fused_computation.42 | convolution fusion | flops 551813120 | bytes 11022336 | tf_op jit(solution)/shard_map/while/body/eval_jaxpr/brn,bnd->brd/dot_general | solution.py:23
  67.2 9.4 %collective-permute-done.4 = bf16[96,2048]{1,0:T(8,128)(2,1)S(1)} collective-permute-done((bf16[96,2048]{1,0:T(8,128)(2,1)S(1)}, bf16[96,2048]{1,0:T(8,128)(2,1)S(1)}, u32[]{:S(2)}, u32[]{:S(2)}) %collective-permute-start.4) | collective-permute-done | bytes 393248 | tf_op jit(solution)/shard_map/ppermute | solution.py:80
  80.7 5.9 %fusion = f32[4,96,2048]{2,1,0:T(8,128)S(1)} fusion(bf16[4,96,2048]{2,1,0:T(8,128)(2,1)S(1)} %bitcast.223, bf16[2048,2048]{1,0:T(8,128)(2,1)} %param.27), kind=kOutput, calls=%fused_computation.3 | convolution fusion | flops 3221225472 | bytes 13107200 | tf_op jit(solution)/shard_map/dot_general | solution.py:234
  88.3 3.8 %collective-permute-start.6 = (bf16[96,2048]{1,0:T(8,128)(2,1)S(1)}, bf16[96,2048]{1,0:T(8,128)(2,1)S(1)}, u32[]{:S(2)}, u32[]{:S(2)}) collective-permute-start(bf16[96,2048]{1,0:T(8,128)(2,1)S(1)} %get-tuple-element.75), channel_id=1, source_target_pairs={{0,1},{1,2},{2,3},{4,5},{5,6},{6,7},{8,9},{9,10},{10,11},{12,13},{... | collective-permute-start | bytes 1179656 | tf_op jit(solution)/shard_map/ppermute | solution.py:112
  93.4 7.3 %collective-permute-done.6 = bf16[96,2048]{1,0:T(8,128)(2,1)S(1)} collective-permute-done((bf16[96,2048]{1,0:T(8,128)(2,1)S(1)}, bf16[96,2048]{1,0:T(8,128)(2,1)S(1)}, u32[]{:S(2)}, u32[]{:S(2)}) %collective-permute-start.6) | collective-permute-done | bytes 393248 | tf_op jit(solution)/shard_map/ppermute | solution.py:112
  101.9 4.4 %collective-permute-start.7 = (bf16[96,2048]{1,0:T(8,128)(2,1)S(1)}, bf16[96,2048]{1,0:T(8,128)(2,1)S(1)}, u32[]{:S(2)}, u32[]{:S(2)}) collective-permute-start(bf16[96,2048]{1,0:T(8,128)(2,1)S(1)} %fusion.44), channel_id=1, source_target_pairs={{0,1},{1,2},{2,3},{4,5},{5,6},{6,7},{8,9},{9,10},{10,11},{12,13},{... | collective-permute-start | bytes 1179656 | tf_op jit(solution)/shard_map/ppermute | solution.py:112
  106.3 7.8 %collective-permute-done.7 = bf16[96,2048]{1,0:T(8,128)(2,1)S(1)} collective-permute-done((bf16[96,2048]{1,0:T(8,128)(2,1)S(1)}, bf16[96,2048]{1,0:T(8,128)(2,1)S(1)}, u32[]{:S(2)}, u32[]{:S(2)}) %collective-permute-start.7) | collective-permute-done | bytes 393248 | tf_op jit(solution)/shard_map/ppermute | solution.py:112
  117.0 5.0 %collective-permute-start.8 = (bf16[96,2048]{1,0:T(8,128)(2,1)S(1)}, bf16[96,2048]{1,0:T(8,128)(2,1)S(1)}, u32[]{:S(2)}, u32[]{:S(2)}) collective-permute-start(bf16[96,2048]{1,0:T(8,128)(2,1)S(1)} %get-tuple-element.73), channel_id=1, source_target_pairs={{0,1},{1,2},{2,3},{4,5},{5,6},{6,7},{8,9},{9,10},{10,11},{12,13},{... | collective-permute-start | bytes 1179656 | tf_op jit(solution)/shard_map/ppermute | solution.py:112
  122.0 5.7 %collective-permute-done.10 = bf16[96,2048]{1,0:T(8,128)(2,1)S(1)} collective-permute-done((bf16[96,2048]{1,0:T(8,128)(2,1)S(1)}, bf16[96,2048]{1,0:T(8,128)(2,1)S(1)}, u32[]{:S(2)}, u32[]{:S(2)}) %collective-permute-start.10) | collective-permute-done | bytes 393248 | tf_op jit(solution)/shard_map/ppermute | solution.py:113
  130.2 9.3 %collective-permute-done.11 = bf16[96,2048]{1,0:T(8,128)(2,1)S(1)} collective-permute-done((bf16[96,2048]{1,0:T(8,128)(2,1)S(1)}, bf16[96,2048]{1,0:T(8,128)(2,1)S(1)}, u32[]{:S(2)}, u32[]{:S(2)}) %collective-permute-start.11) | collective-permute-done | bytes 393248 | tf_op jit(solution)/shard_map/ppermute | solution.py:113
  141.6 3.4 %collective-permute-start.12 = (bf16[96,2048]{1,0:T(8,128)(2,1)S(1)}, bf16[96,2048]{1,0:T(8,128)(2,1)S(1)}, u32[]{:S(2)}, u32[]{:S(2)}) collective-permute-start(bf16[96,2048]{1,0:T(8,128)(2,1)S(1)} %get-tuple-element.57), channel_id=1, source_target_pairs={{0,1},{1,2},{2,3},{4,5},{5,6},{6,7},{8,9},{9,10},{10,11},{12,13},{... | collective-permute-start | bytes 1179656 | tf_op jit(solution)/shard_map/ppermute | solution.py:119
  146.4 3.9 %collective-permute-done.12 = bf16[96,2048]{1,0:T(8,128)(2,1)S(1)} collective-permute-done((bf16[96,2048]{1,0:T(8,128)(2,1)S(1)}, bf16[96,2048]{1,0:T(8,128)(2,1)S(1)}, u32[]{:S(2)}, u32[]{:S(2)}) %collective-permute-start.12) | collective-permute-done | bytes 393248 | tf_op jit(solution)/shard_map/ppermute | solution.py:119
  150.3 4.5 %collective-permute-start.13 = (bf16[96,2048]{1,0:T(8,128)(2,1)S(1)}, bf16[96,2048]{1,0:T(8,128)(2,1)S(1)}, u32[]{:S(2)}, u32[]{:S(2)}) collective-permute-start(bf16[96,2048]{1,0:T(8,128)(2,1)S(1)} %collective-permute-done.12), channel_id=1, source_target_pairs={{0,1},{1,2},{2,3},{4,5},{5,6},{6,7},{8,9},{9,10},{10,11},{12,13},{... | collective-permute-start | bytes 1179656 | tf_op jit(solution)/shard_map/ppermute | solution.py:119
  157.0 4.2 %collective-permute-done.13 = bf16[96,2048]{1,0:T(8,128)(2,1)S(1)} collective-permute-done((bf16[96,2048]{1,0:T(8,128)(2,1)S(1)}, bf16[96,2048]{1,0:T(8,128)(2,1)S(1)}, u32[]{:S(2)}, u32[]{:S(2)}) %collective-permute-start.13) | collective-permute-done | bytes 393248 | tf_op jit(solution)/shard_map/ppermute | solution.py:119
  161.1 4.4 %collective-permute-start.14 = (bf16[96,2048]{1,0:T(8,128)(2,1)S(1)}, bf16[96,2048]{1,0:T(8,128)(2,1)S(1)}, u32[]{:S(2)}, u32[]{:S(2)}) collective-permute-start(bf16[96,2048]{1,0:T(8,128)(2,1)S(1)} %collective-permute-done.13), channel_id=1, source_target_pairs={{0,1},{1,2},{2,3},{4,5},{5,6},{6,7},{8,9},{9,10},{10,11},{12,13},{... | collective-permute-start | bytes 1179656 | tf_op jit(solution)/shard_map/ppermute | solution.py:119
  167.8 3.0 %collective-permute-done.14 = bf16[96,2048]{1,0:T(8,128)(2,1)S(1)} collective-permute-done((bf16[96,2048]{1,0:T(8,128)(2,1)S(1)}, bf16[96,2048]{1,0:T(8,128)(2,1)S(1)}, u32[]{:S(2)}, u32[]{:S(2)}) %collective-permute-start.14) | collective-permute-done | bytes 393248 | tf_op jit(solution)/shard_map/ppermute | solution.py:119
  176.2 2.4 %gather_fusion = bf16[4,96,2048]{2,1,0:T(8,128)(2,1)S(1)} fusion(bf16[7,96,2048]{2,1,0:T(8,128)(2,1)} %bitcast_dynamic-update-slice_fusion, s32[1024]{0:T(1024)S(1)} %pad_clamp_fusion), kind=kCustom, calls=%fused_computation.2 | custom fusion | bytes 3145744 | tf_op jit(solution)/shard_map/jit(_take)/gather | solution.py:130
  (136 shorter events, 47.7 us)
Async XLA Ops:
  8.2 27.0 %collective-permute-start = (bf16[2,2,2,512,128]{4,3,2,1,0:T(8,128)(2,1)}, bf16[2,2,2,512,128]{4,3,2,1,0:T(8,128)(2,1)S(1)}, u32[]{:S(2)}, u32[]{:S(2)}) collective-permute-start(bf16[2,2,2,512,128]{4,3,2,1,0:T(8,128)(2,1)} %get-tuple-element.93), channel_id=1, source_target_pairs={{0,8},{4,12},{8,0},{12,4},{1,9},{5,13},{9,1},{13,5},{2,10},{6,14},... | collective-permute-start | bytes 3145736 | tf_op jit(solution)/shard_map/ppermute | solution.py:80
  11.2 25.8 %collective-permute-start.2 = (bf16[2,2,32,2,128]{4,2,3,1,0:T(8,128)(2,1)S(1)}, bf16[2,2,32,2,128]{4,2,3,1,0:T(8,128)(2,1)S(1)}, u32[]{:S(2)}, u32[]{:S(2)}) collective-permute-start(bf16[2,2,32,2,128]{4,2,3,1,0:T(8,128)(2,1)S(1)} %get-tuple-element.97), channel_id=1, source_target_pairs={{0,8},{4,12},{8,0},{12,4},{1,9},{5,13},{9,1},{13,5},{2,10},{6,14},... | collective-permute-start | bytes 196616 | tf_op jit(solution)/shard_map/ppermute | solution.py:80
  12.1 24.8 %copy-start.10 = (bf16[2,32,16,128]{3,2,1,0:T(8,128)(2,1)S(1)}, bf16[2,32,16,128]{3,2,1,0:T(8,128)(2,1)}, u32[]{:S(2)}) copy-start(bf16[2,32,16,128]{3,2,1,0:T(8,128)(2,1)} %param.17) | copy-start | bytes 786436
  12.9 24.0 %copy-start.16 = (s32[32]{0:T(128)S(1)}, s32[32]{0:T(128)}, u32[]{:S(2)}) copy-start(s32[32]{0:T(128)} %param.26) | copy-start | bytes 388
  36.8 5.4 %collective-permute-start.1 = (bf16[2,2,2,2,512,128]{5,4,3,2,1,0:T(8,128)(2,1)}, bf16[2,2,2,2,512,128]{5,4,3,2,1,0:T(8,128)(2,1)}, u32[]{:S(2)}, u32[]{:S(2)}) collective-permute-start(bf16[2,2,2,2,512,128]{5,4,3,2,1,0:T(8,128)(2,1)} %pad_maximum_fusion), channel_id=1, source_target_pairs={{0,4},{4,0},{8,12},{12,8},{1,5},{5,1},{9,13},{13,9},{2,6},{6,2},{1... | collective-permute-start | bytes 6291464 | tf_op jit(solution)/shard_map/ppermute | solution.py:82
  37.1 4.1 %collective-permute-start.3 = (bf16[2,2,2,32,2,128]{5,3,4,2,1,0:T(8,128)(2,1)S(1)}, bf16[2,2,2,32,2,128]{5,3,4,2,1,0:T(8,128)(2,1)S(1)}, u32[]{:S(2)}, u32[]{:S(2)}) collective-permute-start(bf16[2,2,2,32,2,128]{5,3,4,2,1,0:T(8,128)(2,1)S(1)} %pad_maximum_fusion.11), channel_id=1, source_target_pairs={{0,4},{4,0},{8,12},{12,8},{1,5},{5,1},{9,13},{13,9},{2,6},{6,2},{1... | collective-permute-start | bytes 393224 | tf_op jit(solution)/shard_map/ppermute | solution.py:82
  42.2 9.1 %copy-start.4 = (bf16[1,1,2,2,512,128]{5,4,3,2,1,0:T(8,128)(2,1)}, bf16[1,1,2,2,512,128]{5,4,3,2,1,0:T(8,128)(2,1)S(1)}, u32[]{:S(2)}) copy-start(bf16[1,1,2,2,512,128]{5,4,3,2,1,0:T(8,128)(2,1)S(1)} %get-tuple-element.90) | copy-start | bytes 1572868
  44.1 7.2 %copy-start.6 = (bf16[1,1,2,2,512,128]{5,4,3,2,1,0:T(8,128)(2,1)}, bf16[1,1,2,2,512,128]{5,4,3,2,1,0:T(8,128)(2,1)S(1)}, u32[]{:S(2)}) copy-start(bf16[1,1,2,2,512,128]{5,4,3,2,1,0:T(8,128)(2,1)S(1)} %get-tuple-element.84) | copy-start | bytes 1572868
  44.1 7.2 %copy-start.8 = (bf16[1,1,2,2,512,128]{5,4,3,2,1,0:T(8,128)(2,1)}, bf16[1,1,2,2,512,128]{5,4,3,2,1,0:T(8,128)(2,1)S(1)}, u32[]{:S(2)}) copy-start(bf16[1,1,2,2,512,128]{5,4,3,2,1,0:T(8,128)(2,1)S(1)} %get-tuple-element.85) | copy-start | bytes 1572868
  54.5 4.9 %copy-start.5 = (bf16[1,1,2,2,512,128]{5,4,3,2,1,0:T(8,128)(2,1)S(1)}, bf16[1,1,2,2,512,128]{5,4,3,2,1,0:T(8,128)(2,1)}, u32[]{:S(2)}) copy-start(bf16[1,1,2,2,512,128]{5,4,3,2,1,0:T(8,128)(2,1)} %copy-done.4) | copy-start | bytes 1572868
  65.4 11.2 %collective-permute-start.4 = (bf16[96,2048]{1,0:T(8,128)(2,1)S(1)}, bf16[96,2048]{1,0:T(8,128)(2,1)S(1)}, u32[]{:S(2)}, u32[]{:S(2)}) collective-permute-start(bf16[96,2048]{1,0:T(8,128)(2,1)S(1)} %constant_dynamic-update-slice_fusion), channel_id=1, source_target_pairs={{0,8},{4,12},{8,0},{12,4},{1,9},{5,13},{9,1},{13,5},{2,10},{6,14},... | collective-permute-start | bytes 1179656 | tf_op jit(solution)/shard_map/ppermute | solution.py:80
  76.7 2.4 %collective-permute-start.5 = (bf16[2,96,2048]{2,1,0:T(8,128)(2,1)S(1)}, bf16[2,96,2048]{2,1,0:T(8,128)(2,1)S(1)}, u32[]{:S(2)}, u32[]{:S(2)}) collective-permute-start(bf16[2,96,2048]{2,1,0:T(8,128)(2,1)S(1)} %pad_maximum_fusion.5), channel_id=1, source_target_pairs={{0,4},{4,0},{8,12},{12,8},{1,5},{5,1},{9,13},{13,9},{2,6},{6,2},{1... | collective-permute-start | bytes 2359304 | tf_op jit(solution)/shard_map/ppermute | solution.py:82
  88.3 12.4 %collective-permute-start.6 = (bf16[96,2048]{1,0:T(8,128)(2,1)S(1)}, bf16[96,2048]{1,0:T(8,128)(2,1)S(1)}, u32[]{:S(2)}, u32[]{:S(2)}) collective-permute-start(bf16[96,2048]{1,0:T(8,128)(2,1)S(1)} %get-tuple-element.75), channel_id=1, source_target_pairs={{0,1},{1,2},{2,3},{4,5},{5,6},{6,7},{8,9},{9,10},{10,11},{12,13},{... | collective-permute-start | bytes 1179656 | tf_op jit(solution)/shard_map/ppermute | solution.py:112
  92.1 14.3 %collective-permute-start.9 = (bf16[96,2048]{1,0:T(8,128)(2,1)S(1)}, bf16[96,2048]{1,0:T(8,128)(2,1)S(1)}, u32[]{:S(2)}, u32[]{:S(2)}) collective-permute-start(bf16[96,2048]{1,0:T(8,128)(2,1)S(1)} %get-tuple-element.76), channel_id=1, source_target_pairs={{1,0},{2,1},{3,2},{5,4},{6,5},{7,6},{9,8},{10,9},{11,10},{13,12},{... | collective-permute-start | bytes 1179656 | tf_op jit(solution)/shard_map/ppermute | solution.py:113
  101.9 12.2 %collective-permute-start.7 = (bf16[96,2048]{1,0:T(8,128)(2,1)S(1)}, bf16[96,2048]{1,0:T(8,128)(2,1)S(1)}, u32[]{:S(2)}, u32[]{:S(2)}) collective-permute-start(bf16[96,2048]{1,0:T(8,128)(2,1)S(1)} %fusion.44), channel_id=1, source_target_pairs={{0,1},{1,2},{2,3},{4,5},{5,6},{6,7},{8,9},{9,10},{10,11},{12,13},{... | collective-permute-start | bytes 1179656 | tf_op jit(solution)/shard_map/ppermute | solution.py:112
  115.7 12.0 %collective-permute-start.10 = (bf16[96,2048]{1,0:T(8,128)(2,1)S(1)}, bf16[96,2048]{1,0:T(8,128)(2,1)S(1)}, u32[]{:S(2)}, u32[]{:S(2)}) collective-permute-start(bf16[96,2048]{1,0:T(8,128)(2,1)S(1)} %get-tuple-element.74), channel_id=1, source_target_pairs={{1,0},{2,1},{3,2},{5,4},{6,5},{7,6},{9,8},{10,9},{11,10},{13,12},{... | collective-permute-start | bytes 1179656 | tf_op jit(solution)/shard_map/ppermute | solution.py:113
  117.0 13.3 %collective-permute-start.8 = (bf16[96,2048]{1,0:T(8,128)(2,1)S(1)}, bf16[96,2048]{1,0:T(8,128)(2,1)S(1)}, u32[]{:S(2)}, u32[]{:S(2)}) collective-permute-start(bf16[96,2048]{1,0:T(8,128)(2,1)S(1)} %get-tuple-element.73), channel_id=1, source_target_pairs={{0,1},{1,2},{2,3},{4,5},{5,6},{6,7},{8,9},{9,10},{10,11},{12,13},{... | collective-permute-start | bytes 1179656 | tf_op jit(solution)/shard_map/ppermute | solution.py:112
  128.9 10.7 %collective-permute-start.11 = (bf16[96,2048]{1,0:T(8,128)(2,1)S(1)}, bf16[96,2048]{1,0:T(8,128)(2,1)S(1)}, u32[]{:S(2)}, u32[]{:S(2)}) collective-permute-start(bf16[96,2048]{1,0:T(8,128)(2,1)S(1)} %fusion.43), channel_id=1, source_target_pairs={{1,0},{2,1},{3,2},{5,4},{6,5},{7,6},{9,8},{10,9},{11,10},{13,12},{... | collective-permute-start | bytes 1179656 | tf_op jit(solution)/shard_map/ppermute | solution.py:113
  141.6 8.6 %collective-permute-start.12 = (bf16[96,2048]{1,0:T(8,128)(2,1)S(1)}, bf16[96,2048]{1,0:T(8,128)(2,1)S(1)}, u32[]{:S(2)}, u32[]{:S(2)}) collective-permute-start(bf16[96,2048]{1,0:T(8,128)(2,1)S(1)} %get-tuple-element.57), channel_id=1, source_target_pairs={{0,1},{1,2},{2,3},{4,5},{5,6},{6,7},{8,9},{9,10},{10,11},{12,13},{... | collective-permute-start | bytes 1179656 | tf_op jit(solution)/shard_map/ppermute | solution.py:119
  145.0 9.9 %collective-permute-start.15 = (bf16[96,2048]{1,0:T(8,128)(2,1)S(1)}, bf16[96,2048]{1,0:T(8,128)(2,1)S(1)}, u32[]{:S(2)}, u32[]{:S(2)}) collective-permute-start(bf16[96,2048]{1,0:T(8,128)(2,1)S(1)} %get-tuple-element.57), channel_id=1, source_target_pairs={{1,0},{2,1},{3,2},{5,4},{6,5},{7,6},{9,8},{10,9},{11,10},{13,12},{... | collective-permute-start | bytes 1179656 | tf_op jit(solution)/shard_map/ppermute | solution.py:120
  150.3 10.9 %collective-permute-start.13 = (bf16[96,2048]{1,0:T(8,128)(2,1)S(1)}, bf16[96,2048]{1,0:T(8,128)(2,1)S(1)}, u32[]{:S(2)}, u32[]{:S(2)}) collective-permute-start(bf16[96,2048]{1,0:T(8,128)(2,1)S(1)} %collective-permute-done.12), channel_id=1, source_target_pairs={{0,1},{1,2},{2,3},{4,5},{5,6},{6,7},{8,9},{9,10},{10,11},{12,13},{... | collective-permute-start | bytes 1179656 | tf_op jit(solution)/shard_map/ppermute | solution.py:119
  154.9 10.8 %collective-permute-start.16 = (bf16[96,2048]{1,0:T(8,128)(2,1)S(1)}, bf16[96,2048]{1,0:T(8,128)(2,1)S(1)}, u32[]{:S(2)}, u32[]{:S(2)}) collective-permute-start(bf16[96,2048]{1,0:T(8,128)(2,1)S(1)} %collective-permute-done.15), channel_id=1, source_target_pairs={{1,0},{2,1},{3,2},{5,4},{6,5},{7,6},{9,8},{10,9},{11,10},{13,12},{... | collective-permute-start | bytes 1179656 | tf_op jit(solution)/shard_map/ppermute | solution.py:120
  161.1 9.7 %collective-permute-start.14 = (bf16[96,2048]{1,0:T(8,128)(2,1)S(1)}, bf16[96,2048]{1,0:T(8,128)(2,1)S(1)}, u32[]{:S(2)}, u32[]{:S(2)}) collective-permute-start(bf16[96,2048]{1,0:T(8,128)(2,1)S(1)} %collective-permute-done.13), channel_id=1, source_target_pairs={{0,1},{1,2},{2,3},{4,5},{5,6},{6,7},{8,9},{9,10},{10,11},{12,13},{... | collective-permute-start | bytes 1179656 | tf_op jit(solution)/shard_map/ppermute | solution.py:119
  165.8 9.7 %collective-permute-start.17 = (bf16[96,2048]{1,0:T(8,128)(2,1)S(1)}, bf16[96,2048]{1,0:T(8,128)(2,1)S(1)}, u32[]{:S(2)}, u32[]{:S(2)}) collective-permute-start(bf16[96,2048]{1,0:T(8,128)(2,1)S(1)} %collective-permute-done.16), channel_id=1, source_target_pairs={{1,0},{2,1},{3,2},{5,4},{6,5},{7,6},{9,8},{10,9},{11,10},{13,12},{... | collective-permute-start | bytes 1179656 | tf_op jit(solution)/shard_map/ppermute | solution.py:120
  (11 other events, 35.0 us)

commit v7 on v6

--- a/solution.py
+++ b/solution.py
@@ -188,22 +188,25 @@
         steps_count, samples_dev, kv_heads, group_size, head_depth
     ).transpose(2, 0, 1, 3, 4)
     prefill_state = empty_state(head_batch, span_dev * group_size, head_depth)
-    along_x, other_core = ctx_shards(jnp.stack([local_keys, local_values]), ctx_count)
-    arrived = jnp.concatenate([along_x, other_core], axis=0)
-    prompt_keys_all, prompt_values_all = (
-        jnp.concatenate([arrived[shard, member] for shard in range(ctx_count)], axis=2)
-        for member in range(2)
-    )
-    prefix_len = prompt_keys_all.shape[2]
-    key_rows = prompt_keys_all.reshape(head_batch, prefix_len, head_depth)
-    value_rows = prompt_values_all.reshape(head_batch, prefix_len, head_depth)
-    prefill_state = sweep(prefill_state, span_rows, key_rows, value_rows, 2048)
+    own_pages = jnp.stack([local_keys, local_values])
+    core_pairs = [(dev, dev ^ 1) for dev in range(ctx_count)]
+    near_pages = jnp.concatenate([own_pages, lax.ppermute(own_pages, "ctx", core_pairs)], axis=3)
+    along_x = [
+        lax.ppermute(own_pages, "ctx", [(dev, (dev - 2 * shift) % ctx_count) for dev in range(ctx_count)])
+        for shift in range(1, ctx_count // 2)
+    ]
+    far_pages = jnp.concatenate(along_x, axis=3)
+    far_pages = jnp.concatenate([far_pages, lax.ppermute(far_pages, "ctx", core_pairs)], axis=3)
     decode_flat = decode_five.reshape(kv_heads, -1, head_depth)
     decode_batch = jnp.broadcast_to(decode_flat[None], (prompts,) + decode_flat.shape).reshape(
         head_batch, -1, head_depth
     )
     decode_state = empty_state(head_batch, decode_flat.shape[1], head_depth)
-    decode_state = sweep(decode_state, decode_batch, key_rows, value_rows, 2048)
+    for pages in (near_pages, far_pages):
+        key_rows = pages[0].reshape(head_batch, -1, head_depth)
+        value_rows = pages[1].reshape(head_batch, -1, head_depth)
+        prefill_state = absorb(prefill_state, span_rows, key_rows, value_rows, None)
+        decode_state = absorb(decode_state, decode_batch, key_rows, value_rows, None)
     decode_state = sweep(decode_state, decode_batch, span_key_rows, span_value_rows, span_total)
     own_prompts = lax.dynamic_slice_in_dim(sample_prompt, ctx_index * samples_dev, samples_dev)
     chosen = (

time: 182 us -> 190 us (1.044)
  matrix products: 20.6 us -> 28.4 us
  other arithmetic: 18.6 us -> 21.6 us
    dot_general x4 -> x6, matrix products: 6.1 us -> 11.2 us  [absorb(): jnp.einsum('brd,bnd->brn', queries, key_rows, preferred_element_type=jnp....]
    reduce_sum x4 -> x6, other arithmetic: 6.44 us -> 9.7 us  [absorb(): running_sum = running_sum * factor + jnp.sum(weights, axis=-1)]
    ppermute x0 -> x3, starting transfers between devices: none -> 3.15 us  [the longest x1 2.94 us: shards(): lax.ppermute(own_pages, 'ctx', [(dev, (dev - 2 * shift) % ctx_count) for...]
    ppermute x3 -> x2, starting transfers between devices: 4.82 us -> 1.9 us  [ctx_shards(): received.append(lax.ppermute(block, 'ctx', pairs))]
    another operation x5 -> x3, other arithmetic: 2.73 us -> 0.1 us  [ctx_shards(): along_x = jnp.stack(received)]
    slice x3 -> x2, local copies, waits for them, and re-layouts: 2.83 us -> 0.27 us  [shards(): value_rows = pages[1].reshape(head_batch, -1, head_depth)]
    ppermute x3 -> x2, waiting for transfers between devices: 5.74 us -> 3.58 us  [ctx_shards(): lax.ppermute(along_x, 'ctx', [(dev, dev ^ 1) for dev in range(ctx_count)])]
    dot_general x4 -> x6, matrix products: 7.69 us -> 9.74 us  [absorb(): jnp.einsum('brn,bnd->brd', weights.astype(jnp.bfloat16), value_rows, pref...]
  transfers between devices with their start and end apart: 18 -> 19, of which waited for: 14 -> 14; matrix products, arithmetic and copies ran while one was open for 6% -> 9% of each run, Pallas kernels for 0% -> 0%
where the time goes in v7:
time: 190 us
  waiting for transfers between devices  80 us (42%)
  starting transfers between devices  38.4 us (20%)
  matrix products  28.4 us (15%)
  other arithmetic  21.6 us (11%)
  local copies, waits for them, and re-layouts  19.7 us (10%)
    ppermute x2, waiting for transfers between devices, ctx_shards(): received.append(lax.ppermute(block, 'ctx', pairs))  32.6 us
    ppermute x3, waiting for transfers between devices, head_sum_line(): lax.ppermute(going_right.astype(jnp.bfloat16), 'head', rightward)  15.1 us
    ppermute x3, waiting for transfers between devices, head_sum_line(): from_right = lax.ppermute(going_left.astype(jnp.bfloat16), 'head', leftward)  15 us
    ppermute x3, starting transfers between devices, head_sum_line(): lax.ppermute(going_right.astype(jnp.bfloat16), 'head', rightward)  13.2 us
    ppermute x3, starting transfers between devices, head_sum_line(): send_right = lax.ppermute(send_right, 'head', rightward)  12.2 us
    dot_general x6, matrix products, absorb(): jnp.einsum('brd,bnd->brn', queries, key_rows, preferred_element_type=jnp....  11.2 us
    ppermute x3, waiting for transfers between devices, head_sum_line(): send_right = lax.ppermute(send_right, 'head', rightward)  11.1 us
    dot_general x6, matrix products, absorb(): jnp.einsum('brn,bnd->brd', weights.astype(jnp.bfloat16), value_rows, pref...  9.74 us
  transfers between devices with their start and end apart: 19, of which 14 were waited for; matrix products, arithmetic and copies ran while one was open for 9% of the time, Pallas kernels for 0%

profile of v7, /device:TPU:0, one launch (start us, length us, event | category | flops | bytes accessed | tf_op | source)
XLA Modules:
  0.0 189.6 jit_solution(17795390253003861352)
XLA Ops:
  3.3 2.7 %gather_fusion.2 = bf16[8,128,2,128]{3,2,1,0:T(2,128)(2,1)S(1)} fusion(bf16[8,128,2,128]{3,2,1,0:T(2,128)(2,1)} %param.21, s32[1024]{0:T(1024)S(1)} %pad_clamp_fusion.1), kind=kCustom, calls=%fused_computation.1.clone | custom fusion | bytes 1048608 | tf_op jit(solution)/shard_map/jit(_take)/gather | solution.py:161
  8.2 2.9 %collective-permute-start.1 = (bf16[2,2,2,512,128]{4,3,2,1,0:T(8,128)(2,1)}, bf16[2,2,2,512,128]{4,3,2,1,0:T(8,128)(2,1)}, u32[]{:S(2)}, u32[]{:S(2)}) collective-permute-start(bf16[2,2,2,512,128]{4,3,2,1,0:T(8,128)(2,1)} %pad_maximum_fusion.2), channel_id=1, source_target_pairs={{0,8},{4,12},{8,0},{12,4},{1,9},{5,13},{9,1},{13,5},{2,10},{6,14},... | collective-permute-start | bytes 3145736 | tf_op jit(solution)/shard_map/ppermute | solution.py:195
  13.0 23.0 %collective-permute-done.3 = bf16[2,2,32,2,128]{4,2,3,1,0:T(8,128)(2,1)S(1)} collective-permute-done((bf16[2,2,32,2,128]{4,2,3,1,0:T(8,128)(2,1)S(1)}, bf16[2,2,32,2,128]{4,2,3,1,0:T(8,128)(2,1)S(1)}, u32[]{:S(2)}, u32[]{:S(2)}) %collective-permute-start.3) | collective-permute-done | bytes 65568 | tf_op jit(solution)/shard_map/ppermute | solution.py:80
  41.4 2.7 %bitcast_reduce_fusion.3 = (f32[4,256]{1,0:T(4,128)S(1)}, f32[4,1024,256]{2,1,0:T(8,128)}) fusion(bf16[4,1024,128]{2,1,0:T(8,128)(2,1)S(1)} %bitcast.258, bf16[4,256,128]{2,1,0:T(8,128)(2,1)S(1)} %bitcast.264), kind=kOutput, calls=%fused_computation.15 | convolution fusion | flops 270531584 | bytes 5509120 | tf_op jit(solution)/shard_map/brd,bnd->brn/dot_general | solution.py:14
  49.7 2.7 %bitcast_reduce_fusion = (f32[4,256]{1,0:T(4,128)S(1)}, f32[4,1024,256]{2,1,0:T(8,128)}) fusion(bf16[4,1024,128]{2,1,0:T(8,128)(2,1)S(1)} %bitcast.257, bf16[4,256,128]{2,1,0:T(8,128)(2,1)S(1)} %bitcast.262), kind=kOutput, calls=%fused_computation.6 | convolution fusion | flops 270531584 | bytes 5509120 | tf_op jit(solution)/shard_map/brd,bnd->brn/dot_general | solution.py:14
  54.1 3.0 %fusion.8 = f32[4,256]{1,0:T(4,128)S(1)} fusion(f32[4,1024,256]{2,1,0:T(8,128)} %get-tuple-element.66, f32[4,256]{1,0:T(4,128)S(1)} %get-tuple-element.41), kind=kLoop, calls=%fused_computation.19 | loop fusion | flops 3144704 | bytes 4202496 | tf_op jit(solution)/shard_map/reduce_sum | solution.py:22
  61.3 2.9 %fusion.12 = f32[4,256]{1,0:T(4,128)S(1)} fusion(f32[4,1024,256]{2,1,0:T(8,128)} %get-tuple-element.72, f32[4,256]{1,0:T(4,128)S(1)} %get-tuple-element.36), kind=kLoop, calls=%fused_computation.23 | loop fusion | flops 3144704 | bytes 4202496 | tf_op jit(solution)/shard_map/reduce_sum | solution.py:22
  64.4 2.9 %fusion.10 = f32[4,256]{1,0:T(4,128)S(1)} fusion(f32[4,1024,256]{2,1,0:T(8,128)} %get-tuple-element.74, f32[4,256]{1,0:T(4,128)S(1)} %get-tuple-element.58), kind=kLoop, calls=%fused_computation.21 | loop fusion | flops 3144704 | bytes 4202496 | tf_op jit(solution)/shard_map/reduce_sum | solution.py:22
  67.4 3.5 %fusion.45 = f32[4,256,128]{2,1,0:T(8,128)S(1)} fusion(bf16[4,1024,128]{2,1,0:T(8,128)(2,1)S(1)} %bitcast.255, f32[4,1024,256]{2,1,0:T(8,128)} %get-tuple-element.74, f32[4,256]{1,0:T(4,128)S(1)} %get-tuple-element.58, f32[4,256]{1,0:T(4,128)S(1)} %get-tuple-element.57, f32[4,256]{1,0:T(4,128)S(1)} %get-tuple-element.56), kind=kOutput, calls=%fused_computation.51 | convolution fusion | flops 271843328 | bytes 5779456 | tf_op jit(solution)/shard_map/brn,bnd->brd/dot_general | solution.py:23
  75.8 9.6 %collective-permute-done.5 = bf16[96,2048]{1,0:T(8,128)(2,1)S(1)} collective-permute-done((bf16[96,2048]{1,0:T(8,128)(2,1)S(1)}, bf16[96,2048]{1,0:T(8,128)(2,1)S(1)}, u32[]{:S(2)}, u32[]{:S(2)}) %collective-permute-start.5) | collective-permute-done | bytes 393248 | tf_op jit(solution)/shard_map/ppermute | solution.py:80
  89.4 5.9 %fusion = f32[4,96,2048]{2,1,0:T(8,128)S(1)} fusion(bf16[4,96,2048]{2,1,0:T(8,128)(2,1)S(1)} %bitcast.274, bf16[2048,2048]{1,0:T(8,128)(2,1)} %param.27), kind=kOutput, calls=%fused_computation.3 | convolution fusion | flops 3221225472 | bytes 13107200 | tf_op jit(solution)/shard_map/dot_general | solution.py:237
  97.0 3.8 %collective-permute-start.7 = (bf16[96,2048]{1,0:T(8,128)(2,1)S(1)}, bf16[96,2048]{1,0:T(8,128)(2,1)S(1)}, u32[]{:S(2)}, u32[]{:S(2)}) collective-permute-start(bf16[96,2048]{1,0:T(8,128)(2,1)S(1)} %get-tuple-element.46), channel_id=1, source_target_pairs={{0,1},{1,2},{2,3},{4,5},{5,6},{6,7},{8,9},{9,10},{10,11},{12,13},{... | collective-permute-start | bytes 1179656 | tf_op jit(solution)/shard_map/ppermute | solution.py:112
  102.1 7.3 %collective-permute-done.7 = bf16[96,2048]{1,0:T(8,128)(2,1)S(1)} collective-permute-done((bf16[96,2048]{1,0:T(8,128)(2,1)S(1)}, bf16[96,2048]{1,0:T(8,128)(2,1)S(1)}, u32[]{:S(2)}, u32[]{:S(2)}) %collective-permute-start.7) | collective-permute-done | bytes 393248 | tf_op jit(solution)/shard_map/ppermute | solution.py:112
  110.6 4.4 %collective-permute-start.8 = (bf16[96,2048]{1,0:T(8,128)(2,1)S(1)}, bf16[96,2048]{1,0:T(8,128)(2,1)S(1)}, u32[]{:S(2)}, u32[]{:S(2)}) collective-permute-start(bf16[96,2048]{1,0:T(8,128)(2,1)S(1)} %fusion.80), channel_id=1, source_target_pairs={{0,1},{1,2},{2,3},{4,5},{5,6},{6,7},{8,9},{9,10},{10,11},{12,13},{... | collective-permute-start | bytes 1179656 | tf_op jit(solution)/shard_map/ppermute | solution.py:112
  115.1 7.8 %collective-permute-done.8 = bf16[96,2048]{1,0:T(8,128)(2,1)S(1)} collective-permute-done((bf16[96,2048]{1,0:T(8,128)(2,1)S(1)}, bf16[96,2048]{1,0:T(8,128)(2,1)S(1)}, u32[]{:S(2)}, u32[]{:S(2)}) %collective-permute-start.8) | collective-permute-done | bytes 393248 | tf_op jit(solution)/shard_map/ppermute | solution.py:112
  125.7 5.0 %collective-permute-start.9 = (bf16[96,2048]{1,0:T(8,128)(2,1)S(1)}, bf16[96,2048]{1,0:T(8,128)(2,1)S(1)}, u32[]{:S(2)}, u32[]{:S(2)}) collective-permute-start(bf16[96,2048]{1,0:T(8,128)(2,1)S(1)} %get-tuple-element.44), channel_id=1, source_target_pairs={{0,1},{1,2},{2,3},{4,5},{5,6},{6,7},{8,9},{9,10},{10,11},{12,13},{... | collective-permute-start | bytes 1179656 | tf_op jit(solution)/shard_map/ppermute | solution.py:112
  130.8 5.7 %collective-permute-done.11 = bf16[96,2048]{1,0:T(8,128)(2,1)S(1)} collective-permute-done((bf16[96,2048]{1,0:T(8,128)(2,1)S(1)}, bf16[96,2048]{1,0:T(8,128)(2,1)S(1)}, u32[]{:S(2)}, u32[]{:S(2)}) %collective-permute-start.11) | collective-permute-done | bytes 393248 | tf_op jit(solution)/shard_map/ppermute | solution.py:113
  139.0 9.3 %collective-permute-done.12 = bf16[96,2048]{1,0:T(8,128)(2,1)S(1)} collective-permute-done((bf16[96,2048]{1,0:T(8,128)(2,1)S(1)}, bf16[96,2048]{1,0:T(8,128)(2,1)S(1)}, u32[]{:S(2)}, u32[]{:S(2)}) %collective-permute-start.12) | collective-permute-done | bytes 393248 | tf_op jit(solution)/shard_map/ppermute | solution.py:113
  150.3 3.4 %collective-permute-start.13 = (bf16[96,2048]{1,0:T(8,128)(2,1)S(1)}, bf16[96,2048]{1,0:T(8,128)(2,1)S(1)}, u32[]{:S(2)}, u32[]{:S(2)}) collective-permute-start(bf16[96,2048]{1,0:T(8,128)(2,1)S(1)} %get-tuple-element.29), channel_id=1, source_target_pairs={{0,1},{1,2},{2,3},{4,5},{5,6},{6,7},{8,9},{9,10},{10,11},{12,13},{... | collective-permute-start | bytes 1179656 | tf_op jit(solution)/shard_map/ppermute | solution.py:119
  155.1 3.9 %collective-permute-done.13 = bf16[96,2048]{1,0:T(8,128)(2,1)S(1)} collective-permute-done((bf16[96,2048]{1,0:T(8,128)(2,1)S(1)}, bf16[96,2048]{1,0:T(8,128)(2,1)S(1)}, u32[]{:S(2)}, u32[]{:S(2)}) %collective-permute-start.13) | collective-permute-done | bytes 393248 | tf_op jit(solution)/shard_map/ppermute | solution.py:119
  159.0 4.5 %collective-permute-start.14 = (bf16[96,2048]{1,0:T(8,128)(2,1)S(1)}, bf16[96,2048]{1,0:T(8,128)(2,1)S(1)}, u32[]{:S(2)}, u32[]{:S(2)}) collective-permute-start(bf16[96,2048]{1,0:T(8,128)(2,1)S(1)} %collective-permute-done.13), channel_id=1, source_target_pairs={{0,1},{1,2},{2,3},{4,5},{5,6},{6,7},{8,9},{9,10},{10,11},{12,13},{... | collective-permute-start | bytes 1179656 | tf_op jit(solution)/shard_map/ppermute | solution.py:119
  165.7 4.2 %collective-permute-done.14 = bf16[96,2048]{1,0:T(8,128)(2,1)S(1)} collective-permute-done((bf16[96,2048]{1,0:T(8,128)(2,1)S(1)}, bf16[96,2048]{1,0:T(8,128)(2,1)S(1)}, u32[]{:S(2)}, u32[]{:S(2)}) %collective-permute-start.14) | collective-permute-done | bytes 393248 | tf_op jit(solution)/shard_map/ppermute | solution.py:119
  169.8 4.4 %collective-permute-start.15 = (bf16[96,2048]{1,0:T(8,128)(2,1)S(1)}, bf16[96,2048]{1,0:T(8,128)(2,1)S(1)}, u32[]{:S(2)}, u32[]{:S(2)}) collective-permute-start(bf16[96,2048]{1,0:T(8,128)(2,1)S(1)} %collective-permute-done.14), channel_id=1, source_target_pairs={{0,1},{1,2},{2,3},{4,5},{5,6},{6,7},{8,9},{9,10},{10,11},{12,13},{... | collective-permute-start | bytes 1179656 | tf_op jit(solution)/shard_map/ppermute | solution.py:119
  176.5 3.0 %collective-permute-done.15 = bf16[96,2048]{1,0:T(8,128)(2,1)S(1)} collective-permute-done((bf16[96,2048]{1,0:T(8,128)(2,1)S(1)}, bf16[96,2048]{1,0:T(8,128)(2,1)S(1)}, u32[]{:S(2)}, u32[]{:S(2)}) %collective-permute-start.15) | collective-permute-done | bytes 393248 | tf_op jit(solution)/shard_map/ppermute | solution.py:119
  (142 shorter events, 59.7 us)
Async XLA Ops:
  1.7 9.5 %copy-start.9 = (bf16[2,32,2,128]{3,2,1,0:T(2,128)(2,1)S(1)}, bf16[2,32,2,128]{3,2,1,0:T(2,128)(2,1)}, u32[]{:S(2)}) copy-start(bf16[2,32,2,128]{3,2,1,0:T(2,128)(2,1)} %param.19) | copy-start | bytes 98308
  1.7 9.5 %copy-start.10 = (bf16[2,32,2,128]{3,2,1,0:T(2,128)(2,1)S(1)}, bf16[2,32,2,128]{3,2,1,0:T(2,128)(2,1)}, u32[]{:S(2)}) copy-start(bf16[2,32,2,128]{3,2,1,0:T(2,128)(2,1)} %param.18) | copy-start | bytes 98308
  1.7 9.6 %copy-start.8 = (bf16[4,8,16,128]{3,2,1,0:T(8,128)(2,1)S(1)}, bf16[4,8,16,128]{3,2,1,0:T(8,128)(2,1)}, u32[]{:S(2)}) copy-start(bf16[4,8,16,128]{3,2,1,0:T(8,128)(2,1)} %param.23) | copy-start | bytes 393220
  1.7 9.6 %copy-start.11 = (bf16[4,8,2,128]{3,2,1,0:T(2,128)(2,1)S(1)}, bf16[4,8,2,128]{3,2,1,0:T(2,128)(2,1)}, u32[]{:S(2)}) copy-start(bf16[4,8,2,128]{3,2,1,0:T(2,128)(2,1)} %param.24) | copy-start | bytes 49156
  3.3 9.5 %copy-start.6 = (bf16[2,32,16,128]{3,2,1,0:T(8,128)(2,1)S(1)}, bf16[2,32,16,128]{3,2,1,0:T(8,128)(2,1)}, u32[]{:S(2)}) copy-start(bf16[2,32,16,128]{3,2,1,0:T(8,128)(2,1)} %param.17) | copy-start | bytes 786436
  8.2 30.1 %collective-permute-start.1 = (bf16[2,2,2,512,128]{4,3,2,1,0:T(8,128)(2,1)}, bf16[2,2,2,512,128]{4,3,2,1,0:T(8,128)(2,1)}, u32[]{:S(2)}, u32[]{:S(2)}) collective-permute-start(bf16[2,2,2,512,128]{4,3,2,1,0:T(8,128)(2,1)} %pad_maximum_fusion.2), channel_id=1, source_target_pairs={{0,8},{4,12},{8,0},{12,4},{1,9},{5,13},{9,1},{13,5},{2,10},{6,14},... | collective-permute-start | bytes 3145736 | tf_op jit(solution)/shard_map/ppermute | solution.py:195
  11.2 27.4 %collective-permute-start = (bf16[2,2,2,512,128]{4,3,2,1,0:T(8,128)(2,1)}, bf16[2,2,2,512,128]{4,3,2,1,0:T(8,128)(2,1)}, u32[]{:S(2)}, u32[]{:S(2)}) collective-permute-start(bf16[2,2,2,512,128]{4,3,2,1,0:T(8,128)(2,1)} %pad_maximum_fusion.2), channel_id=1, source_target_pairs={{0,4},{4,0},{8,12},{12,8},{1,5},{5,1},{9,13},{13,9},{2,6},{6,2},{1... | collective-permute-start | bytes 3145736 | tf_op jit(solution)/shard_map/ppermute | solution.py:193
  11.2 24.7 %collective-permute-start.3 = (bf16[2,2,32,2,128]{4,2,3,1,0:T(8,128)(2,1)S(1)}, bf16[2,2,32,2,128]{4,2,3,1,0:T(8,128)(2,1)S(1)}, u32[]{:S(2)}, u32[]{:S(2)}) collective-permute-start(bf16[2,2,32,2,128]{4,2,3,1,0:T(8,128)(2,1)S(1)} %get-tuple-element.55), channel_id=1, source_target_pairs={{0,8},{4,12},{8,0},{12,4},{1,9},{5,13},{9,1},{13,5},{2,10},{6,14},... | collective-permute-start | bytes 196616 | tf_op jit(solution)/shard_map/ppermute | solution.py:80
  36.0 1.4 collective-permute-start.4
  38.4 8.4 %collective-permute-start.2 = (bf16[2,2,2,512,128]{4,3,2,1,0:T(8,128)(2,1)}, bf16[2,2,2,512,128]{4,3,2,1,0:T(8,128)(2,1)S(1)}, u32[]{:S(2)}, u32[]{:S(2)}) collective-permute-start(bf16[2,2,2,512,128]{4,3,2,1,0:T(8,128)(2,1)} %collective-permute-done.1), channel_id=1, source_target_pairs={{0,4},{4,0},{8,12},{12,8},{1,5},{5,1},{9,13},{13,9},{2,6},{6,2},{1... | collective-permute-start | bytes 3145736 | tf_op jit(solution)/shard_map/ppermute | solution.py:199
  73.9 11.5 %collective-permute-start.5 = (bf16[96,2048]{1,0:T(8,128)(2,1)S(1)}, bf16[96,2048]{1,0:T(8,128)(2,1)S(1)}, u32[]{:S(2)}, u32[]{:S(2)}) collective-permute-start(bf16[96,2048]{1,0:T(8,128)(2,1)S(1)} %constant_dynamic-update-slice_fusion.2), channel_id=1, source_target_pairs={{0,8},{4,12},{8,0},{12,4},{1,9},{5,13},{9,1},{13,5},{2,10},{6,14},... | collective-permute-start | bytes 1179656 | tf_op jit(solution)/shard_map/ppermute | solution.py:80
  85.5 2.4 %collective-permute-start.6 = (bf16[2,96,2048]{2,1,0:T(8,128)(2,1)S(1)}, bf16[2,96,2048]{2,1,0:T(8,128)(2,1)S(1)}, u32[]{:S(2)}, u32[]{:S(2)}) collective-permute-start(bf16[2,96,2048]{2,1,0:T(8,128)(2,1)S(1)} %pad_maximum_fusion.3), channel_id=1, source_target_pairs={{0,4},{4,0},{8,12},{12,8},{1,5},{5,1},{9,13},{13,9},{2,6},{6,2},{1... | collective-permute-start | bytes 2359304 | tf_op jit(solution)/shard_map/ppermute | solution.py:82
  97.0 12.4 %collective-permute-start.7 = (bf16[96,2048]{1,0:T(8,128)(2,1)S(1)}, bf16[96,2048]{1,0:T(8,128)(2,1)S(1)}, u32[]{:S(2)}, u32[]{:S(2)}) collective-permute-start(bf16[96,2048]{1,0:T(8,128)(2,1)S(1)} %get-tuple-element.46), channel_id=1, source_target_pairs={{0,1},{1,2},{2,3},{4,5},{5,6},{6,7},{8,9},{9,10},{10,11},{12,13},{... | collective-permute-start | bytes 1179656 | tf_op jit(solution)/shard_map/ppermute | solution.py:112
  100.8 14.3 %collective-permute-start.10 = (bf16[96,2048]{1,0:T(8,128)(2,1)S(1)}, bf16[96,2048]{1,0:T(8,128)(2,1)S(1)}, u32[]{:S(2)}, u32[]{:S(2)}) collective-permute-start(bf16[96,2048]{1,0:T(8,128)(2,1)S(1)} %get-tuple-element.47), channel_id=1, source_target_pairs={{1,0},{2,1},{3,2},{5,4},{6,5},{7,6},{9,8},{10,9},{11,10},{13,12},{... | collective-permute-start | bytes 1179656 | tf_op jit(solution)/shard_map/ppermute | solution.py:113
  110.6 12.2 %collective-permute-start.8 = (bf16[96,2048]{1,0:T(8,128)(2,1)S(1)}, bf16[96,2048]{1,0:T(8,128)(2,1)S(1)}, u32[]{:S(2)}, u32[]{:S(2)}) collective-permute-start(bf16[96,2048]{1,0:T(8,128)(2,1)S(1)} %fusion.80), channel_id=1, source_target_pairs={{0,1},{1,2},{2,3},{4,5},{5,6},{6,7},{8,9},{9,10},{10,11},{12,13},{... | collective-permute-start | bytes 1179656 | tf_op jit(solution)/shard_map/ppermute | solution.py:112
  124.4 12.0 %collective-permute-start.11 = (bf16[96,2048]{1,0:T(8,128)(2,1)S(1)}, bf16[96,2048]{1,0:T(8,128)(2,1)S(1)}, u32[]{:S(2)}, u32[]{:S(2)}) collective-permute-start(bf16[96,2048]{1,0:T(8,128)(2,1)S(1)} %get-tuple-element.45), channel_id=1, source_target_pairs={{1,0},{2,1},{3,2},{5,4},{6,5},{7,6},{9,8},{10,9},{11,10},{13,12},{... | collective-permute-start | bytes 1179656 | tf_op jit(solution)/shard_map/ppermute | solution.py:113
  125.7 13.3 %collective-permute-start.9 = (bf16[96,2048]{1,0:T(8,128)(2,1)S(1)}, bf16[96,2048]{1,0:T(8,128)(2,1)S(1)}, u32[]{:S(2)}, u32[]{:S(2)}) collective-permute-start(bf16[96,2048]{1,0:T(8,128)(2,1)S(1)} %get-tuple-element.44), channel_id=1, source_target_pairs={{0,1},{1,2},{2,3},{4,5},{5,6},{6,7},{8,9},{9,10},{10,11},{12,13},{... | collective-permute-start | bytes 1179656 | tf_op jit(solution)/shard_map/ppermute | solution.py:112
  137.7 10.7 %collective-permute-start.12 = (bf16[96,2048]{1,0:T(8,128)(2,1)S(1)}, bf16[96,2048]{1,0:T(8,128)(2,1)S(1)}, u32[]{:S(2)}, u32[]{:S(2)}) collective-permute-start(bf16[96,2048]{1,0:T(8,128)(2,1)S(1)} %fusion.79), channel_id=1, source_target_pairs={{1,0},{2,1},{3,2},{5,4},{6,5},{7,6},{9,8},{10,9},{11,10},{13,12},{... | collective-permute-start | bytes 1179656 | tf_op jit(solution)/shard_map/ppermute | solution.py:113
  150.3 8.6 %collective-permute-start.13 = (bf16[96,2048]{1,0:T(8,128)(2,1)S(1)}, bf16[96,2048]{1,0:T(8,128)(2,1)S(1)}, u32[]{:S(2)}, u32[]{:S(2)}) collective-permute-start(bf16[96,2048]{1,0:T(8,128)(2,1)S(1)} %get-tuple-element.29), channel_id=1, source_target_pairs={{0,1},{1,2},{2,3},{4,5},{5,6},{6,7},{8,9},{9,10},{10,11},{12,13},{... | collective-permute-start | bytes 1179656 | tf_op jit(solution)/shard_map/ppermute | solution.py:119
  153.7 9.9 %collective-permute-start.16 = (bf16[96,2048]{1,0:T(8,128)(2,1)S(1)}, bf16[96,2048]{1,0:T(8,128)(2,1)S(1)}, u32[]{:S(2)}, u32[]{:S(2)}) collective-permute-start(bf16[96,2048]{1,0:T(8,128)(2,1)S(1)} %get-tuple-element.29), channel_id=1, source_target_pairs={{1,0},{2,1},{3,2},{5,4},{6,5},{7,6},{9,8},{10,9},{11,10},{13,12},{... | collective-permute-start | bytes 1179656 | tf_op jit(solution)/shard_map/ppermute | solution.py:120
  159.0 10.9 %collective-permute-start.14 = (bf16[96,2048]{1,0:T(8,128)(2,1)S(1)}, bf16[96,2048]{1,0:T(8,128)(2,1)S(1)}, u32[]{:S(2)}, u32[]{:S(2)}) collective-permute-start(bf16[96,2048]{1,0:T(8,128)(2,1)S(1)} %collective-permute-done.13), channel_id=1, source_target_pairs={{0,1},{1,2},{2,3},{4,5},{5,6},{6,7},{8,9},{9,10},{10,11},{12,13},{... | collective-permute-start | bytes 1179656 | tf_op jit(solution)/shard_map/ppermute | solution.py:119
  163.6 10.8 %collective-permute-start.17 = (bf16[96,2048]{1,0:T(8,128)(2,1)S(1)}, bf16[96,2048]{1,0:T(8,128)(2,1)S(1)}, u32[]{:S(2)}, u32[]{:S(2)}) collective-permute-start(bf16[96,2048]{1,0:T(8,128)(2,1)S(1)} %collective-permute-done.16), channel_id=1, source_target_pairs={{1,0},{2,1},{3,2},{5,4},{6,5},{7,6},{9,8},{10,9},{11,10},{13,12},{... | collective-permute-start | bytes 1179656 | tf_op jit(solution)/shard_map/ppermute | solution.py:120
  169.8 9.7 %collective-permute-start.15 = (bf16[96,2048]{1,0:T(8,128)(2,1)S(1)}, bf16[96,2048]{1,0:T(8,128)(2,1)S(1)}, u32[]{:S(2)}, u32[]{:S(2)}) collective-permute-start(bf16[96,2048]{1,0:T(8,128)(2,1)S(1)} %collective-permute-done.14), channel_id=1, source_target_pairs={{0,1},{1,2},{2,3},{4,5},{5,6},{6,7},{8,9},{9,10},{10,11},{12,13},{... | collective-permute-start | bytes 1179656 | tf_op jit(solution)/shard_map/ppermute | solution.py:119
  174.5 9.7 %collective-permute-start.18 = (bf16[96,2048]{1,0:T(8,128)(2,1)S(1)}, bf16[96,2048]{1,0:T(8,128)(2,1)S(1)}, u32[]{:S(2)}, u32[]{:S(2)}) collective-permute-start(bf16[96,2048]{1,0:T(8,128)(2,1)S(1)} %collective-permute-done.17), channel_id=1, source_target_pairs={{1,0},{2,1},{3,2},{5,4},{6,5},{7,6},{9,8},{10,9},{11,10},{13,12},{... | collective-permute-start | bytes 1179656 | tf_op jit(solution)/shard_map/ppermute | solution.py:120
  (9 other events, 28.5 us)

commit v8 on v6

--- a/solution.py
+++ b/solution.py
@@ -151,16 +151,14 @@
     samples_dev = decode_query.shape[1]
     head_batch = prompts * kv_heads
     ctx_index = lax.axis_index("ctx")
-    slot_rows = page_table.reshape(-1)
-    local_keys = (
-        jnp.take(prefix_key, slot_rows, axis=0)
-        .reshape(prompts, -1, kv_heads, head_depth)
-        .transpose(0, 2, 1, 3)
-    )
-    local_values = (
-        jnp.take(prefix_value, slot_rows, axis=0)
-        .reshape(prompts, -1, kv_heads, head_depth)
-        .transpose(0, 2, 1, 3)
+    slot_pick = (
+        page_table[:, :, None] == jnp.arange(prefix_key.shape[0], dtype=jnp.int32)
+    ).astype(prefix_key.dtype)
+    local_keys, local_values = (
+        jnp.einsum("pjs,sqkd->pkjqd", slot_pick, pages, preferred_element_type=jnp.float32)
+        .astype(pages.dtype)
+        .reshape(prompts, kv_heads, -1, head_depth)
+        for pages in (prefix_key, prefix_value)
     )
     span_rows = (
         span_query.reshape(prompts, span_dev, kv_heads, group_size, head_depth)

time: 182 us -> 179 us (0.984)
  local copies, waits for them, and re-layouts: 20.2 us -> 14.1 us
  matrix products: 20.6 us -> 25 us
  waiting for transfers between devices: 81.3 us -> 79 us
    gather x2 -> x0, local copies, waits for them, and re-layouts: 4.24 us -> none  [the longest x1 2.64 us: shards(): jnp.take(prefix_value, slot_rows, axis=0)]
    dot_general x0 -> x2, matrix products: none -> 3.1 us  [shards(): jnp.einsum('pjs,sqkd->pkjqd', slot_pick, pages, preferred_element_type=jn...]
    ppermute x3, waiting for transfers between devices: 31.7 us -> 29.6 us  [ctx_shards(): received.append(lax.ppermute(block, 'ctx', pairs))]
    unnamed x40 -> x38, local copies, waits for them, and re-layouts: 5.87 us -> 4.07 us
  transfers between devices with their start and end apart: 18 -> 18, of which waited for: 14 -> 14; matrix products, arithmetic and copies ran while one was open for 6% -> 8% of each run, Pallas kernels for 0% -> 0%
where the time goes in v8:
time: 179 us
  waiting for transfers between devices  79 us (44%)
  starting transfers between devices  40 us (22%)
  matrix products  25 us (14%)
  other arithmetic  18.9 us (11%)
  local copies, waits for them, and re-layouts  14.1 us (8%)
    ppermute x3, waiting for transfers between devices, ctx_shards(): received.append(lax.ppermute(block, 'ctx', pairs))  29.6 us
    ppermute x3, waiting for transfers between devices, head_sum_line(): from_right = lax.ppermute(going_left.astype(jnp.bfloat16), 'head', leftward)  15.7 us
    ppermute x3, starting transfers between devices, head_sum_line(): lax.ppermute(going_right.astype(jnp.bfloat16), 'head', rightward)  14.6 us
    ppermute x3, waiting for transfers between devices, head_sum_line(): lax.ppermute(going_right.astype(jnp.bfloat16), 'head', rightward)  14.3 us
    ppermute x3, starting transfers between devices, head_sum_line(): send_right = lax.ppermute(send_right, 'head', rightward)  12.2 us
    ppermute x3, waiting for transfers between devices, head_sum_line(): send_right = lax.ppermute(send_right, 'head', rightward)  11 us
    dot_general x4, matrix products, absorb(): jnp.einsum('brn,bnd->brd', weights.astype(jnp.bfloat16), value_rows, pref...  7.71 us
    reduce_sum x4, other arithmetic, absorb(): running_sum = running_sum * factor + jnp.sum(weights, axis=-1)  6.41 us
  transfers between devices with their start and end apart: 18, of which 14 were waited for; matrix products, arithmetic and copies ran while one was open for 8% of the time, Pallas kernels for 0%

profile of v8, /device:TPU:0, one launch (start us, length us, event | category | flops | bytes accessed | tf_op | source)
XLA Modules:
  0.0 178.5 jit_solution(7754824097295286219)
XLA Ops:
  4.1 3.0 %collective-permute-start = (bf16[2,2,2,512,128]{4,3,2,1,0:T(8,128)(2,1)S(1)}, bf16[2,2,2,512,128]{4,3,2,1,0:T(8,128)(2,1)S(1)}, u32[]{:S(2)}, u32[]{:S(2)}) collective-permute-start(bf16[2,2,2,512,128]{4,3,2,1,0:T(8,128)(2,1)S(1)} %get-tuple-element.92), channel_id=1, source_target_pairs={{0,8},{4,12},{8,0},{12,4},{1,9},{5,13},{9,1},{13,5},{2,10},{6,14},... | collective-permute-start | bytes 3145736 | tf_op jit(solution)/shard_map/ppermute | solution.py:80
  10.9 20.2 %collective-permute-done = bf16[2,2,2,512,128]{4,3,2,1,0:T(8,128)(2,1)S(1)} collective-permute-done((bf16[2,2,2,512,128]{4,3,2,1,0:T(8,128)(2,1)S(1)}, bf16[2,2,2,512,128]{4,3,2,1,0:T(8,128)(2,1)S(1)}, u32[]{:S(2)}, u32[]{:S(2)}) %collective-permute-start) | collective-permute-done | bytes 1048608 | tf_op jit(solution)/shard_map/ppermute | solution.py:80
  33.4 3.5 %collective-permute-done.3 = bf16[2,2,2,32,2,128]{5,3,4,2,1,0:T(8,128)(2,1)S(1)} collective-permute-done((bf16[2,2,2,32,2,128]{5,3,4,2,1,0:T(8,128)(2,1)S(1)}, bf16[2,2,2,32,2,128]{5,3,4,2,1,0:T(8,128)(2,1)S(1)}, u32[]{:S(2)}, u32[]{:S(2)}) %collective-permute-start.3) | collective-permute-done | bytes 131104 | tf_op jit(solution)/shard_map/ppermute | solution.py:82
  41.4 4.0 %bitcast_reduce_fusion = (f32[4,256]{1,0:T(4,128)S(1)}, f32[4,2048,256]{2,1,0:T(8,128)}) fusion(bf16[4,256,128]{2,1,0:T(8,128)(2,1)S(1)} %bitcast.238, bf16[4,512,128]{2,1,0:T(8,128)(2,1)S(1)} %bitcast.260, bf16[4,512,128]{2,1,0:T(8,128)(2,1)S(1)} %bitcast.262, bf16[4,512,128]{2,1,0:T(8,128)(2,1)S(1)} %bitcast.252, bf16[4,512,128]{2,1,0:T(8,128)(2,1)S(1)} %bitcast.248), kind=kOutput, calls=%fused_computation.4 | convolution fusion | flops 549452800 | bytes 10752000 | tf_op jit(solution)/shard_map/while/body/eval_jaxpr/brd,bnd->brn/dot_general | solution.py:14
  46.9 2.5 %fusion.31 = f32[4,256,128]{2,1,0:T(8,128)S(1)} fusion(f32[4,2048,256]{2,1,0:T(8,128)S(1)} %get-tuple-element.105, f32[4,256]{1,0:T(4,128)S(1)} %get-tuple-element.103, bf16[4,512,128]{2,1,0:T(8,128)(2,1)S(1)} %bitcast.257, bf16[4,512,128]{2,1,0:T(8,128)(2,1)S(1)} %bitcast.255, bf16[4,512,128]{2,1,0:T(8,128)(2,1)S(1)} %bitcast.249, ...), kind=kOutput, calls=%fused_computation.45 | convolution fusion | flops 551813120 | bytes 11022336 | tf_op jit(solution)/shard_map/while/body/eval_jaxpr/brn,bnd->brd/dot_general | solution.py:23
  50.1 4.8 %fusion.6 = f32[4,256]{1,0:T(4,128)S(1)} fusion(f32[4,2048,256]{2,1,0:T(8,128)} %get-tuple-element.111, f32[4,256]{1,0:T(4,128)S(1)} %get-tuple-element.100), kind=kLoop, calls=%fused_computation.11 | loop fusion | flops 6290432 | bytes 8396800 | tf_op jit(solution)/shard_map/while/body/eval_jaxpr/reduce_sum | solution.py:22
  54.9 4.6 %fusion.28 = f32[4,256,128]{2,1,0:T(8,128)S(1)} fusion(f32[4,2048,256]{2,1,0:T(8,128)} %get-tuple-element.111, f32[4,256]{1,0:T(4,128)S(1)} %get-tuple-element.100, bf16[4,512,128]{2,1,0:T(8,128)(2,1)S(1)} %bitcast.258, bf16[4,512,128]{2,1,0:T(8,128)(2,1)S(1)} %bitcast.256, bf16[4,512,128]{2,1,0:T(8,128)(2,1)S(1)} %bitcast.250, ...), kind=kOutput, calls=%fused_computation.44 | convolution fusion | flops 551813120 | bytes 11022336 | tf_op jit(solution)/shard_map/while/body/eval_jaxpr/brn,bnd->brd/dot_general | solution.py:23
  62.9 9.4 %collective-permute-done.4 = bf16[96,2048]{1,0:T(8,128)(2,1)S(1)} collective-permute-done((bf16[96,2048]{1,0:T(8,128)(2,1)S(1)}, bf16[96,2048]{1,0:T(8,128)(2,1)S(1)}, u32[]{:S(2)}, u32[]{:S(2)}) %collective-permute-start.4) | collective-permute-done | bytes 393248 | tf_op jit(solution)/shard_map/ppermute | solution.py:80
  76.3 5.9 %fusion = f32[4,96,2048]{2,1,0:T(8,128)S(1)} fusion(bf16[4,96,2048]{2,1,0:T(8,128)(2,1)S(1)} %bitcast.232, bf16[2048,2048]{1,0:T(8,128)(2,1)} %param.25), kind=kOutput, calls=%fused_computation.1 | convolution fusion | flops 3221225472 | bytes 13107200 | tf_op jit(solution)/shard_map/dot_general | solution.py:232
  83.0 4.5 %collective-permute-start.6 = (bf16[96,2048]{1,0:T(8,128)(2,1)}, bf16[96,2048]{1,0:T(8,128)(2,1)}, u32[]{:S(2)}, u32[]{:S(2)}) collective-permute-start(bf16[96,2048]{1,0:T(8,128)(2,1)} %get-tuple-element.74), channel_id=1, source_target_pairs={{0,1},{1,2},{2,3},{4,5},{5,6},{6,7},{8,9},{9,10},{10,11},{12,13},{... | collective-permute-start | bytes 1179656 | tf_op jit(solution)/shard_map/ppermute | solution.py:112
  88.8 6.9 %collective-permute-done.6 = bf16[96,2048]{1,0:T(8,128)(2,1)} collective-permute-done((bf16[96,2048]{1,0:T(8,128)(2,1)}, bf16[96,2048]{1,0:T(8,128)(2,1)}, u32[]{:S(2)}, u32[]{:S(2)}) %collective-permute-start.6) | collective-permute-done | bytes 393248 | tf_op jit(solution)/shard_map/ppermute | solution.py:112
  97.6 5.1 %collective-permute-start.7 = (bf16[96,2048]{1,0:T(8,128)(2,1)}, bf16[96,2048]{1,0:T(8,128)(2,1)}, u32[]{:S(2)}, u32[]{:S(2)}) collective-permute-start(bf16[96,2048]{1,0:T(8,128)(2,1)} %fusion.46), channel_id=1, source_target_pairs={{0,1},{1,2},{2,3},{4,5},{5,6},{6,7},{8,9},{9,10},{10,11},{12,13},{... | collective-permute-start | bytes 1179656 | tf_op jit(solution)/shard_map/ppermute | solution.py:112
  102.7 7.4 %collective-permute-done.7 = bf16[96,2048]{1,0:T(8,128)(2,1)} collective-permute-done((bf16[96,2048]{1,0:T(8,128)(2,1)}, bf16[96,2048]{1,0:T(8,128)(2,1)}, u32[]{:S(2)}, u32[]{:S(2)}) %collective-permute-start.7) | collective-permute-done | bytes 393248 | tf_op jit(solution)/shard_map/ppermute | solution.py:112
  113.6 5.0 %collective-permute-start.8 = (bf16[96,2048]{1,0:T(8,128)(2,1)}, bf16[96,2048]{1,0:T(8,128)(2,1)S(1)}, u32[]{:S(2)}, u32[]{:S(2)}) collective-permute-start(bf16[96,2048]{1,0:T(8,128)(2,1)} %get-tuple-element.72), channel_id=1, source_target_pairs={{0,1},{1,2},{2,3},{4,5},{5,6},{6,7},{8,9},{9,10},{10,11},{12,13},{... | collective-permute-start | bytes 1179656 | tf_op jit(solution)/shard_map/ppermute | solution.py:112
  118.6 6.0 %collective-permute-done.10 = bf16[96,2048]{1,0:T(8,128)(2,1)} collective-permute-done((bf16[96,2048]{1,0:T(8,128)(2,1)}, bf16[96,2048]{1,0:T(8,128)(2,1)}, u32[]{:S(2)}, u32[]{:S(2)}) %collective-permute-start.10) | collective-permute-done | bytes 393248 | tf_op jit(solution)/shard_map/ppermute | solution.py:113
  127.7 9.7 %collective-permute-done.11 = bf16[96,2048]{1,0:T(8,128)(2,1)} collective-permute-done((bf16[96,2048]{1,0:T(8,128)(2,1)}, bf16[96,2048]{1,0:T(8,128)(2,1)}, u32[]{:S(2)}, u32[]{:S(2)}) %collective-permute-start.11) | collective-permute-done | bytes 393248 | tf_op jit(solution)/shard_map/ppermute | solution.py:113
  139.3 3.4 %collective-permute-start.12 = (bf16[96,2048]{1,0:T(8,128)(2,1)S(1)}, bf16[96,2048]{1,0:T(8,128)(2,1)S(1)}, u32[]{:S(2)}, u32[]{:S(2)}) collective-permute-start(bf16[96,2048]{1,0:T(8,128)(2,1)S(1)} %get-tuple-element.56), channel_id=1, source_target_pairs={{0,1},{1,2},{2,3},{4,5},{5,6},{6,7},{8,9},{9,10},{10,11},{12,13},{... | collective-permute-start | bytes 1179656 | tf_op jit(solution)/shard_map/ppermute | solution.py:119
  144.0 3.9 %collective-permute-done.12 = bf16[96,2048]{1,0:T(8,128)(2,1)S(1)} collective-permute-done((bf16[96,2048]{1,0:T(8,128)(2,1)S(1)}, bf16[96,2048]{1,0:T(8,128)(2,1)S(1)}, u32[]{:S(2)}, u32[]{:S(2)}) %collective-permute-start.12) | collective-permute-done | bytes 393248 | tf_op jit(solution)/shard_map/ppermute | solution.py:119
  147.9 4.5 %collective-permute-start.13 = (bf16[96,2048]{1,0:T(8,128)(2,1)S(1)}, bf16[96,2048]{1,0:T(8,128)(2,1)S(1)}, u32[]{:S(2)}, u32[]{:S(2)}) collective-permute-start(bf16[96,2048]{1,0:T(8,128)(2,1)S(1)} %collective-permute-done.12), channel_id=1, source_target_pairs={{0,1},{1,2},{2,3},{4,5},{5,6},{6,7},{8,9},{9,10},{10,11},{12,13},{... | collective-permute-start | bytes 1179656 | tf_op jit(solution)/shard_map/ppermute | solution.py:119
  154.6 4.2 %collective-permute-done.13 = bf16[96,2048]{1,0:T(8,128)(2,1)S(1)} collective-permute-done((bf16[96,2048]{1,0:T(8,128)(2,1)S(1)}, bf16[96,2048]{1,0:T(8,128)(2,1)S(1)}, u32[]{:S(2)}, u32[]{:S(2)}) %collective-permute-start.13) | collective-permute-done | bytes 393248 | tf_op jit(solution)/shard_map/ppermute | solution.py:119
  158.8 4.4 %collective-permute-start.14 = (bf16[96,2048]{1,0:T(8,128)(2,1)S(1)}, bf16[96,2048]{1,0:T(8,128)(2,1)S(1)}, u32[]{:S(2)}, u32[]{:S(2)}) collective-permute-start(bf16[96,2048]{1,0:T(8,128)(2,1)S(1)} %collective-permute-done.13), channel_id=1, source_target_pairs={{0,1},{1,2},{2,3},{4,5},{5,6},{6,7},{8,9},{9,10},{10,11},{12,13},{... | collective-permute-start | bytes 1179656 | tf_op jit(solution)/shard_map/ppermute | solution.py:119
  165.5 3.0 %collective-permute-done.14 = bf16[96,2048]{1,0:T(8,128)(2,1)S(1)} collective-permute-done((bf16[96,2048]{1,0:T(8,128)(2,1)S(1)}, bf16[96,2048]{1,0:T(8,128)(2,1)S(1)}, u32[]{:S(2)}, u32[]{:S(2)}) %collective-permute-start.14) | collective-permute-done | bytes 393248 | tf_op jit(solution)/shard_map/ppermute | solution.py:119
  170.8 2.3 %collective-permute-done.17 = bf16[96,2048]{1,0:T(8,128)(2,1)S(1)} collective-permute-done((bf16[96,2048]{1,0:T(8,128)(2,1)S(1)}, bf16[96,2048]{1,0:T(8,128)(2,1)S(1)}, u32[]{:S(2)}, u32[]{:S(2)}) %collective-permute-start.17) | collective-permute-done | bytes 393248 | tf_op jit(solution)/shard_map/ppermute | solution.py:120
  173.9 2.4 %gather_fusion = bf16[4,96,2048]{2,1,0:T(8,128)(2,1)S(1)} fusion(bf16[7,96,2048]{2,1,0:T(8,128)(2,1)} %bitcast_dynamic-update-slice_fusion, s32[1024]{0:T(1024)S(1)} %pad_clamp_fusion), kind=kCustom, calls=%fused_computation | custom fusion | bytes 3145744 | tf_op jit(solution)/shard_map/jit(_take)/gather | solution.py:130
  (130 shorter events, 46.7 us)
Async XLA Ops:
  0.6 60.0 %copy-start = (bf16[4,8,2,128]{3,2,1,0:T(2,128)(2,1)S(1)}, bf16[4,8,2,128]{3,2,1,0:T(2,128)(2,1)}, u32[]{:S(2)}) copy-start(bf16[4,8,2,128]{3,2,1,0:T(2,128)(2,1)} %param.23) | copy-start | bytes 49156
  2.3 5.5 %copy-start.9 = (bf16[4,8,16,128]{3,2,1,0:T(8,128)(2,1)S(1)}, bf16[4,8,16,128]{3,2,1,0:T(8,128)(2,1)}, u32[]{:S(2)}) copy-start(bf16[4,8,16,128]{3,2,1,0:T(8,128)(2,1)} %param.21) | copy-start | bytes 393220
  2.3 5.5 %copy-start.14 = (bf16[4,8,2,128]{3,2,1,0:T(2,128)(2,1)S(1)}, bf16[4,8,2,128]{3,2,1,0:T(2,128)(2,1)}, u32[]{:S(2)}) copy-start(bf16[4,8,2,128]{3,2,1,0:T(2,128)(2,1)} %param.22) | copy-start | bytes 49156
  4.1 26.9 %collective-permute-start = (bf16[2,2,2,512,128]{4,3,2,1,0:T(8,128)(2,1)S(1)}, bf16[2,2,2,512,128]{4,3,2,1,0:T(8,128)(2,1)S(1)}, u32[]{:S(2)}, u32[]{:S(2)}) collective-permute-start(bf16[2,2,2,512,128]{4,3,2,1,0:T(8,128)(2,1)S(1)} %get-tuple-element.92), channel_id=1, source_target_pairs={{0,8},{4,12},{8,0},{12,4},{1,9},{5,13},{9,1},{13,5},{2,10},{6,14},... | collective-permute-start | bytes 3145736 | tf_op jit(solution)/shard_map/ppermute | solution.py:80
  7.8 25.0 %collective-permute-start.2 = (bf16[2,2,32,2,128]{4,2,3,1,0:T(8,128)(2,1)}, bf16[2,2,32,2,128]{4,2,3,1,0:T(8,128)(2,1)S(1)}, u32[]{:S(2)}, u32[]{:S(2)}) collective-permute-start(bf16[2,2,32,2,128]{4,2,3,1,0:T(8,128)(2,1)} %get-tuple-element.96), channel_id=1, source_target_pairs={{0,8},{4,12},{8,0},{12,4},{1,9},{5,13},{9,1},{13,5},{2,10},{6,14},... | collective-permute-start | bytes 196616 | tf_op jit(solution)/shard_map/ppermute | solution.py:80
  9.8 22.8 %copy-start.7 = (bf16[2,32,16,128]{3,2,1,0:T(8,128)(2,1)S(1)}, bf16[2,32,16,128]{3,2,1,0:T(8,128)(2,1)}, u32[]{:S(2)}) copy-start(bf16[2,32,16,128]{3,2,1,0:T(8,128)(2,1)} %param.15) | copy-start | bytes 786436
  32.5 5.4 %collective-permute-start.1 = (bf16[2,2,2,2,512,128]{5,4,3,2,1,0:T(8,128)(2,1)}, bf16[2,2,2,2,512,128]{5,4,3,2,1,0:T(8,128)(2,1)}, u32[]{:S(2)}, u32[]{:S(2)}) collective-permute-start(bf16[2,2,2,2,512,128]{5,4,3,2,1,0:T(8,128)(2,1)} %pad_maximum_fusion), channel_id=1, source_target_pairs={{0,4},{4,0},{8,12},{12,8},{1,5},{5,1},{9,13},{13,9},{2,6},{6,2},{1... | collective-permute-start | bytes 6291464 | tf_op jit(solution)/shard_map/ppermute | solution.py:82
  32.8 4.0 %collective-permute-start.3 = (bf16[2,2,2,32,2,128]{5,3,4,2,1,0:T(8,128)(2,1)S(1)}, bf16[2,2,2,32,2,128]{5,3,4,2,1,0:T(8,128)(2,1)S(1)}, u32[]{:S(2)}, u32[]{:S(2)}) collective-permute-start(bf16[2,2,2,32,2,128]{5,3,4,2,1,0:T(8,128)(2,1)S(1)} %pad_maximum_fusion.11), channel_id=1, source_target_pairs={{0,4},{4,0},{8,12},{12,8},{1,5},{5,1},{9,13},{13,9},{2,6},{6,2},{1... | collective-permute-start | bytes 393224 | tf_op jit(solution)/shard_map/ppermute | solution.py:82
  39.7 7.2 %copy-start.3 = (bf16[1,1,2,2,512,128]{5,4,3,2,1,0:T(8,128)(2,1)}, bf16[1,1,2,2,512,128]{5,4,3,2,1,0:T(8,128)(2,1)S(1)}, u32[]{:S(2)}) copy-start(bf16[1,1,2,2,512,128]{5,4,3,2,1,0:T(8,128)(2,1)S(1)} %get-tuple-element.76) | copy-start | bytes 1572868
  39.7 7.2 %copy-start.5 = (bf16[1,1,2,2,512,128]{5,4,3,2,1,0:T(8,128)(2,1)}, bf16[1,1,2,2,512,128]{5,4,3,2,1,0:T(8,128)(2,1)S(1)}, u32[]{:S(2)}) copy-start(bf16[1,1,2,2,512,128]{5,4,3,2,1,0:T(8,128)(2,1)S(1)} %get-tuple-element.84) | copy-start | bytes 1572868
  61.1 11.2 %collective-permute-start.4 = (bf16[96,2048]{1,0:T(8,128)(2,1)S(1)}, bf16[96,2048]{1,0:T(8,128)(2,1)S(1)}, u32[]{:S(2)}, u32[]{:S(2)}) collective-permute-start(bf16[96,2048]{1,0:T(8,128)(2,1)S(1)} %constant_dynamic-update-slice_fusion), channel_id=1, source_target_pairs={{0,8},{4,12},{8,0},{12,4},{1,9},{5,13},{9,1},{13,5},{2,10},{6,14},... | collective-permute-start | bytes 1179656 | tf_op jit(solution)/shard_map/ppermute | solution.py:80
  72.4 2.4 %collective-permute-start.5 = (bf16[2,96,2048]{2,1,0:T(8,128)(2,1)S(1)}, bf16[2,96,2048]{2,1,0:T(8,128)(2,1)S(1)}, u32[]{:S(2)}, u32[]{:S(2)}) collective-permute-start(bf16[2,96,2048]{2,1,0:T(8,128)(2,1)S(1)} %pad_maximum_fusion.5), channel_id=1, source_target_pairs={{0,4},{4,0},{8,12},{12,8},{1,5},{5,1},{9,13},{13,9},{2,6},{6,2},{1... | collective-permute-start | bytes 2359304 | tf_op jit(solution)/shard_map/ppermute | solution.py:82
  83.0 12.7 %collective-permute-start.6 = (bf16[96,2048]{1,0:T(8,128)(2,1)}, bf16[96,2048]{1,0:T(8,128)(2,1)}, u32[]{:S(2)}, u32[]{:S(2)}) collective-permute-start(bf16[96,2048]{1,0:T(8,128)(2,1)} %get-tuple-element.74), channel_id=1, source_target_pairs={{0,1},{1,2},{2,3},{4,5},{5,6},{6,7},{8,9},{9,10},{10,11},{12,13},{... | collective-permute-start | bytes 1179656 | tf_op jit(solution)/shard_map/ppermute | solution.py:112
  87.5 15.2 %collective-permute-start.9 = (bf16[96,2048]{1,0:T(8,128)(2,1)S(1)}, bf16[96,2048]{1,0:T(8,128)(2,1)}, u32[]{:S(2)}, u32[]{:S(2)}) collective-permute-start(bf16[96,2048]{1,0:T(8,128)(2,1)S(1)} %get-tuple-element.75), channel_id=1, source_target_pairs={{1,0},{2,1},{3,2},{5,4},{6,5},{7,6},{9,8},{10,9},{11,10},{13,12},{... | collective-permute-start | bytes 1179656 | tf_op jit(solution)/shard_map/ppermute | solution.py:113
  97.6 12.5 %collective-permute-start.7 = (bf16[96,2048]{1,0:T(8,128)(2,1)}, bf16[96,2048]{1,0:T(8,128)(2,1)}, u32[]{:S(2)}, u32[]{:S(2)}) collective-permute-start(bf16[96,2048]{1,0:T(8,128)(2,1)} %fusion.46), channel_id=1, source_target_pairs={{0,1},{1,2},{2,3},{4,5},{5,6},{6,7},{8,9},{9,10},{10,11},{12,13},{... | collective-permute-start | bytes 1179656 | tf_op jit(solution)/shard_map/ppermute | solution.py:112
  112.3 12.4 %collective-permute-start.10 = (bf16[96,2048]{1,0:T(8,128)(2,1)}, bf16[96,2048]{1,0:T(8,128)(2,1)}, u32[]{:S(2)}, u32[]{:S(2)}) collective-permute-start(bf16[96,2048]{1,0:T(8,128)(2,1)} %get-tuple-element.73), channel_id=1, source_target_pairs={{1,0},{2,1},{3,2},{5,4},{6,5},{7,6},{9,8},{10,9},{11,10},{13,12},{... | collective-permute-start | bytes 1179656 | tf_op jit(solution)/shard_map/ppermute | solution.py:113
  113.6 14.2 %collective-permute-start.8 = (bf16[96,2048]{1,0:T(8,128)(2,1)}, bf16[96,2048]{1,0:T(8,128)(2,1)S(1)}, u32[]{:S(2)}, u32[]{:S(2)}) collective-permute-start(bf16[96,2048]{1,0:T(8,128)(2,1)} %get-tuple-element.72), channel_id=1, source_target_pairs={{0,1},{1,2},{2,3},{4,5},{5,6},{6,7},{8,9},{9,10},{10,11},{12,13},{... | collective-permute-start | bytes 1179656 | tf_op jit(solution)/shard_map/ppermute | solution.py:112
  126.4 11.0 %collective-permute-start.11 = (bf16[96,2048]{1,0:T(8,128)(2,1)}, bf16[96,2048]{1,0:T(8,128)(2,1)}, u32[]{:S(2)}, u32[]{:S(2)}) collective-permute-start(bf16[96,2048]{1,0:T(8,128)(2,1)} %fusion.45), channel_id=1, source_target_pairs={{1,0},{2,1},{3,2},{5,4},{6,5},{7,6},{9,8},{10,9},{11,10},{13,12},{... | collective-permute-start | bytes 1179656 | tf_op jit(solution)/shard_map/ppermute | solution.py:113
  139.3 8.6 %collective-permute-start.12 = (bf16[96,2048]{1,0:T(8,128)(2,1)S(1)}, bf16[96,2048]{1,0:T(8,128)(2,1)S(1)}, u32[]{:S(2)}, u32[]{:S(2)}) collective-permute-start(bf16[96,2048]{1,0:T(8,128)(2,1)S(1)} %get-tuple-element.56), channel_id=1, source_target_pairs={{0,1},{1,2},{2,3},{4,5},{5,6},{6,7},{8,9},{9,10},{10,11},{12,13},{... | collective-permute-start | bytes 1179656 | tf_op jit(solution)/shard_map/ppermute | solution.py:119
  142.7 9.9 %collective-permute-start.15 = (bf16[96,2048]{1,0:T(8,128)(2,1)S(1)}, bf16[96,2048]{1,0:T(8,128)(2,1)S(1)}, u32[]{:S(2)}, u32[]{:S(2)}) collective-permute-start(bf16[96,2048]{1,0:T(8,128)(2,1)S(1)} %get-tuple-element.56), channel_id=1, source_target_pairs={{1,0},{2,1},{3,2},{5,4},{6,5},{7,6},{9,8},{10,9},{11,10},{13,12},{... | collective-permute-start | bytes 1179656 | tf_op jit(solution)/shard_map/ppermute | solution.py:120
  147.9 10.9 %collective-permute-start.13 = (bf16[96,2048]{1,0:T(8,128)(2,1)S(1)}, bf16[96,2048]{1,0:T(8,128)(2,1)S(1)}, u32[]{:S(2)}, u32[]{:S(2)}) collective-permute-start(bf16[96,2048]{1,0:T(8,128)(2,1)S(1)} %collective-permute-done.12), channel_id=1, source_target_pairs={{0,1},{1,2},{2,3},{4,5},{5,6},{6,7},{8,9},{9,10},{10,11},{12,13},{... | collective-permute-start | bytes 1179656 | tf_op jit(solution)/shard_map/ppermute | solution.py:119
  152.6 10.8 %collective-permute-start.16 = (bf16[96,2048]{1,0:T(8,128)(2,1)S(1)}, bf16[96,2048]{1,0:T(8,128)(2,1)S(1)}, u32[]{:S(2)}, u32[]{:S(2)}) collective-permute-start(bf16[96,2048]{1,0:T(8,128)(2,1)S(1)} %collective-permute-done.15), channel_id=1, source_target_pairs={{1,0},{2,1},{3,2},{5,4},{6,5},{7,6},{9,8},{10,9},{11,10},{13,12},{... | collective-permute-start | bytes 1179656 | tf_op jit(solution)/shard_map/ppermute | solution.py:120
  158.8 9.7 %collective-permute-start.14 = (bf16[96,2048]{1,0:T(8,128)(2,1)S(1)}, bf16[96,2048]{1,0:T(8,128)(2,1)S(1)}, u32[]{:S(2)}, u32[]{:S(2)}) collective-permute-start(bf16[96,2048]{1,0:T(8,128)(2,1)S(1)} %collective-permute-done.13), channel_id=1, source_target_pairs={{0,1},{1,2},{2,3},{4,5},{5,6},{6,7},{8,9},{9,10},{10,11},{12,13},{... | collective-permute-start | bytes 1179656 | tf_op jit(solution)/shard_map/ppermute | solution.py:119
  163.4 9.7 %collective-permute-start.17 = (bf16[96,2048]{1,0:T(8,128)(2,1)S(1)}, bf16[96,2048]{1,0:T(8,128)(2,1)S(1)}, u32[]{:S(2)}, u32[]{:S(2)}) collective-permute-start(bf16[96,2048]{1,0:T(8,128)(2,1)S(1)} %collective-permute-done.16), channel_id=1, source_target_pairs={{1,0},{2,1},{3,2},{5,4},{6,5},{7,6},{9,8},{10,9},{11,10},{13,12},{... | collective-permute-start | bytes 1179656 | tf_op jit(solution)/shard_map/ppermute | solution.py:120
  (10 other events, 27.9 us)

commit v9 on v8

--- a/solution.py
+++ b/solution.py
@@ -154,11 +154,15 @@
     slot_pick = (
         page_table[:, :, None] == jnp.arange(prefix_key.shape[0], dtype=jnp.int32)
     ).astype(prefix_key.dtype)
-    local_keys, local_values = (
-        jnp.einsum("pjs,sqkd->pkjqd", slot_pick, pages, preferred_element_type=jnp.float32)
-        .astype(pages.dtype)
-        .reshape(prompts, kv_heads, -1, head_depth)
-        for pages in (prefix_key, prefix_value)
+    own_pages = (
+        jnp.einsum(
+            "pjs,msqkd->mpkjqd",
+            slot_pick,
+            jnp.stack([prefix_key, prefix_value]),
+            preferred_element_type=jnp.float32,
+        )
+        .astype(prefix_key.dtype)
+        .reshape(2, prompts, kv_heads, -1, head_depth)
     )
     span_rows = (
         span_query.reshape(prompts, span_dev, kv_heads, group_size, head_depth)
@@ -186,7 +190,7 @@
         steps_count, samples_dev, kv_heads, group_size, head_depth
     ).transpose(2, 0, 1, 3, 4)
     prefill_state = empty_state(head_batch, span_dev * group_size, head_depth)
-    along_x, other_core = ctx_shards(jnp.stack([local_keys, local_values]), ctx_count)
+    along_x, other_core = ctx_shards(own_pages, ctx_count)
     arrived = jnp.concatenate([along_x, other_core], axis=0)
     prompt_keys_all, prompt_values_all = (
         jnp.concatenate([arrived[shard, member] for shard in range(ctx_count)], axis=2)

time: 179 us -> 180 us (level)
  matrix products: 25 us -> 22.1 us
  local copies, waits for them, and re-layouts: 14.1 us -> 16.5 us
  waiting for transfers between devices: 79 us -> 81 us
    another operation x0 -> x1, local copies, waits for them, and re-layouts: none -> 2.44 us  [shards(): jnp.stack([prefix_key, prefix_value])]
    ppermute x3, waiting for transfers between devices: 29.6 us -> 31.5 us  [ctx_shards(): received.append(lax.ppermute(block, 'ctx', pairs))]
    unnamed x38 -> x30, local copies, waits for them, and re-layouts: 4.07 us -> 3.96 us
  transfers between devices with their start and end apart: 18 -> 18, of which waited for: 14 -> 14; matrix products, arithmetic and copies ran while one was open for 8% -> 7% of each run, Pallas kernels for 0% -> 0%
where the time goes in v9:
time: 180 us; the launch traced here: 179 us
  waiting for transfers between devices  81 us (45%)
  starting transfers between devices  40.1 us (22%)
  matrix products  22.1 us (12%)
  other arithmetic  18.1 us (10%)
  local copies, waits for them, and re-layouts  16.5 us (9%)
    ppermute x3, waiting for transfers between devices, ctx_shards(): received.append(lax.ppermute(block, 'ctx', pairs))  31.5 us
    ppermute x3, waiting for transfers between devices, head_sum_line(): from_right = lax.ppermute(going_left.astype(jnp.bfloat16), 'head', leftward)  15.7 us
    ppermute x3, starting transfers between devices, head_sum_line(): lax.ppermute(going_right.astype(jnp.bfloat16), 'head', rightward)  14.6 us
    ppermute x3, waiting for transfers between devices, head_sum_line(): lax.ppermute(going_right.astype(jnp.bfloat16), 'head', rightward)  14.3 us
    ppermute x3, starting transfers between devices, head_sum_line(): send_right = lax.ppermute(send_right, 'head', rightward)  12.2 us
    ppermute x3, waiting for transfers between devices, head_sum_line(): send_right = lax.ppermute(send_right, 'head', rightward)  11 us
    dot_general x4, matrix products, absorb(): jnp.einsum('brn,bnd->brd', weights.astype(jnp.bfloat16), value_rows, pref...  7.7 us
    reduce_sum x4, other arithmetic, absorb(): running_sum = running_sum * factor + jnp.sum(weights, axis=-1)  6.41 us
  transfers between devices with their start and end apart: 18, of which 14 were waited for; matrix products, arithmetic and copies ran while one was open for 7% of the time, Pallas kernels for 0%

profile of v9, /device:TPU:0, one launch (start us, length us, event | category | flops | bytes accessed | tf_op | source)
XLA Modules:
  0.0 179.2 jit_solution(5714643591866387372)
XLA Ops:
  0.7 2.4 %copy_bitcast_fusion.1 = (bf16[1,8,128,2,128]{4,1,3,2,0:T(8,128)(2,1)S(1)}, bf16[1,8,128,2,128]{4,1,3,2,0:T(8,128)(2,1)S(1)}) fusion(bf16[8,128,2,128]{3,2,1,0:T(2,128)(2,1)} %param.19, bf16[8,128,2,128]{3,2,1,0:T(2,128)(2,1)} %param.18), kind=kLoop, calls=%fused_computation.77 | loop fusion | bytes 2097152 | tf_op jit(solution)/shard_map/stack | solution.py:161
  4.9 3.0 %collective-permute-start = (bf16[2,2,2,512,128]{4,3,2,1,0:T(8,128)(2,1)S(1)}, bf16[2,2,2,512,128]{4,3,2,1,0:T(8,128)(2,1)S(1)}, u32[]{:S(2)}, u32[]{:S(2)}) collective-permute-start(bf16[2,2,2,512,128]{4,3,2,1,0:T(8,128)(2,1)S(1)} %bitcast.222), channel_id=1, source_target_pairs={{0,8},{4,12},{8,0},{12,4},{1,9},{5,13},{9,1},{13,5},{2,10},{6,14},... | collective-permute-start | bytes 3145736 | tf_op jit(solution)/shard_map/ppermute | solution.py:80
  9.6 22.1 %collective-permute-done = bf16[2,2,2,512,128]{4,3,2,1,0:T(8,128)(2,1)S(1)} collective-permute-done((bf16[2,2,2,512,128]{4,3,2,1,0:T(8,128)(2,1)S(1)}, bf16[2,2,2,512,128]{4,3,2,1,0:T(8,128)(2,1)S(1)}, u32[]{:S(2)}, u32[]{:S(2)}) %collective-permute-start) | collective-permute-done | bytes 1048608 | tf_op jit(solution)/shard_map/ppermute | solution.py:80
  34.1 3.5 %collective-permute-done.3 = bf16[2,2,2,32,2,128]{5,3,4,2,1,0:T(8,128)(2,1)S(1)} collective-permute-done((bf16[2,2,2,32,2,128]{5,3,4,2,1,0:T(8,128)(2,1)S(1)}, bf16[2,2,2,32,2,128]{5,3,4,2,1,0:T(8,128)(2,1)S(1)}, u32[]{:S(2)}, u32[]{:S(2)}) %collective-permute-start.3) | collective-permute-done | bytes 131104 | tf_op jit(solution)/shard_map/ppermute | solution.py:82
  42.3 4.0 %bitcast_reduce_fusion = (f32[4,256]{1,0:T(4,128)S(1)}, f32[4,2048,256]{2,1,0:T(8,128)}) fusion(bf16[4,256,128]{2,1,0:T(8,128)(2,1)S(1)} %bitcast.237, bf16[4,512,128]{2,1,0:T(8,128)(2,1)S(1)} %bitcast.259, bf16[4,512,128]{2,1,0:T(8,128)(2,1)S(1)} %bitcast.261, bf16[4,512,128]{2,1,0:T(8,128)(2,1)S(1)} %bitcast.251, bf16[4,512,128]{2,1,0:T(8,128)(2,1)S(1)} %bitcast.247), kind=kOutput, calls=%fused_computation.4 | convolution fusion | flops 549452800 | bytes 10752000 | tf_op jit(solution)/shard_map/while/body/eval_jaxpr/brd,bnd->brn/dot_general | solution.py:14
  47.8 2.5 %fusion.30 = f32[4,256,128]{2,1,0:T(8,128)S(1)} fusion(f32[4,2048,256]{2,1,0:T(8,128)S(1)} %get-tuple-element.103, f32[4,256]{1,0:T(4,128)S(1)} %get-tuple-element.101, bf16[4,512,128]{2,1,0:T(8,128)(2,1)S(1)} %bitcast.256, bf16[4,512,128]{2,1,0:T(8,128)(2,1)S(1)} %bitcast.254, bf16[4,512,128]{2,1,0:T(8,128)(2,1)S(1)} %bitcast.248, ...), kind=kOutput, calls=%fused_computation.43 | convolution fusion | flops 551813120 | bytes 11022336 | tf_op jit(solution)/shard_map/while/body/eval_jaxpr/brn,bnd->brd/dot_general | solution.py:23
  50.9 4.8 %fusion.6 = f32[4,256]{1,0:T(4,128)S(1)} fusion(f32[4,2048,256]{2,1,0:T(8,128)} %get-tuple-element.109, f32[4,256]{1,0:T(4,128)S(1)} %get-tuple-element.98), kind=kLoop, calls=%fused_computation.11 | loop fusion | flops 6290432 | bytes 8396800 | tf_op jit(solution)/shard_map/while/body/eval_jaxpr/reduce_sum | solution.py:22
  55.8 4.6 %fusion.27 = f32[4,256,128]{2,1,0:T(8,128)S(1)} fusion(f32[4,2048,256]{2,1,0:T(8,128)} %get-tuple-element.109, f32[4,256]{1,0:T(4,128)S(1)} %get-tuple-element.98, bf16[4,512,128]{2,1,0:T(8,128)(2,1)S(1)} %bitcast.257, bf16[4,512,128]{2,1,0:T(8,128)(2,1)S(1)} %bitcast.255, bf16[4,512,128]{2,1,0:T(8,128)(2,1)S(1)} %bitcast.249, ...), kind=kOutput, calls=%fused_computation.42 | convolution fusion | flops 551813120 | bytes 11022336 | tf_op jit(solution)/shard_map/while/body/eval_jaxpr/brn,bnd->brd/dot_general | solution.py:23
  63.6 9.4 %collective-permute-done.4 = bf16[96,2048]{1,0:T(8,128)(2,1)S(1)} collective-permute-done((bf16[96,2048]{1,0:T(8,128)(2,1)S(1)}, bf16[96,2048]{1,0:T(8,128)(2,1)S(1)}, u32[]{:S(2)}, u32[]{:S(2)}) %collective-permute-start.4) | collective-permute-done | bytes 393248 | tf_op jit(solution)/shard_map/ppermute | solution.py:80
  77.1 5.9 %fusion = f32[4,96,2048]{2,1,0:T(8,128)S(1)} fusion(bf16[4,96,2048]{2,1,0:T(8,128)(2,1)S(1)} %bitcast.231, bf16[2048,2048]{1,0:T(8,128)(2,1)} %param.25), kind=kOutput, calls=%fused_computation.1 | convolution fusion | flops 3221225472 | bytes 13107200 | tf_op jit(solution)/shard_map/dot_general | solution.py:236
  83.8 4.5 %collective-permute-start.6 = (bf16[96,2048]{1,0:T(8,128)(2,1)}, bf16[96,2048]{1,0:T(8,128)(2,1)}, u32[]{:S(2)}, u32[]{:S(2)}) collective-permute-start(bf16[96,2048]{1,0:T(8,128)(2,1)} %get-tuple-element.74), channel_id=1, source_target_pairs={{0,1},{1,2},{2,3},{4,5},{5,6},{6,7},{8,9},{9,10},{10,11},{12,13},{... | collective-permute-start | bytes 1179656 | tf_op jit(solution)/shard_map/ppermute | solution.py:112
  89.6 6.9 %collective-permute-done.6 = bf16[96,2048]{1,0:T(8,128)(2,1)} collective-permute-done((bf16[96,2048]{1,0:T(8,128)(2,1)}, bf16[96,2048]{1,0:T(8,128)(2,1)}, u32[]{:S(2)}, u32[]{:S(2)}) %collective-permute-start.6) | collective-permute-done | bytes 393248 | tf_op jit(solution)/shard_map/ppermute | solution.py:112
  98.3 5.1 %collective-permute-start.7 = (bf16[96,2048]{1,0:T(8,128)(2,1)}, bf16[96,2048]{1,0:T(8,128)(2,1)}, u32[]{:S(2)}, u32[]{:S(2)}) collective-permute-start(bf16[96,2048]{1,0:T(8,128)(2,1)} %fusion.47), channel_id=1, source_target_pairs={{0,1},{1,2},{2,3},{4,5},{5,6},{6,7},{8,9},{9,10},{10,11},{12,13},{... | collective-permute-start | bytes 1179656 | tf_op jit(solution)/shard_map/ppermute | solution.py:112
  103.4 7.4 %collective-permute-done.7 = bf16[96,2048]{1,0:T(8,128)(2,1)} collective-permute-done((bf16[96,2048]{1,0:T(8,128)(2,1)}, bf16[96,2048]{1,0:T(8,128)(2,1)}, u32[]{:S(2)}, u32[]{:S(2)}) %collective-permute-start.7) | collective-permute-done | bytes 393248 | tf_op jit(solution)/shard_map/ppermute | solution.py:112
  114.3 5.0 %collective-permute-start.8 = (bf16[96,2048]{1,0:T(8,128)(2,1)}, bf16[96,2048]{1,0:T(8,128)(2,1)S(1)}, u32[]{:S(2)}, u32[]{:S(2)}) collective-permute-start(bf16[96,2048]{1,0:T(8,128)(2,1)} %get-tuple-element.72), channel_id=1, source_target_pairs={{0,1},{1,2},{2,3},{4,5},{5,6},{6,7},{8,9},{9,10},{10,11},{12,13},{... | collective-permute-start | bytes 1179656 | tf_op jit(solution)/shard_map/ppermute | solution.py:112
  119.3 6.0 %collective-permute-done.10 = bf16[96,2048]{1,0:T(8,128)(2,1)} collective-permute-done((bf16[96,2048]{1,0:T(8,128)(2,1)}, bf16[96,2048]{1,0:T(8,128)(2,1)}, u32[]{:S(2)}, u32[]{:S(2)}) %collective-permute-start.10) | collective-permute-done | bytes 393248 | tf_op jit(solution)/shard_map/ppermute | solution.py:113
  128.5 9.7 %collective-permute-done.11 = bf16[96,2048]{1,0:T(8,128)(2,1)} collective-permute-done((bf16[96,2048]{1,0:T(8,128)(2,1)}, bf16[96,2048]{1,0:T(8,128)(2,1)}, u32[]{:S(2)}, u32[]{:S(2)}) %collective-permute-start.11) | collective-permute-done | bytes 393248 | tf_op jit(solution)/shard_map/ppermute | solution.py:113
  140.0 3.4 %collective-permute-start.12 = (bf16[96,2048]{1,0:T(8,128)(2,1)S(1)}, bf16[96,2048]{1,0:T(8,128)(2,1)S(1)}, u32[]{:S(2)}, u32[]{:S(2)}) collective-permute-start(bf16[96,2048]{1,0:T(8,128)(2,1)S(1)} %get-tuple-element.56), channel_id=1, source_target_pairs={{0,1},{1,2},{2,3},{4,5},{5,6},{6,7},{8,9},{9,10},{10,11},{12,13},{... | collective-permute-start | bytes 1179656 | tf_op jit(solution)/shard_map/ppermute | solution.py:119
  144.7 3.9 %collective-permute-done.12 = bf16[96,2048]{1,0:T(8,128)(2,1)S(1)} collective-permute-done((bf16[96,2048]{1,0:T(8,128)(2,1)S(1)}, bf16[96,2048]{1,0:T(8,128)(2,1)S(1)}, u32[]{:S(2)}, u32[]{:S(2)}) %collective-permute-start.12) | collective-permute-done | bytes 393248 | tf_op jit(solution)/shard_map/ppermute | solution.py:119
  148.7 4.5 %collective-permute-start.13 = (bf16[96,2048]{1,0:T(8,128)(2,1)S(1)}, bf16[96,2048]{1,0:T(8,128)(2,1)S(1)}, u32[]{:S(2)}, u32[]{:S(2)}) collective-permute-start(bf16[96,2048]{1,0:T(8,128)(2,1)S(1)} %collective-permute-done.12), channel_id=1, source_target_pairs={{0,1},{1,2},{2,3},{4,5},{5,6},{6,7},{8,9},{9,10},{10,11},{12,13},{... | collective-permute-start | bytes 1179656 | tf_op jit(solution)/shard_map/ppermute | solution.py:119
  155.4 4.2 %collective-permute-done.13 = bf16[96,2048]{1,0:T(8,128)(2,1)S(1)} collective-permute-done((bf16[96,2048]{1,0:T(8,128)(2,1)S(1)}, bf16[96,2048]{1,0:T(8,128)(2,1)S(1)}, u32[]{:S(2)}, u32[]{:S(2)}) %collective-permute-start.13) | collective-permute-done | bytes 393248 | tf_op jit(solution)/shard_map/ppermute | solution.py:119
  159.5 4.4 %collective-permute-start.14 = (bf16[96,2048]{1,0:T(8,128)(2,1)S(1)}, bf16[96,2048]{1,0:T(8,128)(2,1)S(1)}, u32[]{:S(2)}, u32[]{:S(2)}) collective-permute-start(bf16[96,2048]{1,0:T(8,128)(2,1)S(1)} %collective-permute-done.13), channel_id=1, source_target_pairs={{0,1},{1,2},{2,3},{4,5},{5,6},{6,7},{8,9},{9,10},{10,11},{12,13},{... | collective-permute-start | bytes 1179656 | tf_op jit(solution)/shard_map/ppermute | solution.py:119
  166.2 3.0 %collective-permute-done.14 = bf16[96,2048]{1,0:T(8,128)(2,1)S(1)} collective-permute-done((bf16[96,2048]{1,0:T(8,128)(2,1)S(1)}, bf16[96,2048]{1,0:T(8,128)(2,1)S(1)}, u32[]{:S(2)}, u32[]{:S(2)}) %collective-permute-start.14) | collective-permute-done | bytes 393248 | tf_op jit(solution)/shard_map/ppermute | solution.py:119
  174.6 2.4 %gather_fusion = bf16[4,96,2048]{2,1,0:T(8,128)(2,1)S(1)} fusion(bf16[7,96,2048]{2,1,0:T(8,128)(2,1)} %bitcast_dynamic-update-slice_fusion, s32[1024]{0:T(1024)S(1)} %pad_clamp_fusion), kind=kCustom, calls=%fused_computation | custom fusion | bytes 3145744 | tf_op jit(solution)/shard_map/jit(_take)/gather | solution.py:130
  (120 shorter events, 45.4 us)
Async XLA Ops:
  0.6 60.8 %copy-start = (bf16[4,8,2,128]{3,2,1,0:T(2,128)(2,1)S(1)}, bf16[4,8,2,128]{3,2,1,0:T(2,128)(2,1)}, u32[]{:S(2)}) copy-start(bf16[4,8,2,128]{3,2,1,0:T(2,128)(2,1)} %param.23) | copy-start | bytes 49156
  0.6 7.2 %copy-start.8 = (bf16[2,32,2,128]{3,2,1,0:T(2,128)(2,1)S(1)}, bf16[2,32,2,128]{3,2,1,0:T(2,128)(2,1)}, u32[]{:S(2)}) copy-start(bf16[2,32,2,128]{3,2,1,0:T(2,128)(2,1)} %param.17) | copy-start | bytes 98308
  0.7 7.2 %copy-start.9 = (bf16[2,32,2,128]{3,2,1,0:T(2,128)(2,1)S(1)}, bf16[2,32,2,128]{3,2,1,0:T(2,128)(2,1)}, u32[]{:S(2)}) copy-start(bf16[2,32,2,128]{3,2,1,0:T(2,128)(2,1)} %param.16) | copy-start | bytes 98308
  4.9 26.9 %collective-permute-start = (bf16[2,2,2,512,128]{4,3,2,1,0:T(8,128)(2,1)S(1)}, bf16[2,2,2,512,128]{4,3,2,1,0:T(8,128)(2,1)S(1)}, u32[]{:S(2)}, u32[]{:S(2)}) collective-permute-start(bf16[2,2,2,512,128]{4,3,2,1,0:T(8,128)(2,1)S(1)} %bitcast.222), channel_id=1, source_target_pairs={{0,8},{4,12},{8,0},{12,4},{1,9},{5,13},{9,1},{13,5},{2,10},{6,14},... | collective-permute-start | bytes 3145736 | tf_op jit(solution)/shard_map/ppermute | solution.py:80
  7.9 25.6 %collective-permute-start.2 = (bf16[2,2,32,2,128]{4,2,3,1,0:T(8,128)(2,1)S(1)}, bf16[2,2,32,2,128]{4,2,3,1,0:T(8,128)(2,1)S(1)}, u32[]{:S(2)}, u32[]{:S(2)}) collective-permute-start(bf16[2,2,32,2,128]{4,2,3,1,0:T(8,128)(2,1)S(1)} %get-tuple-element.94), channel_id=1, source_target_pairs={{0,8},{4,12},{8,0},{12,4},{1,9},{5,13},{9,1},{13,5},{2,10},{6,14},... | collective-permute-start | bytes 196616 | tf_op jit(solution)/shard_map/ppermute | solution.py:80
  8.8 24.6 %copy-start.6 = (bf16[2,32,16,128]{3,2,1,0:T(8,128)(2,1)S(1)}, bf16[2,32,16,128]{3,2,1,0:T(8,128)(2,1)}, u32[]{:S(2)}) copy-start(bf16[2,32,16,128]{3,2,1,0:T(8,128)(2,1)} %param.15) | copy-start | bytes 786436
  9.6 23.8 %copy-start.11 = (s32[32]{0:T(128)S(1)}, s32[32]{0:T(128)}, u32[]{:S(2)}) copy-start(s32[32]{0:T(128)} %param.24) | copy-start | bytes 388
  33.3 5.4 %collective-permute-start.1 = (bf16[2,2,2,2,512,128]{5,4,3,2,1,0:T(8,128)(2,1)}, bf16[2,2,2,2,512,128]{5,4,3,2,1,0:T(8,128)(2,1)}, u32[]{:S(2)}, u32[]{:S(2)}) collective-permute-start(bf16[2,2,2,2,512,128]{5,4,3,2,1,0:T(8,128)(2,1)} %pad_maximum_fusion), channel_id=1, source_target_pairs={{0,4},{4,0},{8,12},{12,8},{1,5},{5,1},{9,13},{13,9},{2,6},{6,2},{1... | collective-permute-start | bytes 6291464 | tf_op jit(solution)/shard_map/ppermute | solution.py:82
  33.5 4.1 %collective-permute-start.3 = (bf16[2,2,2,32,2,128]{5,3,4,2,1,0:T(8,128)(2,1)S(1)}, bf16[2,2,2,32,2,128]{5,3,4,2,1,0:T(8,128)(2,1)S(1)}, u32[]{:S(2)}, u32[]{:S(2)}) collective-permute-start(bf16[2,2,2,32,2,128]{5,3,4,2,1,0:T(8,128)(2,1)S(1)} %pad_maximum_fusion.10), channel_id=1, source_target_pairs={{0,4},{4,0},{8,12},{12,8},{1,5},{5,1},{9,13},{13,9},{2,6},{6,2},{1... | collective-permute-start | bytes 393224 | tf_op jit(solution)/shard_map/ppermute | solution.py:82
  38.7 9.1 %copy-start.2 = (bf16[1,1,2,2,512,128]{5,4,3,2,1,0:T(8,128)(2,1)}, bf16[1,1,2,2,512,128]{5,4,3,2,1,0:T(8,128)(2,1)S(1)}, u32[]{:S(2)}) copy-start(bf16[1,1,2,2,512,128]{5,4,3,2,1,0:T(8,128)(2,1)S(1)} %get-tuple-element.89) | copy-start | bytes 1572868
  61.8 11.2 %collective-permute-start.4 = (bf16[96,2048]{1,0:T(8,128)(2,1)S(1)}, bf16[96,2048]{1,0:T(8,128)(2,1)S(1)}, u32[]{:S(2)}, u32[]{:S(2)}) collective-permute-start(bf16[96,2048]{1,0:T(8,128)(2,1)S(1)} %constant_dynamic-update-slice_fusion), channel_id=1, source_target_pairs={{0,8},{4,12},{8,0},{12,4},{1,9},{5,13},{9,1},{13,5},{2,10},{6,14},... | collective-permute-start | bytes 1179656 | tf_op jit(solution)/shard_map/ppermute | solution.py:80
  73.1 2.4 %collective-permute-start.5 = (bf16[2,96,2048]{2,1,0:T(8,128)(2,1)S(1)}, bf16[2,96,2048]{2,1,0:T(8,128)(2,1)S(1)}, u32[]{:S(2)}, u32[]{:S(2)}) collective-permute-start(bf16[2,96,2048]{2,1,0:T(8,128)(2,1)S(1)} %pad_maximum_fusion.4), channel_id=1, source_target_pairs={{0,4},{4,0},{8,12},{12,8},{1,5},{5,1},{9,13},{13,9},{2,6},{6,2},{1... | collective-permute-start | bytes 2359304 | tf_op jit(solution)/shard_map/ppermute | solution.py:82
  83.8 12.7 %collective-permute-start.6 = (bf16[96,2048]{1,0:T(8,128)(2,1)}, bf16[96,2048]{1,0:T(8,128)(2,1)}, u32[]{:S(2)}, u32[]{:S(2)}) collective-permute-start(bf16[96,2048]{1,0:T(8,128)(2,1)} %get-tuple-element.74), channel_id=1, source_target_pairs={{0,1},{1,2},{2,3},{4,5},{5,6},{6,7},{8,9},{9,10},{10,11},{12,13},{... | collective-permute-start | bytes 1179656 | tf_op jit(solution)/shard_map/ppermute | solution.py:112
  88.3 15.2 %collective-permute-start.9 = (bf16[96,2048]{1,0:T(8,128)(2,1)S(1)}, bf16[96,2048]{1,0:T(8,128)(2,1)}, u32[]{:S(2)}, u32[]{:S(2)}) collective-permute-start(bf16[96,2048]{1,0:T(8,128)(2,1)S(1)} %get-tuple-element.75), channel_id=1, source_target_pairs={{1,0},{2,1},{3,2},{5,4},{6,5},{7,6},{9,8},{10,9},{11,10},{13,12},{... | collective-permute-start | bytes 1179656 | tf_op jit(solution)/shard_map/ppermute | solution.py:113
  98.3 12.5 %collective-permute-start.7 = (bf16[96,2048]{1,0:T(8,128)(2,1)}, bf16[96,2048]{1,0:T(8,128)(2,1)}, u32[]{:S(2)}, u32[]{:S(2)}) collective-permute-start(bf16[96,2048]{1,0:T(8,128)(2,1)} %fusion.47), channel_id=1, source_target_pairs={{0,1},{1,2},{2,3},{4,5},{5,6},{6,7},{8,9},{9,10},{10,11},{12,13},{... | collective-permute-start | bytes 1179656 | tf_op jit(solution)/shard_map/ppermute | solution.py:112
  113.0 12.3 %collective-permute-start.10 = (bf16[96,2048]{1,0:T(8,128)(2,1)}, bf16[96,2048]{1,0:T(8,128)(2,1)}, u32[]{:S(2)}, u32[]{:S(2)}) collective-permute-start(bf16[96,2048]{1,0:T(8,128)(2,1)} %get-tuple-element.73), channel_id=1, source_target_pairs={{1,0},{2,1},{3,2},{5,4},{6,5},{7,6},{9,8},{10,9},{11,10},{13,12},{... | collective-permute-start | bytes 1179656 | tf_op jit(solution)/shard_map/ppermute | solution.py:113
  114.3 14.2 %collective-permute-start.8 = (bf16[96,2048]{1,0:T(8,128)(2,1)}, bf16[96,2048]{1,0:T(8,128)(2,1)S(1)}, u32[]{:S(2)}, u32[]{:S(2)}) collective-permute-start(bf16[96,2048]{1,0:T(8,128)(2,1)} %get-tuple-element.72), channel_id=1, source_target_pairs={{0,1},{1,2},{2,3},{4,5},{5,6},{6,7},{8,9},{9,10},{10,11},{12,13},{... | collective-permute-start | bytes 1179656 | tf_op jit(solution)/shard_map/ppermute | solution.py:112
  127.2 11.0 %collective-permute-start.11 = (bf16[96,2048]{1,0:T(8,128)(2,1)}, bf16[96,2048]{1,0:T(8,128)(2,1)}, u32[]{:S(2)}, u32[]{:S(2)}) collective-permute-start(bf16[96,2048]{1,0:T(8,128)(2,1)} %fusion.46), channel_id=1, source_target_pairs={{1,0},{2,1},{3,2},{5,4},{6,5},{7,6},{9,8},{10,9},{11,10},{13,12},{... | collective-permute-start | bytes 1179656 | tf_op jit(solution)/shard_map/ppermute | solution.py:113
  140.0 8.6 %collective-permute-start.12 = (bf16[96,2048]{1,0:T(8,128)(2,1)S(1)}, bf16[96,2048]{1,0:T(8,128)(2,1)S(1)}, u32[]{:S(2)}, u32[]{:S(2)}) collective-permute-start(bf16[96,2048]{1,0:T(8,128)(2,1)S(1)} %get-tuple-element.56), channel_id=1, source_target_pairs={{0,1},{1,2},{2,3},{4,5},{5,6},{6,7},{8,9},{9,10},{10,11},{12,13},{... | collective-permute-start | bytes 1179656 | tf_op jit(solution)/shard_map/ppermute | solution.py:119
  143.4 9.9 %collective-permute-start.15 = (bf16[96,2048]{1,0:T(8,128)(2,1)S(1)}, bf16[96,2048]{1,0:T(8,128)(2,1)S(1)}, u32[]{:S(2)}, u32[]{:S(2)}) collective-permute-start(bf16[96,2048]{1,0:T(8,128)(2,1)S(1)} %get-tuple-element.56), channel_id=1, source_target_pairs={{1,0},{2,1},{3,2},{5,4},{6,5},{7,6},{9,8},{10,9},{11,10},{13,12},{... | collective-permute-start | bytes 1179656 | tf_op jit(solution)/shard_map/ppermute | solution.py:120
  148.7 10.9 %collective-permute-start.13 = (bf16[96,2048]{1,0:T(8,128)(2,1)S(1)}, bf16[96,2048]{1,0:T(8,128)(2,1)S(1)}, u32[]{:S(2)}, u32[]{:S(2)}) collective-permute-start(bf16[96,2048]{1,0:T(8,128)(2,1)S(1)} %collective-permute-done.12), channel_id=1, source_target_pairs={{0,1},{1,2},{2,3},{4,5},{5,6},{6,7},{8,9},{9,10},{10,11},{12,13},{... | collective-permute-start | bytes 1179656 | tf_op jit(solution)/shard_map/ppermute | solution.py:119
  153.3 10.8 %collective-permute-start.16 = (bf16[96,2048]{1,0:T(8,128)(2,1)S(1)}, bf16[96,2048]{1,0:T(8,128)(2,1)S(1)}, u32[]{:S(2)}, u32[]{:S(2)}) collective-permute-start(bf16[96,2048]{1,0:T(8,128)(2,1)S(1)} %collective-permute-done.15), channel_id=1, source_target_pairs={{1,0},{2,1},{3,2},{5,4},{6,5},{7,6},{9,8},{10,9},{11,10},{13,12},{... | collective-permute-start | bytes 1179656 | tf_op jit(solution)/shard_map/ppermute | solution.py:120
  159.5 9.7 %collective-permute-start.14 = (bf16[96,2048]{1,0:T(8,128)(2,1)S(1)}, bf16[96,2048]{1,0:T(8,128)(2,1)S(1)}, u32[]{:S(2)}, u32[]{:S(2)}) collective-permute-start(bf16[96,2048]{1,0:T(8,128)(2,1)S(1)} %collective-permute-done.13), channel_id=1, source_target_pairs={{0,1},{1,2},{2,3},{4,5},{5,6},{6,7},{8,9},{9,10},{10,11},{12,13},{... | collective-permute-start | bytes 1179656 | tf_op jit(solution)/shard_map/ppermute | solution.py:119
  164.2 9.7 %collective-permute-start.17 = (bf16[96,2048]{1,0:T(8,128)(2,1)S(1)}, bf16[96,2048]{1,0:T(8,128)(2,1)S(1)}, u32[]{:S(2)}, u32[]{:S(2)}) collective-permute-start(bf16[96,2048]{1,0:T(8,128)(2,1)S(1)} %collective-permute-done.16), channel_id=1, source_target_pairs={{1,0},{2,1},{3,2},{5,4},{6,5},{7,6},{9,8},{10,9},{11,10},{13,12},{... | collective-permute-start | bytes 1179656 | tf_op jit(solution)/shard_map/ppermute | solution.py:120
  (6 other events, 28.8 us)

commit v10 on v8

--- a/solution.py
+++ b/solution.py
@@ -186,11 +186,16 @@
         steps_count, samples_dev, kv_heads, group_size, head_depth
     ).transpose(2, 0, 1, 3, 4)
     prefill_state = empty_state(head_batch, span_dev * group_size, head_depth)
-    along_x, other_core = ctx_shards(jnp.stack([local_keys, local_values]), ctx_count)
-    arrived = jnp.concatenate([along_x, other_core], axis=0)
+    own_pages = jnp.stack([local_keys, local_values])
+    core_pairs = [(dev, dev ^ 1) for dev in range(ctx_count)]
+    along_x = [
+        lax.ppermute(own_pages, "ctx", [(dev, (dev - 2 * shift) % ctx_count) for dev in range(ctx_count)])
+        for shift in range(1, ctx_count // 2)
+    ]
+    arrived = [own_pages, lax.ppermute(own_pages, "ctx", core_pairs)] + along_x
+    arrived += [lax.ppermute(pages, "ctx", core_pairs) for pages in along_x]
     prompt_keys_all, prompt_values_all = (
-        jnp.concatenate([arrived[shard, member] for shard in range(ctx_count)], axis=2)
-        for member in range(2)
+        jnp.concatenate([pages[member] for pages in arrived], axis=2) for member in range(2)
     )
     prefix_len = prompt_keys_all.shape[2]
     key_rows = prompt_keys_all.reshape(head_batch, prefix_len, head_depth)

time: 179 us -> 180 us (level)
    ppermute x0 -> x3, starting transfers between devices: none -> 3.15 us  [the longest x1 2.94 us: shards(): lax.ppermute(own_pages, 'ctx', [(dev, (dev - 2 * shift) % ctx_count) for...]
    ppermute x3 -> x2, waiting for transfers between devices: 29.6 us -> 32.6 us  [ctx_shards(): received.append(lax.ppermute(block, 'ctx', pairs))]
    ppermute x3 -> x2, starting transfers between devices: 4.84 us -> 1.9 us  [ctx_shards(): received.append(lax.ppermute(block, 'ctx', pairs))]
    ppermute x3 -> x2, waiting for transfers between devices: 5.73 us -> 3.09 us  [ctx_shards(): lax.ppermute(along_x, 'ctx', [(dev, dev ^ 1) for dev in range(ctx_count)])]
    another operation x5 -> x3, other arithmetic: 2.38 us -> 0.1 us  [ctx_shards(): along_x = jnp.stack(received)]
    unnamed x38 -> x34, local copies, waits for them, and re-layouts: 4.07 us -> 4.18 us
  transfers between devices with their start and end apart: 18 -> 19, of which waited for: 14 -> 14; matrix products, arithmetic and copies ran while one was open for 8% -> 7% of each run, Pallas kernels for 0% -> 0%
where the time goes in v10:
time: 180 us; the launch traced here: 179 us
  waiting for transfers between devices  79.4 us (44%)
  starting transfers between devices  39.8 us (22%)
  matrix products  25 us (14%)
  other arithmetic  18.2 us (10%)
  local copies, waits for them, and re-layouts  15 us (8%)
    ppermute x2, waiting for transfers between devices, ctx_shards(): received.append(lax.ppermute(block, 'ctx', pairs))  32.6 us
    ppermute x3, waiting for transfers between devices, head_sum_line(): from_right = lax.ppermute(going_left.astype(jnp.bfloat16), 'head', leftward)  15.7 us
    ppermute x3, starting transfers between devices, head_sum_line(): lax.ppermute(going_right.astype(jnp.bfloat16), 'head', rightward)  14.6 us
    ppermute x3, waiting for transfers between devices, head_sum_line(): lax.ppermute(going_right.astype(jnp.bfloat16), 'head', rightward)  14.3 us
    ppermute x3, starting transfers between devices, head_sum_line(): send_right = lax.ppermute(send_right, 'head', rightward)  12.2 us
    ppermute x3, waiting for transfers between devices, head_sum_line(): send_right = lax.ppermute(send_right, 'head', rightward)  11 us
    dot_general x4, matrix products, absorb(): jnp.einsum('brn,bnd->brd', weights.astype(jnp.bfloat16), value_rows, pref...  7.72 us
    dot_general x4, matrix products, absorb(): jnp.einsum('brd,bnd->brn', queries, key_rows, preferred_element_type=jnp....  6.66 us
  transfers between devices with their start and end apart: 19, of which 14 were waited for; matrix products, arithmetic and copies ran while one was open for 7% of the time, Pallas kernels for 0%

profile of v10, /device:TPU:0, one launch (start us, length us, event | category | flops | bytes accessed | tf_op | source)
XLA Modules:
  0.0 178.8 jit_solution(14593340486584158951)
XLA Ops:
  5.1 2.9 %collective-permute-start.1 = (bf16[2,2,2,512,128]{4,3,2,1,0:T(8,128)(2,1)}, bf16[2,2,2,512,128]{4,3,2,1,0:T(8,128)(2,1)S(1)}, u32[]{:S(2)}, u32[]{:S(2)}) collective-permute-start(bf16[2,2,2,512,128]{4,3,2,1,0:T(8,128)(2,1)} %pad_maximum_fusion.3), channel_id=1, source_target_pairs={{0,8},{4,12},{8,0},{12,4},{1,9},{5,13},{9,1},{13,5},{2,10},{6,14},... | collective-permute-start | bytes 3145736 | tf_op jit(solution)/shard_map/ppermute | solution.py:192
  9.8 23.0 %collective-permute-done.3 = bf16[2,2,32,2,128]{4,2,3,1,0:T(8,128)(2,1)S(1)} collective-permute-done((bf16[2,2,32,2,128]{4,2,3,1,0:T(8,128)(2,1)S(1)}, bf16[2,2,32,2,128]{4,2,3,1,0:T(8,128)(2,1)S(1)}, u32[]{:S(2)}, u32[]{:S(2)}) %collective-permute-start.3) | collective-permute-done | bytes 65568 | tf_op jit(solution)/shard_map/ppermute | solution.py:80
  41.4 3.9 %bitcast_reduce_fusion = (f32[4,256]{1,0:T(4,128)S(1)}, f32[4,2048,256]{2,1,0:T(8,128)}) fusion(bf16[4,256,128]{2,1,0:T(8,128)(2,1)S(1)} %bitcast.237, bf16[4,512,128]{2,1,0:T(8,128)(2,1)S(1)} %bitcast.255, bf16[4,512,128]{2,1,0:T(8,128)(2,1)S(1)} %bitcast.251, bf16[4,512,128]{2,1,0:T(8,128)(2,1)S(1)} %bitcast.253, bf16[4,512,128]{2,1,0:T(8,128)(2,1)S(1)} %bitcast.230), kind=kOutput, calls=%fused_computation.4 | convolution fusion | flops 549452800 | bytes 10752000 | tf_op jit(solution)/shard_map/while/body/eval_jaxpr/brd,bnd->brn/dot_general | solution.py:14
  46.9 2.5 %fusion.31 = f32[4,256,128]{2,1,0:T(8,128)S(1)} fusion(f32[4,2048,256]{2,1,0:T(8,128)S(1)} %get-tuple-element.101, f32[4,256]{1,0:T(4,128)S(1)} %get-tuple-element.99, bf16[4,512,128]{2,1,0:T(8,128)(2,1)S(1)} %bitcast.248, bf16[4,512,128]{2,1,0:T(8,128)(2,1)S(1)} %bitcast.244, bf16[4,512,128]{2,1,0:T(8,128)(2,1)S(1)} %bitcast.246, ...), kind=kOutput, calls=%fused_computation.44 | convolution fusion | flops 551813120 | bytes 11022336 | tf_op jit(solution)/shard_map/while/body/eval_jaxpr/brn,bnd->brd/dot_general | solution.py:23
  50.2 4.8 %fusion.6 = f32[4,256]{1,0:T(4,128)S(1)} fusion(f32[4,2048,256]{2,1,0:T(8,128)} %get-tuple-element.107, f32[4,256]{1,0:T(4,128)S(1)} %get-tuple-element.96), kind=kLoop, calls=%fused_computation.11 | loop fusion | flops 6290432 | bytes 8396800 | tf_op jit(solution)/shard_map/while/body/eval_jaxpr/reduce_sum | solution.py:22
  55.1 4.6 %fusion.28 = f32[4,256,128]{2,1,0:T(8,128)S(1)} fusion(f32[4,2048,256]{2,1,0:T(8,128)} %get-tuple-element.107, f32[4,256]{1,0:T(4,128)S(1)} %get-tuple-element.96, bf16[4,512,128]{2,1,0:T(8,128)(2,1)S(1)} %bitcast.249, bf16[4,512,128]{2,1,0:T(8,128)(2,1)S(1)} %bitcast.245, bf16[4,512,128]{2,1,0:T(8,128)(2,1)S(1)} %bitcast.247, ...), kind=kOutput, calls=%fused_computation.43 | convolution fusion | flops 551813120 | bytes 11022336 | tf_op jit(solution)/shard_map/while/body/eval_jaxpr/brn,bnd->brd/dot_general | solution.py:23
  63.0 9.6 %collective-permute-done.5 = bf16[96,2048]{1,0:T(8,128)(2,1)S(1)} collective-permute-done((bf16[96,2048]{1,0:T(8,128)(2,1)S(1)}, bf16[96,2048]{1,0:T(8,128)(2,1)S(1)}, u32[]{:S(2)}, u32[]{:S(2)}) %collective-permute-start.5) | collective-permute-done | bytes 393248 | tf_op jit(solution)/shard_map/ppermute | solution.py:80
  72.8 2.3 %collective-permute-done.6 = bf16[2,96,2048]{2,1,0:T(8,128)(2,1)S(1)} collective-permute-done((bf16[2,96,2048]{2,1,0:T(8,128)(2,1)S(1)}, bf16[2,96,2048]{2,1,0:T(8,128)(2,1)S(1)}, u32[]{:S(2)}, u32[]{:S(2)}) %collective-permute-start.6) | collective-permute-done | bytes 786464 | tf_op jit(solution)/shard_map/ppermute | solution.py:82
  76.7 5.9 %fusion = f32[4,96,2048]{2,1,0:T(8,128)S(1)} fusion(bf16[4,96,2048]{2,1,0:T(8,128)(2,1)S(1)} %bitcast.231, bf16[2048,2048]{1,0:T(8,128)(2,1)} %param.25), kind=kOutput, calls=%fused_computation.1 | convolution fusion | flops 3221225472 | bytes 13107200 | tf_op jit(solution)/shard_map/dot_general | solution.py:237
  83.4 4.5 %collective-permute-start.7 = (bf16[96,2048]{1,0:T(8,128)(2,1)}, bf16[96,2048]{1,0:T(8,128)(2,1)}, u32[]{:S(2)}, u32[]{:S(2)}) collective-permute-start(bf16[96,2048]{1,0:T(8,128)(2,1)} %get-tuple-element.74), channel_id=1, source_target_pairs={{0,1},{1,2},{2,3},{4,5},{5,6},{6,7},{8,9},{9,10},{10,11},{12,13},{... | collective-permute-start | bytes 1179656 | tf_op jit(solution)/shard_map/ppermute | solution.py:112
  89.1 6.9 %collective-permute-done.7 = bf16[96,2048]{1,0:T(8,128)(2,1)} collective-permute-done((bf16[96,2048]{1,0:T(8,128)(2,1)}, bf16[96,2048]{1,0:T(8,128)(2,1)}, u32[]{:S(2)}, u32[]{:S(2)}) %collective-permute-start.7) | collective-permute-done | bytes 393248 | tf_op jit(solution)/shard_map/ppermute | solution.py:112
  97.9 5.1 %collective-permute-start.8 = (bf16[96,2048]{1,0:T(8,128)(2,1)}, bf16[96,2048]{1,0:T(8,128)(2,1)}, u32[]{:S(2)}, u32[]{:S(2)}) collective-permute-start(bf16[96,2048]{1,0:T(8,128)(2,1)} %fusion.46), channel_id=1, source_target_pairs={{0,1},{1,2},{2,3},{4,5},{5,6},{6,7},{8,9},{9,10},{10,11},{12,13},{... | collective-permute-start | bytes 1179656 | tf_op jit(solution)/shard_map/ppermute | solution.py:112
  103.0 7.4 %collective-permute-done.8 = bf16[96,2048]{1,0:T(8,128)(2,1)} collective-permute-done((bf16[96,2048]{1,0:T(8,128)(2,1)}, bf16[96,2048]{1,0:T(8,128)(2,1)}, u32[]{:S(2)}, u32[]{:S(2)}) %collective-permute-start.8) | collective-permute-done | bytes 393248 | tf_op jit(solution)/shard_map/ppermute | solution.py:112
  113.9 5.0 %collective-permute-start.9 = (bf16[96,2048]{1,0:T(8,128)(2,1)}, bf16[96,2048]{1,0:T(8,128)(2,1)S(1)}, u32[]{:S(2)}, u32[]{:S(2)}) collective-permute-start(bf16[96,2048]{1,0:T(8,128)(2,1)} %get-tuple-element.72), channel_id=1, source_target_pairs={{0,1},{1,2},{2,3},{4,5},{5,6},{6,7},{8,9},{9,10},{10,11},{12,13},{... | collective-permute-start | bytes 1179656 | tf_op jit(solution)/shard_map/ppermute | solution.py:112
  118.9 6.0 %collective-permute-done.11 = bf16[96,2048]{1,0:T(8,128)(2,1)} collective-permute-done((bf16[96,2048]{1,0:T(8,128)(2,1)}, bf16[96,2048]{1,0:T(8,128)(2,1)}, u32[]{:S(2)}, u32[]{:S(2)}) %collective-permute-start.11) | collective-permute-done | bytes 393248 | tf_op jit(solution)/shard_map/ppermute | solution.py:113
  128.1 9.7 %collective-permute-done.12 = bf16[96,2048]{1,0:T(8,128)(2,1)} collective-permute-done((bf16[96,2048]{1,0:T(8,128)(2,1)}, bf16[96,2048]{1,0:T(8,128)(2,1)}, u32[]{:S(2)}, u32[]{:S(2)}) %collective-permute-start.12) | collective-permute-done | bytes 393248 | tf_op jit(solution)/shard_map/ppermute | solution.py:113
  139.6 3.4 %collective-permute-start.13 = (bf16[96,2048]{1,0:T(8,128)(2,1)S(1)}, bf16[96,2048]{1,0:T(8,128)(2,1)S(1)}, u32[]{:S(2)}, u32[]{:S(2)}) collective-permute-start(bf16[96,2048]{1,0:T(8,128)(2,1)S(1)} %get-tuple-element.56), channel_id=1, source_target_pairs={{0,1},{1,2},{2,3},{4,5},{5,6},{6,7},{8,9},{9,10},{10,11},{12,13},{... | collective-permute-start | bytes 1179656 | tf_op jit(solution)/shard_map/ppermute | solution.py:119
  144.4 3.9 %collective-permute-done.13 = bf16[96,2048]{1,0:T(8,128)(2,1)S(1)} collective-permute-done((bf16[96,2048]{1,0:T(8,128)(2,1)S(1)}, bf16[96,2048]{1,0:T(8,128)(2,1)S(1)}, u32[]{:S(2)}, u32[]{:S(2)}) %collective-permute-start.13) | collective-permute-done | bytes 393248 | tf_op jit(solution)/shard_map/ppermute | solution.py:119
  148.3 4.5 %collective-permute-start.14 = (bf16[96,2048]{1,0:T(8,128)(2,1)S(1)}, bf16[96,2048]{1,0:T(8,128)(2,1)S(1)}, u32[]{:S(2)}, u32[]{:S(2)}) collective-permute-start(bf16[96,2048]{1,0:T(8,128)(2,1)S(1)} %collective-permute-done.13), channel_id=1, source_target_pairs={{0,1},{1,2},{2,3},{4,5},{5,6},{6,7},{8,9},{9,10},{10,11},{12,13},{... | collective-permute-start | bytes 1179656 | tf_op jit(solution)/shard_map/ppermute | solution.py:119
  155.0 4.1 %collective-permute-done.14 = bf16[96,2048]{1,0:T(8,128)(2,1)S(1)} collective-permute-done((bf16[96,2048]{1,0:T(8,128)(2,1)S(1)}, bf16[96,2048]{1,0:T(8,128)(2,1)S(1)}, u32[]{:S(2)}, u32[]{:S(2)}) %collective-permute-start.14) | collective-permute-done | bytes 393248 | tf_op jit(solution)/shard_map/ppermute | solution.py:119
  159.1 4.4 %collective-permute-start.15 = (bf16[96,2048]{1,0:T(8,128)(2,1)S(1)}, bf16[96,2048]{1,0:T(8,128)(2,1)S(1)}, u32[]{:S(2)}, u32[]{:S(2)}) collective-permute-start(bf16[96,2048]{1,0:T(8,128)(2,1)S(1)} %collective-permute-done.14), channel_id=1, source_target_pairs={{0,1},{1,2},{2,3},{4,5},{5,6},{6,7},{8,9},{9,10},{10,11},{12,13},{... | collective-permute-start | bytes 1179656 | tf_op jit(solution)/shard_map/ppermute | solution.py:119
  165.8 3.0 %collective-permute-done.15 = bf16[96,2048]{1,0:T(8,128)(2,1)S(1)} collective-permute-done((bf16[96,2048]{1,0:T(8,128)(2,1)S(1)}, bf16[96,2048]{1,0:T(8,128)(2,1)S(1)}, u32[]{:S(2)}, u32[]{:S(2)}) %collective-permute-start.15) | collective-permute-done | bytes 393248 | tf_op jit(solution)/shard_map/ppermute | solution.py:119
  171.1 2.3 %collective-permute-done.18 = bf16[96,2048]{1,0:T(8,128)(2,1)S(1)} collective-permute-done((bf16[96,2048]{1,0:T(8,128)(2,1)S(1)}, bf16[96,2048]{1,0:T(8,128)(2,1)S(1)}, u32[]{:S(2)}, u32[]{:S(2)}) %collective-permute-start.18) | collective-permute-done | bytes 393248 | tf_op jit(solution)/shard_map/ppermute | solution.py:120
  174.2 2.4 %gather_fusion = bf16[4,96,2048]{2,1,0:T(8,128)(2,1)S(1)} fusion(bf16[7,96,2048]{2,1,0:T(8,128)(2,1)} %bitcast_dynamic-update-slice_fusion, s32[1024]{0:T(1024)S(1)} %pad_clamp_fusion), kind=kCustom, calls=%fused_computation | custom fusion | bytes 3145744 | tf_op jit(solution)/shard_map/jit(_take)/gather | solution.py:130
  (127 shorter events, 45.2 us)
Async XLA Ops:
  0.6 60.1 %copy-start = (bf16[4,8,2,128]{3,2,1,0:T(2,128)(2,1)S(1)}, bf16[4,8,2,128]{3,2,1,0:T(2,128)(2,1)}, u32[]{:S(2)}) copy-start(bf16[4,8,2,128]{3,2,1,0:T(2,128)(2,1)} %param.23) | copy-start | bytes 49156
  0.7 7.5 %copy-start.7 = (bf16[4,8,16,128]{3,2,1,0:T(8,128)(2,1)S(1)}, bf16[4,8,16,128]{3,2,1,0:T(8,128)(2,1)}, u32[]{:S(2)}) copy-start(bf16[4,8,16,128]{3,2,1,0:T(8,128)(2,1)} %param.21) | copy-start | bytes 393220
  0.7 7.5 %copy-start.12 = (bf16[4,8,2,128]{3,2,1,0:T(2,128)(2,1)S(1)}, bf16[4,8,2,128]{3,2,1,0:T(2,128)(2,1)}, u32[]{:S(2)}) copy-start(bf16[4,8,2,128]{3,2,1,0:T(2,128)(2,1)} %param.22) | copy-start | bytes 49156
  5.1 29.4 %collective-permute-start.1 = (bf16[2,2,2,512,128]{4,3,2,1,0:T(8,128)(2,1)}, bf16[2,2,2,512,128]{4,3,2,1,0:T(8,128)(2,1)S(1)}, u32[]{:S(2)}, u32[]{:S(2)}) collective-permute-start(bf16[2,2,2,512,128]{4,3,2,1,0:T(8,128)(2,1)} %pad_maximum_fusion.3), channel_id=1, source_target_pairs={{0,8},{4,12},{8,0},{12,4},{1,9},{5,13},{9,1},{13,5},{2,10},{6,14},... | collective-permute-start | bytes 3145736 | tf_op jit(solution)/shard_map/ppermute | solution.py:192
  8.0 28.7 %collective-permute-start = (bf16[2,2,2,512,128]{4,3,2,1,0:T(8,128)(2,1)}, bf16[2,2,2,512,128]{4,3,2,1,0:T(8,128)(2,1)}, u32[]{:S(2)}, u32[]{:S(2)}) collective-permute-start(bf16[2,2,2,512,128]{4,3,2,1,0:T(8,128)(2,1)} %pad_maximum_fusion.3), channel_id=1, source_target_pairs={{0,4},{4,0},{8,12},{12,8},{1,5},{5,1},{9,13},{13,9},{2,6},{6,2},{1... | collective-permute-start | bytes 3145736 | tf_op jit(solution)/shard_map/ppermute | solution.py:195
  8.1 24.7 %collective-permute-start.3 = (bf16[2,2,32,2,128]{4,2,3,1,0:T(8,128)(2,1)S(1)}, bf16[2,2,32,2,128]{4,2,3,1,0:T(8,128)(2,1)S(1)}, u32[]{:S(2)}, u32[]{:S(2)}) collective-permute-start(bf16[2,2,32,2,128]{4,2,3,1,0:T(8,128)(2,1)S(1)} %get-tuple-element.92), channel_id=1, source_target_pairs={{0,8},{4,12},{8,0},{12,4},{1,9},{5,13},{9,1},{13,5},{2,10},{6,14},... | collective-permute-start | bytes 196616 | tf_op jit(solution)/shard_map/ppermute | solution.py:80
  32.8 1.4 collective-permute-start.4
  34.5 3.7 %collective-permute-start.2 = (bf16[2,2,2,512,128]{4,3,2,1,0:T(8,128)(2,1)S(1)}, bf16[2,2,2,512,128]{4,3,2,1,0:T(8,128)(2,1)}, u32[]{:S(2)}, u32[]{:S(2)}) collective-permute-start(bf16[2,2,2,512,128]{4,3,2,1,0:T(8,128)(2,1)S(1)} %collective-permute-done.1), channel_id=1, source_target_pairs={{0,4},{4,0},{8,12},{12,8},{1,5},{5,1},{9,13},{13,9},{2,6},{6,2},{1... | collective-permute-start | bytes 3145736 | tf_op jit(solution)/shard_map/ppermute | solution.py:196
  36.8 10.1 %copy-start.1 = (bf16[1,2,2,512,128]{4,3,2,1,0:T(8,128)(2,1)}, bf16[1,2,2,512,128]{4,3,2,1,0:T(8,128)(2,1)S(1)}, u32[]{:S(2)}) copy-start(bf16[1,2,2,512,128]{4,3,2,1,0:T(8,128)(2,1)S(1)} %get-tuple-element.85) | copy-start | bytes 1572868
  38.3 8.6 %copy-start.3 = (bf16[1,2,2,512,128]{4,3,2,1,0:T(8,128)(2,1)}, bf16[1,2,2,512,128]{4,3,2,1,0:T(8,128)(2,1)S(1)}, u32[]{:S(2)}) copy-start(bf16[1,2,2,512,128]{4,3,2,1,0:T(8,128)(2,1)S(1)} %get-tuple-element.76) | copy-start | bytes 1572868
  61.2 11.5 %collective-permute-start.5 = (bf16[96,2048]{1,0:T(8,128)(2,1)S(1)}, bf16[96,2048]{1,0:T(8,128)(2,1)S(1)}, u32[]{:S(2)}, u32[]{:S(2)}) collective-permute-start(bf16[96,2048]{1,0:T(8,128)(2,1)S(1)} %constant_dynamic-update-slice_fusion), channel_id=1, source_target_pairs={{0,8},{4,12},{8,0},{12,4},{1,9},{5,13},{9,1},{13,5},{2,10},{6,14},... | collective-permute-start | bytes 1179656 | tf_op jit(solution)/shard_map/ppermute | solution.py:80
  72.7 2.4 %collective-permute-start.6 = (bf16[2,96,2048]{2,1,0:T(8,128)(2,1)S(1)}, bf16[2,96,2048]{2,1,0:T(8,128)(2,1)S(1)}, u32[]{:S(2)}, u32[]{:S(2)}) collective-permute-start(bf16[2,96,2048]{2,1,0:T(8,128)(2,1)S(1)} %pad_maximum_fusion.4), channel_id=1, source_target_pairs={{0,4},{4,0},{8,12},{12,8},{1,5},{5,1},{9,13},{13,9},{2,6},{6,2},{1... | collective-permute-start | bytes 2359304 | tf_op jit(solution)/shard_map/ppermute | solution.py:82
  83.4 12.7 %collective-permute-start.7 = (bf16[96,2048]{1,0:T(8,128)(2,1)}, bf16[96,2048]{1,0:T(8,128)(2,1)}, u32[]{:S(2)}, u32[]{:S(2)}) collective-permute-start(bf16[96,2048]{1,0:T(8,128)(2,1)} %get-tuple-element.74), channel_id=1, source_target_pairs={{0,1},{1,2},{2,3},{4,5},{5,6},{6,7},{8,9},{9,10},{10,11},{12,13},{... | collective-permute-start | bytes 1179656 | tf_op jit(solution)/shard_map/ppermute | solution.py:112
  87.9 15.2 %collective-permute-start.10 = (bf16[96,2048]{1,0:T(8,128)(2,1)S(1)}, bf16[96,2048]{1,0:T(8,128)(2,1)}, u32[]{:S(2)}, u32[]{:S(2)}) collective-permute-start(bf16[96,2048]{1,0:T(8,128)(2,1)S(1)} %get-tuple-element.75), channel_id=1, source_target_pairs={{1,0},{2,1},{3,2},{5,4},{6,5},{7,6},{9,8},{10,9},{11,10},{13,12},{... | collective-permute-start | bytes 1179656 | tf_op jit(solution)/shard_map/ppermute | solution.py:113
  97.9 12.5 %collective-permute-start.8 = (bf16[96,2048]{1,0:T(8,128)(2,1)}, bf16[96,2048]{1,0:T(8,128)(2,1)}, u32[]{:S(2)}, u32[]{:S(2)}) collective-permute-start(bf16[96,2048]{1,0:T(8,128)(2,1)} %fusion.46), channel_id=1, source_target_pairs={{0,1},{1,2},{2,3},{4,5},{5,6},{6,7},{8,9},{9,10},{10,11},{12,13},{... | collective-permute-start | bytes 1179656 | tf_op jit(solution)/shard_map/ppermute | solution.py:112
  112.6 12.4 %collective-permute-start.11 = (bf16[96,2048]{1,0:T(8,128)(2,1)}, bf16[96,2048]{1,0:T(8,128)(2,1)}, u32[]{:S(2)}, u32[]{:S(2)}) collective-permute-start(bf16[96,2048]{1,0:T(8,128)(2,1)} %get-tuple-element.73), channel_id=1, source_target_pairs={{1,0},{2,1},{3,2},{5,4},{6,5},{7,6},{9,8},{10,9},{11,10},{13,12},{... | collective-permute-start | bytes 1179656 | tf_op jit(solution)/shard_map/ppermute | solution.py:113
  113.9 14.2 %collective-permute-start.9 = (bf16[96,2048]{1,0:T(8,128)(2,1)}, bf16[96,2048]{1,0:T(8,128)(2,1)S(1)}, u32[]{:S(2)}, u32[]{:S(2)}) collective-permute-start(bf16[96,2048]{1,0:T(8,128)(2,1)} %get-tuple-element.72), channel_id=1, source_target_pairs={{0,1},{1,2},{2,3},{4,5},{5,6},{6,7},{8,9},{9,10},{10,11},{12,13},{... | collective-permute-start | bytes 1179656 | tf_op jit(solution)/shard_map/ppermute | solution.py:112
  126.8 11.0 %collective-permute-start.12 = (bf16[96,2048]{1,0:T(8,128)(2,1)}, bf16[96,2048]{1,0:T(8,128)(2,1)}, u32[]{:S(2)}, u32[]{:S(2)}) collective-permute-start(bf16[96,2048]{1,0:T(8,128)(2,1)} %fusion.45), channel_id=1, source_target_pairs={{1,0},{2,1},{3,2},{5,4},{6,5},{7,6},{9,8},{10,9},{11,10},{13,12},{... | collective-permute-start | bytes 1179656 | tf_op jit(solution)/shard_map/ppermute | solution.py:113
  139.6 8.6 %collective-permute-start.13 = (bf16[96,2048]{1,0:T(8,128)(2,1)S(1)}, bf16[96,2048]{1,0:T(8,128)(2,1)S(1)}, u32[]{:S(2)}, u32[]{:S(2)}) collective-permute-start(bf16[96,2048]{1,0:T(8,128)(2,1)S(1)} %get-tuple-element.56), channel_id=1, source_target_pairs={{0,1},{1,2},{2,3},{4,5},{5,6},{6,7},{8,9},{9,10},{10,11},{12,13},{... | collective-permute-start | bytes 1179656 | tf_op jit(solution)/shard_map/ppermute | solution.py:119
  143.0 9.9 %collective-permute-start.16 = (bf16[96,2048]{1,0:T(8,128)(2,1)S(1)}, bf16[96,2048]{1,0:T(8,128)(2,1)S(1)}, u32[]{:S(2)}, u32[]{:S(2)}) collective-permute-start(bf16[96,2048]{1,0:T(8,128)(2,1)S(1)} %get-tuple-element.56), channel_id=1, source_target_pairs={{1,0},{2,1},{3,2},{5,4},{6,5},{7,6},{9,8},{10,9},{11,10},{13,12},{... | collective-permute-start | bytes 1179656 | tf_op jit(solution)/shard_map/ppermute | solution.py:120
  148.3 10.8 %collective-permute-start.14 = (bf16[96,2048]{1,0:T(8,128)(2,1)S(1)}, bf16[96,2048]{1,0:T(8,128)(2,1)S(1)}, u32[]{:S(2)}, u32[]{:S(2)}) collective-permute-start(bf16[96,2048]{1,0:T(8,128)(2,1)S(1)} %collective-permute-done.13), channel_id=1, source_target_pairs={{0,1},{1,2},{2,3},{4,5},{5,6},{6,7},{8,9},{9,10},{10,11},{12,13},{... | collective-permute-start | bytes 1179656 | tf_op jit(solution)/shard_map/ppermute | solution.py:119
  152.9 10.8 %collective-permute-start.17 = (bf16[96,2048]{1,0:T(8,128)(2,1)S(1)}, bf16[96,2048]{1,0:T(8,128)(2,1)S(1)}, u32[]{:S(2)}, u32[]{:S(2)}) collective-permute-start(bf16[96,2048]{1,0:T(8,128)(2,1)S(1)} %collective-permute-done.16), channel_id=1, source_target_pairs={{1,0},{2,1},{3,2},{5,4},{6,5},{7,6},{9,8},{10,9},{11,10},{13,12},{... | collective-permute-start | bytes 1179656 | tf_op jit(solution)/shard_map/ppermute | solution.py:120
  159.1 9.7 %collective-permute-start.15 = (bf16[96,2048]{1,0:T(8,128)(2,1)S(1)}, bf16[96,2048]{1,0:T(8,128)(2,1)S(1)}, u32[]{:S(2)}, u32[]{:S(2)}) collective-permute-start(bf16[96,2048]{1,0:T(8,128)(2,1)S(1)} %collective-permute-done.14), channel_id=1, source_target_pairs={{0,1},{1,2},{2,3},{4,5},{5,6},{6,7},{8,9},{9,10},{10,11},{12,13},{... | collective-permute-start | bytes 1179656 | tf_op jit(solution)/shard_map/ppermute | solution.py:119
  163.8 9.7 %collective-permute-start.18 = (bf16[96,2048]{1,0:T(8,128)(2,1)S(1)}, bf16[96,2048]{1,0:T(8,128)(2,1)S(1)}, u32[]{:S(2)}, u32[]{:S(2)}) collective-permute-start(bf16[96,2048]{1,0:T(8,128)(2,1)S(1)} %collective-permute-done.17), channel_id=1, source_target_pairs={{1,0},{2,1},{3,2},{5,4},{6,5},{7,6},{9,8},{10,9},{11,10},{13,12},{... | collective-permute-start | bytes 1179656 | tf_op jit(solution)/shard_map/ppermute | solution.py:120
  (9 other events, 46.0 us)

commit v11 on v10

--- a/solution.py
+++ b/solution.py
@@ -83,7 +83,7 @@
     return along_x, other_core
 
 
-def ctx_gather(block, ctx_count):
+def ctx_gather(block, ctx_count, axis=0):
     ctx_index = lax.axis_index("ctx")
     chip, core = ctx_index // 2, ctx_index % 2
     along_x, other_core = ctx_shards(block, ctx_count)
@@ -91,27 +91,34 @@
     other_core = jnp.roll(other_core, chip, axis=0)
     core_zero = jnp.where(core == 0, along_x, other_core)
     core_one = jnp.where(core == 0, other_core, along_x)
-    return jnp.stack([core_zero, core_one], axis=1).reshape((ctx_count,) + block.shape)
-
-
-def head_sum_line(partial, head_count):
+    joined = jnp.moveaxis(jnp.stack([core_zero, core_one], axis=1), (0, 1), (axis, axis + 1))
+    return joined.reshape(block.shape[:axis] + (-1,) + block.shape[axis + 1 :])
+
+
+def head_sum_line(partials, head_count):
     last = head_count - 1
     head_index = lax.axis_index("head")
-    blocks = partial.reshape((head_count, -1) + partial.shape[1:])
+    pieces = [part.reshape((head_count, -1) + part.shape[1:]) for part in partials]
+
+    def take_block(index):
+        return jnp.concatenate(
+            [lax.dynamic_index_in_dim(piece, index, 0, False) for piece in pieces], axis=0
+        )
+
     rightward = [(dev, dev + 1) for dev in range(last)]
     leftward = [(dev + 1, dev) for dev in range(last)]
     from_left = from_right = None
     for step in range(1, head_count):
         right_block = jnp.clip(head_index + head_count - step, 0, last)
         left_block = jnp.clip(head_index - head_count + step, 0, last)
-        going_right = lax.dynamic_index_in_dim(blocks, right_block, 0, False)
-        going_left = lax.dynamic_index_in_dim(blocks, left_block, 0, False)
+        going_right = take_block(right_block)
+        going_left = take_block(left_block)
         if from_left is not None:
             going_right = going_right + from_left.astype(jnp.float32)
             going_left = going_left + from_right.astype(jnp.float32)
         from_left = lax.ppermute(going_right.astype(jnp.bfloat16), "head", rightward)
         from_right = lax.ppermute(going_left.astype(jnp.bfloat16), "head", leftward)
-    own = lax.dynamic_index_in_dim(blocks, head_index, 0, False)
+    own = take_block(head_index)
     mine = (own + from_left.astype(jnp.float32) + from_right.astype(jnp.float32)).astype(jnp.bfloat16)
     lefts, rights = [], []
     send_right = send_left = mine
@@ -127,7 +134,7 @@
         0,
         jnp.where(wanted < head_index, head_index - wanted, last + wanted - head_index),
     )
-    return jnp.take(candidates, pick, axis=0).reshape(partial.shape)
+    return jnp.take(candidates, pick, axis=0)
 
 
 def shards(
@@ -166,13 +173,8 @@
         .reshape(head_batch, span_dev * group_size, head_depth)
     )
     ctx_count = sample_prompt.shape[0] // samples_dev
-    span_pair = ctx_gather(jnp.stack([span_key, span_value]), ctx_count)
-    span_keys_all, span_values_all = (
-        span_pair[:, member].transpose(1, 0, 2, 3, 4).reshape(
-            (prompts, ctx_count * span_dev) + span_key.shape[2:]
-        )
-        for member in range(2)
-    )
+    span_pair = ctx_gather(jnp.stack([span_key, span_value]), ctx_count, axis=2)
+    span_keys_all, span_values_all = span_pair[0], span_pair[1]
     span_total = span_keys_all.shape[1]
     span_key_rows = span_keys_all.transpose(0, 2, 1, 3).reshape(head_batch, span_total, head_depth)
     span_value_rows = span_values_all.transpose(0, 2, 1, 3).reshape(
@@ -227,33 +229,24 @@
     span_attn = (
         span_mixed.reshape(prompts, kv_heads, span_dev, group_size, head_depth)
         .transpose(0, 2, 1, 3, 4)
-        .reshape(prompts * span_dev, heads_dev * head_depth)
+        .reshape(prompts, span_dev, heads_dev * head_depth)
+    )
+    span_rows_all = ctx_gather(span_attn, ctx_count, axis=1)
+    span_partial = jnp.dot(
+        span_rows_all.reshape(-1, span_rows_all.shape[-1]), out_weight, preferred_element_type=jnp.float32
     )
     decode_mixed = own_steps(decode_state, decode_five, decode_key, decode_value)
     decode_attn = decode_mixed.transpose(1, 2, 0, 3, 4).reshape(
-        steps_count * samples_dev, heads_dev * head_depth
-    )
-    rows_local = jnp.concatenate([span_attn, decode_attn], axis=0)
-    projected = jnp.dot(
-        ctx_gather(rows_local, ctx_count).reshape(-1, rows_local.shape[-1]),
-        out_weight,
-        preferred_element_type=jnp.float32,
-    )
-    summed = head_sum_line(projected, head_count)
-    rows_dev = rows_local.shape[0]
-    blocks_by_ctx = summed.reshape(-1, rows_dev, summed.shape[-1])
-    span_out = (
-        blocks_by_ctx[:, : prompts * span_dev]
-        .reshape(ctx_count, prompts, span_dev, -1)
-        .transpose(1, 0, 2, 3)
-        .reshape(prompts, ctx_count * span_dev, -1)
-    )
-    decode_out = (
-        blocks_by_ctx[:, prompts * span_dev :]
-        .reshape(ctx_count, steps_count, samples_dev, -1)
-        .transpose(1, 0, 2, 3)
-        .reshape(steps_count, ctx_count * samples_dev, -1)
-    )
+        steps_count, samples_dev, heads_dev * head_depth
+    )
+    decode_rows_all = ctx_gather(decode_attn, ctx_count, axis=1)
+    decode_partial = jnp.dot(
+        decode_rows_all.reshape(-1, decode_rows_all.shape[-1]), out_weight, preferred_element_type=jnp.float32
+    )
+    summed = head_sum_line((span_partial, decode_partial), head_count)
+    span_block = span_partial.shape[0] // head_count
+    span_out = summed[:, :span_block].reshape(span_rows_all.shape[:-1] + (-1,))
+    decode_out = summed[:, span_block:].reshape(decode_rows_all.shape[:-1] + (-1,))
     return (span_out, decode_out)
 
 

time: 180 us -> 173 us (0.961)
  waiting for transfers between devices: 79.4 us -> 63.7 us
  matrix products: 25 us -> 33.5 us
  local copies, waits for them, and re-layouts: 15 us -> 17.9 us
  other arithmetic: 18.2 us -> 15.9 us
    ppermute x3, waiting for transfers between devices: 14.3 us -> 1.29 us  [head_sum_line(): lax.ppermute(going_right.astype(jnp.bfloat16), 'head', rightward)]
    ppermute x3, waiting for transfers between devices: 15.7 us -> 19.5 us  [head_sum_line(): from_right = lax.ppermute(going_left.astype(jnp.bfloat16), 'head', leftward)]
    convert_element_type x2, other arithmetic: 3.99 us -> 0.18 us  [head_sum_line(): going_right.astype(jnp.bfloat16)]
    ppermute x2 -> x3, waiting for transfers between devices: 32.6 us -> 28.8 us  [ctx_shards(): received.append(lax.ppermute(block, 'ctx', pairs))]
    reduce_sum x4, other arithmetic: 6.41 us -> 9.86 us  [absorb(): running_sum = running_sum * factor + jnp.sum(weights, axis=-1)]
    dot_general x4, matrix products: 6.66 us -> 9.95 us  [absorb(): jnp.einsum('brd,bnd->brn', queries, key_rows, preferred_element_type=jnp....]
    dot_general x4, matrix products: 7.72 us -> 10.9 us  [absorb(): jnp.einsum('brn,bnd->brd', weights.astype(jnp.bfloat16), value_rows, pref...]
    slice x1 -> x3, local copies, waits for them, and re-layouts: 0.1 us -> 2.54 us  [the longest x1 1.04 us: shards(): span_out = summed[:, :span_block].reshape(span_rows_all.shape[:-1] + (-1,))]
  transfers between devices with their start and end apart: 19 -> 21, of which waited for: 14 -> 12; matrix products, arithmetic and copies ran while one was open for 7% -> 18% of each run, Pallas kernels for 0% -> 0%
where the time goes in v11:
time: 173 us
  waiting for transfers between devices  63.7 us (37%)
  starting transfers between devices  40.3 us (23%)
  matrix products  33.5 us (19%)
  local copies, waits for them, and re-layouts  17.9 us (10%)
  other arithmetic  15.9 us (9%)
    ppermute x3, waiting for transfers between devices, ctx_shards(): received.append(lax.ppermute(block, 'ctx', pairs))  28.8 us
    ppermute x3, waiting for transfers between devices, head_sum_line(): from_right = lax.ppermute(going_left.astype(jnp.bfloat16), 'head', leftward)  19.5 us
    ppermute x3, starting transfers between devices, head_sum_line(): lax.ppermute(going_right.astype(jnp.bfloat16), 'head', rightward)  13.7 us
    ppermute x3, starting transfers between devices, head_sum_line(): send_right = lax.ppermute(send_right, 'head', rightward)  13.2 us
    ppermute x3, waiting for transfers between devices, head_sum_line(): send_right = lax.ppermute(send_right, 'head', rightward)  11 us
    dot_general x4, matrix products, absorb(): jnp.einsum('brn,bnd->brd', weights.astype(jnp.bfloat16), value_rows, pref...  10.9 us
    dot_general x4, matrix products, absorb(): jnp.einsum('brd,bnd->brn', queries, key_rows, preferred_element_type=jnp....  9.95 us
    reduce_sum x4, other arithmetic, absorb(): running_sum = running_sum * factor + jnp.sum(weights, axis=-1)  9.86 us
  transfers between devices with their start and end apart: 21, of which 12 were waited for; matrix products, arithmetic and copies ran while one was open for 18% of the time, Pallas kernels for 0%

profile of v11, /device:TPU:0, one launch (start us, length us, event | category | flops | bytes accessed | tf_op | source)
XLA Modules:
  0.0 172.8 jit_solution(7072916400336914487)
XLA Ops:
  5.1 2.9 %collective-permute-start.1 = (bf16[2,2,2,512,128]{4,3,2,1,0:T(8,128)(2,1)}, bf16[2,2,2,512,128]{4,3,2,1,0:T(8,128)(2,1)S(1)}, u32[]{:S(2)}, u32[]{:S(2)}) collective-permute-start(bf16[2,2,2,512,128]{4,3,2,1,0:T(8,128)(2,1)} %pad_maximum_fusion.2), channel_id=1, source_target_pairs={{0,8},{4,12},{8,0},{12,4},{1,9},{5,13},{9,1},{13,5},{2,10},{6,14},... | collective-permute-start | bytes 3145736 | tf_op jit(solution)/shard_map/ppermute | solution.py:194
  11.7 21.1 %collective-permute-done.3 = bf16[2,2,32,2,128]{4,2,3,1,0:T(8,128)(2,1)S(1)} collective-permute-done((bf16[2,2,32,2,128]{4,2,3,1,0:T(8,128)(2,1)S(1)}, bf16[2,2,32,2,128]{4,2,3,1,0:T(8,128)(2,1)S(1)}, u32[]{:S(2)}, u32[]{:S(2)}) %collective-permute-start.3) | collective-permute-done | bytes 65568 | tf_op jit(solution)/shard_map/ppermute | solution.py:80
  43.2 3.9 %bitcast_reduce_fusion = (f32[4,256]{1,0:T(4,128)S(1)}, f32[4,2048,256]{2,1,0:T(8,128)}) fusion(bf16[4,256,128]{2,1,0:T(8,128)(2,1)S(1)} %bitcast.238, bf16[4,512,128]{2,1,0:T(8,128)(2,1)S(1)} %bitcast.258, bf16[4,512,128]{2,1,0:T(8,128)(2,1)S(1)} %bitcast.254, bf16[4,512,128]{2,1,0:T(8,128)(2,1)S(1)} %bitcast.256, bf16[4,512,128]{2,1,0:T(8,128)(2,1)S(1)} %bitcast.233), kind=kOutput, calls=%fused_computation.2 | convolution fusion | flops 549452800 | bytes 10752000 | tf_op jit(solution)/shard_map/while/body/eval_jaxpr/brd,bnd->brn/dot_general | solution.py:14
  47.1 4.0 %bitcast_reduce_fusion.1 = (f32[4,256]{1,0:T(4,128)S(1)}, f32[4,2048,256]{2,1,0:T(8,128)}) fusion(bf16[4,256,128]{2,1,0:T(8,128)(2,1)S(1)} %bitcast.242, bf16[4,512,128]{2,1,0:T(8,128)(2,1)S(1)} %bitcast.259, bf16[4,512,128]{2,1,0:T(8,128)(2,1)S(1)} %bitcast.255, bf16[4,512,128]{2,1,0:T(8,128)(2,1)S(1)} %bitcast.257, bf16[4,512,128]{2,1,0:T(8,128)(2,1)S(1)} %bitcast.234), kind=kOutput, calls=%fused_computation.9 | convolution fusion | flops 549452800 | bytes 10752000 | tf_op jit(solution)/shard_map/while/body/eval_jaxpr/brd,bnd->brn/dot_general | solution.py:14
  51.3 4.8 %fusion.8 = f32[4,256]{1,0:T(4,128)S(1)} fusion(f32[4,2048,256]{2,1,0:T(8,128)} %get-tuple-element.116, f32[4,256]{1,0:T(4,128)S(1)} %get-tuple-element.112), kind=kLoop, calls=%fused_computation.13 | loop fusion | flops 6290432 | bytes 8396800 | tf_op jit(solution)/shard_map/while/body/eval_jaxpr/reduce_sum | solution.py:22
  56.5 5.5 %fusion.30 = f32[4,256,128]{2,1,0:T(8,128)S(1)} fusion(f32[4,2048,256]{2,1,0:T(8,128)} %get-tuple-element.116, f32[4,256]{1,0:T(4,128)S(1)} %get-tuple-element.112, bf16[4,512,128]{2,1,0:T(8,128)(2,1)} %bitcast.252, bf16[4,512,128]{2,1,0:T(8,128)(2,1)S(1)} %bitcast.248, bf16[4,512,128]{2,1,0:T(8,128)(2,1)S(1)} %bitcast.250, ...), kind=kOutput, calls=%fused_computation.38 | convolution fusion | flops 551813120 | bytes 11022336 | tf_op jit(solution)/shard_map/while/body/eval_jaxpr/brn,bnd->brd/dot_general | solution.py:23
  65.2 4.8 %fusion.6 = f32[4,256]{1,0:T(4,128)S(1)} fusion(f32[4,2048,256]{2,1,0:T(8,128)} %get-tuple-element.120, f32[4,256]{1,0:T(4,128)S(1)} %get-tuple-element.110), kind=kLoop, calls=%fused_computation.11 | loop fusion | flops 6290432 | bytes 8396800 | tf_op jit(solution)/shard_map/while/body/eval_jaxpr/reduce_sum | solution.py:22
  70.0 4.8 %fusion.33 = f32[4,256,128]{2,1,0:T(8,128)S(1)} fusion(f32[4,2048,256]{2,1,0:T(8,128)} %get-tuple-element.120, f32[4,256]{1,0:T(4,128)S(1)} %get-tuple-element.110, bf16[4,512,128]{2,1,0:T(8,128)(2,1)S(1)} %bitcast.253, bf16[4,512,128]{2,1,0:T(8,128)(2,1)S(1)} %bitcast.249, bf16[4,512,128]{2,1,0:T(8,128)(2,1)S(1)} %bitcast.251, ...), kind=kOutput, calls=%fused_computation.39 | convolution fusion | flops 551813120 | bytes 11022336 | tf_op jit(solution)/shard_map/while/body/eval_jaxpr/brn,bnd->brd/dot_general | solution.py:23
  76.0 7.7 %collective-permute-done.5 = bf16[2,32,2048]{2,1,0:T(8,128)(2,1)S(1)} collective-permute-done((bf16[2,32,2048]{2,1,0:T(8,128)(2,1)S(1)}, bf16[2,32,2048]{2,1,0:T(8,128)(2,1)S(1)}, u32[]{:S(2)}, u32[]{:S(2)}) %collective-permute-start.5) | collective-permute-done | bytes 262176 | tf_op jit(solution)/shard_map/ppermute | solution.py:80
  84.5 4.8 %fusion.1 = f32[4,32,2048]{2,1,0:T(8,128)S(1)} fusion(bf16[4,32,2048]{2,1,0:T(8,128)(2,1)S(1)} %bitcast.225, bf16[2048,2048]{1,0:T(8,128)(2,1)} %param.27), kind=kOutput, calls=%fused_computation.4 | convolution fusion | flops 1073741824 | bytes 9961472 | tf_op jit(solution)/shard_map/dot_general | solution.py:243
  90.6 2.4 %fusion.3 = f32[4,64,2048]{2,1,0:T(8,128)S(1)} fusion(bf16[4,64,2048]{2,1,0:T(8,128)(2,1)S(1)} %bitcast.240, bf16[2048,2048]{1,0:T(8,128)(2,1)S(1)} %bitcast.224), kind=kOutput, calls=%fused_computation.6 | convolution fusion | flops 2147483648 | bytes 11534336 | tf_op jit(solution)/shard_map/dot_general | solution.py:235
  94.4 4.6 %collective-permute-start.9 = (bf16[96,2048]{1,0:T(8,128)(2,1)S(1)}, bf16[96,2048]{1,0:T(8,128)(2,1)S(1)}, u32[]{:S(2)}, u32[]{:S(2)}) collective-permute-start(bf16[96,2048]{1,0:T(8,128)(2,1)S(1)} %pad_maximum_fusion.4), channel_id=1, source_target_pairs={{0,1},{1,2},{2,3},{4,5},{5,6},{6,7},{8,9},{9,10},{10,11},{12,13},{... | collective-permute-start | bytes 1179656 | tf_op jit(solution)/shard_map/ppermute | solution.py:119
  99.3 7.2 %collective-permute-done.12 = bf16[96,2048]{1,0:T(8,128)(2,1)S(1)} collective-permute-done((bf16[96,2048]{1,0:T(8,128)(2,1)S(1)}, bf16[96,2048]{1,0:T(8,128)(2,1)S(1)}, u32[]{:S(2)}, u32[]{:S(2)}) %collective-permute-start.12) | collective-permute-done | bytes 393248 | tf_op jit(solution)/shard_map/ppermute | solution.py:120
  108.0 4.6 %collective-permute-start.10 = (bf16[96,2048]{1,0:T(8,128)(2,1)S(1)}, bf16[96,2048]{1,0:T(8,128)(2,1)S(1)}, u32[]{:S(2)}, u32[]{:S(2)}) collective-permute-start(bf16[96,2048]{1,0:T(8,128)(2,1)S(1)} %fusion.45), channel_id=1, source_target_pairs={{0,1},{1,2},{2,3},{4,5},{5,6},{6,7},{8,9},{9,10},{10,11},{12,13},{... | collective-permute-start | bytes 1179656 | tf_op jit(solution)/shard_map/ppermute | solution.py:119
  112.6 6.6 %collective-permute-done.13 = bf16[96,2048]{1,0:T(8,128)(2,1)S(1)} collective-permute-done((bf16[96,2048]{1,0:T(8,128)(2,1)S(1)}, bf16[96,2048]{1,0:T(8,128)(2,1)S(1)}, u32[]{:S(2)}, u32[]{:S(2)}) %collective-permute-start.13) | collective-permute-done | bytes 393248 | tf_op jit(solution)/shard_map/ppermute | solution.py:120
  120.7 4.6 %collective-permute-start.11 = (bf16[96,2048]{1,0:T(8,128)(2,1)S(1)}, bf16[96,2048]{1,0:T(8,128)(2,1)S(1)}, u32[]{:S(2)}, u32[]{:S(2)}) collective-permute-start(bf16[96,2048]{1,0:T(8,128)(2,1)S(1)} %fusion.44), channel_id=1, source_target_pairs={{0,1},{1,2},{2,3},{4,5},{5,6},{6,7},{8,9},{9,10},{10,11},{12,13},{... | collective-permute-start | bytes 1179656 | tf_op jit(solution)/shard_map/ppermute | solution.py:119
  125.3 5.7 %collective-permute-done.14 = bf16[96,2048]{1,0:T(8,128)(2,1)S(1)} collective-permute-done((bf16[96,2048]{1,0:T(8,128)(2,1)S(1)}, bf16[96,2048]{1,0:T(8,128)(2,1)S(1)}, u32[]{:S(2)}, u32[]{:S(2)}) %collective-permute-start.14) | collective-permute-done | bytes 393248 | tf_op jit(solution)/shard_map/ppermute | solution.py:120
  133.2 4.4 %collective-permute-start.15 = (bf16[96,2048]{1,0:T(8,128)(2,1)S(1)}, bf16[96,2048]{1,0:T(8,128)(2,1)S(1)}, u32[]{:S(2)}, u32[]{:S(2)}) collective-permute-start(bf16[96,2048]{1,0:T(8,128)(2,1)S(1)} %get-tuple-element.57), channel_id=1, source_target_pairs={{0,1},{1,2},{2,3},{4,5},{5,6},{6,7},{8,9},{9,10},{10,11},{12,13},{... | collective-permute-start | bytes 1179656 | tf_op jit(solution)/shard_map/ppermute | solution.py:126
  138.9 4.7 %collective-permute-done.15 = bf16[96,2048]{1,0:T(8,128)(2,1)S(1)} collective-permute-done((bf16[96,2048]{1,0:T(8,128)(2,1)S(1)}, bf16[96,2048]{1,0:T(8,128)(2,1)S(1)}, u32[]{:S(2)}, u32[]{:S(2)}) %collective-permute-start.15) | collective-permute-done | bytes 393248 | tf_op jit(solution)/shard_map/ppermute | solution.py:126
  143.7 4.4 %collective-permute-start.16 = (bf16[96,2048]{1,0:T(8,128)(2,1)S(1)}, bf16[96,2048]{1,0:T(8,128)(2,1)S(1)}, u32[]{:S(2)}, u32[]{:S(2)}) collective-permute-start(bf16[96,2048]{1,0:T(8,128)(2,1)S(1)} %collective-permute-done.15), channel_id=1, source_target_pairs={{0,1},{1,2},{2,3},{4,5},{5,6},{6,7},{8,9},{9,10},{10,11},{12,13},{... | collective-permute-start | bytes 1179656 | tf_op jit(solution)/shard_map/ppermute | solution.py:126
  150.2 3.2 %collective-permute-done.16 = bf16[96,2048]{1,0:T(8,128)(2,1)S(1)} collective-permute-done((bf16[96,2048]{1,0:T(8,128)(2,1)S(1)}, bf16[96,2048]{1,0:T(8,128)(2,1)S(1)}, u32[]{:S(2)}, u32[]{:S(2)}) %collective-permute-start.16) | collective-permute-done | bytes 393248 | tf_op jit(solution)/shard_map/ppermute | solution.py:126
  153.3 4.4 %collective-permute-start.17 = (bf16[96,2048]{1,0:T(8,128)(2,1)S(1)}, bf16[96,2048]{1,0:T(8,128)(2,1)S(1)}, u32[]{:S(2)}, u32[]{:S(2)}) collective-permute-start(bf16[96,2048]{1,0:T(8,128)(2,1)S(1)} %collective-permute-done.16), channel_id=1, source_target_pairs={{0,1},{1,2},{2,3},{4,5},{5,6},{6,7},{8,9},{9,10},{10,11},{12,13},{... | collective-permute-start | bytes 1179656 | tf_op jit(solution)/shard_map/ppermute | solution.py:126
  159.9 3.1 %collective-permute-done.17 = bf16[96,2048]{1,0:T(8,128)(2,1)S(1)} collective-permute-done((bf16[96,2048]{1,0:T(8,128)(2,1)S(1)}, bf16[96,2048]{1,0:T(8,128)(2,1)S(1)}, u32[]{:S(2)}, u32[]{:S(2)}) %collective-permute-start.17) | collective-permute-done | bytes 393248 | tf_op jit(solution)/shard_map/ppermute | solution.py:126
  168.3 2.4 %gather_fusion = bf16[4,96,2048]{2,1,0:T(8,128)(2,1)S(1)} fusion(bf16[7,96,2048]{2,1,0:T(8,128)(2,1)} %bitcast_dynamic-update-slice_fusion, s32[1024]{0:T(1024)S(1)} %pad_clamp_fusion), kind=kCustom, calls=%fused_computation | custom fusion | bytes 3145744 | tf_op jit(solution)/shard_map/jit(_take)/gather | solution.py:137
  (159 shorter events, 44.5 us)
Async XLA Ops:
  0.6 62.2 %copy-start = (bf16[4,8,2,128]{3,2,1,0:T(2,128)(2,1)S(1)}, bf16[4,8,2,128]{3,2,1,0:T(2,128)(2,1)}, u32[]{:S(2)}) copy-start(bf16[4,8,2,128]{3,2,1,0:T(2,128)(2,1)} %param.25) | copy-start | bytes 49156
  0.7 10.2 %copy-start.9 = (bf16[2,32,16,128]{3,2,1,0:T(8,128)(2,1)S(1)}, bf16[2,32,16,128]{3,2,1,0:T(8,128)(2,1)}, u32[]{:S(2)}) copy-start(bf16[2,32,16,128]{3,2,1,0:T(8,128)(2,1)} %param.17) | copy-start | bytes 786436
  0.7 10.9 %copy-start.20 = (s32[32]{0:T(128)S(1)}, s32[32]{0:T(128)}, u32[]{:S(2)}) copy-start(s32[32]{0:T(128)} %param.26) | copy-start | bytes 388
  5.1 29.4 %collective-permute-start.1 = (bf16[2,2,2,512,128]{4,3,2,1,0:T(8,128)(2,1)}, bf16[2,2,2,512,128]{4,3,2,1,0:T(8,128)(2,1)S(1)}, u32[]{:S(2)}, u32[]{:S(2)}) collective-permute-start(bf16[2,2,2,512,128]{4,3,2,1,0:T(8,128)(2,1)} %pad_maximum_fusion.2), channel_id=1, source_target_pairs={{0,8},{4,12},{8,0},{12,4},{1,9},{5,13},{9,1},{13,5},{2,10},{6,14},... | collective-permute-start | bytes 3145736 | tf_op jit(solution)/shard_map/ppermute | solution.py:194
  8.0 31.0 %collective-permute-start = (bf16[2,2,2,512,128]{4,3,2,1,0:T(8,128)(2,1)}, bf16[2,2,2,512,128]{4,3,2,1,0:T(8,128)(2,1)}, u32[]{:S(2)}, u32[]{:S(2)}) collective-permute-start(bf16[2,2,2,512,128]{4,3,2,1,0:T(8,128)(2,1)} %pad_maximum_fusion.2), channel_id=1, source_target_pairs={{0,4},{4,0},{8,12},{12,8},{1,5},{5,1},{9,13},{13,9},{2,6},{6,2},{1... | collective-permute-start | bytes 3145736 | tf_op jit(solution)/shard_map/ppermute | solution.py:197
  8.1 24.7 %collective-permute-start.3 = (bf16[2,2,32,2,128]{4,2,3,1,0:T(8,128)(2,1)S(1)}, bf16[2,2,32,2,128]{4,2,3,1,0:T(8,128)(2,1)S(1)}, u32[]{:S(2)}, u32[]{:S(2)}) collective-permute-start(bf16[2,2,32,2,128]{4,2,3,1,0:T(8,128)(2,1)S(1)} %get-tuple-element.105), channel_id=1, source_target_pairs={{0,8},{4,12},{8,0},{12,4},{1,9},{5,13},{9,1},{13,5},{2,10},{6,14},... | collective-permute-start | bytes 196616 | tf_op jit(solution)/shard_map/ppermute | solution.py:80
  32.8 1.4 collective-permute-start.4
  34.5 6.6 %collective-permute-start.2 = (bf16[2,2,2,512,128]{4,3,2,1,0:T(8,128)(2,1)S(1)}, bf16[2,2,2,512,128]{4,3,2,1,0:T(8,128)(2,1)}, u32[]{:S(2)}, u32[]{:S(2)}) collective-permute-start(bf16[2,2,2,512,128]{4,3,2,1,0:T(8,128)(2,1)S(1)} %collective-permute-done.1), channel_id=1, source_target_pairs={{0,4},{4,0},{8,12},{12,8},{1,5},{5,1},{9,13},{13,9},{2,6},{6,2},{1... | collective-permute-start | bytes 3145736 | tf_op jit(solution)/shard_map/ppermute | solution.py:198
  63.2 12.6 %collective-permute-start.7 = (bf16[4,8,2048]{2,1,0:T(8,128)(2,1)S(1)}, bf16[4,8,2048]{2,1,0:T(8,128)(2,1)S(1)}, u32[]{:S(2)}, u32[]{:S(2)}) collective-permute-start(bf16[4,8,2048]{2,1,0:T(8,128)(2,1)S(1)} %reshape.284), channel_id=1, source_target_pairs={{0,8},{4,12},{8,0},{12,4},{1,9},{5,13},{9,1},{13,5},{2,10},{6,14},... | collective-permute-start | bytes 393224 | tf_op jit(solution)/shard_map/ppermute | solution.py:80
  75.4 8.3 %collective-permute-start.5 = (bf16[2,32,2048]{2,1,0:T(8,128)(2,1)S(1)}, bf16[2,32,2048]{2,1,0:T(8,128)(2,1)S(1)}, u32[]{:S(2)}, u32[]{:S(2)}) collective-permute-start(bf16[2,32,2048]{2,1,0:T(8,128)(2,1)S(1)} %reshape.280), channel_id=1, source_target_pairs={{0,8},{4,12},{8,0},{12,4},{1,9},{5,13},{9,1},{13,5},{2,10},{6,14},... | collective-permute-start | bytes 786440 | tf_op jit(solution)/shard_map/ppermute | solution.py:80
  75.8 8.0 %collective-permute-start.8 = (bf16[2,4,8,2048]{3,2,1,0:T(8,128)(2,1)S(1)}, bf16[2,4,8,2048]{3,2,1,0:T(8,128)(2,1)S(1)}, u32[]{:S(2)}, u32[]{:S(2)}) collective-permute-start(bf16[2,4,8,2048]{3,2,1,0:T(8,128)(2,1)S(1)} %pad_maximum_fusion.10), channel_id=1, source_target_pairs={{0,4},{4,0},{8,12},{12,8},{1,5},{5,1},{9,13},{13,9},{2,6},{6,2},{1... | collective-permute-start | bytes 786440 | tf_op jit(solution)/shard_map/ppermute | solution.py:82
  83.8 5.7 %collective-permute-start.6 = (bf16[2,2,32,2048]{3,2,1,0:T(8,128)(2,1)S(1)}, bf16[2,2,32,2048]{3,2,1,0:T(8,128)(2,1)S(1)}, u32[]{:S(2)}, u32[]{:S(2)}) collective-permute-start(bf16[2,2,32,2048]{3,2,1,0:T(8,128)(2,1)S(1)} %pad_maximum_fusion.3), channel_id=1, source_target_pairs={{0,4},{4,0},{8,12},{12,8},{1,5},{5,1},{9,13},{13,9},{2,6},{6,2},{1... | collective-permute-start | bytes 1572872 | tf_op jit(solution)/shard_map/ppermute | solution.py:82
  93.1 13.4 %collective-permute-start.12 = (bf16[96,2048]{1,0:T(8,128)(2,1)S(1)}, bf16[96,2048]{1,0:T(8,128)(2,1)S(1)}, u32[]{:S(2)}, u32[]{:S(2)}) collective-permute-start(bf16[96,2048]{1,0:T(8,128)(2,1)S(1)} %pad_maximum_fusion.5), channel_id=1, source_target_pairs={{1,0},{2,1},{3,2},{5,4},{6,5},{7,6},{9,8},{10,9},{11,10},{13,12},{... | collective-permute-start | bytes 1179656 | tf_op jit(solution)/shard_map/ppermute | solution.py:120
  94.4 13.5 %collective-permute-start.9 = (bf16[96,2048]{1,0:T(8,128)(2,1)S(1)}, bf16[96,2048]{1,0:T(8,128)(2,1)S(1)}, u32[]{:S(2)}, u32[]{:S(2)}) collective-permute-start(bf16[96,2048]{1,0:T(8,128)(2,1)S(1)} %pad_maximum_fusion.4), channel_id=1, source_target_pairs={{0,1},{1,2},{2,3},{4,5},{5,6},{6,7},{8,9},{9,10},{10,11},{12,13},{... | collective-permute-start | bytes 1179656 | tf_op jit(solution)/shard_map/ppermute | solution.py:119
  106.6 12.6 %collective-permute-start.13 = (bf16[96,2048]{1,0:T(8,128)(2,1)S(1)}, bf16[96,2048]{1,0:T(8,128)(2,1)S(1)}, u32[]{:S(2)}, u32[]{:S(2)}) collective-permute-start(bf16[96,2048]{1,0:T(8,128)(2,1)S(1)} %fusion.47), channel_id=1, source_target_pairs={{1,0},{2,1},{3,2},{5,4},{6,5},{7,6},{9,8},{10,9},{11,10},{13,12},{... | collective-permute-start | bytes 1179656 | tf_op jit(solution)/shard_map/ppermute | solution.py:120
  108.0 12.6 %collective-permute-start.10 = (bf16[96,2048]{1,0:T(8,128)(2,1)S(1)}, bf16[96,2048]{1,0:T(8,128)(2,1)S(1)}, u32[]{:S(2)}, u32[]{:S(2)}) collective-permute-start(bf16[96,2048]{1,0:T(8,128)(2,1)S(1)} %fusion.45), channel_id=1, source_target_pairs={{0,1},{1,2},{2,3},{4,5},{5,6},{6,7},{8,9},{9,10},{10,11},{12,13},{... | collective-permute-start | bytes 1179656 | tf_op jit(solution)/shard_map/ppermute | solution.py:119
  119.3 11.7 %collective-permute-start.14 = (bf16[96,2048]{1,0:T(8,128)(2,1)S(1)}, bf16[96,2048]{1,0:T(8,128)(2,1)S(1)}, u32[]{:S(2)}, u32[]{:S(2)}) collective-permute-start(bf16[96,2048]{1,0:T(8,128)(2,1)S(1)} %fusion.46), channel_id=1, source_target_pairs={{1,0},{2,1},{3,2},{5,4},{6,5},{7,6},{9,8},{10,9},{11,10},{13,12},{... | collective-permute-start | bytes 1179656 | tf_op jit(solution)/shard_map/ppermute | solution.py:120
  120.7 11.6 %collective-permute-start.11 = (bf16[96,2048]{1,0:T(8,128)(2,1)S(1)}, bf16[96,2048]{1,0:T(8,128)(2,1)S(1)}, u32[]{:S(2)}, u32[]{:S(2)}) collective-permute-start(bf16[96,2048]{1,0:T(8,128)(2,1)S(1)} %fusion.44), channel_id=1, source_target_pairs={{0,1},{1,2},{2,3},{4,5},{5,6},{6,7},{8,9},{9,10},{10,11},{12,13},{... | collective-permute-start | bytes 1179656 | tf_op jit(solution)/shard_map/ppermute | solution.py:119
  133.2 10.5 %collective-permute-start.15 = (bf16[96,2048]{1,0:T(8,128)(2,1)S(1)}, bf16[96,2048]{1,0:T(8,128)(2,1)S(1)}, u32[]{:S(2)}, u32[]{:S(2)}) collective-permute-start(bf16[96,2048]{1,0:T(8,128)(2,1)S(1)} %get-tuple-element.57), channel_id=1, source_target_pairs={{0,1},{1,2},{2,3},{4,5},{5,6},{6,7},{8,9},{9,10},{10,11},{12,13},{... | collective-permute-start | bytes 1179656 | tf_op jit(solution)/shard_map/ppermute | solution.py:126
  137.6 10.5 %collective-permute-start.18 = (bf16[96,2048]{1,0:T(8,128)(2,1)S(1)}, bf16[96,2048]{1,0:T(8,128)(2,1)S(1)}, u32[]{:S(2)}, u32[]{:S(2)}) collective-permute-start(bf16[96,2048]{1,0:T(8,128)(2,1)S(1)} %get-tuple-element.57), channel_id=1, source_target_pairs={{1,0},{2,1},{3,2},{5,4},{6,5},{7,6},{9,8},{10,9},{11,10},{13,12},{... | collective-permute-start | bytes 1179656 | tf_op jit(solution)/shard_map/ppermute | solution.py:127
  143.7 9.7 %collective-permute-start.16 = (bf16[96,2048]{1,0:T(8,128)(2,1)S(1)}, bf16[96,2048]{1,0:T(8,128)(2,1)S(1)}, u32[]{:S(2)}, u32[]{:S(2)}) collective-permute-start(bf16[96,2048]{1,0:T(8,128)(2,1)S(1)} %collective-permute-done.15), channel_id=1, source_target_pairs={{0,1},{1,2},{2,3},{4,5},{5,6},{6,7},{8,9},{9,10},{10,11},{12,13},{... | collective-permute-start | bytes 1179656 | tf_op jit(solution)/shard_map/ppermute | solution.py:126
  148.1 9.8 %collective-permute-start.19 = (bf16[96,2048]{1,0:T(8,128)(2,1)S(1)}, bf16[96,2048]{1,0:T(8,128)(2,1)S(1)}, u32[]{:S(2)}, u32[]{:S(2)}) collective-permute-start(bf16[96,2048]{1,0:T(8,128)(2,1)S(1)} %collective-permute-done.18), channel_id=1, source_target_pairs={{1,0},{2,1},{3,2},{5,4},{6,5},{7,6},{9,8},{10,9},{11,10},{13,12},{... | collective-permute-start | bytes 1179656 | tf_op jit(solution)/shard_map/ppermute | solution.py:127
  153.3 9.7 %collective-permute-start.17 = (bf16[96,2048]{1,0:T(8,128)(2,1)S(1)}, bf16[96,2048]{1,0:T(8,128)(2,1)S(1)}, u32[]{:S(2)}, u32[]{:S(2)}) collective-permute-start(bf16[96,2048]{1,0:T(8,128)(2,1)S(1)} %collective-permute-done.16), channel_id=1, source_target_pairs={{0,1},{1,2},{2,3},{4,5},{5,6},{6,7},{8,9},{9,10},{10,11},{12,13},{... | collective-permute-start | bytes 1179656 | tf_op jit(solution)/shard_map/ppermute | solution.py:126
  157.8 9.7 %collective-permute-start.20 = (bf16[96,2048]{1,0:T(8,128)(2,1)S(1)}, bf16[96,2048]{1,0:T(8,128)(2,1)S(1)}, u32[]{:S(2)}, u32[]{:S(2)}) collective-permute-start(bf16[96,2048]{1,0:T(8,128)(2,1)S(1)} %collective-permute-done.19), channel_id=1, source_target_pairs={{1,0},{2,1},{3,2},{5,4},{6,5},{7,6},{9,8},{10,9},{11,10},{13,12},{... | collective-permute-start | bytes 1179656 | tf_op jit(solution)/shard_map/ppermute | solution.py:127
  (20 other events, 108.9 us)

commit v12 on v11

--- a/solution.py
+++ b/solution.py
@@ -120,21 +120,27 @@
         from_right = lax.ppermute(going_left.astype(jnp.bfloat16), "head", leftward)
     own = take_block(head_index)
     mine = (own + from_left.astype(jnp.float32) + from_right.astype(jnp.float32)).astype(jnp.bfloat16)
-    lefts, rights = [], []
+    sizes = [piece.shape[1] for piece in pieces]
+    outs = [jnp.zeros((head_count,) + piece.shape[1:], mine.dtype) for piece in pieces]
+
+    def place(outs, block, index, valid):
+        safe = jnp.clip(index, 0, last)
+        placed, start = [], 0
+        for out, size in zip(outs, sizes):
+            part = block[start : start + size]
+            start += size
+            current = lax.dynamic_index_in_dim(out, safe, 0, False)
+            placed.append(lax.dynamic_update_index_in_dim(out, jnp.where(valid, part, current), safe, 0))
+        return placed
+
+    outs = place(outs, mine, head_index, True)
     send_right = send_left = mine
     for step in range(1, head_count):
         send_right = lax.ppermute(send_right, "head", rightward)
         send_left = lax.ppermute(send_left, "head", leftward)
-        lefts.append(send_right)
-        rights.append(send_left)
-    candidates = jnp.stack([mine] + lefts + rights)
-    wanted = jnp.arange(head_count, dtype=jnp.int32)
-    pick = jnp.where(
-        wanted == head_index,
-        0,
-        jnp.where(wanted < head_index, head_index - wanted, last + wanted - head_index),
-    )
-    return jnp.take(candidates, pick, axis=0)
+        outs = place(outs, send_right, head_index - step, head_index >= step)
+        outs = place(outs, send_left, head_index + step, head_index + step <= last)
+    return outs
 
 
 def shards(
@@ -243,10 +249,9 @@
     decode_partial = jnp.dot(
         decode_rows_all.reshape(-1, decode_rows_all.shape[-1]), out_weight, preferred_element_type=jnp.float32
     )
-    summed = head_sum_line((span_partial, decode_partial), head_count)
-    span_block = span_partial.shape[0] // head_count
-    span_out = summed[:, :span_block].reshape(span_rows_all.shape[:-1] + (-1,))
-    decode_out = summed[:, span_block:].reshape(decode_rows_all.shape[:-1] + (-1,))
+    span_sum, decode_sum = head_sum_line((span_partial, decode_partial), head_count)
+    span_out = span_sum.reshape(span_rows_all.shape[:-1] + (-1,))
+    decode_out = decode_sum.reshape(decode_rows_all.shape[:-1] + (-1,))
     return (span_out, decode_out)
 
 

time: 173 us -> 173 us (level)
  local copies, waits for them, and re-layouts: 17.9 us -> 10.4 us
  waiting for transfers between devices: 63.7 us -> 70 us
  matrix products: 33.5 us -> 37 us
  starting transfers between devices: 40.3 us -> 38 us
    ppermute x3, waiting for transfers between devices: 1.29 us -> 20 us  [head_sum_line(): lax.ppermute(going_right.astype(jnp.bfloat16), 'head', rightward)]
    ppermute x3, waiting for transfers between devices: 19.5 us -> 4.24 us  [head_sum_line(): from_right = lax.ppermute(going_left.astype(jnp.bfloat16), 'head', leftward)]
    dot_general x4, matrix products: 9.95 us -> 13.5 us  [absorb(): jnp.einsum('brd,bnd->brn', queries, key_rows, preferred_element_type=jnp....]
    unnamed x51 -> x48, local copies, waits for them, and re-layouts: 4.03 us -> 1.16 us
    gather x1 -> x0, local copies, waits for them, and re-layouts: 2.42 us -> none  [head_sum_line(): return jnp.take(candidates, pick, axis=0)]
    ppermute x3, waiting for transfers between devices: 2.3 us -> 4.65 us  [head_sum_line(): send_left = lax.ppermute(send_left, 'head', leftward)]
    slice x2 -> x0, local copies, waits for them, and re-layouts: 1.87 us -> none  [the longest x1 1.04 us: shards(): span_out = summed[:, :span_block].reshape(span_rows_all.shape[:-1] + (-1,))]
  transfers between devices with their start and end apart: 21 -> 21, of which waited for: 12 -> 12; matrix products, arithmetic and copies ran while one was open for 18% -> 16% of each run, Pallas kernels for 0% -> 0%
where the time goes in v12:
time: 173 us
  waiting for transfers between devices  70 us (40%)
  starting transfers between devices  38 us (22%)
  matrix products  37 us (21%)
  other arithmetic  15.5 us (9%)
  local copies, waits for them, and re-layouts  10.4 us (6%)
  between operations  1.81 us (1%)
    ppermute x3, waiting for transfers between devices, ctx_shards(): received.append(lax.ppermute(block, 'ctx', pairs))  28.8 us
    ppermute x3, waiting for transfers between devices, head_sum_line(): lax.ppermute(going_right.astype(jnp.bfloat16), 'head', rightward)  20 us
    dot_general x4, matrix products, absorb(): jnp.einsum('brd,bnd->brn', queries, key_rows, preferred_element_type=jnp....  13.5 us
    ppermute x3, starting transfers between devices, head_sum_line(): lax.ppermute(going_right.astype(jnp.bfloat16), 'head', rightward)  12.3 us
    ppermute x3, starting transfers between devices, head_sum_line(): send_right = lax.ppermute(send_right, 'head', rightward)  12.3 us
    ppermute x3, waiting for transfers between devices, head_sum_line(): send_right = lax.ppermute(send_right, 'head', rightward)  11.6 us
    dot_general x4, matrix products, absorb(): jnp.einsum('brn,bnd->brd', weights.astype(jnp.bfloat16), value_rows, pref...  10.9 us
    reduce_sum x4, other arithmetic, absorb(): running_sum = running_sum * factor + jnp.sum(weights, axis=-1)  9.87 us
  transfers between devices with their start and end apart: 21, of which 12 were waited for; matrix products, arithmetic and copies ran while one was open for 16% of the time, Pallas kernels for 0%

profile of v12, /device:TPU:0, one launch (start us, length us, event | category | flops | bytes accessed | tf_op | source)
XLA Modules:
  0.0 172.8 jit_solution(6229175658256004401)
XLA Ops:
  5.1 2.9 %collective-permute-start.1 = (bf16[2,2,2,512,128]{4,3,2,1,0:T(8,128)(2,1)}, bf16[2,2,2,512,128]{4,3,2,1,0:T(8,128)(2,1)S(1)}, u32[]{:S(2)}, u32[]{:S(2)}) collective-permute-start(bf16[2,2,2,512,128]{4,3,2,1,0:T(8,128)(2,1)} %pad_maximum_fusion.2), channel_id=1, source_target_pairs={{0,8},{4,12},{8,0},{12,4},{1,9},{5,13},{9,1},{13,5},{2,10},{6,14},... | collective-permute-start | bytes 3145736 | tf_op jit(solution)/shard_map/ppermute | solution.py:200
  11.7 21.1 %collective-permute-done.3 = bf16[2,2,32,2,128]{4,2,3,1,0:T(8,128)(2,1)S(1)} collective-permute-done((bf16[2,2,32,2,128]{4,2,3,1,0:T(8,128)(2,1)S(1)}, bf16[2,2,32,2,128]{4,2,3,1,0:T(8,128)(2,1)S(1)}, u32[]{:S(2)}, u32[]{:S(2)}) %collective-permute-start.3) | collective-permute-done | bytes 65568 | tf_op jit(solution)/shard_map/ppermute | solution.py:80
  43.2 7.6 %bitcast_reduce_fusion.1 = (f32[4,256]{1,0:T(4,128)S(1)}, f32[4,2048,256]{2,1,0:T(8,128)}) fusion(bf16[4,256,128]{2,1,0:T(8,128)(2,1)} %bitcast.306, bf16[4,512,128]{2,1,0:T(8,128)(2,1)S(1)} %bitcast.322, bf16[4,512,128]{2,1,0:T(8,128)(2,1)S(1)} %bitcast.318, bf16[4,512,128]{2,1,0:T(8,128)(2,1)S(1)} %bitcast.320, bf16[4,512,128]{2,1,0:T(8,128)(2,1)S(1)} %bitcast.298), kind=kOutput, calls=%fused_computation.8 | convolution fusion | flops 549452800 | bytes 10752000 | tf_op jit(solution)/shard_map/while/body/eval_jaxpr/brd,bnd->brn/dot_general | solution.py:14
  50.8 3.9 %bitcast_reduce_fusion = (f32[4,256]{1,0:T(4,128)S(1)}, f32[4,2048,256]{2,1,0:T(8,128)}) fusion(bf16[4,256,128]{2,1,0:T(8,128)(2,1)S(1)} %bitcast.303, bf16[4,512,128]{2,1,0:T(8,128)(2,1)S(1)} %bitcast.323, bf16[4,512,128]{2,1,0:T(8,128)(2,1)S(1)} %bitcast.319, bf16[4,512,128]{2,1,0:T(8,128)(2,1)S(1)} %bitcast.321, bf16[4,512,128]{2,1,0:T(8,128)(2,1)S(1)} %bitcast.299), kind=kOutput, calls=%fused_computation.1 | convolution fusion | flops 549452800 | bytes 10752000 | tf_op jit(solution)/shard_map/while/body/eval_jaxpr/brd,bnd->brn/dot_general | solution.py:14
  54.9 4.8 %fusion.8 = f32[4,256]{1,0:T(4,128)S(1)} fusion(f32[4,2048,256]{2,1,0:T(8,128)} %get-tuple-element.114, f32[4,256]{1,0:T(4,128)S(1)} %get-tuple-element.110), kind=kLoop, calls=%fused_computation.12 | loop fusion | flops 6290432 | bytes 8396800 | tf_op jit(solution)/shard_map/while/body/eval_jaxpr/reduce_sum | solution.py:22
  60.4 5.5 %fusion.30 = f32[4,256,128]{2,1,0:T(8,128)S(1)} fusion(f32[4,2048,256]{2,1,0:T(8,128)} %get-tuple-element.114, f32[4,256]{1,0:T(4,128)S(1)} %get-tuple-element.110, bf16[4,512,128]{2,1,0:T(8,128)(2,1)} %bitcast.316, bf16[4,512,128]{2,1,0:T(8,128)(2,1)S(1)} %bitcast.312, bf16[4,512,128]{2,1,0:T(8,128)(2,1)S(1)} %bitcast.314, ...), kind=kOutput, calls=%fused_computation.36 | convolution fusion | flops 551813120 | bytes 11022336 | tf_op jit(solution)/shard_map/while/body/eval_jaxpr/brn,bnd->brd/dot_general | solution.py:23
  68.6 4.8 %fusion.6 = f32[4,256]{1,0:T(4,128)S(1)} fusion(f32[4,2048,256]{2,1,0:T(8,128)} %get-tuple-element.118, f32[4,256]{1,0:T(4,128)S(1)} %get-tuple-element.108), kind=kLoop, calls=%fused_computation.10 | loop fusion | flops 6290432 | bytes 8396800 | tf_op jit(solution)/shard_map/while/body/eval_jaxpr/reduce_sum | solution.py:22
  73.6 4.8 %fusion.33 = f32[4,256,128]{2,1,0:T(8,128)S(1)} fusion(f32[4,2048,256]{2,1,0:T(8,128)} %get-tuple-element.118, f32[4,256]{1,0:T(4,128)S(1)} %get-tuple-element.108, bf16[4,512,128]{2,1,0:T(8,128)(2,1)S(1)} %bitcast.317, bf16[4,512,128]{2,1,0:T(8,128)(2,1)S(1)} %bitcast.313, bf16[4,512,128]{2,1,0:T(8,128)(2,1)S(1)} %bitcast.315, ...), kind=kOutput, calls=%fused_computation.37 | convolution fusion | flops 551813120 | bytes 11022336 | tf_op jit(solution)/shard_map/while/body/eval_jaxpr/brn,bnd->brd/dot_general | solution.py:23
  79.6 7.7 %collective-permute-done.5 = bf16[2,32,2048]{2,1,0:T(8,128)(2,1)S(1)} collective-permute-done((bf16[2,32,2048]{2,1,0:T(8,128)(2,1)S(1)}, bf16[2,32,2048]{2,1,0:T(8,128)(2,1)S(1)}, u32[]{:S(2)}, u32[]{:S(2)}) %collective-permute-start.5) | collective-permute-done | bytes 262176 | tf_op jit(solution)/shard_map/ppermute | solution.py:80
  88.0 4.8 %fusion.1 = f32[4,32,2048]{2,1,0:T(8,128)S(1)} fusion(bf16[4,32,2048]{2,1,0:T(8,128)(2,1)S(1)} %bitcast.290, bf16[2048,2048]{1,0:T(8,128)(2,1)} %param.27), kind=kOutput, calls=%fused_computation.3 | convolution fusion | flops 1073741824 | bytes 9961472 | tf_op jit(solution)/shard_map/dot_general | solution.py:249
  96.6 3.5 %collective-permute-start.9 = (bf16[96,2048]{1,0:T(8,128)(2,1)S(1)}, bf16[96,2048]{1,0:T(8,128)(2,1)S(1)}, u32[]{:S(2)}, u32[]{:S(2)}) collective-permute-start(bf16[96,2048]{1,0:T(8,128)(2,1)S(1)} %pad_maximum_fusion.4), channel_id=1, source_target_pairs={{0,1},{1,2},{2,3},{4,5},{5,6},{6,7},{8,9},{9,10},{10,11},{12,13},{... | collective-permute-start | bytes 1179656 | tf_op jit(solution)/shard_map/ppermute | solution.py:119
  101.7 7.4 %collective-permute-done.9 = bf16[96,2048]{1,0:T(8,128)(2,1)S(1)} collective-permute-done((bf16[96,2048]{1,0:T(8,128)(2,1)S(1)}, bf16[96,2048]{1,0:T(8,128)(2,1)S(1)}, u32[]{:S(2)}, u32[]{:S(2)}) %collective-permute-start.9) | collective-permute-done | bytes 393248 | tf_op jit(solution)/shard_map/ppermute | solution.py:119
  109.2 4.4 %collective-permute-start.10 = (bf16[96,2048]{1,0:T(8,128)(2,1)S(1)}, bf16[96,2048]{1,0:T(8,128)(2,1)S(1)}, u32[]{:S(2)}, u32[]{:S(2)}) collective-permute-start(bf16[96,2048]{1,0:T(8,128)(2,1)S(1)} %fusion.45), channel_id=1, source_target_pairs={{0,1},{1,2},{2,3},{4,5},{5,6},{6,7},{8,9},{9,10},{10,11},{12,13},{... | collective-permute-start | bytes 1179656 | tf_op jit(solution)/shard_map/ppermute | solution.py:119
  115.0 6.8 %collective-permute-done.10 = bf16[96,2048]{1,0:T(8,128)(2,1)S(1)} collective-permute-done((bf16[96,2048]{1,0:T(8,128)(2,1)S(1)}, bf16[96,2048]{1,0:T(8,128)(2,1)S(1)}, u32[]{:S(2)}, u32[]{:S(2)}) %collective-permute-start.10) | collective-permute-done | bytes 393248 | tf_op jit(solution)/shard_map/ppermute | solution.py:119
  121.9 4.4 %collective-permute-start.11 = (bf16[96,2048]{1,0:T(8,128)(2,1)S(1)}, bf16[96,2048]{1,0:T(8,128)(2,1)S(1)}, u32[]{:S(2)}, u32[]{:S(2)}) collective-permute-start(bf16[96,2048]{1,0:T(8,128)(2,1)S(1)} %fusion.44), channel_id=1, source_target_pairs={{0,1},{1,2},{2,3},{4,5},{5,6},{6,7},{8,9},{9,10},{10,11},{12,13},{... | collective-permute-start | bytes 1179656 | tf_op jit(solution)/shard_map/ppermute | solution.py:119
  127.7 5.9 %collective-permute-done.11 = bf16[96,2048]{1,0:T(8,128)(2,1)S(1)} collective-permute-done((bf16[96,2048]{1,0:T(8,128)(2,1)S(1)}, bf16[96,2048]{1,0:T(8,128)(2,1)S(1)}, u32[]{:S(2)}, u32[]{:S(2)}) %collective-permute-start.11) | collective-permute-done | bytes 393248 | tf_op jit(solution)/shard_map/ppermute | solution.py:119
  133.6 4.2 %collective-permute-done.14 = bf16[96,2048]{1,0:T(8,128)(2,1)S(1)} collective-permute-done((bf16[96,2048]{1,0:T(8,128)(2,1)S(1)}, bf16[96,2048]{1,0:T(8,128)(2,1)S(1)}, u32[]{:S(2)}, u32[]{:S(2)}) %collective-permute-start.14) | collective-permute-done | bytes 393248 | tf_op jit(solution)/shard_map/ppermute | solution.py:120
  138.0 3.5 %collective-permute-start.15 = (bf16[96,2048]{1,0:T(8,128)(2,1)S(1)}, bf16[96,2048]{1,0:T(8,128)(2,1)S(1)}, u32[]{:S(2)}, u32[]{:S(2)}) collective-permute-start(bf16[96,2048]{1,0:T(8,128)(2,1)S(1)} %fusion.43), channel_id=1, source_target_pairs={{0,1},{1,2},{2,3},{4,5},{5,6},{6,7},{8,9},{9,10},{10,11},{12,13},{... | collective-permute-start | bytes 1179656 | tf_op jit(solution)/shard_map/ppermute | solution.py:139
  143.1 4.5 %collective-permute-done.15 = bf16[96,2048]{1,0:T(8,128)(2,1)S(1)} collective-permute-done((bf16[96,2048]{1,0:T(8,128)(2,1)S(1)}, bf16[96,2048]{1,0:T(8,128)(2,1)S(1)}, u32[]{:S(2)}, u32[]{:S(2)}) %collective-permute-start.15) | collective-permute-done | bytes 393248 | tf_op jit(solution)/shard_map/ppermute | solution.py:139
  147.6 4.4 %collective-permute-start.17 = (bf16[96,2048]{1,0:T(8,128)(2,1)S(1)}, bf16[96,2048]{1,0:T(8,128)(2,1)S(1)}, u32[]{:S(2)}, u32[]{:S(2)}) collective-permute-start(bf16[96,2048]{1,0:T(8,128)(2,1)S(1)} %collective-permute-done.15), channel_id=1, source_target_pairs={{0,1},{1,2},{2,3},{4,5},{5,6},{6,7},{8,9},{9,10},{10,11},{12,13},{... | collective-permute-start | bytes 1179656 | tf_op jit(solution)/shard_map/ppermute | solution.py:139
  153.7 3.6 %collective-permute-done.17 = bf16[96,2048]{1,0:T(8,128)(2,1)S(1)} collective-permute-done((bf16[96,2048]{1,0:T(8,128)(2,1)S(1)}, bf16[96,2048]{1,0:T(8,128)(2,1)S(1)}, u32[]{:S(2)}, u32[]{:S(2)}) %collective-permute-start.17) | collective-permute-done | bytes 393248 | tf_op jit(solution)/shard_map/ppermute | solution.py:139
  157.2 4.4 %collective-permute-start.19 = (bf16[96,2048]{1,0:T(8,128)(2,1)S(1)}, bf16[96,2048]{1,0:T(8,128)(2,1)S(1)}, u32[]{:S(2)}, u32[]{:S(2)}) collective-permute-start(bf16[96,2048]{1,0:T(8,128)(2,1)S(1)} %collective-permute-done.17), channel_id=1, source_target_pairs={{0,1},{1,2},{2,3},{4,5},{5,6},{6,7},{8,9},{9,10},{10,11},{12,13},{... | collective-permute-start | bytes 1179656 | tf_op jit(solution)/shard_map/ppermute | solution.py:139
  163.4 3.5 %collective-permute-done.19 = bf16[96,2048]{1,0:T(8,128)(2,1)S(1)} collective-permute-done((bf16[96,2048]{1,0:T(8,128)(2,1)S(1)}, bf16[96,2048]{1,0:T(8,128)(2,1)S(1)}, u32[]{:S(2)}, u32[]{:S(2)}) %collective-permute-start.19) | collective-permute-done | bytes 393248 | tf_op jit(solution)/shard_map/ppermute | solution.py:139
  167.1 4.5 %collective-permute-done.20 = bf16[96,2048]{1,0:T(8,128)(2,1)S(1)} collective-permute-done((bf16[96,2048]{1,0:T(8,128)(2,1)S(1)}, bf16[96,2048]{1,0:T(8,128)(2,1)S(1)}, u32[]{:S(2)}, u32[]{:S(2)}) %collective-permute-start.20) | collective-permute-done | bytes 393248 | tf_op jit(solution)/shard_map/ppermute | solution.py:140
  (176 shorter events, 38.0 us)
Async XLA Ops:
  0.6 65.7 %copy-start = (bf16[4,8,2,128]{3,2,1,0:T(2,128)(2,1)S(1)}, bf16[4,8,2,128]{3,2,1,0:T(2,128)(2,1)}, u32[]{:S(2)}) copy-start(bf16[4,8,2,128]{3,2,1,0:T(2,128)(2,1)} %param.25) | copy-start | bytes 49156
  0.7 10.9 %copy-start.21 = (s32[32]{0:T(128)S(1)}, s32[32]{0:T(128)}, u32[]{:S(2)}) copy-start(s32[32]{0:T(128)} %param.26) | copy-start | bytes 388
  5.1 29.4 %collective-permute-start.1 = (bf16[2,2,2,512,128]{4,3,2,1,0:T(8,128)(2,1)}, bf16[2,2,2,512,128]{4,3,2,1,0:T(8,128)(2,1)S(1)}, u32[]{:S(2)}, u32[]{:S(2)}) collective-permute-start(bf16[2,2,2,512,128]{4,3,2,1,0:T(8,128)(2,1)} %pad_maximum_fusion.2), channel_id=1, source_target_pairs={{0,8},{4,12},{8,0},{12,4},{1,9},{5,13},{9,1},{13,5},{2,10},{6,14},... | collective-permute-start | bytes 3145736 | tf_op jit(solution)/shard_map/ppermute | solution.py:200
  8.0 31.0 %collective-permute-start = (bf16[2,2,2,512,128]{4,3,2,1,0:T(8,128)(2,1)}, bf16[2,2,2,512,128]{4,3,2,1,0:T(8,128)(2,1)}, u32[]{:S(2)}, u32[]{:S(2)}) collective-permute-start(bf16[2,2,2,512,128]{4,3,2,1,0:T(8,128)(2,1)} %pad_maximum_fusion.2), channel_id=1, source_target_pairs={{0,4},{4,0},{8,12},{12,8},{1,5},{5,1},{9,13},{13,9},{2,6},{6,2},{1... | collective-permute-start | bytes 3145736 | tf_op jit(solution)/shard_map/ppermute | solution.py:203
  8.1 24.7 %collective-permute-start.3 = (bf16[2,2,32,2,128]{4,2,3,1,0:T(8,128)(2,1)S(1)}, bf16[2,2,32,2,128]{4,2,3,1,0:T(8,128)(2,1)S(1)}, u32[]{:S(2)}, u32[]{:S(2)}) collective-permute-start(bf16[2,2,32,2,128]{4,2,3,1,0:T(8,128)(2,1)S(1)} %get-tuple-element.103), channel_id=1, source_target_pairs={{0,8},{4,12},{8,0},{12,4},{1,9},{5,13},{9,1},{13,5},{2,10},{6,14},... | collective-permute-start | bytes 196616 | tf_op jit(solution)/shard_map/ppermute | solution.py:80
  32.8 1.4 collective-permute-start.4
  34.5 6.6 %collective-permute-start.2 = (bf16[2,2,2,512,128]{4,3,2,1,0:T(8,128)(2,1)S(1)}, bf16[2,2,2,512,128]{4,3,2,1,0:T(8,128)(2,1)}, u32[]{:S(2)}, u32[]{:S(2)}) collective-permute-start(bf16[2,2,2,512,128]{4,3,2,1,0:T(8,128)(2,1)S(1)} %collective-permute-done.1), channel_id=1, source_target_pairs={{0,4},{4,0},{8,12},{12,8},{1,5},{5,1},{9,13},{13,9},{2,6},{6,2},{1... | collective-permute-start | bytes 3145736 | tf_op jit(solution)/shard_map/ppermute | solution.py:204
  66.7 12.6 %collective-permute-start.7 = (bf16[4,8,2048]{2,1,0:T(8,128)(2,1)S(1)}, bf16[4,8,2048]{2,1,0:T(8,128)(2,1)S(1)}, u32[]{:S(2)}, u32[]{:S(2)}) collective-permute-start(bf16[4,8,2048]{2,1,0:T(8,128)(2,1)S(1)} %reshape.236), channel_id=1, source_target_pairs={{0,8},{4,12},{8,0},{12,4},{1,9},{5,13},{9,1},{13,5},{2,10},{6,14},... | collective-permute-start | bytes 393224 | tf_op jit(solution)/shard_map/ppermute | solution.py:80
  78.9 8.3 %collective-permute-start.5 = (bf16[2,32,2048]{2,1,0:T(8,128)(2,1)S(1)}, bf16[2,32,2048]{2,1,0:T(8,128)(2,1)S(1)}, u32[]{:S(2)}, u32[]{:S(2)}) collective-permute-start(bf16[2,32,2048]{2,1,0:T(8,128)(2,1)S(1)} %reshape.232), channel_id=1, source_target_pairs={{0,8},{4,12},{8,0},{12,4},{1,9},{5,13},{9,1},{13,5},{2,10},{6,14},... | collective-permute-start | bytes 786440 | tf_op jit(solution)/shard_map/ppermute | solution.py:80
  79.3 8.0 %collective-permute-start.8 = (bf16[2,4,8,2048]{3,2,1,0:T(8,128)(2,1)S(1)}, bf16[2,4,8,2048]{3,2,1,0:T(8,128)(2,1)S(1)}, u32[]{:S(2)}, u32[]{:S(2)}) collective-permute-start(bf16[2,4,8,2048]{3,2,1,0:T(8,128)(2,1)S(1)} %pad_maximum_fusion.10), channel_id=1, source_target_pairs={{0,4},{4,0},{8,12},{12,8},{1,5},{5,1},{9,13},{13,9},{2,6},{6,2},{1... | collective-permute-start | bytes 786440 | tf_op jit(solution)/shard_map/ppermute | solution.py:82
  87.3 5.7 %collective-permute-start.6 = (bf16[2,2,32,2048]{3,2,1,0:T(8,128)(2,1)S(1)}, bf16[2,2,32,2048]{3,2,1,0:T(8,128)(2,1)S(1)}, u32[]{:S(2)}, u32[]{:S(2)}) collective-permute-start(bf16[2,2,32,2048]{3,2,1,0:T(8,128)(2,1)S(1)} %pad_maximum_fusion.3), channel_id=1, source_target_pairs={{0,4},{4,0},{8,12},{12,8},{1,5},{5,1},{9,13},{13,9},{2,6},{6,2},{1... | collective-permute-start | bytes 1572872 | tf_op jit(solution)/shard_map/ppermute | solution.py:82
  96.6 12.5 %collective-permute-start.9 = (bf16[96,2048]{1,0:T(8,128)(2,1)S(1)}, bf16[96,2048]{1,0:T(8,128)(2,1)S(1)}, u32[]{:S(2)}, u32[]{:S(2)}) collective-permute-start(bf16[96,2048]{1,0:T(8,128)(2,1)S(1)} %pad_maximum_fusion.4), channel_id=1, source_target_pairs={{0,1},{1,2},{2,3},{4,5},{5,6},{6,7},{8,9},{9,10},{10,11},{12,13},{... | collective-permute-start | bytes 1179656 | tf_op jit(solution)/shard_map/ppermute | solution.py:119
  100.2 13.5 %collective-permute-start.12 = (bf16[96,2048]{1,0:T(8,128)(2,1)S(1)}, bf16[96,2048]{1,0:T(8,128)(2,1)S(1)}, u32[]{:S(2)}, u32[]{:S(2)}) collective-permute-start(bf16[96,2048]{1,0:T(8,128)(2,1)S(1)} %pad_maximum_fusion.5), channel_id=1, source_target_pairs={{1,0},{2,1},{3,2},{5,4},{6,5},{7,6},{9,8},{10,9},{11,10},{13,12},{... | collective-permute-start | bytes 1179656 | tf_op jit(solution)/shard_map/ppermute | solution.py:120
  109.2 12.6 %collective-permute-start.10 = (bf16[96,2048]{1,0:T(8,128)(2,1)S(1)}, bf16[96,2048]{1,0:T(8,128)(2,1)S(1)}, u32[]{:S(2)}, u32[]{:S(2)}) collective-permute-start(bf16[96,2048]{1,0:T(8,128)(2,1)S(1)} %fusion.45), channel_id=1, source_target_pairs={{0,1},{1,2},{2,3},{4,5},{5,6},{6,7},{8,9},{9,10},{10,11},{12,13},{... | collective-permute-start | bytes 1179656 | tf_op jit(solution)/shard_map/ppermute | solution.py:119
  113.7 12.6 %collective-permute-start.13 = (bf16[96,2048]{1,0:T(8,128)(2,1)S(1)}, bf16[96,2048]{1,0:T(8,128)(2,1)S(1)}, u32[]{:S(2)}, u32[]{:S(2)}) collective-permute-start(bf16[96,2048]{1,0:T(8,128)(2,1)S(1)} %fusion.47), channel_id=1, source_target_pairs={{1,0},{2,1},{3,2},{5,4},{6,5},{7,6},{9,8},{10,9},{11,10},{13,12},{... | collective-permute-start | bytes 1179656 | tf_op jit(solution)/shard_map/ppermute | solution.py:120
  121.9 11.7 %collective-permute-start.11 = (bf16[96,2048]{1,0:T(8,128)(2,1)S(1)}, bf16[96,2048]{1,0:T(8,128)(2,1)S(1)}, u32[]{:S(2)}, u32[]{:S(2)}) collective-permute-start(bf16[96,2048]{1,0:T(8,128)(2,1)S(1)} %fusion.44), channel_id=1, source_target_pairs={{0,1},{1,2},{2,3},{4,5},{5,6},{6,7},{8,9},{9,10},{10,11},{12,13},{... | collective-permute-start | bytes 1179656 | tf_op jit(solution)/shard_map/ppermute | solution.py:119
  126.4 11.4 %collective-permute-start.14 = (bf16[96,2048]{1,0:T(8,128)(2,1)S(1)}, bf16[96,2048]{1,0:T(8,128)(2,1)S(1)}, u32[]{:S(2)}, u32[]{:S(2)}) collective-permute-start(bf16[96,2048]{1,0:T(8,128)(2,1)S(1)} %fusion.46), channel_id=1, source_target_pairs={{1,0},{2,1},{3,2},{5,4},{6,5},{7,6},{9,8},{10,9},{11,10},{13,12},{... | collective-permute-start | bytes 1179656 | tf_op jit(solution)/shard_map/ppermute | solution.py:120
  138.0 9.6 %collective-permute-start.15 = (bf16[96,2048]{1,0:T(8,128)(2,1)S(1)}, bf16[96,2048]{1,0:T(8,128)(2,1)S(1)}, u32[]{:S(2)}, u32[]{:S(2)}) collective-permute-start(bf16[96,2048]{1,0:T(8,128)(2,1)S(1)} %fusion.43), channel_id=1, source_target_pairs={{0,1},{1,2},{2,3},{4,5},{5,6},{6,7},{8,9},{9,10},{10,11},{12,13},{... | collective-permute-start | bytes 1179656 | tf_op jit(solution)/shard_map/ppermute | solution.py:139
  141.5 10.7 %collective-permute-start.16 = (bf16[96,2048]{1,0:T(8,128)(2,1)S(1)}, bf16[96,2048]{1,0:T(8,128)(2,1)S(1)}, u32[]{:S(2)}, u32[]{:S(2)}) collective-permute-start(bf16[96,2048]{1,0:T(8,128)(2,1)S(1)} %fusion.43), channel_id=1, source_target_pairs={{1,0},{2,1},{3,2},{5,4},{6,5},{7,6},{9,8},{10,9},{11,10},{13,12},{... | collective-permute-start | bytes 1179656 | tf_op jit(solution)/shard_map/ppermute | solution.py:140
  147.6 9.7 %collective-permute-start.17 = (bf16[96,2048]{1,0:T(8,128)(2,1)S(1)}, bf16[96,2048]{1,0:T(8,128)(2,1)S(1)}, u32[]{:S(2)}, u32[]{:S(2)}) collective-permute-start(bf16[96,2048]{1,0:T(8,128)(2,1)S(1)} %collective-permute-done.15), channel_id=1, source_target_pairs={{0,1},{1,2},{2,3},{4,5},{5,6},{6,7},{8,9},{9,10},{10,11},{12,13},{... | collective-permute-start | bytes 1179656 | tf_op jit(solution)/shard_map/ppermute | solution.py:139
  152.2 9.8 %collective-permute-start.18 = (bf16[96,2048]{1,0:T(8,128)(2,1)S(1)}, bf16[96,2048]{1,0:T(8,128)(2,1)S(1)}, u32[]{:S(2)}, u32[]{:S(2)}) collective-permute-start(bf16[96,2048]{1,0:T(8,128)(2,1)S(1)} %collective-permute-done.16), channel_id=1, source_target_pairs={{1,0},{2,1},{3,2},{5,4},{6,5},{7,6},{9,8},{10,9},{11,10},{13,12},{... | collective-permute-start | bytes 1179656 | tf_op jit(solution)/shard_map/ppermute | solution.py:140
  153.5 19.3 %copy-start.1 = (bf16[4,8,2,128]{3,2,1,0:T(2,128)(2,1)S(1)}, bf16[4,8,2,128]{3,2,1,0:T(2,128)(2,1)}, u32[]{:S(2)}) copy-start(bf16[4,8,2,128]{3,2,1,0:T(2,128)(2,1)} %param.25) | copy-start | bytes 49156
  157.2 9.7 %collective-permute-start.19 = (bf16[96,2048]{1,0:T(8,128)(2,1)S(1)}, bf16[96,2048]{1,0:T(8,128)(2,1)S(1)}, u32[]{:S(2)}, u32[]{:S(2)}) collective-permute-start(bf16[96,2048]{1,0:T(8,128)(2,1)S(1)} %collective-permute-done.17), channel_id=1, source_target_pairs={{0,1},{1,2},{2,3},{4,5},{5,6},{6,7},{8,9},{9,10},{10,11},{12,13},{... | collective-permute-start | bytes 1179656 | tf_op jit(solution)/shard_map/ppermute | solution.py:139
  161.9 9.7 %collective-permute-start.20 = (bf16[96,2048]{1,0:T(8,128)(2,1)S(1)}, bf16[96,2048]{1,0:T(8,128)(2,1)S(1)}, u32[]{:S(2)}, u32[]{:S(2)}) collective-permute-start(bf16[96,2048]{1,0:T(8,128)(2,1)S(1)} %collective-permute-done.18), channel_id=1, source_target_pairs={{1,0},{2,1},{3,2},{5,4},{6,5},{7,6},{9,8},{10,9},{11,10},{13,12},{... | collective-permute-start | bytes 1179656 | tf_op jit(solution)/shard_map/ppermute | solution.py:140
  (21 other events, 108.9 us)

commit v13 on v11

--- a/solution.py
+++ b/solution.py
@@ -107,19 +107,12 @@
 
     rightward = [(dev, dev + 1) for dev in range(last)]
     leftward = [(dev + 1, dev) for dev in range(last)]
-    from_left = from_right = None
-    for step in range(1, head_count):
-        right_block = jnp.clip(head_index + head_count - step, 0, last)
-        left_block = jnp.clip(head_index - head_count + step, 0, last)
-        going_right = take_block(right_block)
-        going_left = take_block(left_block)
-        if from_left is not None:
-            going_right = going_right + from_left.astype(jnp.float32)
-            going_left = going_left + from_right.astype(jnp.float32)
-        from_left = lax.ppermute(going_right.astype(jnp.bfloat16), "head", rightward)
-        from_right = lax.ppermute(going_left.astype(jnp.bfloat16), "head", leftward)
-    own = take_block(head_index)
-    mine = (own + from_left.astype(jnp.float32) + from_right.astype(jnp.float32)).astype(jnp.bfloat16)
+    total = take_block(head_index)
+    for offset in [step for step in range(1, head_count)] + [-step for step in range(1, head_count)]:
+        pairs = [(dev, dev + offset) for dev in range(head_count) if 0 <= dev + offset <= last]
+        outgoing = take_block(jnp.clip(head_index + offset, 0, last)).astype(jnp.bfloat16)
+        total = total + lax.ppermute(outgoing, "head", pairs).astype(jnp.float32)
+    mine = total.astype(jnp.bfloat16)
     lefts, rights = [], []
     send_right = send_left = mine
     for step in range(1, head_count):

time: 173 us -> 181 us (1.046)
  starting transfers between devices: 40.3 us -> 50.8 us
  waiting for transfers between devices: 63.7 us -> 60.8 us
    ppermute x6, starting transfers between devices: 17.6 us -> 30.5 us  [head_sum_line(): total = total + lax.ppermute(outgoing, 'head', pairs).astype(jnp.float32)]
    ppermute x6, waiting for transfers between devices: 20.8 us -> 13.9 us  [head_sum_line(): total = total + lax.ppermute(outgoing, 'head', pairs).astype(jnp.float32)]
    ppermute x3, waiting for transfers between devices: 11 us -> 14.5 us  [head_sum_line(): send_right = lax.ppermute(send_right, 'head', rightward)]
    ppermute x3, starting transfers between devices: 13.2 us -> 10.8 us  [head_sum_line(): send_right = lax.ppermute(send_right, 'head', rightward)]
    unnamed x51 -> x49, local copies, waits for them, and re-layouts: 4.03 us -> 4.06 us
  transfers between devices with their start and end apart: 21 -> 21, of which waited for: 12 -> 10; matrix products, arithmetic and copies ran while one was open for 18% -> 17% of each run, Pallas kernels for 0% -> 0%
where the time goes in v13:
time: 181 us; the launch traced here: 180 us
  waiting for transfers between devices  60.8 us (34%)
  starting transfers between devices  50.8 us (28%)
  matrix products  33.6 us (19%)
  local copies, waits for them, and re-layouts  17.8 us (10%)
  other arithmetic  15.9 us (9%)
    ppermute x6, starting transfers between devices, head_sum_line(): total = total + lax.ppermute(outgoing, 'head', pairs).astype(jnp.float32)  30.5 us
    ppermute x3, waiting for transfers between devices, ctx_shards(): received.append(lax.ppermute(block, 'ctx', pairs))  28.8 us
    ppermute x3, waiting for transfers between devices, head_sum_line(): send_right = lax.ppermute(send_right, 'head', rightward)  14.5 us
    ppermute x6, waiting for transfers between devices, head_sum_line(): total = total + lax.ppermute(outgoing, 'head', pairs).astype(jnp.float32)  13.9 us
    dot_general x4, matrix products, absorb(): jnp.einsum('brn,bnd->brd', weights.astype(jnp.bfloat16), value_rows, pref...  11 us
    ppermute x3, starting transfers between devices, head_sum_line(): send_right = lax.ppermute(send_right, 'head', rightward)  10.8 us
    dot_general x4, matrix products, absorb(): jnp.einsum('brd,bnd->brn', queries, key_rows, preferred_element_type=jnp....  9.97 us
    reduce_sum x4, other arithmetic, absorb(): running_sum = running_sum * factor + jnp.sum(weights, axis=-1)  9.84 us
  transfers between devices with their start and end apart: 21, of which 10 were waited for; matrix products, arithmetic and copies ran while one was open for 17% of the time, Pallas kernels for 0%

profile of v13, /device:TPU:0, one launch (start us, length us, event | category | flops | bytes accessed | tf_op | source)
XLA Modules:
  0.0 180.5 jit_solution(15829477214905366736)
XLA Ops:
  5.1 2.9 %collective-permute-start.1 = (bf16[2,2,2,512,128]{4,3,2,1,0:T(8,128)(2,1)}, bf16[2,2,2,512,128]{4,3,2,1,0:T(8,128)(2,1)S(1)}, u32[]{:S(2)}, u32[]{:S(2)}) collective-permute-start(bf16[2,2,2,512,128]{4,3,2,1,0:T(8,128)(2,1)} %pad_maximum_fusion.2), channel_id=1, source_target_pairs={{0,8},{4,12},{8,0},{12,4},{1,9},{5,13},{9,1},{13,5},{2,10},{6,14},... | collective-permute-start | bytes 3145736 | tf_op jit(solution)/shard_map/ppermute | solution.py:187
  11.7 21.1 %collective-permute-done.3 = bf16[2,2,32,2,128]{4,2,3,1,0:T(8,128)(2,1)S(1)} collective-permute-done((bf16[2,2,32,2,128]{4,2,3,1,0:T(8,128)(2,1)S(1)}, bf16[2,2,32,2,128]{4,2,3,1,0:T(8,128)(2,1)S(1)}, u32[]{:S(2)}, u32[]{:S(2)}) %collective-permute-start.3) | collective-permute-done | bytes 65568 | tf_op jit(solution)/shard_map/ppermute | solution.py:80
  41.1 2.1 %fusion.117 = (bf16[1,2,2,512,128]{4,3,2,1,0:T(8,128)(2,1)}, bf16[1,2,2,512,128]{4,3,2,1,0:T(8,128)(2,1)S(1)}) fusion(bf16[2,2,2,512,128]{4,3,2,1,0:T(8,128)(2,1)} %collective-permute-done.2), kind=kLoop, calls=%fused_computation.210 | loop fusion | bytes 2097152 | tf_op jit(solution)/shard_map/slice | solution.py:193
  43.2 3.9 %bitcast_reduce_fusion = (f32[4,256]{1,0:T(4,128)S(1)}, f32[4,2048,256]{2,1,0:T(8,128)}) fusion(bf16[4,256,128]{2,1,0:T(8,128)(2,1)S(1)} %bitcast.238, bf16[4,512,128]{2,1,0:T(8,128)(2,1)S(1)} %bitcast.258, bf16[4,512,128]{2,1,0:T(8,128)(2,1)S(1)} %bitcast.254, bf16[4,512,128]{2,1,0:T(8,128)(2,1)S(1)} %bitcast.256, bf16[4,512,128]{2,1,0:T(8,128)(2,1)S(1)} %bitcast.233), kind=kOutput, calls=%fused_computation.2 | convolution fusion | flops 549452800 | bytes 10752000 | tf_op jit(solution)/shard_map/while/body/eval_jaxpr/brd,bnd->brn/dot_general | solution.py:14
  47.1 4.0 %bitcast_reduce_fusion.1 = (f32[4,256]{1,0:T(4,128)S(1)}, f32[4,2048,256]{2,1,0:T(8,128)}) fusion(bf16[4,256,128]{2,1,0:T(8,128)(2,1)S(1)} %bitcast.242, bf16[4,512,128]{2,1,0:T(8,128)(2,1)S(1)} %bitcast.259, bf16[4,512,128]{2,1,0:T(8,128)(2,1)S(1)} %bitcast.255, bf16[4,512,128]{2,1,0:T(8,128)(2,1)S(1)} %bitcast.257, bf16[4,512,128]{2,1,0:T(8,128)(2,1)S(1)} %bitcast.234), kind=kOutput, calls=%fused_computation.9 | convolution fusion | flops 549452800 | bytes 10752000 | tf_op jit(solution)/shard_map/while/body/eval_jaxpr/brd,bnd->brn/dot_general | solution.py:14
  51.3 4.8 %fusion.8 = f32[4,256]{1,0:T(4,128)S(1)} fusion(f32[4,2048,256]{2,1,0:T(8,128)} %get-tuple-element.114, f32[4,256]{1,0:T(4,128)S(1)} %get-tuple-element.110), kind=kLoop, calls=%fused_computation.13 | loop fusion | flops 6290432 | bytes 8396800 | tf_op jit(solution)/shard_map/while/body/eval_jaxpr/reduce_sum | solution.py:22
  56.5 5.6 %fusion.30 = f32[4,256,128]{2,1,0:T(8,128)S(1)} fusion(f32[4,2048,256]{2,1,0:T(8,128)} %get-tuple-element.114, f32[4,256]{1,0:T(4,128)S(1)} %get-tuple-element.110, bf16[4,512,128]{2,1,0:T(8,128)(2,1)} %bitcast.252, bf16[4,512,128]{2,1,0:T(8,128)(2,1)S(1)} %bitcast.248, bf16[4,512,128]{2,1,0:T(8,128)(2,1)S(1)} %bitcast.250, ...), kind=kOutput, calls=%fused_computation.38 | convolution fusion | flops 551813120 | bytes 11022336 | tf_op jit(solution)/shard_map/while/body/eval_jaxpr/brn,bnd->brd/dot_general | solution.py:23
  65.3 4.8 %fusion.6 = f32[4,256]{1,0:T(4,128)S(1)} fusion(f32[4,2048,256]{2,1,0:T(8,128)} %get-tuple-element.118, f32[4,256]{1,0:T(4,128)S(1)} %get-tuple-element.108), kind=kLoop, calls=%fused_computation.11 | loop fusion | flops 6290432 | bytes 8396800 | tf_op jit(solution)/shard_map/while/body/eval_jaxpr/reduce_sum | solution.py:22
  70.1 4.8 %fusion.33 = f32[4,256,128]{2,1,0:T(8,128)S(1)} fusion(f32[4,2048,256]{2,1,0:T(8,128)} %get-tuple-element.118, f32[4,256]{1,0:T(4,128)S(1)} %get-tuple-element.108, bf16[4,512,128]{2,1,0:T(8,128)(2,1)S(1)} %bitcast.253, bf16[4,512,128]{2,1,0:T(8,128)(2,1)S(1)} %bitcast.249, bf16[4,512,128]{2,1,0:T(8,128)(2,1)S(1)} %bitcast.251, ...), kind=kOutput, calls=%fused_computation.39 | convolution fusion | flops 551813120 | bytes 11022336 | tf_op jit(solution)/shard_map/while/body/eval_jaxpr/brn,bnd->brd/dot_general | solution.py:23
  76.1 7.7 %collective-permute-done.5 = bf16[2,32,2048]{2,1,0:T(8,128)(2,1)S(1)} collective-permute-done((bf16[2,32,2048]{2,1,0:T(8,128)(2,1)S(1)}, bf16[2,32,2048]{2,1,0:T(8,128)(2,1)S(1)}, u32[]{:S(2)}, u32[]{:S(2)}) %collective-permute-start.5) | collective-permute-done | bytes 262176 | tf_op jit(solution)/shard_map/ppermute | solution.py:80
  84.5 4.8 %fusion.1 = f32[4,32,2048]{2,1,0:T(8,128)S(1)} fusion(bf16[4,32,2048]{2,1,0:T(8,128)(2,1)S(1)} %bitcast.225, bf16[2048,2048]{1,0:T(8,128)(2,1)} %param.27), kind=kOutput, calls=%fused_computation.4 | convolution fusion | flops 1073741824 | bytes 9961472 | tf_op jit(solution)/shard_map/dot_general | solution.py:236
  90.6 2.4 %fusion.3 = f32[4,64,2048]{2,1,0:T(8,128)S(1)} fusion(bf16[4,64,2048]{2,1,0:T(8,128)(2,1)S(1)} %bitcast.240, bf16[2048,2048]{1,0:T(8,128)(2,1)S(1)} %bitcast.224), kind=kOutput, calls=%fused_computation.6 | convolution fusion | flops 2147483648 | bytes 11534336 | tf_op jit(solution)/shard_map/dot_general | solution.py:228
  93.2 4.5 %collective-permute-start.10 = (bf16[96,2048]{1,0:T(8,128)(2,1)S(1)}, bf16[96,2048]{1,0:T(8,128)(2,1)S(1)}, u32[]{:S(2)}, u32[]{:S(2)}) collective-permute-start(bf16[96,2048]{1,0:T(8,128)(2,1)S(1)} %pad_maximum_fusion.5), channel_id=1, source_target_pairs={{0,2},{1,3},{4,6},{5,7},{8,10},{9,11},{12,14},{13,15},{16,18},{17,... | collective-permute-start | bytes 1179656 | tf_op jit(solution)/shard_map/ppermute | solution.py:114
  97.8 2.3 %collective-permute-start.11 = (bf16[96,2048]{1,0:T(8,128)(2,1)S(1)}, bf16[96,2048]{1,0:T(8,128)(2,1)S(1)}, u32[]{:S(2)}, u32[]{:S(2)}) collective-permute-start(bf16[96,2048]{1,0:T(8,128)(2,1)S(1)} %pad_maximum_fusion.6), channel_id=1, source_target_pairs={{0,3},{4,7},{8,11},{12,15},{16,19},{20,23},{24,27},{28,31}} | collective-permute-start | bytes 1179656 | tf_op jit(solution)/shard_map/ppermute | solution.py:114
  104.1 3.0 %collective-permute-done.10 = bf16[96,2048]{1,0:T(8,128)(2,1)S(1)} collective-permute-done((bf16[96,2048]{1,0:T(8,128)(2,1)S(1)}, bf16[96,2048]{1,0:T(8,128)(2,1)S(1)}, u32[]{:S(2)}, u32[]{:S(2)}) %collective-permute-start.10) | collective-permute-done | bytes 393248 | tf_op jit(solution)/shard_map/ppermute | solution.py:114
  107.2 19.8 %collective-permute-start.9 = (bf16[96,2048]{1,0:T(8,128)(2,1)S(1)}, bf16[96,2048]{1,0:T(8,128)(2,1)S(1)}, u32[]{:S(2)}, u32[]{:S(2)}) collective-permute-start(bf16[96,2048]{1,0:T(8,128)(2,1)S(1)} %pad_maximum_fusion.4), channel_id=1, source_target_pairs={{0,1},{1,2},{2,3},{4,5},{5,6},{6,7},{8,9},{9,10},{10,11},{12,13},{... | collective-permute-start | bytes 1179656 | tf_op jit(solution)/shard_map/ppermute | solution.py:114
  127.1 10.8 %collective-permute-done.13 = bf16[96,2048]{1,0:T(8,128)(2,1)S(1)} collective-permute-done((bf16[96,2048]{1,0:T(8,128)(2,1)S(1)}, bf16[96,2048]{1,0:T(8,128)(2,1)S(1)}, u32[]{:S(2)}, u32[]{:S(2)}) %collective-permute-start.13) | collective-permute-done | bytes 393248 | tf_op jit(solution)/shard_map/ppermute | solution.py:114
  142.5 6.4 %collective-permute-done.15 = bf16[96,2048]{1,0:T(8,128)(2,1)S(1)} collective-permute-done((bf16[96,2048]{1,0:T(8,128)(2,1)S(1)}, bf16[96,2048]{1,0:T(8,128)(2,1)S(1)}, u32[]{:S(2)}, u32[]{:S(2)}) %collective-permute-start.15) | collective-permute-done | bytes 393248 | tf_op jit(solution)/shard_map/ppermute | solution.py:119
  148.8 4.4 %collective-permute-start.16 = (bf16[96,2048]{1,0:T(8,128)(2,1)S(1)}, bf16[96,2048]{1,0:T(8,128)(2,1)S(1)}, u32[]{:S(2)}, u32[]{:S(2)}) collective-permute-start(bf16[96,2048]{1,0:T(8,128)(2,1)S(1)} %collective-permute-done.15), channel_id=1, source_target_pairs={{0,1},{1,2},{2,3},{4,5},{5,6},{6,7},{8,9},{9,10},{10,11},{12,13},{... | collective-permute-start | bytes 1179656 | tf_op jit(solution)/shard_map/ppermute | solution.py:119
  155.3 4.7 %collective-permute-done.16 = bf16[96,2048]{1,0:T(8,128)(2,1)S(1)} collective-permute-done((bf16[96,2048]{1,0:T(8,128)(2,1)S(1)}, bf16[96,2048]{1,0:T(8,128)(2,1)S(1)}, u32[]{:S(2)}, u32[]{:S(2)}) %collective-permute-start.16) | collective-permute-done | bytes 393248 | tf_op jit(solution)/shard_map/ppermute | solution.py:119
  160.0 4.4 %collective-permute-start.17 = (bf16[96,2048]{1,0:T(8,128)(2,1)S(1)}, bf16[96,2048]{1,0:T(8,128)(2,1)S(1)}, u32[]{:S(2)}, u32[]{:S(2)}) collective-permute-start(bf16[96,2048]{1,0:T(8,128)(2,1)S(1)} %collective-permute-done.16), channel_id=1, source_target_pairs={{0,1},{1,2},{2,3},{4,5},{5,6},{6,7},{8,9},{9,10},{10,11},{12,13},{... | collective-permute-start | bytes 1179656 | tf_op jit(solution)/shard_map/ppermute | solution.py:119
  166.8 3.5 %collective-permute-done.17 = bf16[96,2048]{1,0:T(8,128)(2,1)S(1)} collective-permute-done((bf16[96,2048]{1,0:T(8,128)(2,1)S(1)}, bf16[96,2048]{1,0:T(8,128)(2,1)S(1)}, u32[]{:S(2)}, u32[]{:S(2)}) %collective-permute-start.17) | collective-permute-done | bytes 393248 | tf_op jit(solution)/shard_map/ppermute | solution.py:119
  172.6 2.5 %collective-permute-done.20 = bf16[96,2048]{1,0:T(8,128)(2,1)S(1)} collective-permute-done((bf16[96,2048]{1,0:T(8,128)(2,1)S(1)}, bf16[96,2048]{1,0:T(8,128)(2,1)S(1)}, u32[]{:S(2)}, u32[]{:S(2)}) %collective-permute-start.20) | collective-permute-done | bytes 393248 | tf_op jit(solution)/shard_map/ppermute | solution.py:120
  176.0 2.4 %gather_fusion = bf16[4,96,2048]{2,1,0:T(8,128)(2,1)S(1)} fusion(bf16[7,96,2048]{2,1,0:T(8,128)(2,1)} %bitcast_dynamic-update-slice_fusion, s32[1024]{0:T(1024)S(1)} %pad_clamp_fusion), kind=kCustom, calls=%fused_computation | custom fusion | bytes 3145744 | tf_op jit(solution)/shard_map/jit(_take)/gather | solution.py:130
  (157 shorter events, 41.2 us)
Async XLA Ops:
  0.6 62.3 %copy-start = (bf16[4,8,2,128]{3,2,1,0:T(2,128)(2,1)S(1)}, bf16[4,8,2,128]{3,2,1,0:T(2,128)(2,1)}, u32[]{:S(2)}) copy-start(bf16[4,8,2,128]{3,2,1,0:T(2,128)(2,1)} %param.25) | copy-start | bytes 49156
  0.7 10.2 %copy-start.8 = (bf16[2,32,16,128]{3,2,1,0:T(8,128)(2,1)S(1)}, bf16[2,32,16,128]{3,2,1,0:T(8,128)(2,1)}, u32[]{:S(2)}) copy-start(bf16[2,32,16,128]{3,2,1,0:T(8,128)(2,1)} %param.17) | copy-start | bytes 786436
  0.7 10.9 %copy-start.19 = (s32[32]{0:T(128)S(1)}, s32[32]{0:T(128)}, u32[]{:S(2)}) copy-start(s32[32]{0:T(128)} %param.26) | copy-start | bytes 388
  5.1 29.4 %collective-permute-start.1 = (bf16[2,2,2,512,128]{4,3,2,1,0:T(8,128)(2,1)}, bf16[2,2,2,512,128]{4,3,2,1,0:T(8,128)(2,1)S(1)}, u32[]{:S(2)}, u32[]{:S(2)}) collective-permute-start(bf16[2,2,2,512,128]{4,3,2,1,0:T(8,128)(2,1)} %pad_maximum_fusion.2), channel_id=1, source_target_pairs={{0,8},{4,12},{8,0},{12,4},{1,9},{5,13},{9,1},{13,5},{2,10},{6,14},... | collective-permute-start | bytes 3145736 | tf_op jit(solution)/shard_map/ppermute | solution.py:187
  8.0 31.0 %collective-permute-start = (bf16[2,2,2,512,128]{4,3,2,1,0:T(8,128)(2,1)}, bf16[2,2,2,512,128]{4,3,2,1,0:T(8,128)(2,1)}, u32[]{:S(2)}, u32[]{:S(2)}) collective-permute-start(bf16[2,2,2,512,128]{4,3,2,1,0:T(8,128)(2,1)} %pad_maximum_fusion.2), channel_id=1, source_target_pairs={{0,4},{4,0},{8,12},{12,8},{1,5},{5,1},{9,13},{13,9},{2,6},{6,2},{1... | collective-permute-start | bytes 3145736 | tf_op jit(solution)/shard_map/ppermute | solution.py:190
  8.1 24.7 %collective-permute-start.3 = (bf16[2,2,32,2,128]{4,2,3,1,0:T(8,128)(2,1)S(1)}, bf16[2,2,32,2,128]{4,2,3,1,0:T(8,128)(2,1)S(1)}, u32[]{:S(2)}, u32[]{:S(2)}) collective-permute-start(bf16[2,2,32,2,128]{4,2,3,1,0:T(8,128)(2,1)S(1)} %get-tuple-element.103), channel_id=1, source_target_pairs={{0,8},{4,12},{8,0},{12,4},{1,9},{5,13},{9,1},{13,5},{2,10},{6,14},... | collective-permute-start | bytes 196616 | tf_op jit(solution)/shard_map/ppermute | solution.py:80
  32.8 1.4 collective-permute-start.4
  34.5 6.6 %collective-permute-start.2 = (bf16[2,2,2,512,128]{4,3,2,1,0:T(8,128)(2,1)S(1)}, bf16[2,2,2,512,128]{4,3,2,1,0:T(8,128)(2,1)}, u32[]{:S(2)}, u32[]{:S(2)}) collective-permute-start(bf16[2,2,2,512,128]{4,3,2,1,0:T(8,128)(2,1)S(1)} %collective-permute-done.1), channel_id=1, source_target_pairs={{0,4},{4,0},{8,12},{12,8},{1,5},{5,1},{9,13},{13,9},{2,6},{6,2},{1... | collective-permute-start | bytes 3145736 | tf_op jit(solution)/shard_map/ppermute | solution.py:191
  63.3 12.5 %collective-permute-start.7 = (bf16[4,8,2048]{2,1,0:T(8,128)(2,1)S(1)}, bf16[4,8,2048]{2,1,0:T(8,128)(2,1)S(1)}, u32[]{:S(2)}, u32[]{:S(2)}) collective-permute-start(bf16[4,8,2048]{2,1,0:T(8,128)(2,1)S(1)} %reshape.284), channel_id=1, source_target_pairs={{0,8},{4,12},{8,0},{12,4},{1,9},{5,13},{9,1},{13,5},{2,10},{6,14},... | collective-permute-start | bytes 393224 | tf_op jit(solution)/shard_map/ppermute | solution.py:80
  75.4 8.3 %collective-permute-start.5 = (bf16[2,32,2048]{2,1,0:T(8,128)(2,1)S(1)}, bf16[2,32,2048]{2,1,0:T(8,128)(2,1)S(1)}, u32[]{:S(2)}, u32[]{:S(2)}) collective-permute-start(bf16[2,32,2048]{2,1,0:T(8,128)(2,1)S(1)} %reshape.280), channel_id=1, source_target_pairs={{0,8},{4,12},{8,0},{12,4},{1,9},{5,13},{9,1},{13,5},{2,10},{6,14},... | collective-permute-start | bytes 786440 | tf_op jit(solution)/shard_map/ppermute | solution.py:80
  75.9 8.0 %collective-permute-start.8 = (bf16[2,4,8,2048]{3,2,1,0:T(8,128)(2,1)S(1)}, bf16[2,4,8,2048]{3,2,1,0:T(8,128)(2,1)S(1)}, u32[]{:S(2)}, u32[]{:S(2)}) collective-permute-start(bf16[2,4,8,2048]{3,2,1,0:T(8,128)(2,1)S(1)} %pad_maximum_fusion.14), channel_id=1, source_target_pairs={{0,4},{4,0},{8,12},{12,8},{1,5},{5,1},{9,13},{13,9},{2,6},{6,2},{1... | collective-permute-start | bytes 786440 | tf_op jit(solution)/shard_map/ppermute | solution.py:82
  83.8 5.6 %collective-permute-start.6 = (bf16[2,2,32,2048]{3,2,1,0:T(8,128)(2,1)S(1)}, bf16[2,2,32,2048]{3,2,1,0:T(8,128)(2,1)S(1)}, u32[]{:S(2)}, u32[]{:S(2)}) collective-permute-start(bf16[2,2,32,2048]{3,2,1,0:T(8,128)(2,1)S(1)} %pad_maximum_fusion.3), channel_id=1, source_target_pairs={{0,4},{4,0},{8,12},{12,8},{1,5},{5,1},{9,13},{13,9},{2,6},{6,2},{1... | collective-permute-start | bytes 1572872 | tf_op jit(solution)/shard_map/ppermute | solution.py:82
  93.2 14.0 %collective-permute-start.10 = (bf16[96,2048]{1,0:T(8,128)(2,1)S(1)}, bf16[96,2048]{1,0:T(8,128)(2,1)S(1)}, u32[]{:S(2)}, u32[]{:S(2)}) collective-permute-start(bf16[96,2048]{1,0:T(8,128)(2,1)S(1)} %pad_maximum_fusion.5), channel_id=1, source_target_pairs={{0,2},{1,3},{4,6},{5,7},{8,10},{9,11},{12,14},{13,15},{16,18},{17,... | collective-permute-start | bytes 1179656 | tf_op jit(solution)/shard_map/ppermute | solution.py:114
  97.8 29.3 %collective-permute-start.11 = (bf16[96,2048]{1,0:T(8,128)(2,1)S(1)}, bf16[96,2048]{1,0:T(8,128)(2,1)S(1)}, u32[]{:S(2)}, u32[]{:S(2)}) collective-permute-start(bf16[96,2048]{1,0:T(8,128)(2,1)S(1)} %pad_maximum_fusion.6), channel_id=1, source_target_pairs={{0,3},{4,7},{8,11},{12,15},{16,19},{20,23},{24,27},{28,31}} | collective-permute-start | bytes 1179656 | tf_op jit(solution)/shard_map/ppermute | solution.py:114
  100.1 27.0 %collective-permute-start.12 = (bf16[96,2048]{1,0:T(8,128)(2,1)S(1)}, bf16[96,2048]{1,0:T(8,128)(2,1)S(1)}, u32[]{:S(2)}, u32[]{:S(2)}) collective-permute-start(bf16[96,2048]{1,0:T(8,128)(2,1)S(1)} %pad_maximum_fusion.7), channel_id=1, source_target_pairs={{1,0},{2,1},{3,2},{5,4},{6,5},{7,6},{9,8},{10,9},{11,10},{13,12},{... | collective-permute-start | bytes 1179656 | tf_op jit(solution)/shard_map/ppermute | solution.py:114
  101.4 36.4 %collective-permute-start.13 = (bf16[96,2048]{1,0:T(8,128)(2,1)S(1)}, bf16[96,2048]{1,0:T(8,128)(2,1)S(1)}, u32[]{:S(2)}, u32[]{:S(2)}) collective-permute-start(bf16[96,2048]{1,0:T(8,128)(2,1)S(1)} %pad_maximum_fusion.8), channel_id=1, source_target_pairs={{2,0},{3,1},{6,4},{7,5},{10,8},{11,9},{14,12},{15,13},{18,16},{19,... | collective-permute-start | bytes 1179656 | tf_op jit(solution)/shard_map/ppermute | solution.py:114
  102.8 35.1 %collective-permute-start.14 = (bf16[96,2048]{1,0:T(8,128)(2,1)S(1)}, bf16[96,2048]{1,0:T(8,128)(2,1)S(1)}, u32[]{:S(2)}, u32[]{:S(2)}) collective-permute-start(bf16[96,2048]{1,0:T(8,128)(2,1)S(1)} %pad_maximum_fusion.9), channel_id=1, source_target_pairs={{3,0},{7,4},{11,8},{15,12},{19,16},{23,20},{27,24},{31,28}} | collective-permute-start | bytes 1179656 | tf_op jit(solution)/shard_map/ppermute | solution.py:114
  107.2 30.7 %collective-permute-start.9 = (bf16[96,2048]{1,0:T(8,128)(2,1)S(1)}, bf16[96,2048]{1,0:T(8,128)(2,1)S(1)}, u32[]{:S(2)}, u32[]{:S(2)}) collective-permute-start(bf16[96,2048]{1,0:T(8,128)(2,1)S(1)} %pad_maximum_fusion.4), channel_id=1, source_target_pairs={{0,1},{1,2},{2,3},{4,5},{5,6},{6,7},{8,9},{9,10},{10,11},{12,13},{... | collective-permute-start | bytes 1179656 | tf_op jit(solution)/shard_map/ppermute | solution.py:114
  139.1 9.7 %collective-permute-start.15 = (bf16[96,2048]{1,0:T(8,128)(2,1)S(1)}, bf16[96,2048]{1,0:T(8,128)(2,1)S(1)}, u32[]{:S(2)}, u32[]{:S(2)}) collective-permute-start(bf16[96,2048]{1,0:T(8,128)(2,1)S(1)} %get-tuple-element.57), channel_id=1, source_target_pairs={{0,1},{1,2},{2,3},{4,5},{5,6},{6,7},{8,9},{9,10},{10,11},{12,13},{... | collective-permute-start | bytes 1179656 | tf_op jit(solution)/shard_map/ppermute | solution.py:119
  141.1 12.1 %collective-permute-start.18 = (bf16[96,2048]{1,0:T(8,128)(2,1)S(1)}, bf16[96,2048]{1,0:T(8,128)(2,1)S(1)}, u32[]{:S(2)}, u32[]{:S(2)}) collective-permute-start(bf16[96,2048]{1,0:T(8,128)(2,1)S(1)} %get-tuple-element.57), channel_id=1, source_target_pairs={{1,0},{2,1},{3,2},{5,4},{6,5},{7,6},{9,8},{10,9},{11,10},{13,12},{... | collective-permute-start | bytes 1179656 | tf_op jit(solution)/shard_map/ppermute | solution.py:120
  148.8 11.2 %collective-permute-start.16 = (bf16[96,2048]{1,0:T(8,128)(2,1)S(1)}, bf16[96,2048]{1,0:T(8,128)(2,1)S(1)}, u32[]{:S(2)}, u32[]{:S(2)}) collective-permute-start(bf16[96,2048]{1,0:T(8,128)(2,1)S(1)} %collective-permute-done.15), channel_id=1, source_target_pairs={{0,1},{1,2},{2,3},{4,5},{5,6},{6,7},{8,9},{9,10},{10,11},{12,13},{... | collective-permute-start | bytes 1179656 | tf_op jit(solution)/shard_map/ppermute | solution.py:119
  153.2 11.4 %collective-permute-start.19 = (bf16[96,2048]{1,0:T(8,128)(2,1)S(1)}, bf16[96,2048]{1,0:T(8,128)(2,1)S(1)}, u32[]{:S(2)}, u32[]{:S(2)}) collective-permute-start(bf16[96,2048]{1,0:T(8,128)(2,1)S(1)} %collective-permute-done.18), channel_id=1, source_target_pairs={{1,0},{2,1},{3,2},{5,4},{6,5},{7,6},{9,8},{10,9},{11,10},{13,12},{... | collective-permute-start | bytes 1179656 | tf_op jit(solution)/shard_map/ppermute | solution.py:120
  160.0 10.3 %collective-permute-start.17 = (bf16[96,2048]{1,0:T(8,128)(2,1)S(1)}, bf16[96,2048]{1,0:T(8,128)(2,1)S(1)}, u32[]{:S(2)}, u32[]{:S(2)}) collective-permute-start(bf16[96,2048]{1,0:T(8,128)(2,1)S(1)} %collective-permute-done.16), channel_id=1, source_target_pairs={{0,1},{1,2},{2,3},{4,5},{5,6},{6,7},{8,9},{9,10},{10,11},{12,13},{... | collective-permute-start | bytes 1179656 | tf_op jit(solution)/shard_map/ppermute | solution.py:119
  164.7 10.5 %collective-permute-start.20 = (bf16[96,2048]{1,0:T(8,128)(2,1)S(1)}, bf16[96,2048]{1,0:T(8,128)(2,1)S(1)}, u32[]{:S(2)}, u32[]{:S(2)}) collective-permute-start(bf16[96,2048]{1,0:T(8,128)(2,1)S(1)} %collective-permute-done.19), channel_id=1, source_target_pairs={{1,0},{2,1},{3,2},{5,4},{6,5},{7,6},{9,8},{10,9},{11,10},{13,12},{... | collective-permute-start | bytes 1179656 | tf_op jit(solution)/shard_map/ppermute | solution.py:120
  (19 other events, 104.3 us)

commit v14 on v11

--- a/solution.py
+++ b/solution.py
@@ -188,7 +188,7 @@
         steps_count, samples_dev, kv_heads, group_size, head_depth
     ).transpose(2, 0, 1, 3, 4)
     prefill_state = empty_state(head_batch, span_dev * group_size, head_depth)
-    own_pages = jnp.stack([local_keys, local_values])
+    own_pages = (local_keys, local_values)
     core_pairs = [(dev, dev ^ 1) for dev in range(ctx_count)]
     along_x = [
         lax.ppermute(own_pages, "ctx", [(dev, (dev - 2 * shift) % ctx_count) for dev in range(ctx_count)])

time: 173 us -> 164 us (0.948)
  local copies, waits for them, and re-layouts: 17.9 us -> 10.9 us
  other arithmetic: 15.9 us -> 10.1 us
  starting transfers between devices: 40.3 us -> 43 us
    slice x3 -> x0, local copies, waits for them, and re-layouts: 5.01 us -> none  [shards(): pages[member]]
    reduce_sum x4, other arithmetic: 9.86 us -> 6.32 us  [absorb(): running_sum = running_sum * factor + jnp.sum(weights, axis=-1)]
    unnamed x51 -> x27, local copies, waits for them, and re-layouts: 4.03 us -> 3.94 us
  transfers between devices with their start and end apart: 21 -> 24, of which waited for: 12 -> 13; matrix products, arithmetic and copies ran while one was open for 18% -> 23% of each run, Pallas kernels for 0% -> 0%
where the time goes in v14:
time: 164 us; the launch traced here: 163 us
  waiting for transfers between devices  63.4 us (39%)
  starting transfers between devices  43 us (26%)
  matrix products  34.2 us (21%)
  local copies, waits for them, and re-layouts  10.9 us (7%)
  other arithmetic  10.1 us (6%)
    ppermute x3, waiting for transfers between devices, ctx_shards(): received.append(lax.ppermute(block, 'ctx', pairs))  27.1 us
    ppermute x3, waiting for transfers between devices, head_sum_line(): from_right = lax.ppermute(going_left.astype(jnp.bfloat16), 'head', leftward)  19.5 us
    ppermute x3, starting transfers between devices, head_sum_line(): lax.ppermute(going_right.astype(jnp.bfloat16), 'head', rightward)  13.7 us
    ppermute x3, starting transfers between devices, head_sum_line(): send_right = lax.ppermute(send_right, 'head', rightward)  13.2 us
    dot_general x4, matrix products, absorb(): jnp.einsum('brn,bnd->brd', weights.astype(jnp.bfloat16), value_rows, pref...  12.4 us
    ppermute x3, waiting for transfers between devices, head_sum_line(): send_right = lax.ppermute(send_right, 'head', rightward)  11 us
    dot_general x4, matrix products, absorb(): jnp.einsum('brd,bnd->brn', queries, key_rows, preferred_element_type=jnp....  10.3 us
    reduce_sum x4, other arithmetic, absorb(): running_sum = running_sum * factor + jnp.sum(weights, axis=-1)  6.32 us
  transfers between devices with their start and end apart: 24, of which 13 were waited for; matrix products, arithmetic and copies ran while one was open for 23% of the time, Pallas kernels for 0%

profile of v14, /device:TPU:0, one launch (start us, length us, event | category | flops | bytes accessed | tf_op | source)
XLA Modules:
  0.0 163.2 jit_solution(6679206623217854000)
XLA Ops:
  2.4 3.0 %collective-permute-start.4 = (bf16[2,2,512,128]{3,2,1,0:T(8,128)(2,1)S(1)}, bf16[2,2,512,128]{3,2,1,0:T(8,128)(2,1)}, u32[]{:S(2)}, u32[]{:S(2)}) collective-permute-start(bf16[2,2,512,128]{3,2,1,0:T(8,128)(2,1)S(1)} %bitcast.249), channel_id=1, source_target_pairs={{0,8},{4,12},{8,0},{12,4},{1,9},{5,13},{9,1},{13,5},{2,10},{6,14},... | collective-permute-start | bytes 1572872 | tf_op jit(solution)/shard_map/ppermute | solution.py:194
  10.4 19.6 %collective-permute-done.6 = bf16[2,2,32,2,128]{4,2,3,1,0:T(8,128)(2,1)S(1)} collective-permute-done((bf16[2,2,32,2,128]{4,2,3,1,0:T(8,128)(2,1)S(1)}, bf16[2,2,32,2,128]{4,2,3,1,0:T(8,128)(2,1)S(1)}, u32[]{:S(2)}, u32[]{:S(2)}) %collective-permute-start.6) | collective-permute-done | bytes 65568 | tf_op jit(solution)/shard_map/ppermute | solution.py:80
  34.0 2.7 %bitcast_reduce_fusion = (f32[4,256]{1,0:T(4,128)S(1)}, f32[4,2048,256]{2,1,0:T(8,128)S(1)}) fusion(bf16[4,256,128]{2,1,0:T(8,128)(2,1)S(1)} %bitcast.241, bf16[4,512,128]{2,1,0:T(8,128)(2,1)} %bitcast.8, bf16[4,512,128]{2,1,0:T(8,128)(2,1)} %bitcast.7, bf16[4,512,128]{2,1,0:T(8,128)(2,1)} %bitcast.6, bf16[4,512,128]{2,1,0:T(8,128)(2,1)S(1)} %bitcast.255), kind=kOutput, calls=%fused_computation.2 | convolution fusion | flops 549452800 | bytes 10752000 | tf_op jit(solution)/shard_map/while/body/eval_jaxpr/brd,bnd->brn/dot_general | solution.py:14
  36.8 7.0 %bitcast_reduce_fusion.1 = (f32[4,256]{1,0:T(4,128)S(1)}, f32[4,2048,256]{2,1,0:T(8,128)}) fusion(bf16[4,256,128]{2,1,0:T(8,128)(2,1)S(1)} %bitcast.245, bf16[4,512,128]{2,1,0:T(8,128)(2,1)} %bitcast.8, bf16[4,512,128]{2,1,0:T(8,128)(2,1)} %bitcast.7, bf16[4,512,128]{2,1,0:T(8,128)(2,1)} %bitcast.6, bf16[4,512,128]{2,1,0:T(8,128)(2,1)S(1)} %bitcast.256), kind=kOutput, calls=%fused_computation.9 | convolution fusion | flops 549452800 | bytes 10752000 | tf_op jit(solution)/shard_map/while/body/eval_jaxpr/brd,bnd->brn/dot_general | solution.py:14
  46.3 5.9 %fusion.32 = f32[4,256,128]{2,1,0:T(8,128)S(1)} fusion(f32[4,256,128]{2,1,0:T(8,128)S(1)} %fusion.72, f32[4,2048,256]{2,1,0:T(8,128)} %copy-done.2, f32[4,256]{1,0:T(4,128)S(1)} %get-tuple-element.106, bf16[4,512,128]{2,1,0:T(8,128)(2,1)} %bitcast.20, bf16[4,512,128]{2,1,0:T(8,128)(2,1)} %bitcast.19, bf16[4,512,128]{2,1,0:T(8,128)(2,1)} %bitcast.18, ...), kind=kOutput, calls=%fused_computation.36 | convolution fusion | flops 551944192 | bytes 11546624 | tf_op jit(solution)/shard_map/while/body/eval_jaxpr/brn,bnd->brd/dot_general | solution.py:23
  54.8 4.8 %fusion.6 = f32[4,256]{1,0:T(4,128)S(1)} fusion(f32[4,2048,256]{2,1,0:T(8,128)} %get-tuple-element.114, f32[4,256]{1,0:T(4,128)S(1)} %get-tuple-element.104), kind=kLoop, calls=%fused_computation.11 | loop fusion | flops 6290432 | bytes 8396800 | tf_op jit(solution)/shard_map/while/body/eval_jaxpr/reduce_sum | solution.py:22
  59.6 5.9 %fusion.49 = bf16[4,256,128]{2,1,0:T(8,128)(2,1)S(1)} fusion(f32[4,256,128]{2,1,0:T(8,128)S(1)} %fusion.74, f32[4,2048,256]{2,1,0:T(8,128)} %get-tuple-element.114, f32[4,256]{1,0:T(4,128)S(1)} %get-tuple-element.104, bf16[4,512,128]{2,1,0:T(8,128)(2,1)} %bitcast.20, bf16[4,512,128]{2,1,0:T(8,128)(2,1)} %bitcast.19, bf16[4,512,128]{2,1,0:T(8,128)(2,1)} %bitcast.18, ...), kind=kOutput, calls=%fused_computation.54 | convolution fusion | flops 552206336 | bytes 11288576 | tf_op jit(solution)/shard_map/while/body/eval_jaxpr/brn,bnd->brd/dot_general | solution.py:23
  66.4 7.5 %collective-permute-done.8 = bf16[2,32,2048]{2,1,0:T(8,128)(2,1)S(1)} collective-permute-done((bf16[2,32,2048]{2,1,0:T(8,128)(2,1)S(1)}, bf16[2,32,2048]{2,1,0:T(8,128)(2,1)S(1)}, u32[]{:S(2)}, u32[]{:S(2)}) %collective-permute-start.8) | collective-permute-done | bytes 262176 | tf_op jit(solution)/shard_map/ppermute | solution.py:80
  74.6 5.1 %fusion.1 = f32[4,32,2048]{2,1,0:T(8,128)S(1)} fusion(bf16[4,32,2048]{2,1,0:T(8,128)(2,1)S(1)} %bitcast.233, bf16[2048,2048]{1,0:T(8,128)(2,1)} %param.27), kind=kOutput, calls=%fused_computation.4 | convolution fusion | flops 1073741824 | bytes 9961472 | tf_op jit(solution)/shard_map/dot_general | solution.py:243
  81.0 2.4 %fusion.3 = f32[4,64,2048]{2,1,0:T(8,128)S(1)} fusion(bf16[4,64,2048]{2,1,0:T(8,128)(2,1)S(1)} %bitcast.243, bf16[2048,2048]{1,0:T(8,128)(2,1)S(1)} %bitcast.232), kind=kOutput, calls=%fused_computation.6 | convolution fusion | flops 2147483648 | bytes 11534336 | tf_op jit(solution)/shard_map/dot_general | solution.py:235
  84.8 4.6 %collective-permute-start.12 = (bf16[96,2048]{1,0:T(8,128)(2,1)S(1)}, bf16[96,2048]{1,0:T(8,128)(2,1)S(1)}, u32[]{:S(2)}, u32[]{:S(2)}) collective-permute-start(bf16[96,2048]{1,0:T(8,128)(2,1)S(1)} %pad_maximum_fusion.3), channel_id=1, source_target_pairs={{0,1},{1,2},{2,3},{4,5},{5,6},{6,7},{8,9},{9,10},{10,11},{12,13},{... | collective-permute-start | bytes 1179656 | tf_op jit(solution)/shard_map/ppermute | solution.py:119
  89.7 7.2 %collective-permute-done.15 = bf16[96,2048]{1,0:T(8,128)(2,1)S(1)} collective-permute-done((bf16[96,2048]{1,0:T(8,128)(2,1)S(1)}, bf16[96,2048]{1,0:T(8,128)(2,1)S(1)}, u32[]{:S(2)}, u32[]{:S(2)}) %collective-permute-start.15) | collective-permute-done | bytes 393248 | tf_op jit(solution)/shard_map/ppermute | solution.py:120
  98.4 4.6 %collective-permute-start.13 = (bf16[96,2048]{1,0:T(8,128)(2,1)S(1)}, bf16[96,2048]{1,0:T(8,128)(2,1)S(1)}, u32[]{:S(2)}, u32[]{:S(2)}) collective-permute-start(bf16[96,2048]{1,0:T(8,128)(2,1)S(1)} %fusion.55), channel_id=1, source_target_pairs={{0,1},{1,2},{2,3},{4,5},{5,6},{6,7},{8,9},{9,10},{10,11},{12,13},{... | collective-permute-start | bytes 1179656 | tf_op jit(solution)/shard_map/ppermute | solution.py:119
  102.9 6.6 %collective-permute-done.16 = bf16[96,2048]{1,0:T(8,128)(2,1)S(1)} collective-permute-done((bf16[96,2048]{1,0:T(8,128)(2,1)S(1)}, bf16[96,2048]{1,0:T(8,128)(2,1)S(1)}, u32[]{:S(2)}, u32[]{:S(2)}) %collective-permute-start.16) | collective-permute-done | bytes 393248 | tf_op jit(solution)/shard_map/ppermute | solution.py:120
  111.1 4.6 %collective-permute-start.14 = (bf16[96,2048]{1,0:T(8,128)(2,1)S(1)}, bf16[96,2048]{1,0:T(8,128)(2,1)S(1)}, u32[]{:S(2)}, u32[]{:S(2)}) collective-permute-start(bf16[96,2048]{1,0:T(8,128)(2,1)S(1)} %fusion.54), channel_id=1, source_target_pairs={{0,1},{1,2},{2,3},{4,5},{5,6},{6,7},{8,9},{9,10},{10,11},{12,13},{... | collective-permute-start | bytes 1179656 | tf_op jit(solution)/shard_map/ppermute | solution.py:119
  115.6 5.7 %collective-permute-done.17 = bf16[96,2048]{1,0:T(8,128)(2,1)S(1)} collective-permute-done((bf16[96,2048]{1,0:T(8,128)(2,1)S(1)}, bf16[96,2048]{1,0:T(8,128)(2,1)S(1)}, u32[]{:S(2)}, u32[]{:S(2)}) %collective-permute-start.17) | collective-permute-done | bytes 393248 | tf_op jit(solution)/shard_map/ppermute | solution.py:120
  123.5 4.4 %collective-permute-start.18 = (bf16[96,2048]{1,0:T(8,128)(2,1)S(1)}, bf16[96,2048]{1,0:T(8,128)(2,1)S(1)}, u32[]{:S(2)}, u32[]{:S(2)}) collective-permute-start(bf16[96,2048]{1,0:T(8,128)(2,1)S(1)} %get-tuple-element.57), channel_id=1, source_target_pairs={{0,1},{1,2},{2,3},{4,5},{5,6},{6,7},{8,9},{9,10},{10,11},{12,13},{... | collective-permute-start | bytes 1179656 | tf_op jit(solution)/shard_map/ppermute | solution.py:126
  129.3 4.7 %collective-permute-done.18 = bf16[96,2048]{1,0:T(8,128)(2,1)S(1)} collective-permute-done((bf16[96,2048]{1,0:T(8,128)(2,1)S(1)}, bf16[96,2048]{1,0:T(8,128)(2,1)S(1)}, u32[]{:S(2)}, u32[]{:S(2)}) %collective-permute-start.18) | collective-permute-done | bytes 393248 | tf_op jit(solution)/shard_map/ppermute | solution.py:126
  134.0 4.4 %collective-permute-start.19 = (bf16[96,2048]{1,0:T(8,128)(2,1)S(1)}, bf16[96,2048]{1,0:T(8,128)(2,1)S(1)}, u32[]{:S(2)}, u32[]{:S(2)}) collective-permute-start(bf16[96,2048]{1,0:T(8,128)(2,1)S(1)} %collective-permute-done.18), channel_id=1, source_target_pairs={{0,1},{1,2},{2,3},{4,5},{5,6},{6,7},{8,9},{9,10},{10,11},{12,13},{... | collective-permute-start | bytes 1179656 | tf_op jit(solution)/shard_map/ppermute | solution.py:126
  140.5 3.2 %collective-permute-done.19 = bf16[96,2048]{1,0:T(8,128)(2,1)S(1)} collective-permute-done((bf16[96,2048]{1,0:T(8,128)(2,1)S(1)}, bf16[96,2048]{1,0:T(8,128)(2,1)S(1)}, u32[]{:S(2)}, u32[]{:S(2)}) %collective-permute-start.19) | collective-permute-done | bytes 393248 | tf_op jit(solution)/shard_map/ppermute | solution.py:126
  143.7 4.4 %collective-permute-start.20 = (bf16[96,2048]{1,0:T(8,128)(2,1)S(1)}, bf16[96,2048]{1,0:T(8,128)(2,1)S(1)}, u32[]{:S(2)}, u32[]{:S(2)}) collective-permute-start(bf16[96,2048]{1,0:T(8,128)(2,1)S(1)} %collective-permute-done.19), channel_id=1, source_target_pairs={{0,1},{1,2},{2,3},{4,5},{5,6},{6,7},{8,9},{9,10},{10,11},{12,13},{... | collective-permute-start | bytes 1179656 | tf_op jit(solution)/shard_map/ppermute | solution.py:126
  150.3 3.1 %collective-permute-done.20 = bf16[96,2048]{1,0:T(8,128)(2,1)S(1)} collective-permute-done((bf16[96,2048]{1,0:T(8,128)(2,1)S(1)}, bf16[96,2048]{1,0:T(8,128)(2,1)S(1)}, u32[]{:S(2)}, u32[]{:S(2)}) %collective-permute-start.20) | collective-permute-done | bytes 393248 | tf_op jit(solution)/shard_map/ppermute | solution.py:126
  155.7 2.2 %collective-permute-done.23 = bf16[96,2048]{1,0:T(8,128)(2,1)S(1)} collective-permute-done((bf16[96,2048]{1,0:T(8,128)(2,1)S(1)}, bf16[96,2048]{1,0:T(8,128)(2,1)S(1)}, u32[]{:S(2)}, u32[]{:S(2)}) %collective-permute-start.23) | collective-permute-done | bytes 393248 | tf_op jit(solution)/shard_map/ppermute | solution.py:127
  158.7 2.4 %gather_fusion = bf16[4,96,2048]{2,1,0:T(8,128)(2,1)S(1)} fusion(bf16[7,96,2048]{2,1,0:T(8,128)(2,1)} %bitcast_dynamic-update-slice_fusion, s32[1024]{0:T(1024)S(1)} %pad_clamp_fusion), kind=kCustom, calls=%fused_computation | custom fusion | bytes 3145744 | tf_op jit(solution)/shard_map/jit(_take)/gather | solution.py:137
  (137 shorter events, 35.7 us)
Async XLA Ops:
  2.4 30.1 %collective-permute-start.4 = (bf16[2,2,512,128]{3,2,1,0:T(8,128)(2,1)S(1)}, bf16[2,2,512,128]{3,2,1,0:T(8,128)(2,1)}, u32[]{:S(2)}, u32[]{:S(2)}) collective-permute-start(bf16[2,2,512,128]{3,2,1,0:T(8,128)(2,1)S(1)} %bitcast.249), channel_id=1, source_target_pairs={{0,8},{4,12},{8,0},{12,4},{1,9},{5,13},{9,1},{13,5},{2,10},{6,14},... | collective-permute-start | bytes 1572872 | tf_op jit(solution)/shard_map/ppermute | solution.py:194
  5.4 40.9 %collective-permute-start.3 = (bf16[2,2,512,128]{3,2,1,0:T(8,128)(2,1)S(1)}, bf16[2,2,512,128]{3,2,1,0:T(8,128)(2,1)}, u32[]{:S(2)}, u32[]{:S(2)}) collective-permute-start(bf16[2,2,512,128]{3,2,1,0:T(8,128)(2,1)S(1)} %bitcast.250), channel_id=1, source_target_pairs={{0,4},{4,0},{8,12},{12,8},{1,5},{5,1},{9,13},{13,9},{2,6},{6,2},{1... | collective-permute-start | bytes 1572872 | tf_op jit(solution)/shard_map/ppermute | solution.py:197
  7.1 24.6 %collective-permute-start.1 = (bf16[2,2,512,128]{3,2,1,0:T(8,128)(2,1)S(1)}, bf16[2,2,512,128]{3,2,1,0:T(8,128)(2,1)}, u32[]{:S(2)}, u32[]{:S(2)}) collective-permute-start(bf16[2,2,512,128]{3,2,1,0:T(8,128)(2,1)S(1)} %bitcast.253), channel_id=1, source_target_pairs={{0,8},{4,12},{8,0},{12,4},{1,9},{5,13},{9,1},{13,5},{2,10},{6,14},... | collective-permute-start | bytes 1572872 | tf_op jit(solution)/shard_map/ppermute | solution.py:194
  7.2 25.8 %collective-permute-start = (bf16[2,2,512,128]{3,2,1,0:T(8,128)(2,1)S(1)}, bf16[2,2,512,128]{3,2,1,0:T(8,128)(2,1)}, u32[]{:S(2)}, u32[]{:S(2)}) collective-permute-start(bf16[2,2,512,128]{3,2,1,0:T(8,128)(2,1)S(1)} %bitcast.254), channel_id=1, source_target_pairs={{0,4},{4,0},{8,12},{12,8},{1,5},{5,1},{9,13},{13,9},{2,6},{6,2},{1... | collective-permute-start | bytes 1572872 | tf_op jit(solution)/shard_map/ppermute | solution.py:197
  7.8 22.2 %collective-permute-start.6 = (bf16[2,2,32,2,128]{4,2,3,1,0:T(8,128)(2,1)S(1)}, bf16[2,2,32,2,128]{4,2,3,1,0:T(8,128)(2,1)S(1)}, u32[]{:S(2)}, u32[]{:S(2)}) collective-permute-start(bf16[2,2,32,2,128]{4,2,3,1,0:T(8,128)(2,1)S(1)} %get-tuple-element.99), channel_id=1, source_target_pairs={{0,8},{4,12},{8,0},{12,4},{1,9},{5,13},{9,1},{13,5},{2,10},{6,14},... | collective-permute-start | bytes 196616 | tf_op jit(solution)/shard_map/ppermute | solution.py:80
  30.0 1.4 collective-permute-start.7
  31.7 2.3 %collective-permute-start.2 = (bf16[2,2,512,128]{3,2,1,0:T(8,128)(2,1)}, bf16[2,2,512,128]{3,2,1,0:T(8,128)(2,1)}, u32[]{:S(2)}, u32[]{:S(2)}) collective-permute-start(bf16[2,2,512,128]{3,2,1,0:T(8,128)(2,1)} %collective-permute-done.1), channel_id=1, source_target_pairs={{0,4},{4,0},{8,12},{12,8},{1,5},{5,1},{9,13},{13,9},{2,6},{6,2},{1... | collective-permute-start | bytes 1572872 | tf_op jit(solution)/shard_map/ppermute | solution.py:198
  32.6 13.7 %collective-permute-start.5 = (bf16[2,2,512,128]{3,2,1,0:T(8,128)(2,1)}, bf16[2,2,512,128]{3,2,1,0:T(8,128)(2,1)}, u32[]{:S(2)}, u32[]{:S(2)}) collective-permute-start(bf16[2,2,512,128]{3,2,1,0:T(8,128)(2,1)} %collective-permute-done.4), channel_id=1, source_target_pairs={{0,4},{4,0},{8,12},{12,8},{1,5},{5,1},{9,13},{13,9},{2,6},{6,2},{1... | collective-permute-start | bytes 1572872 | tf_op jit(solution)/shard_map/ppermute | solution.py:198
  53.0 13.1 %collective-permute-start.10 = (bf16[4,8,2048]{2,1,0:T(8,128)(2,1)S(1)}, bf16[4,8,2048]{2,1,0:T(8,128)(2,1)S(1)}, u32[]{:S(2)}, u32[]{:S(2)}) collective-permute-start(bf16[4,8,2048]{2,1,0:T(8,128)(2,1)S(1)} %reshape.286), channel_id=1, source_target_pairs={{0,8},{4,12},{8,0},{12,4},{1,9},{5,13},{9,1},{13,5},{2,10},{6,14},... | collective-permute-start | bytes 393224 | tf_op jit(solution)/shard_map/ppermute | solution.py:80
  65.7 8.1 %collective-permute-start.8 = (bf16[2,32,2048]{2,1,0:T(8,128)(2,1)S(1)}, bf16[2,32,2048]{2,1,0:T(8,128)(2,1)S(1)}, u32[]{:S(2)}, u32[]{:S(2)}) collective-permute-start(bf16[2,32,2048]{2,1,0:T(8,128)(2,1)S(1)} %reshape.282), channel_id=1, source_target_pairs={{0,8},{4,12},{8,0},{12,4},{1,9},{5,13},{9,1},{13,5},{2,10},{6,14},... | collective-permute-start | bytes 786440 | tf_op jit(solution)/shard_map/ppermute | solution.py:80
  66.2 7.8 %collective-permute-start.11 = (bf16[2,4,8,2048]{3,2,1,0:T(8,128)(2,1)S(1)}, bf16[2,4,8,2048]{3,2,1,0:T(8,128)(2,1)S(1)}, u32[]{:S(2)}, u32[]{:S(2)}) collective-permute-start(bf16[2,4,8,2048]{3,2,1,0:T(8,128)(2,1)S(1)} %pad_maximum_fusion.9), channel_id=1, source_target_pairs={{0,4},{4,0},{8,12},{12,8},{1,5},{5,1},{9,13},{13,9},{2,6},{6,2},{1... | collective-permute-start | bytes 786440 | tf_op jit(solution)/shard_map/ppermute | solution.py:82
  73.9 5.9 %collective-permute-start.9 = (bf16[2,2,32,2048]{3,2,1,0:T(8,128)(2,1)S(1)}, bf16[2,2,32,2048]{3,2,1,0:T(8,128)(2,1)S(1)}, u32[]{:S(2)}, u32[]{:S(2)}) collective-permute-start(bf16[2,2,32,2048]{3,2,1,0:T(8,128)(2,1)S(1)} %pad_maximum_fusion.2), channel_id=1, source_target_pairs={{0,4},{4,0},{8,12},{12,8},{1,5},{5,1},{9,13},{13,9},{2,6},{6,2},{1... | collective-permute-start | bytes 1572872 | tf_op jit(solution)/shard_map/ppermute | solution.py:82
  83.5 13.4 %collective-permute-start.15 = (bf16[96,2048]{1,0:T(8,128)(2,1)S(1)}, bf16[96,2048]{1,0:T(8,128)(2,1)S(1)}, u32[]{:S(2)}, u32[]{:S(2)}) collective-permute-start(bf16[96,2048]{1,0:T(8,128)(2,1)S(1)} %pad_maximum_fusion.4), channel_id=1, source_target_pairs={{1,0},{2,1},{3,2},{5,4},{6,5},{7,6},{9,8},{10,9},{11,10},{13,12},{... | collective-permute-start | bytes 1179656 | tf_op jit(solution)/shard_map/ppermute | solution.py:120
  84.8 13.4 %collective-permute-start.12 = (bf16[96,2048]{1,0:T(8,128)(2,1)S(1)}, bf16[96,2048]{1,0:T(8,128)(2,1)S(1)}, u32[]{:S(2)}, u32[]{:S(2)}) collective-permute-start(bf16[96,2048]{1,0:T(8,128)(2,1)S(1)} %pad_maximum_fusion.3), channel_id=1, source_target_pairs={{0,1},{1,2},{2,3},{4,5},{5,6},{6,7},{8,9},{9,10},{10,11},{12,13},{... | collective-permute-start | bytes 1179656 | tf_op jit(solution)/shard_map/ppermute | solution.py:119
  97.0 12.6 %collective-permute-start.16 = (bf16[96,2048]{1,0:T(8,128)(2,1)S(1)}, bf16[96,2048]{1,0:T(8,128)(2,1)S(1)}, u32[]{:S(2)}, u32[]{:S(2)}) collective-permute-start(bf16[96,2048]{1,0:T(8,128)(2,1)S(1)} %fusion.57), channel_id=1, source_target_pairs={{1,0},{2,1},{3,2},{5,4},{6,5},{7,6},{9,8},{10,9},{11,10},{13,12},{... | collective-permute-start | bytes 1179656 | tf_op jit(solution)/shard_map/ppermute | solution.py:120
  98.4 12.6 %collective-permute-start.13 = (bf16[96,2048]{1,0:T(8,128)(2,1)S(1)}, bf16[96,2048]{1,0:T(8,128)(2,1)S(1)}, u32[]{:S(2)}, u32[]{:S(2)}) collective-permute-start(bf16[96,2048]{1,0:T(8,128)(2,1)S(1)} %fusion.55), channel_id=1, source_target_pairs={{0,1},{1,2},{2,3},{4,5},{5,6},{6,7},{8,9},{9,10},{10,11},{12,13},{... | collective-permute-start | bytes 1179656 | tf_op jit(solution)/shard_map/ppermute | solution.py:119
  109.7 11.7 %collective-permute-start.17 = (bf16[96,2048]{1,0:T(8,128)(2,1)S(1)}, bf16[96,2048]{1,0:T(8,128)(2,1)S(1)}, u32[]{:S(2)}, u32[]{:S(2)}) collective-permute-start(bf16[96,2048]{1,0:T(8,128)(2,1)S(1)} %fusion.56), channel_id=1, source_target_pairs={{1,0},{2,1},{3,2},{5,4},{6,5},{7,6},{9,8},{10,9},{11,10},{13,12},{... | collective-permute-start | bytes 1179656 | tf_op jit(solution)/shard_map/ppermute | solution.py:120
  111.1 11.6 %collective-permute-start.14 = (bf16[96,2048]{1,0:T(8,128)(2,1)S(1)}, bf16[96,2048]{1,0:T(8,128)(2,1)S(1)}, u32[]{:S(2)}, u32[]{:S(2)}) collective-permute-start(bf16[96,2048]{1,0:T(8,128)(2,1)S(1)} %fusion.54), channel_id=1, source_target_pairs={{0,1},{1,2},{2,3},{4,5},{5,6},{6,7},{8,9},{9,10},{10,11},{12,13},{... | collective-permute-start | bytes 1179656 | tf_op jit(solution)/shard_map/ppermute | solution.py:119
  123.5 10.5 %collective-permute-start.18 = (bf16[96,2048]{1,0:T(8,128)(2,1)S(1)}, bf16[96,2048]{1,0:T(8,128)(2,1)S(1)}, u32[]{:S(2)}, u32[]{:S(2)}) collective-permute-start(bf16[96,2048]{1,0:T(8,128)(2,1)S(1)} %get-tuple-element.57), channel_id=1, source_target_pairs={{0,1},{1,2},{2,3},{4,5},{5,6},{6,7},{8,9},{9,10},{10,11},{12,13},{... | collective-permute-start | bytes 1179656 | tf_op jit(solution)/shard_map/ppermute | solution.py:126
  127.9 10.5 %collective-permute-start.21 = (bf16[96,2048]{1,0:T(8,128)(2,1)S(1)}, bf16[96,2048]{1,0:T(8,128)(2,1)S(1)}, u32[]{:S(2)}, u32[]{:S(2)}) collective-permute-start(bf16[96,2048]{1,0:T(8,128)(2,1)S(1)} %get-tuple-element.57), channel_id=1, source_target_pairs={{1,0},{2,1},{3,2},{5,4},{6,5},{7,6},{9,8},{10,9},{11,10},{13,12},{... | collective-permute-start | bytes 1179656 | tf_op jit(solution)/shard_map/ppermute | solution.py:127
  134.0 9.7 %collective-permute-start.19 = (bf16[96,2048]{1,0:T(8,128)(2,1)S(1)}, bf16[96,2048]{1,0:T(8,128)(2,1)S(1)}, u32[]{:S(2)}, u32[]{:S(2)}) collective-permute-start(bf16[96,2048]{1,0:T(8,128)(2,1)S(1)} %collective-permute-done.18), channel_id=1, source_target_pairs={{0,1},{1,2},{2,3},{4,5},{5,6},{6,7},{8,9},{9,10},{10,11},{12,13},{... | collective-permute-start | bytes 1179656 | tf_op jit(solution)/shard_map/ppermute | solution.py:126
  138.5 9.8 %collective-permute-start.22 = (bf16[96,2048]{1,0:T(8,128)(2,1)S(1)}, bf16[96,2048]{1,0:T(8,128)(2,1)S(1)}, u32[]{:S(2)}, u32[]{:S(2)}) collective-permute-start(bf16[96,2048]{1,0:T(8,128)(2,1)S(1)} %collective-permute-done.21), channel_id=1, source_target_pairs={{1,0},{2,1},{3,2},{5,4},{6,5},{7,6},{9,8},{10,9},{11,10},{13,12},{... | collective-permute-start | bytes 1179656 | tf_op jit(solution)/shard_map/ppermute | solution.py:127
  143.7 9.7 %collective-permute-start.20 = (bf16[96,2048]{1,0:T(8,128)(2,1)S(1)}, bf16[96,2048]{1,0:T(8,128)(2,1)S(1)}, u32[]{:S(2)}, u32[]{:S(2)}) collective-permute-start(bf16[96,2048]{1,0:T(8,128)(2,1)S(1)} %collective-permute-done.19), channel_id=1, source_target_pairs={{0,1},{1,2},{2,3},{4,5},{5,6},{6,7},{8,9},{9,10},{10,11},{12,13},{... | collective-permute-start | bytes 1179656 | tf_op jit(solution)/shard_map/ppermute | solution.py:126
  148.2 9.7 %collective-permute-start.23 = (bf16[96,2048]{1,0:T(8,128)(2,1)S(1)}, bf16[96,2048]{1,0:T(8,128)(2,1)S(1)}, u32[]{:S(2)}, u32[]{:S(2)}) collective-permute-start(bf16[96,2048]{1,0:T(8,128)(2,1)S(1)} %collective-permute-done.22), channel_id=1, source_target_pairs={{1,0},{2,1},{3,2},{5,4},{6,5},{7,6},{9,8},{10,9},{11,10},{13,12},{... | collective-permute-start | bytes 1179656 | tf_op jit(solution)/shard_map/ppermute | solution.py:127
  (11 other events, 148.1 us)

commit v15 on v14

--- a/solution.py
+++ b/solution.py
@@ -74,13 +74,14 @@
 
 def ctx_shards(block, ctx_count):
     chips = ctx_count // 2
-    received = [block]
+    halves = tuple(jnp.split(block, 2)) if block.shape[0] % 2 == 0 else (block,)
+    received = [halves]
     for shift in range(1, chips):
         pairs = [(dev, (dev - 2 * shift) % ctx_count) for dev in range(ctx_count)]
-        received.append(lax.ppermute(block, "ctx", pairs))
-    along_x = jnp.stack(received)
+        received.append(lax.ppermute(halves, "ctx", pairs))
+    along_x = tuple(jnp.stack([parts[half] for parts in received]) for half in range(len(halves)))
     other_core = lax.ppermute(along_x, "ctx", [(dev, dev ^ 1) for dev in range(ctx_count)])
-    return along_x, other_core
+    return jnp.concatenate(along_x, axis=1), jnp.concatenate(other_core, axis=1)
 
 
 def ctx_gather(block, ctx_count, axis=0):

time: 164 us -> 165 us (level)
  waiting for transfers between devices: 63.4 us -> 59.7 us
  local copies, waits for them, and re-layouts: 10.9 us -> 13.2 us
  starting transfers between devices: 43 us -> 45.2 us
    ppermute x3 -> x6, waiting for transfers between devices: 27.1 us -> 14.7 us  [ctx_shards(): received.append(lax.ppermute(halves, 'ctx', pairs))]
    ppermute x2, waiting for transfers between devices: 0.01 us -> 8.93 us  [shards(): lax.ppermute(own_pages, 'ctx', [(dev, (dev - 2 * shift) % ctx_count) for...]
    unnamed x27 -> x25, local copies, waits for them, and re-layouts: 3.94 us -> 6.29 us
    ppermute x3 -> x6, starting transfers between devices: 3.89 us -> 6.21 us  [ctx_shards(): received.append(lax.ppermute(halves, 'ctx', pairs))]
  transfers between devices with their start and end apart: 24 -> 30, of which waited for: 13 -> 18; matrix products, arithmetic and copies ran while one was open for 23% -> 24% of each run, Pallas kernels for 0% -> 0%
where the time goes in v15:
time: 165 us; the launch traced here: 164 us
  waiting for transfers between devices  59.7 us (36%)
  starting transfers between devices  45.2 us (27%)
  matrix products  34.2 us (21%)
  local copies, waits for them, and re-layouts  13.2 us (8%)
  other arithmetic  10.2 us (6%)
    ppermute x3, waiting for transfers between devices, head_sum_line(): from_right = lax.ppermute(going_left.astype(jnp.bfloat16), 'head', leftward)  19.5 us
    ppermute x6, waiting for transfers between devices, ctx_shards(): received.append(lax.ppermute(halves, 'ctx', pairs))  14.7 us
    ppermute x3, starting transfers between devices, head_sum_line(): lax.ppermute(going_right.astype(jnp.bfloat16), 'head', rightward)  13.7 us
    ppermute x3, starting transfers between devices, head_sum_line(): send_right = lax.ppermute(send_right, 'head', rightward)  13.2 us
    dot_general x4, matrix products, absorb(): jnp.einsum('brn,bnd->brd', weights.astype(jnp.bfloat16), value_rows, pref...  12.3 us
    ppermute x3, waiting for transfers between devices, head_sum_line(): send_right = lax.ppermute(send_right, 'head', rightward)  10.9 us
    dot_general x4, matrix products, absorb(): jnp.einsum('brd,bnd->brn', queries, key_rows, preferred_element_type=jnp....  10.3 us
    ppermute x2, waiting for transfers between devices, shards(): lax.ppermute(own_pages, 'ctx', [(dev, (dev - 2 * shift) % ctx_count) for...  8.93 us
  transfers between devices with their start and end apart: 30, of which 18 were waited for; matrix products, arithmetic and copies ran while one was open for 24% of the time, Pallas kernels for 0%

profile of v15, /device:TPU:0, one launch (start us, length us, event | category | flops | bytes accessed | tf_op | source)
XLA Modules:
  0.0 164.1 jit_solution(15490238506624358855)
XLA Ops:
  2.4 3.0 %collective-permute-start.4 = (bf16[2,2,512,128]{3,2,1,0:T(8,128)(2,1)S(1)}, bf16[2,2,512,128]{3,2,1,0:T(8,128)(2,1)}, u32[]{:S(2)}, u32[]{:S(2)}) collective-permute-start(bf16[2,2,512,128]{3,2,1,0:T(8,128)(2,1)S(1)} %bitcast.259), channel_id=1, source_target_pairs={{0,8},{4,12},{8,0},{12,4},{1,9},{5,13},{9,1},{13,5},{2,10},{6,14},... | collective-permute-start | bytes 1572872 | tf_op jit(solution)/shard_map/ppermute | solution.py:195
  11.6 7.2 %collective-permute-done.7 = bf16[1,2,32,2,128]{4,2,3,1,0:T(8,128)(2,1)S(1)} collective-permute-done((bf16[1,2,32,2,128]{4,2,3,1,0:T(8,128)(2,1)S(1)}, bf16[1,2,32,2,128]{4,2,3,1,0:T(8,128)(2,1)S(1)}, u32[]{:S(2)}, u32[]{:S(2)}) %collective-permute-start.7) | collective-permute-done | bytes 32800 | tf_op jit(solution)/shard_map/ppermute | solution.py:81
  21.1 8.9 %collective-permute-done.1 = bf16[2,2,512,128]{3,2,1,0:T(8,128)(2,1)} collective-permute-done((bf16[2,2,512,128]{3,2,1,0:T(8,128)(2,1)S(1)}, bf16[2,2,512,128]{3,2,1,0:T(8,128)(2,1)}, u32[]{:S(2)}, u32[]{:S(2)}) %collective-permute-start.1) | collective-permute-done | bytes 524320 | tf_op jit(solution)/shard_map/ppermute | solution.py:195
  32.3 2.7 %bitcast_reduce_fusion = (f32[4,256]{1,0:T(4,128)S(1)}, f32[4,2048,256]{2,1,0:T(8,128)S(1)}) fusion(bf16[4,256,128]{2,1,0:T(8,128)(2,1)S(1)} %bitcast.252, bf16[4,512,128]{2,1,0:T(8,128)(2,1)} %bitcast.8, bf16[4,512,128]{2,1,0:T(8,128)(2,1)} %bitcast.7, bf16[4,512,128]{2,1,0:T(8,128)(2,1)} %bitcast.6, bf16[4,512,128]{2,1,0:T(8,128)(2,1)S(1)} %bitcast.265), kind=kOutput, calls=%fused_computation.2 | convolution fusion | flops 549452800 | bytes 10752000 | tf_op jit(solution)/shard_map/while/body/eval_jaxpr/brd,bnd->brn/dot_general | solution.py:14
  35.1 7.1 %bitcast_reduce_fusion.1 = (f32[4,256]{1,0:T(4,128)S(1)}, f32[4,2048,256]{2,1,0:T(8,128)}) fusion(bf16[4,256,128]{2,1,0:T(8,128)(2,1)S(1)} %bitcast.257, bf16[4,512,128]{2,1,0:T(8,128)(2,1)} %bitcast.8, bf16[4,512,128]{2,1,0:T(8,128)(2,1)} %bitcast.7, bf16[4,512,128]{2,1,0:T(8,128)(2,1)} %bitcast.6, bf16[4,512,128]{2,1,0:T(8,128)(2,1)S(1)} %bitcast.266), kind=kOutput, calls=%fused_computation.9 | convolution fusion | flops 549452800 | bytes 10752000 | tf_op jit(solution)/shard_map/while/body/eval_jaxpr/brd,bnd->brn/dot_general | solution.py:14
  44.6 5.9 %fusion.32 = f32[4,256,128]{2,1,0:T(8,128)S(1)} fusion(f32[4,256,128]{2,1,0:T(8,128)S(1)} %fusion.78, f32[4,2048,256]{2,1,0:T(8,128)} %copy-done.2, f32[4,256]{1,0:T(4,128)S(1)} %get-tuple-element.115, bf16[4,512,128]{2,1,0:T(8,128)(2,1)} %bitcast.20, bf16[4,512,128]{2,1,0:T(8,128)(2,1)} %bitcast.19, bf16[4,512,128]{2,1,0:T(8,128)(2,1)} %bitcast.18, ...), kind=kOutput, calls=%fused_computation.36 | convolution fusion | flops 551944192 | bytes 11546624 | tf_op jit(solution)/shard_map/while/body/eval_jaxpr/brn,bnd->brd/dot_general | solution.py:23
  53.1 4.8 %fusion.6 = f32[4,256]{1,0:T(4,128)S(1)} fusion(f32[4,2048,256]{2,1,0:T(8,128)} %get-tuple-element.123, f32[4,256]{1,0:T(4,128)S(1)} %get-tuple-element.113), kind=kLoop, calls=%fused_computation.11 | loop fusion | flops 6290432 | bytes 8396800 | tf_op jit(solution)/shard_map/while/body/eval_jaxpr/reduce_sum | solution.py:22
  57.9 5.9 %fusion.49 = bf16[4,256,128]{2,1,0:T(8,128)(2,1)S(1)} fusion(f32[4,256,128]{2,1,0:T(8,128)S(1)} %fusion.80, f32[4,2048,256]{2,1,0:T(8,128)} %get-tuple-element.123, f32[4,256]{1,0:T(4,128)S(1)} %get-tuple-element.113, bf16[4,512,128]{2,1,0:T(8,128)(2,1)} %bitcast.20, bf16[4,512,128]{2,1,0:T(8,128)(2,1)} %bitcast.19, bf16[4,512,128]{2,1,0:T(8,128)(2,1)} %bitcast.18, ...), kind=kOutput, calls=%fused_computation.60 | convolution fusion | flops 552206336 | bytes 11288576 | tf_op jit(solution)/shard_map/while/body/eval_jaxpr/brn,bnd->brd/dot_general | solution.py:23
  66.8 2.6 %collective-permute-done.14 = bf16[2,8,2048]{2,1,0:T(8,128)(2,1)S(1)} collective-permute-done((bf16[2,8,2048]{2,1,0:T(8,128)(2,1)S(1)}, bf16[2,8,2048]{2,1,0:T(8,128)(2,1)S(1)}, u32[]{:S(2)}, u32[]{:S(2)}) %collective-permute-start.14) | collective-permute-done | bytes 65568 | tf_op jit(solution)/shard_map/ppermute | solution.py:81
  69.5 2.7 %collective-permute-done.11 = bf16[1,32,2048]{2,1,0:T(8,128)(2,1)S(1)} collective-permute-done((bf16[1,32,2048]{2,1,0:T(8,128)(2,1)S(1)}, bf16[1,32,2048]{2,1,0:T(8,128)(2,1)S(1)}, u32[]{:S(2)}, u32[]{:S(2)}) %collective-permute-start.11) | collective-permute-done | bytes 131104 | tf_op jit(solution)/shard_map/ppermute | solution.py:81
  74.6 5.1 %fusion.1 = f32[4,32,2048]{2,1,0:T(8,128)S(1)} fusion(bf16[4,32,2048]{2,1,0:T(8,128)(2,1)S(1)} %bitcast.246, bf16[2048,2048]{1,0:T(8,128)(2,1)} %param.27), kind=kOutput, calls=%fused_computation.4 | convolution fusion | flops 1073741824 | bytes 9961472 | tf_op jit(solution)/shard_map/dot_general | solution.py:244
  85.7 4.6 %collective-permute-start.18 = (bf16[96,2048]{1,0:T(8,128)(2,1)S(1)}, bf16[96,2048]{1,0:T(8,128)(2,1)S(1)}, u32[]{:S(2)}, u32[]{:S(2)}) collective-permute-start(bf16[96,2048]{1,0:T(8,128)(2,1)S(1)} %pad_maximum_fusion.2), channel_id=1, source_target_pairs={{0,1},{1,2},{2,3},{4,5},{5,6},{6,7},{8,9},{9,10},{10,11},{12,13},{... | collective-permute-start | bytes 1179656 | tf_op jit(solution)/shard_map/ppermute | solution.py:120
  90.6 7.2 %collective-permute-done.21 = bf16[96,2048]{1,0:T(8,128)(2,1)S(1)} collective-permute-done((bf16[96,2048]{1,0:T(8,128)(2,1)S(1)}, bf16[96,2048]{1,0:T(8,128)(2,1)S(1)}, u32[]{:S(2)}, u32[]{:S(2)}) %collective-permute-start.21) | collective-permute-done | bytes 393248 | tf_op jit(solution)/shard_map/ppermute | solution.py:121
  99.2 4.6 %collective-permute-start.19 = (bf16[96,2048]{1,0:T(8,128)(2,1)S(1)}, bf16[96,2048]{1,0:T(8,128)(2,1)S(1)}, u32[]{:S(2)}, u32[]{:S(2)}) collective-permute-start(bf16[96,2048]{1,0:T(8,128)(2,1)S(1)} %fusion.55), channel_id=1, source_target_pairs={{0,1},{1,2},{2,3},{4,5},{5,6},{6,7},{8,9},{9,10},{10,11},{12,13},{... | collective-permute-start | bytes 1179656 | tf_op jit(solution)/shard_map/ppermute | solution.py:120
  103.8 6.6 %collective-permute-done.22 = bf16[96,2048]{1,0:T(8,128)(2,1)S(1)} collective-permute-done((bf16[96,2048]{1,0:T(8,128)(2,1)S(1)}, bf16[96,2048]{1,0:T(8,128)(2,1)S(1)}, u32[]{:S(2)}, u32[]{:S(2)}) %collective-permute-start.22) | collective-permute-done | bytes 393248 | tf_op jit(solution)/shard_map/ppermute | solution.py:121
  111.9 4.6 %collective-permute-start.20 = (bf16[96,2048]{1,0:T(8,128)(2,1)S(1)}, bf16[96,2048]{1,0:T(8,128)(2,1)S(1)}, u32[]{:S(2)}, u32[]{:S(2)}) collective-permute-start(bf16[96,2048]{1,0:T(8,128)(2,1)S(1)} %fusion.54), channel_id=1, source_target_pairs={{0,1},{1,2},{2,3},{4,5},{5,6},{6,7},{8,9},{9,10},{10,11},{12,13},{... | collective-permute-start | bytes 1179656 | tf_op jit(solution)/shard_map/ppermute | solution.py:120
  116.5 5.7 %collective-permute-done.23 = bf16[96,2048]{1,0:T(8,128)(2,1)S(1)} collective-permute-done((bf16[96,2048]{1,0:T(8,128)(2,1)S(1)}, bf16[96,2048]{1,0:T(8,128)(2,1)S(1)}, u32[]{:S(2)}, u32[]{:S(2)}) %collective-permute-start.23) | collective-permute-done | bytes 393248 | tf_op jit(solution)/shard_map/ppermute | solution.py:121
  124.4 4.4 %collective-permute-start.24 = (bf16[96,2048]{1,0:T(8,128)(2,1)S(1)}, bf16[96,2048]{1,0:T(8,128)(2,1)S(1)}, u32[]{:S(2)}, u32[]{:S(2)}) collective-permute-start(bf16[96,2048]{1,0:T(8,128)(2,1)S(1)} %get-tuple-element.57), channel_id=1, source_target_pairs={{0,1},{1,2},{2,3},{4,5},{5,6},{6,7},{8,9},{9,10},{10,11},{12,13},{... | collective-permute-start | bytes 1179656 | tf_op jit(solution)/shard_map/ppermute | solution.py:127
  130.2 4.7 %collective-permute-done.24 = bf16[96,2048]{1,0:T(8,128)(2,1)S(1)} collective-permute-done((bf16[96,2048]{1,0:T(8,128)(2,1)S(1)}, bf16[96,2048]{1,0:T(8,128)(2,1)S(1)}, u32[]{:S(2)}, u32[]{:S(2)}) %collective-permute-start.24) | collective-permute-done | bytes 393248 | tf_op jit(solution)/shard_map/ppermute | solution.py:127
  134.9 4.4 %collective-permute-start.25 = (bf16[96,2048]{1,0:T(8,128)(2,1)S(1)}, bf16[96,2048]{1,0:T(8,128)(2,1)S(1)}, u32[]{:S(2)}, u32[]{:S(2)}) collective-permute-start(bf16[96,2048]{1,0:T(8,128)(2,1)S(1)} %collective-permute-done.24), channel_id=1, source_target_pairs={{0,1},{1,2},{2,3},{4,5},{5,6},{6,7},{8,9},{9,10},{10,11},{12,13},{... | collective-permute-start | bytes 1179656 | tf_op jit(solution)/shard_map/ppermute | solution.py:127
  141.4 3.2 %collective-permute-done.25 = bf16[96,2048]{1,0:T(8,128)(2,1)S(1)} collective-permute-done((bf16[96,2048]{1,0:T(8,128)(2,1)S(1)}, bf16[96,2048]{1,0:T(8,128)(2,1)S(1)}, u32[]{:S(2)}, u32[]{:S(2)}) %collective-permute-start.25) | collective-permute-done | bytes 393248 | tf_op jit(solution)/shard_map/ppermute | solution.py:127
  144.6 4.4 %collective-permute-start.26 = (bf16[96,2048]{1,0:T(8,128)(2,1)S(1)}, bf16[96,2048]{1,0:T(8,128)(2,1)S(1)}, u32[]{:S(2)}, u32[]{:S(2)}) collective-permute-start(bf16[96,2048]{1,0:T(8,128)(2,1)S(1)} %collective-permute-done.25), channel_id=1, source_target_pairs={{0,1},{1,2},{2,3},{4,5},{5,6},{6,7},{8,9},{9,10},{10,11},{12,13},{... | collective-permute-start | bytes 1179656 | tf_op jit(solution)/shard_map/ppermute | solution.py:127
  151.2 3.0 %collective-permute-done.26 = bf16[96,2048]{1,0:T(8,128)(2,1)S(1)} collective-permute-done((bf16[96,2048]{1,0:T(8,128)(2,1)S(1)}, bf16[96,2048]{1,0:T(8,128)(2,1)S(1)}, u32[]{:S(2)}, u32[]{:S(2)}) %collective-permute-start.26) | collective-permute-done | bytes 393248 | tf_op jit(solution)/shard_map/ppermute | solution.py:127
  159.6 2.4 %gather_fusion = bf16[4,96,2048]{2,1,0:T(8,128)(2,1)S(1)} fusion(bf16[7,96,2048]{2,1,0:T(8,128)(2,1)} %bitcast_dynamic-update-slice_fusion, s32[1024]{0:T(1024)S(1)} %pad_clamp_fusion), kind=kCustom, calls=%fused_computation | custom fusion | bytes 3145744 | tf_op jit(solution)/shard_map/jit(_take)/gather | solution.py:138
  (155 shorter events, 46.9 us)
Async XLA Ops:
  2.4 28.3 %collective-permute-start.4 = (bf16[2,2,512,128]{3,2,1,0:T(8,128)(2,1)S(1)}, bf16[2,2,512,128]{3,2,1,0:T(8,128)(2,1)}, u32[]{:S(2)}, u32[]{:S(2)}) collective-permute-start(bf16[2,2,512,128]{3,2,1,0:T(8,128)(2,1)S(1)} %bitcast.259), channel_id=1, source_target_pairs={{0,8},{4,12},{8,0},{12,4},{1,9},{5,13},{9,1},{13,5},{2,10},{6,14},... | collective-permute-start | bytes 1572872 | tf_op jit(solution)/shard_map/ppermute | solution.py:195
  5.4 39.2 %collective-permute-start.3 = (bf16[2,2,512,128]{3,2,1,0:T(8,128)(2,1)S(1)}, bf16[2,2,512,128]{3,2,1,0:T(8,128)(2,1)}, u32[]{:S(2)}, u32[]{:S(2)}) collective-permute-start(bf16[2,2,512,128]{3,2,1,0:T(8,128)(2,1)S(1)} %bitcast.260), channel_id=1, source_target_pairs={{0,4},{4,0},{8,12},{12,8},{1,5},{5,1},{9,13},{13,9},{2,6},{6,2},{1... | collective-permute-start | bytes 1572872 | tf_op jit(solution)/shard_map/ppermute | solution.py:198
  6.2 12.7 %collective-permute-start.7 = (bf16[1,2,32,2,128]{4,2,3,1,0:T(8,128)(2,1)S(1)}, bf16[1,2,32,2,128]{4,2,3,1,0:T(8,128)(2,1)S(1)}, u32[]{:S(2)}, u32[]{:S(2)}) collective-permute-start(bf16[1,2,32,2,128]{4,2,3,1,0:T(8,128)(2,1)S(1)} %bitcast.272), channel_id=1, source_target_pairs={{0,8},{4,12},{8,0},{12,4},{1,9},{5,13},{9,1},{13,5},{2,10},{6,14},... | collective-permute-start | bytes 98312 | tf_op jit(solution)/shard_map/ppermute | solution.py:81
  7.0 12.5 %collective-permute-start.6 = (bf16[1,2,32,2,128]{4,2,3,1,0:T(8,128)(2,1)S(1)}, bf16[1,2,32,2,128]{4,2,3,1,0:T(8,128)(2,1)S(1)}, u32[]{:S(2)}, u32[]{:S(2)}) collective-permute-start(bf16[1,2,32,2,128]{4,2,3,1,0:T(8,128)(2,1)S(1)} %bitcast.275), channel_id=1, source_target_pairs={{0,8},{4,12},{8,0},{12,4},{1,9},{5,13},{9,1},{13,5},{2,10},{6,14},... | collective-permute-start | bytes 98312 | tf_op jit(solution)/shard_map/ppermute | solution.py:81
  10.6 19.5 %collective-permute-start.1 = (bf16[2,2,512,128]{3,2,1,0:T(8,128)(2,1)S(1)}, bf16[2,2,512,128]{3,2,1,0:T(8,128)(2,1)}, u32[]{:S(2)}, u32[]{:S(2)}) collective-permute-start(bf16[2,2,512,128]{3,2,1,0:T(8,128)(2,1)S(1)} %bitcast.263), channel_id=1, source_target_pairs={{0,8},{4,12},{8,0},{12,4},{1,9},{5,13},{9,1},{13,5},{2,10},{6,14},... | collective-permute-start | bytes 1572872 | tf_op jit(solution)/shard_map/ppermute | solution.py:195
  20.2 11.1 %collective-permute-start = (bf16[2,2,512,128]{3,2,1,0:T(8,128)(2,1)S(1)}, bf16[2,2,512,128]{3,2,1,0:T(8,128)(2,1)}, u32[]{:S(2)}, u32[]{:S(2)}) collective-permute-start(bf16[2,2,512,128]{3,2,1,0:T(8,128)(2,1)S(1)} %bitcast.264), channel_id=1, source_target_pairs={{0,4},{4,0},{8,12},{12,8},{1,5},{5,1},{9,13},{13,9},{2,6},{6,2},{1... | collective-permute-start | bytes 1572872 | tf_op jit(solution)/shard_map/ppermute | solution.py:198
  30.7 13.9 %collective-permute-start.5 = (bf16[2,2,512,128]{3,2,1,0:T(8,128)(2,1)}, bf16[2,2,512,128]{3,2,1,0:T(8,128)(2,1)}, u32[]{:S(2)}, u32[]{:S(2)}) collective-permute-start(bf16[2,2,512,128]{3,2,1,0:T(8,128)(2,1)} %collective-permute-done.4), channel_id=1, source_target_pairs={{0,4},{4,0},{8,12},{12,8},{1,5},{5,1},{9,13},{13,9},{2,6},{6,2},{1... | collective-permute-start | bytes 1572872 | tf_op jit(solution)/shard_map/ppermute | solution.py:199
  51.3 15.4 %collective-permute-start.15 = (bf16[2,8,2048]{2,1,0:T(8,128)(2,1)S(1)}, bf16[2,8,2048]{2,1,0:T(8,128)(2,1)S(1)}, u32[]{:S(2)}, u32[]{:S(2)}) collective-permute-start(bf16[2,8,2048]{2,1,0:T(8,128)(2,1)S(1)} %split.27), channel_id=1, source_target_pairs={{0,8},{4,12},{8,0},{12,4},{1,9},{5,13},{9,1},{13,5},{2,10},{6,14},... | collective-permute-start | bytes 196616 | tf_op jit(solution)/shard_map/ppermute | solution.py:81
  64.7 7.5 %collective-permute-start.11 = (bf16[1,32,2048]{2,1,0:T(8,128)(2,1)S(1)}, bf16[1,32,2048]{2,1,0:T(8,128)(2,1)S(1)}, u32[]{:S(2)}, u32[]{:S(2)}) collective-permute-start(bf16[1,32,2048]{2,1,0:T(8,128)(2,1)S(1)} %split.23), channel_id=1, source_target_pairs={{0,8},{4,12},{8,0},{12,4},{1,9},{5,13},{9,1},{13,5},{2,10},{6,14},... | collective-permute-start | bytes 393224 | tf_op jit(solution)/shard_map/ppermute | solution.py:81
  66.4 7.4 %collective-permute-start.10 = (bf16[1,32,2048]{2,1,0:T(8,128)(2,1)S(1)}, bf16[1,32,2048]{2,1,0:T(8,128)(2,1)S(1)}, u32[]{:S(2)}, u32[]{:S(2)}) collective-permute-start(bf16[1,32,2048]{2,1,0:T(8,128)(2,1)S(1)} %split.21), channel_id=1, source_target_pairs={{0,8},{4,12},{8,0},{12,4},{1,9},{5,13},{9,1},{13,5},{2,10},{6,14},... | collective-permute-start | bytes 393224 | tf_op jit(solution)/shard_map/ppermute | solution.py:81
  66.7 7.3 %collective-permute-start.17 = (bf16[2,2,8,2048]{3,2,1,0:T(8,128)(2,1)S(1)}, bf16[2,2,8,2048]{3,2,1,0:T(8,128)(2,1)S(1)}, u32[]{:S(2)}, u32[]{:S(2)}) collective-permute-start(bf16[2,2,8,2048]{3,2,1,0:T(8,128)(2,1)S(1)} %pad_maximum_fusion.11), channel_id=1, source_target_pairs={{0,4},{4,0},{8,12},{12,8},{1,5},{5,1},{9,13},{13,9},{2,6},{6,2},{1... | collective-permute-start | bytes 393224 | tf_op jit(solution)/shard_map/ppermute | solution.py:83
  72.2 7.6 %collective-permute-start.13 = (bf16[2,1,32,2048]{3,2,1,0:T(8,128)(2,1)S(1)}, bf16[2,1,32,2048]{3,2,1,0:T(8,128)(2,1)S(1)}, u32[]{:S(2)}, u32[]{:S(2)}) collective-permute-start(bf16[2,1,32,2048]{3,2,1,0:T(8,128)(2,1)S(1)} %pad_maximum_fusion.9), channel_id=1, source_target_pairs={{0,4},{4,0},{8,12},{12,8},{1,5},{5,1},{9,13},{13,9},{2,6},{6,2},{1... | collective-permute-start | bytes 786440 | tf_op jit(solution)/shard_map/ppermute | solution.py:83
  84.4 13.4 %collective-permute-start.21 = (bf16[96,2048]{1,0:T(8,128)(2,1)S(1)}, bf16[96,2048]{1,0:T(8,128)(2,1)S(1)}, u32[]{:S(2)}, u32[]{:S(2)}) collective-permute-start(bf16[96,2048]{1,0:T(8,128)(2,1)S(1)} %pad_maximum_fusion.3), channel_id=1, source_target_pairs={{1,0},{2,1},{3,2},{5,4},{6,5},{7,6},{9,8},{10,9},{11,10},{13,12},{... | collective-permute-start | bytes 1179656 | tf_op jit(solution)/shard_map/ppermute | solution.py:121
  85.7 13.4 %collective-permute-start.18 = (bf16[96,2048]{1,0:T(8,128)(2,1)S(1)}, bf16[96,2048]{1,0:T(8,128)(2,1)S(1)}, u32[]{:S(2)}, u32[]{:S(2)}) collective-permute-start(bf16[96,2048]{1,0:T(8,128)(2,1)S(1)} %pad_maximum_fusion.2), channel_id=1, source_target_pairs={{0,1},{1,2},{2,3},{4,5},{5,6},{6,7},{8,9},{9,10},{10,11},{12,13},{... | collective-permute-start | bytes 1179656 | tf_op jit(solution)/shard_map/ppermute | solution.py:120
  97.8 12.6 %collective-permute-start.22 = (bf16[96,2048]{1,0:T(8,128)(2,1)S(1)}, bf16[96,2048]{1,0:T(8,128)(2,1)S(1)}, u32[]{:S(2)}, u32[]{:S(2)}) collective-permute-start(bf16[96,2048]{1,0:T(8,128)(2,1)S(1)} %fusion.57), channel_id=1, source_target_pairs={{1,0},{2,1},{3,2},{5,4},{6,5},{7,6},{9,8},{10,9},{11,10},{13,12},{... | collective-permute-start | bytes 1179656 | tf_op jit(solution)/shard_map/ppermute | solution.py:121
  99.2 12.6 %collective-permute-start.19 = (bf16[96,2048]{1,0:T(8,128)(2,1)S(1)}, bf16[96,2048]{1,0:T(8,128)(2,1)S(1)}, u32[]{:S(2)}, u32[]{:S(2)}) collective-permute-start(bf16[96,2048]{1,0:T(8,128)(2,1)S(1)} %fusion.55), channel_id=1, source_target_pairs={{0,1},{1,2},{2,3},{4,5},{5,6},{6,7},{8,9},{9,10},{10,11},{12,13},{... | collective-permute-start | bytes 1179656 | tf_op jit(solution)/shard_map/ppermute | solution.py:120
  110.5 11.7 %collective-permute-start.23 = (bf16[96,2048]{1,0:T(8,128)(2,1)S(1)}, bf16[96,2048]{1,0:T(8,128)(2,1)S(1)}, u32[]{:S(2)}, u32[]{:S(2)}) collective-permute-start(bf16[96,2048]{1,0:T(8,128)(2,1)S(1)} %fusion.56), channel_id=1, source_target_pairs={{1,0},{2,1},{3,2},{5,4},{6,5},{7,6},{9,8},{10,9},{11,10},{13,12},{... | collective-permute-start | bytes 1179656 | tf_op jit(solution)/shard_map/ppermute | solution.py:121
  111.9 11.6 %collective-permute-start.20 = (bf16[96,2048]{1,0:T(8,128)(2,1)S(1)}, bf16[96,2048]{1,0:T(8,128)(2,1)S(1)}, u32[]{:S(2)}, u32[]{:S(2)}) collective-permute-start(bf16[96,2048]{1,0:T(8,128)(2,1)S(1)} %fusion.54), channel_id=1, source_target_pairs={{0,1},{1,2},{2,3},{4,5},{5,6},{6,7},{8,9},{9,10},{10,11},{12,13},{... | collective-permute-start | bytes 1179656 | tf_op jit(solution)/shard_map/ppermute | solution.py:120
  124.4 10.5 %collective-permute-start.24 = (bf16[96,2048]{1,0:T(8,128)(2,1)S(1)}, bf16[96,2048]{1,0:T(8,128)(2,1)S(1)}, u32[]{:S(2)}, u32[]{:S(2)}) collective-permute-start(bf16[96,2048]{1,0:T(8,128)(2,1)S(1)} %get-tuple-element.57), channel_id=1, source_target_pairs={{0,1},{1,2},{2,3},{4,5},{5,6},{6,7},{8,9},{9,10},{10,11},{12,13},{... | collective-permute-start | bytes 1179656 | tf_op jit(solution)/shard_map/ppermute | solution.py:127
  128.8 10.5 %collective-permute-start.27 = (bf16[96,2048]{1,0:T(8,128)(2,1)S(1)}, bf16[96,2048]{1,0:T(8,128)(2,1)S(1)}, u32[]{:S(2)}, u32[]{:S(2)}) collective-permute-start(bf16[96,2048]{1,0:T(8,128)(2,1)S(1)} %get-tuple-element.57), channel_id=1, source_target_pairs={{1,0},{2,1},{3,2},{5,4},{6,5},{7,6},{9,8},{10,9},{11,10},{13,12},{... | collective-permute-start | bytes 1179656 | tf_op jit(solution)/shard_map/ppermute | solution.py:128
  134.9 9.7 %collective-permute-start.25 = (bf16[96,2048]{1,0:T(8,128)(2,1)S(1)}, bf16[96,2048]{1,0:T(8,128)(2,1)S(1)}, u32[]{:S(2)}, u32[]{:S(2)}) collective-permute-start(bf16[96,2048]{1,0:T(8,128)(2,1)S(1)} %collective-permute-done.24), channel_id=1, source_target_pairs={{0,1},{1,2},{2,3},{4,5},{5,6},{6,7},{8,9},{9,10},{10,11},{12,13},{... | collective-permute-start | bytes 1179656 | tf_op jit(solution)/shard_map/ppermute | solution.py:127
  139.3 9.8 %collective-permute-start.28 = (bf16[96,2048]{1,0:T(8,128)(2,1)S(1)}, bf16[96,2048]{1,0:T(8,128)(2,1)S(1)}, u32[]{:S(2)}, u32[]{:S(2)}) collective-permute-start(bf16[96,2048]{1,0:T(8,128)(2,1)S(1)} %collective-permute-done.27), channel_id=1, source_target_pairs={{1,0},{2,1},{3,2},{5,4},{6,5},{7,6},{9,8},{10,9},{11,10},{13,12},{... | collective-permute-start | bytes 1179656 | tf_op jit(solution)/shard_map/ppermute | solution.py:128
  144.6 9.7 %collective-permute-start.26 = (bf16[96,2048]{1,0:T(8,128)(2,1)S(1)}, bf16[96,2048]{1,0:T(8,128)(2,1)S(1)}, u32[]{:S(2)}, u32[]{:S(2)}) collective-permute-start(bf16[96,2048]{1,0:T(8,128)(2,1)S(1)} %collective-permute-done.25), channel_id=1, source_target_pairs={{0,1},{1,2},{2,3},{4,5},{5,6},{6,7},{8,9},{9,10},{10,11},{12,13},{... | collective-permute-start | bytes 1179656 | tf_op jit(solution)/shard_map/ppermute | solution.py:127
  149.1 9.7 %collective-permute-start.29 = (bf16[96,2048]{1,0:T(8,128)(2,1)S(1)}, bf16[96,2048]{1,0:T(8,128)(2,1)S(1)}, u32[]{:S(2)}, u32[]{:S(2)}) collective-permute-start(bf16[96,2048]{1,0:T(8,128)(2,1)S(1)} %collective-permute-done.28), channel_id=1, source_target_pairs={{1,0},{2,1},{3,2},{5,4},{6,5},{7,6},{9,8},{10,9},{11,10},{13,12},{... | collective-permute-start | bytes 1179656 | tf_op jit(solution)/shard_map/ppermute | solution.py:128
  (15 other events, 142.1 us)

commit v16 on v14

--- a/solution.py
+++ b/solution.py
@@ -190,10 +190,14 @@
     prefill_state = empty_state(head_batch, span_dev * group_size, head_depth)
     own_pages = (local_keys, local_values)
     core_pairs = [(dev, dev ^ 1) for dev in range(ctx_count)]
-    along_x = [
-        lax.ppermute(own_pages, "ctx", [(dev, (dev - 2 * shift) % ctx_count) for dev in range(ctx_count)])
+    x_pairs = [
+        [(dev, (dev - 2 * shift) % ctx_count) for dev in range(ctx_count)]
         for shift in range(1, ctx_count // 2)
     ]
+    keys_x = [lax.ppermute(local_keys, "ctx", pairs) for pairs in x_pairs]
+    values_after_keys, keys_x = lax.optimization_barrier((local_values, keys_x))
+    values_x = [lax.ppermute(values_after_keys, "ctx", pairs) for pairs in x_pairs]
+    along_x = list(zip(keys_x, values_x))
     arrived = [own_pages, lax.ppermute(own_pages, "ctx", core_pairs)] + along_x
     arrived += [lax.ppermute(pages, "ctx", core_pairs) for pages in along_x]
     prompt_keys_all, prompt_values_all = (

time: 164 us -> 159 us (0.970)
  waiting for transfers between devices: 63.4 us -> 53.1 us
  other arithmetic: 10.1 us -> 13.5 us
    ppermute x3, waiting for transfers between devices: 27.1 us -> 16.4 us  [ctx_shards(): received.append(lax.ppermute(block, 'ctx', pairs))]
    reduce_sum x4, other arithmetic: 6.32 us -> 9.71 us  [absorb(): running_sum = running_sum * factor + jnp.sum(weights, axis=-1)]
    dot_general x4, matrix products: 10.3 us -> 12.2 us  [absorb(): jnp.einsum('brd,bnd->brn', queries, key_rows, preferred_element_type=jnp....]
    ppermute x2, starting transfers between devices: 3.16 us -> 4.83 us  [the longest x1 3 us: shards(): keys_x = [lax.ppermute(local_keys, 'ctx', pairs) for pairs in x_pairs]]
    unnamed x27 -> x21, local copies, waits for them, and re-layouts: 3.94 us -> 3.97 us
  transfers between devices with their start and end apart: 24 -> 24, of which waited for: 13 -> 13; matrix products, arithmetic and copies ran while one was open for 23% -> 27% of each run, Pallas kernels for 0% -> 0%
where the time goes in v16:
time: 159 us; the launch traced here: 158 us
  waiting for transfers between devices  53.1 us (33%)
  starting transfers between devices  42.8 us (27%)
  matrix products  35.6 us (22%)
  other arithmetic  13.5 us (8%)
  local copies, waits for them, and re-layouts  11.9 us (7%)
    ppermute x3, waiting for transfers between devices, head_sum_line(): from_right = lax.ppermute(going_left.astype(jnp.bfloat16), 'head', leftward)  19.5 us
    ppermute x3, waiting for transfers between devices, ctx_shards(): received.append(lax.ppermute(block, 'ctx', pairs))  16.4 us
    ppermute x3, starting transfers between devices, head_sum_line(): lax.ppermute(going_right.astype(jnp.bfloat16), 'head', rightward)  13.7 us
    ppermute x3, starting transfers between devices, head_sum_line(): send_right = lax.ppermute(send_right, 'head', rightward)  13.2 us
    dot_general x4, matrix products, absorb(): jnp.einsum('brd,bnd->brn', queries, key_rows, preferred_element_type=jnp....  12.2 us
    dot_general x4, matrix products, absorb(): jnp.einsum('brn,bnd->brd', weights.astype(jnp.bfloat16), value_rows, pref...  12.1 us
    ppermute x3, waiting for transfers between devices, head_sum_line(): send_right = lax.ppermute(send_right, 'head', rightward)  11 us
    reduce_sum x4, other arithmetic, absorb(): running_sum = running_sum * factor + jnp.sum(weights, axis=-1)  9.71 us
  transfers between devices with their start and end apart: 24, of which 13 were waited for; matrix products, arithmetic and copies ran while one was open for 27% of the time, Pallas kernels for 0%

profile of v16, /device:TPU:0, one launch (start us, length us, event | category | flops | bytes accessed | tf_op | source)
XLA Modules:
  0.0 158.4 jit_solution(14165072512842086939)
XLA Ops:
  2.4 3.0 %collective-permute-start.1 = (bf16[2,2,512,128]{3,2,1,0:T(8,128)(2,1)S(1)}, bf16[2,2,512,128]{3,2,1,0:T(8,128)(2,1)}, u32[]{:S(2)}, u32[]{:S(2)}) collective-permute-start(bf16[2,2,512,128]{3,2,1,0:T(8,128)(2,1)S(1)} %bitcast.253), channel_id=1, source_target_pairs={{0,8},{4,12},{8,0},{12,4},{1,9},{5,13},{9,1},{13,5},{2,10},{6,14},... | collective-permute-start | bytes 1572872 | tf_op jit(solution)/shard_map/ppermute | solution.py:197
  9.4 9.4 %collective-permute-done.6 = bf16[2,2,32,2,128]{4,2,3,1,0:T(8,128)(2,1)S(1)} collective-permute-done((bf16[2,2,32,2,128]{4,2,3,1,0:T(8,128)(2,1)S(1)}, bf16[2,2,32,2,128]{4,2,3,1,0:T(8,128)(2,1)S(1)}, u32[]{:S(2)}, u32[]{:S(2)}) %collective-permute-start.6) | collective-permute-done | bytes 65568 | tf_op jit(solution)/shard_map/ppermute | solution.py:80
  23.1 5.9 %bitcast_reduce_fusion = (f32[4,256]{1,0:T(4,128)S(1)}, f32[4,2048,256]{2,1,0:T(8,128)}) fusion(bf16[4,256,128]{2,1,0:T(8,128)(2,1)S(1)} %bitcast.241, bf16[4,512,128]{2,1,0:T(8,128)(2,1)} %bitcast.12, bf16[4,512,128]{2,1,0:T(8,128)(2,1)} %bitcast.11, bf16[4,512,128]{2,1,0:T(8,128)(2,1)} %bitcast.6, bf16[4,512,128]{2,1,0:T(8,128)(2,1)S(1)} %bitcast.255), kind=kOutput, calls=%fused_computation.2 | convolution fusion | flops 549452800 | bytes 10752000 | tf_op jit(solution)/shard_map/while/body/eval_jaxpr/brd,bnd->brn/dot_general | solution.py:14
  29.0 5.8 %bitcast_reduce_fusion.1 = (f32[4,256]{1,0:T(4,128)S(1)}, f32[4,2048,256]{2,1,0:T(8,128)}) fusion(bf16[4,256,128]{2,1,0:T(8,128)(2,1)S(1)} %bitcast.245, bf16[4,512,128]{2,1,0:T(8,128)(2,1)} %bitcast.12, bf16[4,512,128]{2,1,0:T(8,128)(2,1)} %bitcast.11, bf16[4,512,128]{2,1,0:T(8,128)(2,1)} %bitcast.6, bf16[4,512,128]{2,1,0:T(8,128)(2,1)S(1)} %bitcast.256), kind=kOutput, calls=%fused_computation.9 | convolution fusion | flops 549452800 | bytes 10752000 | tf_op jit(solution)/shard_map/while/body/eval_jaxpr/brd,bnd->brn/dot_general | solution.py:14
  34.9 4.8 %fusion.8 = f32[4,256]{1,0:T(4,128)S(1)} fusion(f32[4,2048,256]{2,1,0:T(8,128)} %get-tuple-element.112, f32[4,256]{1,0:T(4,128)S(1)} %get-tuple-element.110), kind=kLoop, calls=%fused_computation.13 | loop fusion | flops 6290432 | bytes 8396800 | tf_op jit(solution)/shard_map/while/body/eval_jaxpr/reduce_sum | solution.py:22
  40.4 4.8 %fusion.6 = f32[4,256]{1,0:T(4,128)S(1)} fusion(f32[4,2048,256]{2,1,0:T(8,128)} %get-tuple-element.118, f32[4,256]{1,0:T(4,128)S(1)} %get-tuple-element.108), kind=kLoop, calls=%fused_computation.11 | loop fusion | flops 6290432 | bytes 8396800 | tf_op jit(solution)/shard_map/while/body/eval_jaxpr/reduce_sum | solution.py:22
  47.3 5.7 %fusion.32 = f32[4,256,128]{2,1,0:T(8,128)S(1)} fusion(f32[4,256,128]{2,1,0:T(8,128)S(1)} %fusion.72, f32[4,2048,256]{2,1,0:T(8,128)} %get-tuple-element.112, f32[4,256]{1,0:T(4,128)S(1)} %get-tuple-element.110, bf16[4,512,128]{2,1,0:T(8,128)(2,1)S(1)} %bitcast.265, bf16[4,512,128]{2,1,0:T(8,128)(2,1)} %bitcast.19, bf16[4,512,128]{2,1,0:T(8,128)(2,1)} %bitcast.18, ...), kind=kOutput, calls=%fused_computation.36 | convolution fusion | flops 551944192 | bytes 11546624 | tf_op jit(solution)/shard_map/while/body/eval_jaxpr/brn,bnd->brd/dot_general | solution.py:23
  55.2 5.8 %fusion.49 = bf16[4,256,128]{2,1,0:T(8,128)(2,1)S(1)} fusion(f32[4,256,128]{2,1,0:T(8,128)S(1)} %fusion.74, f32[4,2048,256]{2,1,0:T(8,128)} %get-tuple-element.118, f32[4,256]{1,0:T(4,128)S(1)} %get-tuple-element.108, bf16[4,512,128]{2,1,0:T(8,128)(2,1)S(1)} %bitcast.266, bf16[4,512,128]{2,1,0:T(8,128)(2,1)} %bitcast.19, bf16[4,512,128]{2,1,0:T(8,128)(2,1)} %bitcast.18, ...), kind=kOutput, calls=%fused_computation.54 | convolution fusion | flops 552206336 | bytes 11288576 | tf_op jit(solution)/shard_map/while/body/eval_jaxpr/brn,bnd->brd/dot_general | solution.py:23
  62.2 7.1 %collective-permute-done.8 = bf16[2,32,2048]{2,1,0:T(8,128)(2,1)S(1)} collective-permute-done((bf16[2,32,2048]{2,1,0:T(8,128)(2,1)S(1)}, bf16[2,32,2048]{2,1,0:T(8,128)(2,1)S(1)}, u32[]{:S(2)}, u32[]{:S(2)}) %collective-permute-start.8) | collective-permute-done | bytes 262176 | tf_op jit(solution)/shard_map/ppermute | solution.py:80
  70.0 4.8 %fusion.1 = f32[4,32,2048]{2,1,0:T(8,128)S(1)} fusion(bf16[4,32,2048]{2,1,0:T(8,128)(2,1)S(1)} %bitcast.233, bf16[2048,2048]{1,0:T(8,128)(2,1)} %param.27), kind=kOutput, calls=%fused_computation.4 | convolution fusion | flops 1073741824 | bytes 9961472 | tf_op jit(solution)/shard_map/dot_general | solution.py:247
  76.2 2.4 %fusion.3 = f32[4,64,2048]{2,1,0:T(8,128)S(1)} fusion(bf16[4,64,2048]{2,1,0:T(8,128)(2,1)S(1)} %bitcast.243, bf16[2048,2048]{1,0:T(8,128)(2,1)S(1)} %bitcast.232), kind=kOutput, calls=%fused_computation.6 | convolution fusion | flops 2147483648 | bytes 11534336 | tf_op jit(solution)/shard_map/dot_general | solution.py:239
  80.1 4.6 %collective-permute-start.12 = (bf16[96,2048]{1,0:T(8,128)(2,1)S(1)}, bf16[96,2048]{1,0:T(8,128)(2,1)S(1)}, u32[]{:S(2)}, u32[]{:S(2)}) collective-permute-start(bf16[96,2048]{1,0:T(8,128)(2,1)S(1)} %pad_maximum_fusion.3), channel_id=1, source_target_pairs={{0,1},{1,2},{2,3},{4,5},{5,6},{6,7},{8,9},{9,10},{10,11},{12,13},{... | collective-permute-start | bytes 1179656 | tf_op jit(solution)/shard_map/ppermute | solution.py:119
  84.9 7.2 %collective-permute-done.15 = bf16[96,2048]{1,0:T(8,128)(2,1)S(1)} collective-permute-done((bf16[96,2048]{1,0:T(8,128)(2,1)S(1)}, bf16[96,2048]{1,0:T(8,128)(2,1)S(1)}, u32[]{:S(2)}, u32[]{:S(2)}) %collective-permute-start.15) | collective-permute-done | bytes 393248 | tf_op jit(solution)/shard_map/ppermute | solution.py:120
  93.6 4.6 %collective-permute-start.13 = (bf16[96,2048]{1,0:T(8,128)(2,1)S(1)}, bf16[96,2048]{1,0:T(8,128)(2,1)S(1)}, u32[]{:S(2)}, u32[]{:S(2)}) collective-permute-start(bf16[96,2048]{1,0:T(8,128)(2,1)S(1)} %fusion.55), channel_id=1, source_target_pairs={{0,1},{1,2},{2,3},{4,5},{5,6},{6,7},{8,9},{9,10},{10,11},{12,13},{... | collective-permute-start | bytes 1179656 | tf_op jit(solution)/shard_map/ppermute | solution.py:119
  98.2 6.6 %collective-permute-done.16 = bf16[96,2048]{1,0:T(8,128)(2,1)S(1)} collective-permute-done((bf16[96,2048]{1,0:T(8,128)(2,1)S(1)}, bf16[96,2048]{1,0:T(8,128)(2,1)S(1)}, u32[]{:S(2)}, u32[]{:S(2)}) %collective-permute-start.16) | collective-permute-done | bytes 393248 | tf_op jit(solution)/shard_map/ppermute | solution.py:120
  106.3 4.6 %collective-permute-start.14 = (bf16[96,2048]{1,0:T(8,128)(2,1)S(1)}, bf16[96,2048]{1,0:T(8,128)(2,1)S(1)}, u32[]{:S(2)}, u32[]{:S(2)}) collective-permute-start(bf16[96,2048]{1,0:T(8,128)(2,1)S(1)} %fusion.54), channel_id=1, source_target_pairs={{0,1},{1,2},{2,3},{4,5},{5,6},{6,7},{8,9},{9,10},{10,11},{12,13},{... | collective-permute-start | bytes 1179656 | tf_op jit(solution)/shard_map/ppermute | solution.py:119
  110.9 5.7 %collective-permute-done.17 = bf16[96,2048]{1,0:T(8,128)(2,1)S(1)} collective-permute-done((bf16[96,2048]{1,0:T(8,128)(2,1)S(1)}, bf16[96,2048]{1,0:T(8,128)(2,1)S(1)}, u32[]{:S(2)}, u32[]{:S(2)}) %collective-permute-start.17) | collective-permute-done | bytes 393248 | tf_op jit(solution)/shard_map/ppermute | solution.py:120
  118.8 4.4 %collective-permute-start.18 = (bf16[96,2048]{1,0:T(8,128)(2,1)S(1)}, bf16[96,2048]{1,0:T(8,128)(2,1)S(1)}, u32[]{:S(2)}, u32[]{:S(2)}) collective-permute-start(bf16[96,2048]{1,0:T(8,128)(2,1)S(1)} %get-tuple-element.61), channel_id=1, source_target_pairs={{0,1},{1,2},{2,3},{4,5},{5,6},{6,7},{8,9},{9,10},{10,11},{12,13},{... | collective-permute-start | bytes 1179656 | tf_op jit(solution)/shard_map/ppermute | solution.py:126
  124.5 4.7 %collective-permute-done.18 = bf16[96,2048]{1,0:T(8,128)(2,1)S(1)} collective-permute-done((bf16[96,2048]{1,0:T(8,128)(2,1)S(1)}, bf16[96,2048]{1,0:T(8,128)(2,1)S(1)}, u32[]{:S(2)}, u32[]{:S(2)}) %collective-permute-start.18) | collective-permute-done | bytes 393248 | tf_op jit(solution)/shard_map/ppermute | solution.py:126
  129.3 4.4 %collective-permute-start.19 = (bf16[96,2048]{1,0:T(8,128)(2,1)S(1)}, bf16[96,2048]{1,0:T(8,128)(2,1)S(1)}, u32[]{:S(2)}, u32[]{:S(2)}) collective-permute-start(bf16[96,2048]{1,0:T(8,128)(2,1)S(1)} %collective-permute-done.18), channel_id=1, source_target_pairs={{0,1},{1,2},{2,3},{4,5},{5,6},{6,7},{8,9},{9,10},{10,11},{12,13},{... | collective-permute-start | bytes 1179656 | tf_op jit(solution)/shard_map/ppermute | solution.py:126
  135.8 3.2 %collective-permute-done.19 = bf16[96,2048]{1,0:T(8,128)(2,1)S(1)} collective-permute-done((bf16[96,2048]{1,0:T(8,128)(2,1)S(1)}, bf16[96,2048]{1,0:T(8,128)(2,1)S(1)}, u32[]{:S(2)}, u32[]{:S(2)}) %collective-permute-start.19) | collective-permute-done | bytes 393248 | tf_op jit(solution)/shard_map/ppermute | solution.py:126
  138.9 4.4 %collective-permute-start.20 = (bf16[96,2048]{1,0:T(8,128)(2,1)S(1)}, bf16[96,2048]{1,0:T(8,128)(2,1)S(1)}, u32[]{:S(2)}, u32[]{:S(2)}) collective-permute-start(bf16[96,2048]{1,0:T(8,128)(2,1)S(1)} %collective-permute-done.19), channel_id=1, source_target_pairs={{0,1},{1,2},{2,3},{4,5},{5,6},{6,7},{8,9},{9,10},{10,11},{12,13},{... | collective-permute-start | bytes 1179656 | tf_op jit(solution)/shard_map/ppermute | solution.py:126
  145.5 3.1 %collective-permute-done.20 = bf16[96,2048]{1,0:T(8,128)(2,1)S(1)} collective-permute-done((bf16[96,2048]{1,0:T(8,128)(2,1)S(1)}, bf16[96,2048]{1,0:T(8,128)(2,1)S(1)}, u32[]{:S(2)}, u32[]{:S(2)}) %collective-permute-start.20) | collective-permute-done | bytes 393248 | tf_op jit(solution)/shard_map/ppermute | solution.py:126
  153.9 2.4 %gather_fusion = bf16[4,96,2048]{2,1,0:T(8,128)(2,1)S(1)} fusion(bf16[7,96,2048]{2,1,0:T(8,128)(2,1)} %bitcast_dynamic-update-slice_fusion, s32[1024]{0:T(1024)S(1)} %pad_clamp_fusion), kind=kCustom, calls=%fused_computation | custom fusion | bytes 3145744 | tf_op jit(solution)/shard_map/jit(_take)/gather | solution.py:137
  (131 shorter events, 37.7 us)
Async XLA Ops:
  2.4 18.0 %collective-permute-start.1 = (bf16[2,2,512,128]{3,2,1,0:T(8,128)(2,1)S(1)}, bf16[2,2,512,128]{3,2,1,0:T(8,128)(2,1)}, u32[]{:S(2)}, u32[]{:S(2)}) collective-permute-start(bf16[2,2,512,128]{3,2,1,0:T(8,128)(2,1)S(1)} %bitcast.253), channel_id=1, source_target_pairs={{0,8},{4,12},{8,0},{12,4},{1,9},{5,13},{9,1},{13,5},{2,10},{6,14},... | collective-permute-start | bytes 1572872 | tf_op jit(solution)/shard_map/ppermute | solution.py:197
  5.4 17.7 %collective-permute-start = (bf16[2,2,512,128]{3,2,1,0:T(8,128)(2,1)S(1)}, bf16[2,2,512,128]{3,2,1,0:T(8,128)(2,1)}, u32[]{:S(2)}, u32[]{:S(2)}) collective-permute-start(bf16[2,2,512,128]{3,2,1,0:T(8,128)(2,1)S(1)} %bitcast.254), channel_id=1, source_target_pairs={{0,4},{4,0},{8,12},{12,8},{1,5},{5,1},{9,13},{13,9},{2,6},{6,2},{1... | collective-permute-start | bytes 1572872 | tf_op jit(solution)/shard_map/ppermute | solution.py:201
  6.2 12.5 %collective-permute-start.6 = (bf16[2,2,32,2,128]{4,2,3,1,0:T(8,128)(2,1)S(1)}, bf16[2,2,32,2,128]{4,2,3,1,0:T(8,128)(2,1)S(1)}, u32[]{:S(2)}, u32[]{:S(2)}) collective-permute-start(bf16[2,2,32,2,128]{4,2,3,1,0:T(8,128)(2,1)S(1)} %get-tuple-element.103), channel_id=1, source_target_pairs={{0,8},{4,12},{8,0},{12,4},{1,9},{5,13},{9,1},{13,5},{2,10},{6,14},... | collective-permute-start | bytes 196616 | tf_op jit(solution)/shard_map/ppermute | solution.py:80
  8.0 37.9 %collective-permute-start.3 = (bf16[2,2,512,128]{3,2,1,0:T(8,128)(2,1)S(1)}, bf16[2,2,512,128]{3,2,1,0:T(8,128)(2,1)}, u32[]{:S(2)}, u32[]{:S(2)}) collective-permute-start(bf16[2,2,512,128]{3,2,1,0:T(8,128)(2,1)S(1)} %bitcast.249), channel_id=1, source_target_pairs={{0,4},{4,0},{8,12},{12,8},{1,5},{5,1},{9,13},{13,9},{2,6},{6,2},{1... | collective-permute-start | bytes 1572872 | tf_op jit(solution)/shard_map/ppermute | solution.py:201
  18.7 1.4 collective-permute-start.7
  20.4 2.7 %collective-permute-start.2 = (bf16[2,2,512,128]{3,2,1,0:T(8,128)(2,1)}, bf16[2,2,512,128]{3,2,1,0:T(8,128)(2,1)}, u32[]{:S(2)}, u32[]{:S(2)}) collective-permute-start(bf16[2,2,512,128]{3,2,1,0:T(8,128)(2,1)} %collective-permute-done.1), channel_id=1, source_target_pairs={{0,4},{4,0},{8,12},{12,8},{1,5},{5,1},{9,13},{13,9},{2,6},{6,2},{1... | collective-permute-start | bytes 1572872 | tf_op jit(solution)/shard_map/ppermute | solution.py:202
  21.3 23.8 %collective-permute-start.4 = (bf16[2,2,512,128]{3,2,1,0:T(8,128)(2,1)S(1)}, bf16[2,2,512,128]{3,2,1,0:T(8,128)(2,1)}, u32[]{:S(2)}, u32[]{:S(2)}) collective-permute-start(bf16[2,2,512,128]{3,2,1,0:T(8,128)(2,1)S(1)} %bitcast.250), channel_id=1, source_target_pairs={{0,8},{4,12},{8,0},{12,4},{1,9},{5,13},{9,1},{13,5},{2,10},{6,14},... | collective-permute-start | bytes 1572872 | tf_op jit(solution)/shard_map/ppermute | solution.py:199
  45.2 2.2 %collective-permute-start.5 = (bf16[2,2,512,128]{3,2,1,0:T(8,128)(2,1)}, bf16[2,2,512,128]{3,2,1,0:T(8,128)(2,1)S(1)}, u32[]{:S(2)}, u32[]{:S(2)}) collective-permute-start(bf16[2,2,512,128]{3,2,1,0:T(8,128)(2,1)} %collective-permute-done.4), channel_id=1, source_target_pairs={{0,4},{4,0},{8,12},{12,8},{1,5},{5,1},{9,13},{13,9},{2,6},{6,2},{1... | collective-permute-start | bytes 1572872 | tf_op jit(solution)/shard_map/ppermute | solution.py:202
  53.8 8.2 %collective-permute-start.10 = (bf16[4,8,2048]{2,1,0:T(8,128)(2,1)S(1)}, bf16[4,8,2048]{2,1,0:T(8,128)(2,1)S(1)}, u32[]{:S(2)}, u32[]{:S(2)}) collective-permute-start(bf16[4,8,2048]{2,1,0:T(8,128)(2,1)S(1)} %reshape.286), channel_id=1, source_target_pairs={{0,8},{4,12},{8,0},{12,4},{1,9},{5,13},{9,1},{13,5},{2,10},{6,14},... | collective-permute-start | bytes 393224 | tf_op jit(solution)/shard_map/ppermute | solution.py:80
  61.2 8.1 %collective-permute-start.8 = (bf16[2,32,2048]{2,1,0:T(8,128)(2,1)S(1)}, bf16[2,32,2048]{2,1,0:T(8,128)(2,1)S(1)}, u32[]{:S(2)}, u32[]{:S(2)}) collective-permute-start(bf16[2,32,2048]{2,1,0:T(8,128)(2,1)S(1)} %reshape.282), channel_id=1, source_target_pairs={{0,8},{4,12},{8,0},{12,4},{1,9},{5,13},{9,1},{13,5},{2,10},{6,14},... | collective-permute-start | bytes 786440 | tf_op jit(solution)/shard_map/ppermute | solution.py:80
  62.0 7.4 %collective-permute-start.11 = (bf16[2,4,8,2048]{3,2,1,0:T(8,128)(2,1)S(1)}, bf16[2,4,8,2048]{3,2,1,0:T(8,128)(2,1)S(1)}, u32[]{:S(2)}, u32[]{:S(2)}) collective-permute-start(bf16[2,4,8,2048]{3,2,1,0:T(8,128)(2,1)S(1)} %pad_maximum_fusion.9), channel_id=1, source_target_pairs={{0,4},{4,0},{8,12},{12,8},{1,5},{5,1},{9,13},{13,9},{2,6},{6,2},{1... | collective-permute-start | bytes 786440 | tf_op jit(solution)/shard_map/ppermute | solution.py:82
  69.4 5.7 %collective-permute-start.9 = (bf16[2,2,32,2048]{3,2,1,0:T(8,128)(2,1)S(1)}, bf16[2,2,32,2048]{3,2,1,0:T(8,128)(2,1)S(1)}, u32[]{:S(2)}, u32[]{:S(2)}) collective-permute-start(bf16[2,2,32,2048]{3,2,1,0:T(8,128)(2,1)S(1)} %pad_maximum_fusion.2), channel_id=1, source_target_pairs={{0,4},{4,0},{8,12},{12,8},{1,5},{5,1},{9,13},{13,9},{2,6},{6,2},{1... | collective-permute-start | bytes 1572872 | tf_op jit(solution)/shard_map/ppermute | solution.py:82
  78.7 13.4 %collective-permute-start.15 = (bf16[96,2048]{1,0:T(8,128)(2,1)S(1)}, bf16[96,2048]{1,0:T(8,128)(2,1)S(1)}, u32[]{:S(2)}, u32[]{:S(2)}) collective-permute-start(bf16[96,2048]{1,0:T(8,128)(2,1)S(1)} %pad_maximum_fusion.4), channel_id=1, source_target_pairs={{1,0},{2,1},{3,2},{5,4},{6,5},{7,6},{9,8},{10,9},{11,10},{13,12},{... | collective-permute-start | bytes 1179656 | tf_op jit(solution)/shard_map/ppermute | solution.py:120
  80.1 13.5 %collective-permute-start.12 = (bf16[96,2048]{1,0:T(8,128)(2,1)S(1)}, bf16[96,2048]{1,0:T(8,128)(2,1)S(1)}, u32[]{:S(2)}, u32[]{:S(2)}) collective-permute-start(bf16[96,2048]{1,0:T(8,128)(2,1)S(1)} %pad_maximum_fusion.3), channel_id=1, source_target_pairs={{0,1},{1,2},{2,3},{4,5},{5,6},{6,7},{8,9},{9,10},{10,11},{12,13},{... | collective-permute-start | bytes 1179656 | tf_op jit(solution)/shard_map/ppermute | solution.py:119
  92.2 12.6 %collective-permute-start.16 = (bf16[96,2048]{1,0:T(8,128)(2,1)S(1)}, bf16[96,2048]{1,0:T(8,128)(2,1)S(1)}, u32[]{:S(2)}, u32[]{:S(2)}) collective-permute-start(bf16[96,2048]{1,0:T(8,128)(2,1)S(1)} %fusion.57), channel_id=1, source_target_pairs={{1,0},{2,1},{3,2},{5,4},{6,5},{7,6},{9,8},{10,9},{11,10},{13,12},{... | collective-permute-start | bytes 1179656 | tf_op jit(solution)/shard_map/ppermute | solution.py:120
  93.6 12.6 %collective-permute-start.13 = (bf16[96,2048]{1,0:T(8,128)(2,1)S(1)}, bf16[96,2048]{1,0:T(8,128)(2,1)S(1)}, u32[]{:S(2)}, u32[]{:S(2)}) collective-permute-start(bf16[96,2048]{1,0:T(8,128)(2,1)S(1)} %fusion.55), channel_id=1, source_target_pairs={{0,1},{1,2},{2,3},{4,5},{5,6},{6,7},{8,9},{9,10},{10,11},{12,13},{... | collective-permute-start | bytes 1179656 | tf_op jit(solution)/shard_map/ppermute | solution.py:119
  104.9 11.7 %collective-permute-start.17 = (bf16[96,2048]{1,0:T(8,128)(2,1)S(1)}, bf16[96,2048]{1,0:T(8,128)(2,1)S(1)}, u32[]{:S(2)}, u32[]{:S(2)}) collective-permute-start(bf16[96,2048]{1,0:T(8,128)(2,1)S(1)} %fusion.56), channel_id=1, source_target_pairs={{1,0},{2,1},{3,2},{5,4},{6,5},{7,6},{9,8},{10,9},{11,10},{13,12},{... | collective-permute-start | bytes 1179656 | tf_op jit(solution)/shard_map/ppermute | solution.py:120
  106.3 11.6 %collective-permute-start.14 = (bf16[96,2048]{1,0:T(8,128)(2,1)S(1)}, bf16[96,2048]{1,0:T(8,128)(2,1)S(1)}, u32[]{:S(2)}, u32[]{:S(2)}) collective-permute-start(bf16[96,2048]{1,0:T(8,128)(2,1)S(1)} %fusion.54), channel_id=1, source_target_pairs={{0,1},{1,2},{2,3},{4,5},{5,6},{6,7},{8,9},{9,10},{10,11},{12,13},{... | collective-permute-start | bytes 1179656 | tf_op jit(solution)/shard_map/ppermute | solution.py:119
  118.8 10.5 %collective-permute-start.18 = (bf16[96,2048]{1,0:T(8,128)(2,1)S(1)}, bf16[96,2048]{1,0:T(8,128)(2,1)S(1)}, u32[]{:S(2)}, u32[]{:S(2)}) collective-permute-start(bf16[96,2048]{1,0:T(8,128)(2,1)S(1)} %get-tuple-element.61), channel_id=1, source_target_pairs={{0,1},{1,2},{2,3},{4,5},{5,6},{6,7},{8,9},{9,10},{10,11},{12,13},{... | collective-permute-start | bytes 1179656 | tf_op jit(solution)/shard_map/ppermute | solution.py:126
  123.2 10.5 %collective-permute-start.21 = (bf16[96,2048]{1,0:T(8,128)(2,1)S(1)}, bf16[96,2048]{1,0:T(8,128)(2,1)S(1)}, u32[]{:S(2)}, u32[]{:S(2)}) collective-permute-start(bf16[96,2048]{1,0:T(8,128)(2,1)S(1)} %get-tuple-element.61), channel_id=1, source_target_pairs={{1,0},{2,1},{3,2},{5,4},{6,5},{7,6},{9,8},{10,9},{11,10},{13,12},{... | collective-permute-start | bytes 1179656 | tf_op jit(solution)/shard_map/ppermute | solution.py:127
  129.3 9.7 %collective-permute-start.19 = (bf16[96,2048]{1,0:T(8,128)(2,1)S(1)}, bf16[96,2048]{1,0:T(8,128)(2,1)S(1)}, u32[]{:S(2)}, u32[]{:S(2)}) collective-permute-start(bf16[96,2048]{1,0:T(8,128)(2,1)S(1)} %collective-permute-done.18), channel_id=1, source_target_pairs={{0,1},{1,2},{2,3},{4,5},{5,6},{6,7},{8,9},{9,10},{10,11},{12,13},{... | collective-permute-start | bytes 1179656 | tf_op jit(solution)/shard_map/ppermute | solution.py:126
  133.7 9.8 %collective-permute-start.22 = (bf16[96,2048]{1,0:T(8,128)(2,1)S(1)}, bf16[96,2048]{1,0:T(8,128)(2,1)S(1)}, u32[]{:S(2)}, u32[]{:S(2)}) collective-permute-start(bf16[96,2048]{1,0:T(8,128)(2,1)S(1)} %collective-permute-done.21), channel_id=1, source_target_pairs={{1,0},{2,1},{3,2},{5,4},{6,5},{7,6},{9,8},{10,9},{11,10},{13,12},{... | collective-permute-start | bytes 1179656 | tf_op jit(solution)/shard_map/ppermute | solution.py:127
  138.9 9.7 %collective-permute-start.20 = (bf16[96,2048]{1,0:T(8,128)(2,1)S(1)}, bf16[96,2048]{1,0:T(8,128)(2,1)S(1)}, u32[]{:S(2)}, u32[]{:S(2)}) collective-permute-start(bf16[96,2048]{1,0:T(8,128)(2,1)S(1)} %collective-permute-done.19), channel_id=1, source_target_pairs={{0,1},{1,2},{2,3},{4,5},{5,6},{6,7},{8,9},{9,10},{10,11},{12,13},{... | collective-permute-start | bytes 1179656 | tf_op jit(solution)/shard_map/ppermute | solution.py:126
  143.5 9.7 %collective-permute-start.23 = (bf16[96,2048]{1,0:T(8,128)(2,1)S(1)}, bf16[96,2048]{1,0:T(8,128)(2,1)S(1)}, u32[]{:S(2)}, u32[]{:S(2)}) collective-permute-start(bf16[96,2048]{1,0:T(8,128)(2,1)S(1)} %collective-permute-done.22), channel_id=1, source_target_pairs={{1,0},{2,1},{3,2},{5,4},{6,5},{7,6},{9,8},{10,9},{11,10},{13,12},{... | collective-permute-start | bytes 1179656 | tf_op jit(solution)/shard_map/ppermute | solution.py:127
  (8 other events, 112.7 us)

commit v17 on v16

--- a/solution.py
+++ b/solution.py
@@ -198,21 +198,22 @@
     values_after_keys, keys_x = lax.optimization_barrier((local_values, keys_x))
     values_x = [lax.ppermute(values_after_keys, "ctx", pairs) for pairs in x_pairs]
     along_x = list(zip(keys_x, values_x))
-    arrived = [own_pages, lax.ppermute(own_pages, "ctx", core_pairs)] + along_x
-    arrived += [lax.ppermute(pages, "ctx", core_pairs) for pages in along_x]
-    prompt_keys_all, prompt_values_all = (
-        jnp.concatenate([pages[member] for pages in arrived], axis=2) for member in range(2)
-    )
-    prefix_len = prompt_keys_all.shape[2]
-    key_rows = prompt_keys_all.reshape(head_batch, prefix_len, head_depth)
-    value_rows = prompt_values_all.reshape(head_batch, prefix_len, head_depth)
-    prefill_state = sweep(prefill_state, span_rows, key_rows, value_rows, 2048)
+    near = [own_pages, lax.ppermute(own_pages, "ctx", core_pairs)]
+    far = along_x + [lax.ppermute(pages, "ctx", core_pairs) for pages in along_x]
     decode_flat = decode_five.reshape(kv_heads, -1, head_depth)
     decode_batch = jnp.broadcast_to(decode_flat[None], (prompts,) + decode_flat.shape).reshape(
         head_batch, -1, head_depth
     )
     decode_state = empty_state(head_batch, decode_flat.shape[1], head_depth)
-    decode_state = sweep(decode_state, decode_batch, key_rows, value_rows, 2048)
+    for group in (near, far):
+        key_rows, value_rows = (
+            jnp.concatenate([pages[member] for pages in group], axis=2).reshape(
+                head_batch, -1, head_depth
+            )
+            for member in range(2)
+        )
+        prefill_state = absorb(prefill_state, span_rows, key_rows, value_rows, None)
+        decode_state = absorb(decode_state, decode_batch, key_rows, value_rows, None)
     decode_state = sweep(decode_state, decode_batch, span_key_rows, span_value_rows, span_total)
     own_prompts = lax.dynamic_slice_in_dim(sample_prompt, ctx_index * samples_dev, samples_dev)
     chosen = (

time: 159 us -> 158 us (level)
  starting transfers between devices: 42.8 us -> 40.6 us
  other arithmetic: 13.5 us -> 15.3 us
    ppermute x3, waiting for transfers between devices: 1.29 us -> 20 us  [head_sum_line(): lax.ppermute(going_right.astype(jnp.bfloat16), 'head', rightward)]
    ppermute x3, waiting for transfers between devices: 19.5 us -> 4.24 us  [head_sum_line(): from_right = lax.ppermute(going_left.astype(jnp.bfloat16), 'head', leftward)]
    ppermute x3, waiting for transfers between devices: 16.4 us -> 14.3 us  [ctx_shards(): received.append(lax.ppermute(block, 'ctx', pairs))]
    dot_general x4 -> x6, matrix products: 12.1 us -> 10.7 us  [absorb(): jnp.einsum('brn,bnd->brd', weights.astype(jnp.bfloat16), value_rows, pref...]
    dot_general x4 -> x6, matrix products: 12.2 us -> 11.7 us  [absorb(): jnp.einsum('brd,bnd->brn', queries, key_rows, preferred_element_type=jnp....]
    reduce_sum x4 -> x6, other arithmetic: 9.71 us -> 9.76 us  [absorb(): running_sum = running_sum * factor + jnp.sum(weights, axis=-1)]
    unnamed x21 -> x33, local copies, waits for them, and re-layouts: 3.97 us -> 4 us
  transfers between devices with their start and end apart: 24 -> 24, of which waited for: 13 -> 13; matrix products, arithmetic and copies ran while one was open for 27% -> 31% of each run, Pallas kernels for 0% -> 0%
where the time goes in v17:
time: 158 us
  waiting for transfers between devices  52.6 us (33%)
  starting transfers between devices  40.6 us (26%)
  matrix products  34.4 us (22%)
  other arithmetic  15.3 us (10%)
  local copies, waits for them, and re-layouts  13.2 us (8%)
  between operations  1.6 us (1%)
    ppermute x3, waiting for transfers between devices, head_sum_line(): lax.ppermute(going_right.astype(jnp.bfloat16), 'head', rightward)  20 us
    ppermute x3, waiting for transfers between devices, ctx_shards(): received.append(lax.ppermute(block, 'ctx', pairs))  14.3 us
    ppermute x3, starting transfers between devices, head_sum_line(): lax.ppermute(going_right.astype(jnp.bfloat16), 'head', rightward)  12.6 us
    ppermute x3, starting transfers between devices, head_sum_line(): send_right = lax.ppermute(send_right, 'head', rightward)  12.3 us
    dot_general x6, matrix products, absorb(): jnp.einsum('brd,bnd->brn', queries, key_rows, preferred_element_type=jnp....  11.7 us
    ppermute x3, waiting for transfers between devices, head_sum_line(): send_right = lax.ppermute(send_right, 'head', rightward)  11 us
    dot_general x6, matrix products, absorb(): jnp.einsum('brn,bnd->brd', weights.astype(jnp.bfloat16), value_rows, pref...  10.7 us
    reduce_sum x6, other arithmetic, absorb(): running_sum = running_sum * factor + jnp.sum(weights, axis=-1)  9.76 us
  transfers between devices with their start and end apart: 24, of which 13 were waited for; matrix products, arithmetic and copies ran while one was open for 31% of the time, Pallas kernels for 0%

profile of v17, /device:TPU:0, one launch (start us, length us, event | category | flops | bytes accessed | tf_op | source)
XLA Modules:
  0.0 157.8 jit_solution(11531702972477166881)
XLA Ops:
  2.4 3.0 %collective-permute-start.2 = (bf16[2,2,512,128]{3,2,1,0:T(8,128)(2,1)S(1)}, bf16[2,2,512,128]{3,2,1,0:T(8,128)(2,1)S(1)}, u32[]{:S(2)}, u32[]{:S(2)}) collective-permute-start(bf16[2,2,512,128]{3,2,1,0:T(8,128)(2,1)S(1)} %bitcast.267), channel_id=1, source_target_pairs={{0,8},{4,12},{8,0},{12,4},{1,9},{5,13},{9,1},{13,5},{2,10},{6,14},... | collective-permute-start | bytes 1572872 | tf_op jit(solution)/shard_map/ppermute | solution.py:197
  10.8 7.9 %collective-permute-done.6 = bf16[2,2,32,2,128]{4,2,3,1,0:T(8,128)(2,1)S(1)} collective-permute-done((bf16[2,2,32,2,128]{4,2,3,1,0:T(8,128)(2,1)S(1)}, bf16[2,2,32,2,128]{4,2,3,1,0:T(8,128)(2,1)S(1)}, u32[]{:S(2)}, u32[]{:S(2)}) %collective-permute-start.6) | collective-permute-done | bytes 65568 | tf_op jit(solution)/shard_map/ppermute | solution.py:80
  26.9 2.7 %bitcast_reduce_fusion.1 = (f32[4,256]{1,0:T(4,128)S(1)}, f32[4,1024,256]{2,1,0:T(8,128)}) fusion(bf16[4,256,128]{2,1,0:T(8,128)(2,1)S(1)} %bitcast.272, bf16[4,512,128]{2,1,0:T(8,128)(2,1)S(1)} %bitcast.283, bf16[4,512,128]{2,1,0:T(8,128)(2,1)S(1)} %bitcast.270), kind=kOutput, calls=%fused_computation.9 | convolution fusion | flops 272628736 | bytes 5509120 | tf_op jit(solution)/shard_map/brd,bnd->brn/dot_general | solution.py:14
  32.4 2.7 %bitcast_reduce_fusion = (f32[4,256]{1,0:T(4,128)S(1)}, f32[4,1024,256]{2,1,0:T(8,128)}) fusion(bf16[4,1024,128]{2,1,0:T(8,128)(2,1)S(1)} %bitcast.266, bf16[4,256,128]{2,1,0:T(8,128)(2,1)S(1)} %bitcast.273), kind=kOutput, calls=%fused_computation.6 | convolution fusion | flops 270531584 | bytes 5509120 | tf_op jit(solution)/shard_map/brd,bnd->brn/dot_general | solution.py:14
  35.7 2.9 %fusion.12 = f32[4,256]{1,0:T(4,128)S(1)} fusion(f32[4,1024,256]{2,1,0:T(8,128)} %get-tuple-element.78, f32[4,256]{1,0:T(4,128)S(1)} %get-tuple-element.72), kind=kLoop, calls=%fused_computation.21 | loop fusion | flops 3144704 | bytes 4202496 | tf_op jit(solution)/shard_map/reduce_sum | solution.py:22
  38.7 2.9 %fusion.14 = f32[4,256]{1,0:T(4,128)S(1)} fusion(f32[4,1024,256]{2,1,0:T(8,128)} %get-tuple-element.76, f32[4,256]{1,0:T(4,128)S(1)} %get-tuple-element.47), kind=kLoop, calls=%fused_computation.23 | loop fusion | flops 3144704 | bytes 4202496 | tf_op jit(solution)/shard_map/reduce_sum | solution.py:22
  42.3 3.1 %fusion.10 = f32[4,256]{1,0:T(4,128)S(1)} fusion(f32[4,1024,256]{2,1,0:T(8,128)} %get-tuple-element.84, f32[4,256]{1,0:T(4,128)S(1)} %get-tuple-element.40), kind=kLoop, calls=%fused_computation.19 | loop fusion | flops 3144704 | bytes 4202496 | tf_op jit(solution)/shard_map/reduce_sum | solution.py:22
  46.1 3.2 %fusion.37 = f32[4,256,128]{2,1,0:T(8,128)} fusion(f32[4,1024,256]{2,1,0:T(8,128)S(1)} %copy-done.4, f32[4,256]{1,0:T(4,128)S(1)} %get-tuple-element.69, bf16[4,512,128]{2,1,0:T(8,128)(2,1)} %bitcast.16, bf16[4,512,128]{2,1,0:T(8,128)(2,1)S(1)} %bitcast.296, f32[4,256]{1,0:T(4,128)S(1)} %get-tuple-element.38, f32[4,256]{1,0:T(4,128)S(1)} %get-tuple-element.68), kind=kOutput, calls=%fused_computation.43 | convolution fusion | flops 273940480 | bytes 5779456 | tf_op jit(solution)/shard_map/brn,bnd->brd/dot_general | solution.py:23
  55.3 3.4 %fusion.75 = bf16[4,256,128]{2,1,0:T(8,128)(2,1)S(1)} fusion(f32[4,256,128]{2,1,0:T(8,128)S(1)} %fusion.100, f32[4,256,128]{2,1,0:T(8,128)S(1)} %copy-done.11, bf16[4,1024,128]{2,1,0:T(8,128)(2,1)S(1)} %bitcast.278, f32[4,1024,256]{2,1,0:T(8,128)} %get-tuple-element.84, f32[4,256]{1,0:T(4,128)S(1)} %get-tuple-element.40, ...), kind=kOutput, calls=%fused_computation.76 | convolution fusion | flops 272236544 | bytes 6565888 | tf_op jit(solution)/shard_map/brn,bnd->brd/dot_general | solution.py:23
  61.1 6.2 %collective-permute-done.8 = bf16[2,32,2048]{2,1,0:T(8,128)(2,1)S(1)} collective-permute-done((bf16[2,32,2048]{2,1,0:T(8,128)(2,1)S(1)}, bf16[2,32,2048]{2,1,0:T(8,128)(2,1)S(1)}, u32[]{:S(2)}, u32[]{:S(2)}) %collective-permute-start.8) | collective-permute-done | bytes 262176 | tf_op jit(solution)/shard_map/ppermute | solution.py:80
  68.0 4.8 %fusion = f32[4,32,2048]{2,1,0:T(8,128)S(1)} fusion(bf16[4,32,2048]{2,1,0:T(8,128)(2,1)S(1)} %bitcast.279, bf16[2048,2048]{1,0:T(8,128)(2,1)} %param.27), kind=kOutput, calls=%fused_computation.1 | convolution fusion | flops 1073741824 | bytes 9961472 | tf_op jit(solution)/shard_map/dot_general | solution.py:248
  76.7 3.7 %collective-permute-start.12 = (bf16[96,2048]{1,0:T(8,128)(2,1)S(1)}, bf16[96,2048]{1,0:T(8,128)(2,1)S(1)}, u32[]{:S(2)}, u32[]{:S(2)}) collective-permute-start(bf16[96,2048]{1,0:T(8,128)(2,1)S(1)} %pad_maximum_fusion.9), channel_id=1, source_target_pairs={{0,1},{1,2},{2,3},{4,5},{5,6},{6,7},{8,9},{9,10},{10,11},{12,13},{... | collective-permute-start | bytes 1179656 | tf_op jit(solution)/shard_map/ppermute | solution.py:119
  82.1 7.3 %collective-permute-done.12 = bf16[96,2048]{1,0:T(8,128)(2,1)S(1)} collective-permute-done((bf16[96,2048]{1,0:T(8,128)(2,1)S(1)}, bf16[96,2048]{1,0:T(8,128)(2,1)S(1)}, u32[]{:S(2)}, u32[]{:S(2)}) %collective-permute-start.12) | collective-permute-done | bytes 393248 | tf_op jit(solution)/shard_map/ppermute | solution.py:119
  89.5 4.4 %collective-permute-start.13 = (bf16[96,2048]{1,0:T(8,128)(2,1)S(1)}, bf16[96,2048]{1,0:T(8,128)(2,1)S(1)}, u32[]{:S(2)}, u32[]{:S(2)}) collective-permute-start(bf16[96,2048]{1,0:T(8,128)(2,1)S(1)} %fusion.81), channel_id=1, source_target_pairs={{0,1},{1,2},{2,3},{4,5},{5,6},{6,7},{8,9},{9,10},{10,11},{12,13},{... | collective-permute-start | bytes 1179656 | tf_op jit(solution)/shard_map/ppermute | solution.py:119
  95.3 6.8 %collective-permute-done.13 = bf16[96,2048]{1,0:T(8,128)(2,1)S(1)} collective-permute-done((bf16[96,2048]{1,0:T(8,128)(2,1)S(1)}, bf16[96,2048]{1,0:T(8,128)(2,1)S(1)}, u32[]{:S(2)}, u32[]{:S(2)}) %collective-permute-start.13) | collective-permute-done | bytes 393248 | tf_op jit(solution)/shard_map/ppermute | solution.py:119
  102.2 4.4 %collective-permute-start.14 = (bf16[96,2048]{1,0:T(8,128)(2,1)S(1)}, bf16[96,2048]{1,0:T(8,128)(2,1)S(1)}, u32[]{:S(2)}, u32[]{:S(2)}) collective-permute-start(bf16[96,2048]{1,0:T(8,128)(2,1)S(1)} %fusion.80), channel_id=1, source_target_pairs={{0,1},{1,2},{2,3},{4,5},{5,6},{6,7},{8,9},{9,10},{10,11},{12,13},{... | collective-permute-start | bytes 1179656 | tf_op jit(solution)/shard_map/ppermute | solution.py:119
  108.0 5.9 %collective-permute-done.14 = bf16[96,2048]{1,0:T(8,128)(2,1)S(1)} collective-permute-done((bf16[96,2048]{1,0:T(8,128)(2,1)S(1)}, bf16[96,2048]{1,0:T(8,128)(2,1)S(1)}, u32[]{:S(2)}, u32[]{:S(2)}) %collective-permute-start.14) | collective-permute-done | bytes 393248 | tf_op jit(solution)/shard_map/ppermute | solution.py:119
  113.9 4.2 %collective-permute-done.17 = bf16[96,2048]{1,0:T(8,128)(2,1)S(1)} collective-permute-done((bf16[96,2048]{1,0:T(8,128)(2,1)S(1)}, bf16[96,2048]{1,0:T(8,128)(2,1)S(1)}, u32[]{:S(2)}, u32[]{:S(2)}) %collective-permute-start.17) | collective-permute-done | bytes 393248 | tf_op jit(solution)/shard_map/ppermute | solution.py:120
  119.0 3.5 %collective-permute-start.18 = (bf16[96,2048]{1,0:T(8,128)(2,1)S(1)}, bf16[96,2048]{1,0:T(8,128)(2,1)S(1)}, u32[]{:S(2)}, u32[]{:S(2)}) collective-permute-start(bf16[96,2048]{1,0:T(8,128)(2,1)S(1)} %get-tuple-element.33), channel_id=1, source_target_pairs={{0,1},{1,2},{2,3},{4,5},{5,6},{6,7},{8,9},{9,10},{10,11},{12,13},{... | collective-permute-start | bytes 1179656 | tf_op jit(solution)/shard_map/ppermute | solution.py:126
  123.9 4.7 %collective-permute-done.18 = bf16[96,2048]{1,0:T(8,128)(2,1)S(1)} collective-permute-done((bf16[96,2048]{1,0:T(8,128)(2,1)S(1)}, bf16[96,2048]{1,0:T(8,128)(2,1)S(1)}, u32[]{:S(2)}, u32[]{:S(2)}) %collective-permute-start.18) | collective-permute-done | bytes 393248 | tf_op jit(solution)/shard_map/ppermute | solution.py:126
  128.6 4.4 %collective-permute-start.19 = (bf16[96,2048]{1,0:T(8,128)(2,1)S(1)}, bf16[96,2048]{1,0:T(8,128)(2,1)S(1)}, u32[]{:S(2)}, u32[]{:S(2)}) collective-permute-start(bf16[96,2048]{1,0:T(8,128)(2,1)S(1)} %collective-permute-done.18), channel_id=1, source_target_pairs={{0,1},{1,2},{2,3},{4,5},{5,6},{6,7},{8,9},{9,10},{10,11},{12,13},{... | collective-permute-start | bytes 1179656 | tf_op jit(solution)/shard_map/ppermute | solution.py:126
  135.1 3.2 %collective-permute-done.19 = bf16[96,2048]{1,0:T(8,128)(2,1)S(1)} collective-permute-done((bf16[96,2048]{1,0:T(8,128)(2,1)S(1)}, bf16[96,2048]{1,0:T(8,128)(2,1)S(1)}, u32[]{:S(2)}, u32[]{:S(2)}) %collective-permute-start.19) | collective-permute-done | bytes 393248 | tf_op jit(solution)/shard_map/ppermute | solution.py:126
  138.3 4.4 %collective-permute-start.20 = (bf16[96,2048]{1,0:T(8,128)(2,1)S(1)}, bf16[96,2048]{1,0:T(8,128)(2,1)S(1)}, u32[]{:S(2)}, u32[]{:S(2)}) collective-permute-start(bf16[96,2048]{1,0:T(8,128)(2,1)S(1)} %collective-permute-done.19), channel_id=1, source_target_pairs={{0,1},{1,2},{2,3},{4,5},{5,6},{6,7},{8,9},{9,10},{10,11},{12,13},{... | collective-permute-start | bytes 1179656 | tf_op jit(solution)/shard_map/ppermute | solution.py:126
  144.9 3.1 %collective-permute-done.20 = bf16[96,2048]{1,0:T(8,128)(2,1)S(1)} collective-permute-done((bf16[96,2048]{1,0:T(8,128)(2,1)S(1)}, bf16[96,2048]{1,0:T(8,128)(2,1)S(1)}, u32[]{:S(2)}, u32[]{:S(2)}) %collective-permute-start.20) | collective-permute-done | bytes 393248 | tf_op jit(solution)/shard_map/ppermute | solution.py:126
  (154 shorter events, 53.4 us)
Async XLA Ops:
  2.4 20.0 %collective-permute-start.2 = (bf16[2,2,512,128]{3,2,1,0:T(8,128)(2,1)S(1)}, bf16[2,2,512,128]{3,2,1,0:T(8,128)(2,1)S(1)}, u32[]{:S(2)}, u32[]{:S(2)}) collective-permute-start(bf16[2,2,512,128]{3,2,1,0:T(8,128)(2,1)S(1)} %bitcast.267), channel_id=1, source_target_pairs={{0,8},{4,12},{8,0},{12,4},{1,9},{5,13},{9,1},{13,5},{2,10},{6,14},... | collective-permute-start | bytes 1572872 | tf_op jit(solution)/shard_map/ppermute | solution.py:197
  5.4 18.9 %collective-permute-start = (bf16[2,2,512,128]{3,2,1,0:T(8,128)(2,1)S(1)}, bf16[2,2,512,128]{3,2,1,0:T(8,128)(2,1)S(1)}, u32[]{:S(2)}, u32[]{:S(2)}) collective-permute-start(bf16[2,2,512,128]{3,2,1,0:T(8,128)(2,1)S(1)} %bitcast.268), channel_id=1, source_target_pairs={{0,4},{4,0},{8,12},{12,8},{1,5},{5,1},{9,13},{13,9},{2,6},{6,2},{1... | collective-permute-start | bytes 1572872 | tf_op jit(solution)/shard_map/ppermute | solution.py:201
  6.2 12.5 %collective-permute-start.6 = (bf16[2,2,32,2,128]{4,2,3,1,0:T(8,128)(2,1)S(1)}, bf16[2,2,32,2,128]{4,2,3,1,0:T(8,128)(2,1)S(1)}, u32[]{:S(2)}, u32[]{:S(2)}) collective-permute-start(bf16[2,2,32,2,128]{4,2,3,1,0:T(8,128)(2,1)S(1)} %get-tuple-element.67), channel_id=1, source_target_pairs={{0,8},{4,12},{8,0},{12,4},{1,9},{5,13},{9,1},{13,5},{2,10},{6,14},... | collective-permute-start | bytes 196616 | tf_op jit(solution)/shard_map/ppermute | solution.py:80
  8.0 38.1 %collective-permute-start.1 = (bf16[2,2,512,128]{3,2,1,0:T(8,128)(2,1)S(1)}, bf16[2,2,512,128]{3,2,1,0:T(8,128)(2,1)}, u32[]{:S(2)}, u32[]{:S(2)}) collective-permute-start(bf16[2,2,512,128]{3,2,1,0:T(8,128)(2,1)S(1)} %bitcast.294), channel_id=1, source_target_pairs={{0,4},{4,0},{8,12},{12,8},{1,5},{5,1},{9,13},{13,9},{2,6},{6,2},{1... | collective-permute-start | bytes 1572872 | tf_op jit(solution)/shard_map/ppermute | solution.py:201
  18.7 1.4 collective-permute-start.7
  22.3 7.3 %collective-permute-start.3 = (bf16[2,2,512,128]{3,2,1,0:T(8,128)(2,1)S(1)}, bf16[2,2,512,128]{3,2,1,0:T(8,128)(2,1)S(1)}, u32[]{:S(2)}, u32[]{:S(2)}) collective-permute-start(bf16[2,2,512,128]{3,2,1,0:T(8,128)(2,1)S(1)} %collective-permute-done.2), channel_id=1, source_target_pairs={{0,4},{4,0},{8,12},{12,8},{1,5},{5,1},{9,13},{13,9},{2,6},{6,2},{1... | collective-permute-start | bytes 1572872 | tf_op jit(solution)/shard_map/ppermute | solution.py:202
  22.6 26.7 %collective-permute-start.4 = (bf16[2,2,512,128]{3,2,1,0:T(8,128)(2,1)S(1)}, bf16[2,2,512,128]{3,2,1,0:T(8,128)(2,1)}, u32[]{:S(2)}, u32[]{:S(2)}) collective-permute-start(bf16[2,2,512,128]{3,2,1,0:T(8,128)(2,1)S(1)} %bitcast.295), channel_id=1, source_target_pairs={{0,8},{4,12},{8,0},{12,4},{1,9},{5,13},{9,1},{13,5},{2,10},{6,14},... | collective-permute-start | bytes 1572872 | tf_op jit(solution)/shard_map/ppermute | solution.py:199
  49.3 2.9 %collective-permute-start.5 = (bf16[2,2,512,128]{3,2,1,0:T(8,128)(2,1)}, bf16[2,2,512,128]{3,2,1,0:T(8,128)(2,1)S(1)}, u32[]{:S(2)}, u32[]{:S(2)}) collective-permute-start(bf16[2,2,512,128]{3,2,1,0:T(8,128)(2,1)} %collective-permute-done.4), channel_id=1, source_target_pairs={{0,4},{4,0},{8,12},{12,8},{1,5},{5,1},{9,13},{13,9},{2,6},{6,2},{1... | collective-permute-start | bytes 1572872 | tf_op jit(solution)/shard_map/ppermute | solution.py:202
  54.9 5.9 %collective-permute-start.10 = (bf16[4,8,2048]{2,1,0:T(8,128)(2,1)S(1)}, bf16[4,8,2048]{2,1,0:T(8,128)(2,1)S(1)}, u32[]{:S(2)}, u32[]{:S(2)}) collective-permute-start(bf16[4,8,2048]{2,1,0:T(8,128)(2,1)S(1)} %reshape.329), channel_id=1, source_target_pairs={{0,8},{4,12},{8,0},{12,4},{1,9},{5,13},{9,1},{13,5},{2,10},{6,14},... | collective-permute-start | bytes 393224 | tf_op jit(solution)/shard_map/ppermute | solution.py:80
  58.9 8.5 %collective-permute-start.8 = (bf16[2,32,2048]{2,1,0:T(8,128)(2,1)S(1)}, bf16[2,32,2048]{2,1,0:T(8,128)(2,1)S(1)}, u32[]{:S(2)}, u32[]{:S(2)}) collective-permute-start(bf16[2,32,2048]{2,1,0:T(8,128)(2,1)S(1)} %reshape.325), channel_id=1, source_target_pairs={{0,8},{4,12},{8,0},{12,4},{1,9},{5,13},{9,1},{13,5},{2,10},{6,14},... | collective-permute-start | bytes 786440 | tf_op jit(solution)/shard_map/ppermute | solution.py:80
  60.9 6.6 %collective-permute-start.11 = (bf16[2,4,8,2048]{3,2,1,0:T(8,128)(2,1)S(1)}, bf16[2,4,8,2048]{3,2,1,0:T(8,128)(2,1)S(1)}, u32[]{:S(2)}, u32[]{:S(2)}) collective-permute-start(bf16[2,4,8,2048]{3,2,1,0:T(8,128)(2,1)S(1)} %pad_maximum_fusion.11), channel_id=1, source_target_pairs={{0,4},{4,0},{8,12},{12,8},{1,5},{5,1},{9,13},{13,9},{2,6},{6,2},{1... | collective-permute-start | bytes 786440 | tf_op jit(solution)/shard_map/ppermute | solution.py:82
  67.4 5.7 %collective-permute-start.9 = (bf16[2,2,32,2048]{3,2,1,0:T(8,128)(2,1)S(1)}, bf16[2,2,32,2048]{3,2,1,0:T(8,128)(2,1)S(1)}, u32[]{:S(2)}, u32[]{:S(2)}) collective-permute-start(bf16[2,2,32,2048]{3,2,1,0:T(8,128)(2,1)S(1)} %pad_maximum_fusion.8), channel_id=1, source_target_pairs={{0,4},{4,0},{8,12},{12,8},{1,5},{5,1},{9,13},{13,9},{2,6},{6,2},{1... | collective-permute-start | bytes 1572872 | tf_op jit(solution)/shard_map/ppermute | solution.py:82
  76.7 12.7 %collective-permute-start.12 = (bf16[96,2048]{1,0:T(8,128)(2,1)S(1)}, bf16[96,2048]{1,0:T(8,128)(2,1)S(1)}, u32[]{:S(2)}, u32[]{:S(2)}) collective-permute-start(bf16[96,2048]{1,0:T(8,128)(2,1)S(1)} %pad_maximum_fusion.9), channel_id=1, source_target_pairs={{0,1},{1,2},{2,3},{4,5},{5,6},{6,7},{8,9},{9,10},{10,11},{12,13},{... | collective-permute-start | bytes 1179656 | tf_op jit(solution)/shard_map/ppermute | solution.py:119
  80.5 13.4 %collective-permute-start.15 = (bf16[96,2048]{1,0:T(8,128)(2,1)S(1)}, bf16[96,2048]{1,0:T(8,128)(2,1)S(1)}, u32[]{:S(2)}, u32[]{:S(2)}) collective-permute-start(bf16[96,2048]{1,0:T(8,128)(2,1)S(1)} %pad_maximum_fusion.10), channel_id=1, source_target_pairs={{1,0},{2,1},{3,2},{5,4},{6,5},{7,6},{9,8},{10,9},{11,10},{13,12},{... | collective-permute-start | bytes 1179656 | tf_op jit(solution)/shard_map/ppermute | solution.py:120
  89.5 12.6 %collective-permute-start.13 = (bf16[96,2048]{1,0:T(8,128)(2,1)S(1)}, bf16[96,2048]{1,0:T(8,128)(2,1)S(1)}, u32[]{:S(2)}, u32[]{:S(2)}) collective-permute-start(bf16[96,2048]{1,0:T(8,128)(2,1)S(1)} %fusion.81), channel_id=1, source_target_pairs={{0,1},{1,2},{2,3},{4,5},{5,6},{6,7},{8,9},{9,10},{10,11},{12,13},{... | collective-permute-start | bytes 1179656 | tf_op jit(solution)/shard_map/ppermute | solution.py:119
  94.0 12.6 %collective-permute-start.16 = (bf16[96,2048]{1,0:T(8,128)(2,1)S(1)}, bf16[96,2048]{1,0:T(8,128)(2,1)S(1)}, u32[]{:S(2)}, u32[]{:S(2)}) collective-permute-start(bf16[96,2048]{1,0:T(8,128)(2,1)S(1)} %fusion.83), channel_id=1, source_target_pairs={{1,0},{2,1},{3,2},{5,4},{6,5},{7,6},{9,8},{10,9},{11,10},{13,12},{... | collective-permute-start | bytes 1179656 | tf_op jit(solution)/shard_map/ppermute | solution.py:120
  102.2 11.7 %collective-permute-start.14 = (bf16[96,2048]{1,0:T(8,128)(2,1)S(1)}, bf16[96,2048]{1,0:T(8,128)(2,1)S(1)}, u32[]{:S(2)}, u32[]{:S(2)}) collective-permute-start(bf16[96,2048]{1,0:T(8,128)(2,1)S(1)} %fusion.80), channel_id=1, source_target_pairs={{0,1},{1,2},{2,3},{4,5},{5,6},{6,7},{8,9},{9,10},{10,11},{12,13},{... | collective-permute-start | bytes 1179656 | tf_op jit(solution)/shard_map/ppermute | solution.py:119
  106.7 11.4 %collective-permute-start.17 = (bf16[96,2048]{1,0:T(8,128)(2,1)S(1)}, bf16[96,2048]{1,0:T(8,128)(2,1)S(1)}, u32[]{:S(2)}, u32[]{:S(2)}) collective-permute-start(bf16[96,2048]{1,0:T(8,128)(2,1)S(1)} %fusion.82), channel_id=1, source_target_pairs={{1,0},{2,1},{3,2},{5,4},{6,5},{7,6},{9,8},{10,9},{11,10},{13,12},{... | collective-permute-start | bytes 1179656 | tf_op jit(solution)/shard_map/ppermute | solution.py:120
  119.0 9.6 %collective-permute-start.18 = (bf16[96,2048]{1,0:T(8,128)(2,1)S(1)}, bf16[96,2048]{1,0:T(8,128)(2,1)S(1)}, u32[]{:S(2)}, u32[]{:S(2)}) collective-permute-start(bf16[96,2048]{1,0:T(8,128)(2,1)S(1)} %get-tuple-element.33), channel_id=1, source_target_pairs={{0,1},{1,2},{2,3},{4,5},{5,6},{6,7},{8,9},{9,10},{10,11},{12,13},{... | collective-permute-start | bytes 1179656 | tf_op jit(solution)/shard_map/ppermute | solution.py:126
  122.5 10.5 %collective-permute-start.21 = (bf16[96,2048]{1,0:T(8,128)(2,1)S(1)}, bf16[96,2048]{1,0:T(8,128)(2,1)S(1)}, u32[]{:S(2)}, u32[]{:S(2)}) collective-permute-start(bf16[96,2048]{1,0:T(8,128)(2,1)S(1)} %get-tuple-element.33), channel_id=1, source_target_pairs={{1,0},{2,1},{3,2},{5,4},{6,5},{7,6},{9,8},{10,9},{11,10},{13,12},{... | collective-permute-start | bytes 1179656 | tf_op jit(solution)/shard_map/ppermute | solution.py:127
  128.6 9.7 %collective-permute-start.19 = (bf16[96,2048]{1,0:T(8,128)(2,1)S(1)}, bf16[96,2048]{1,0:T(8,128)(2,1)S(1)}, u32[]{:S(2)}, u32[]{:S(2)}) collective-permute-start(bf16[96,2048]{1,0:T(8,128)(2,1)S(1)} %collective-permute-done.18), channel_id=1, source_target_pairs={{0,1},{1,2},{2,3},{4,5},{5,6},{6,7},{8,9},{9,10},{10,11},{12,13},{... | collective-permute-start | bytes 1179656 | tf_op jit(solution)/shard_map/ppermute | solution.py:126
  133.0 9.8 %collective-permute-start.22 = (bf16[96,2048]{1,0:T(8,128)(2,1)S(1)}, bf16[96,2048]{1,0:T(8,128)(2,1)S(1)}, u32[]{:S(2)}, u32[]{:S(2)}) collective-permute-start(bf16[96,2048]{1,0:T(8,128)(2,1)S(1)} %collective-permute-done.21), channel_id=1, source_target_pairs={{1,0},{2,1},{3,2},{5,4},{6,5},{7,6},{9,8},{10,9},{11,10},{13,12},{... | collective-permute-start | bytes 1179656 | tf_op jit(solution)/shard_map/ppermute | solution.py:127
  138.3 9.7 %collective-permute-start.20 = (bf16[96,2048]{1,0:T(8,128)(2,1)S(1)}, bf16[96,2048]{1,0:T(8,128)(2,1)S(1)}, u32[]{:S(2)}, u32[]{:S(2)}) collective-permute-start(bf16[96,2048]{1,0:T(8,128)(2,1)S(1)} %collective-permute-done.19), channel_id=1, source_target_pairs={{0,1},{1,2},{2,3},{4,5},{5,6},{6,7},{8,9},{9,10},{10,11},{12,13},{... | collective-permute-start | bytes 1179656 | tf_op jit(solution)/shard_map/ppermute | solution.py:126
  142.8 9.7 %collective-permute-start.23 = (bf16[96,2048]{1,0:T(8,128)(2,1)S(1)}, bf16[96,2048]{1,0:T(8,128)(2,1)S(1)}, u32[]{:S(2)}, u32[]{:S(2)}) collective-permute-start(bf16[96,2048]{1,0:T(8,128)(2,1)S(1)} %collective-permute-done.22), channel_id=1, source_target_pairs={{1,0},{2,1},{3,2},{5,4},{6,5},{7,6},{9,8},{10,9},{11,10},{13,12},{... | collective-permute-start | bytes 1179656 | tf_op jit(solution)/shard_map/ppermute | solution.py:127
  (14 other events, 124.8 us)

commit v18 on v17

--- a/solution.py
+++ b/solution.py
@@ -199,13 +199,13 @@
     values_x = [lax.ppermute(values_after_keys, "ctx", pairs) for pairs in x_pairs]
     along_x = list(zip(keys_x, values_x))
     near = [own_pages, lax.ppermute(own_pages, "ctx", core_pairs)]
-    far = along_x + [lax.ppermute(pages, "ctx", core_pairs) for pages in along_x]
+    forwarded = [lax.ppermute(pages, "ctx", core_pairs) for pages in along_x]
     decode_flat = decode_five.reshape(kv_heads, -1, head_depth)
     decode_batch = jnp.broadcast_to(decode_flat[None], (prompts,) + decode_flat.shape).reshape(
         head_batch, -1, head_depth
     )
     decode_state = empty_state(head_batch, decode_flat.shape[1], head_depth)
-    for group in (near, far):
+    for group in (near, along_x, forwarded):
         key_rows, value_rows = (
             jnp.concatenate([pages[member] for pages in group], axis=2).reshape(
                 head_batch, -1, head_depth

time: 158 us -> 171 us (1.082)
  matrix products: 34.4 us -> 42.7 us
  local copies, waits for them, and re-layouts: 13.2 us -> 15.6 us
    ppermute x3, waiting for transfers between devices: 20 us -> 1.29 us  [head_sum_line(): lax.ppermute(going_right.astype(jnp.bfloat16), 'head', rightward)]
    ppermute x3, waiting for transfers between devices: 4.24 us -> 19.5 us  [head_sum_line(): from_right = lax.ppermute(going_left.astype(jnp.bfloat16), 'head', leftward)]
    dot_general x6 -> x8, matrix products: 11.7 us -> 18.7 us  [absorb(): jnp.einsum('brd,bnd->brn', queries, key_rows, preferred_element_type=jnp....]
    unnamed x33 -> x73, local copies, waits for them, and re-layouts: 4 us -> 7.58 us
    ppermute x3, waiting for transfers between devices: 14.3 us -> 16.9 us  [ctx_shards(): received.append(lax.ppermute(block, 'ctx', pairs))]
    dot_general x6 -> x8, matrix products: 10.7 us -> 13.1 us  [absorb(): jnp.einsum('brn,bnd->brd', weights.astype(jnp.bfloat16), value_rows, pref...]
    reduce_sum x6 -> x8, other arithmetic: 9.76 us -> 10.2 us  [absorb(): running_sum = running_sum * factor + jnp.sum(weights, axis=-1)]
  transfers between devices with their start and end apart: 24 -> 24, of which waited for: 13 -> 13; matrix products, arithmetic and copies ran while one was open for 31% -> 33% of each run, Pallas kernels for 0% -> 0%
where the time goes in v18:
time: 171 us; the launch traced here: 170 us
  waiting for transfers between devices  51.7 us (30%)
  matrix products  42.7 us (25%)
  starting transfers between devices  42 us (25%)
  other arithmetic  16.4 us (10%)
  local copies, waits for them, and re-layouts  15.6 us (9%)
  between operations  1.74 us (1%)
    ppermute x3, waiting for transfers between devices, head_sum_line(): from_right = lax.ppermute(going_left.astype(jnp.bfloat16), 'head', leftward)  19.5 us
    dot_general x8, matrix products, absorb(): jnp.einsum('brd,bnd->brn', queries, key_rows, preferred_element_type=jnp....  18.7 us
    ppermute x3, waiting for transfers between devices, ctx_shards(): received.append(lax.ppermute(block, 'ctx', pairs))  16.9 us
    ppermute x3, starting transfers between devices, head_sum_line(): lax.ppermute(going_right.astype(jnp.bfloat16), 'head', rightward)  13.7 us
    ppermute x3, starting transfers between devices, head_sum_line(): send_right = lax.ppermute(send_right, 'head', rightward)  13.2 us
    dot_general x8, matrix products, absorb(): jnp.einsum('brn,bnd->brd', weights.astype(jnp.bfloat16), value_rows, pref...  13.1 us
    ppermute x3, waiting for transfers between devices, head_sum_line(): send_right = lax.ppermute(send_right, 'head', rightward)  11 us
    reduce_sum x8, other arithmetic, absorb(): running_sum = running_sum * factor + jnp.sum(weights, axis=-1)  10.2 us
  transfers between devices with their start and end apart: 24, of which 13 were waited for; matrix products, arithmetic and copies ran while one was open for 33% of the time, Pallas kernels for 0%

profile of v18, /device:TPU:0, one launch (start us, length us, event | category | flops | bytes accessed | tf_op | source)
XLA Modules:
  0.0 170.3 jit_solution(1680860953450873149)
XLA Ops:
  2.4 3.0 %collective-permute-start.2 = (bf16[2,2,512,128]{3,2,1,0:T(8,128)(2,1)S(1)}, bf16[2,2,512,128]{3,2,1,0:T(8,128)(2,1)}, u32[]{:S(2)}, u32[]{:S(2)}) collective-permute-start(bf16[2,2,512,128]{3,2,1,0:T(8,128)(2,1)S(1)} %bitcast.285), channel_id=1, source_target_pairs={{0,8},{4,12},{8,0},{12,4},{1,9},{5,13},{9,1},{13,5},{2,10},{6,14},... | collective-permute-start | bytes 1572872 | tf_op jit(solution)/shard_map/ppermute | solution.py:197
  9.1 9.7 %collective-permute-done.6 = bf16[2,2,32,2,128]{4,2,3,1,0:T(8,128)(2,1)S(1)} collective-permute-done((bf16[2,2,32,2,128]{4,2,3,1,0:T(8,128)(2,1)S(1)}, bf16[2,2,32,2,128]{4,2,3,1,0:T(8,128)(2,1)S(1)}, u32[]{:S(2)}, u32[]{:S(2)}) %collective-permute-start.6) | collective-permute-done | bytes 65568 | tf_op jit(solution)/shard_map/ppermute | solution.py:80
  24.6 2.9 %bitcast_reduce_fusion.3 = (f32[4,256]{1,0:T(4,128)S(1)}, f32[4,512,256]{2,1,0:T(8,128)}) fusion(bf16[4,512,128]{2,1,0:T(8,128)(2,1)} %bitcast.17, bf16[4,256,128]{2,1,0:T(8,128)(2,1)S(1)} %bitcast.278), kind=kOutput, calls=%fused_computation.21 | convolution fusion | flops 135265280 | bytes 2887680 | tf_op jit(solution)/shard_map/brd,bnd->brn/dot_general | solution.py:14
  28.4 2.6 %bitcast_reduce_fusion = (f32[4,256]{1,0:T(4,128)S(1)}, f32[4,1024,256]{2,1,0:T(8,128)}) fusion(bf16[4,256,128]{2,1,0:T(8,128)(2,1)S(1)} %bitcast.279, bf16[4,512,128]{2,1,0:T(8,128)(2,1)S(1)} %bitcast.292, bf16[4,512,128]{2,1,0:T(8,128)(2,1)S(1)} %bitcast.287), kind=kOutput, calls=%fused_computation.6 | convolution fusion | flops 272628736 | bytes 5509120 | tf_op jit(solution)/shard_map/brd,bnd->brn/dot_general | solution.py:14
  33.2 2.7 %bitcast_reduce_fusion.1 = (f32[4,256]{1,0:T(4,128)S(1)}, f32[4,1024,256]{2,1,0:T(8,128)}) fusion(bf16[4,256,128]{2,1,0:T(8,128)(2,1)S(1)} %bitcast.283, bf16[4,512,128]{2,1,0:T(8,128)(2,1)S(1)} %bitcast.293, bf16[4,512,128]{2,1,0:T(8,128)(2,1)S(1)} %bitcast.288), kind=kOutput, calls=%fused_computation.9 | convolution fusion | flops 272628736 | bytes 5509120 | tf_op jit(solution)/shard_map/brd,bnd->brn/dot_general | solution.py:14
  35.9 2.8 %bitcast_reduce_fusion.2 = (f32[4,256]{1,0:T(4,128)S(1)}, f32[4,512,256]{2,1,0:T(8,128)}) fusion(bf16[4,512,128]{2,1,0:T(8,128)(2,1)} %bitcast.20, bf16[4,256,128]{2,1,0:T(8,128)(2,1)S(1)} %bitcast.280), kind=kOutput, calls=%fused_computation.18 | convolution fusion | flops 135265280 | bytes 2887680 | tf_op jit(solution)/shard_map/brd,bnd->brn/dot_general | solution.py:14
  38.7 3.5 %bitcast_reduce_fusion.4 = (f32[4,256]{1,0:T(4,128)}, f32[4,512,256]{2,1,0:T(8,128)}) fusion(bf16[4,512,128]{2,1,0:T(8,128)(2,1)} %bitcast.20, bf16[4,256,128]{2,1,0:T(8,128)(2,1)S(1)} %bitcast.284), kind=kOutput, calls=%fused_computation.24 | convolution fusion | flops 135265280 | bytes 2887680 | tf_op jit(solution)/shard_map/brd,bnd->brn/dot_general | solution.py:14
  49.0 2.9 %fusion.8 = f32[4,256]{1,0:T(4,128)S(1)} fusion(f32[4,1024,256]{2,1,0:T(8,128)} %get-tuple-element.84, f32[4,256]{1,0:T(4,128)S(1)} %get-tuple-element.76), kind=kLoop, calls=%fused_computation.13 | loop fusion | flops 3144704 | bytes 4202496 | tf_op jit(solution)/shard_map/reduce_sum | solution.py:22
  60.5 2.7 %fusion.39 = f32[4,256,128]{2,1,0:T(8,128)S(1)} fusion(f32[4,1024,256]{2,1,0:T(8,128)S(1)} %copy-done.4, f32[4,256]{1,0:T(4,128)S(1)} %get-tuple-element.72, bf16[4,512,128]{2,1,0:T(8,128)(2,1)} %bitcast.16, bf16[4,512,128]{2,1,0:T(8,128)(2,1)} %bitcast.14, f32[4,256]{1,0:T(4,128)S(1)} %get-tuple-element.39, f32[4,256]{1,0:T(4,128)S(1)} %get-tuple-element.71), kind=kOutput, calls=%fused_computation.55 | convolution fusion | flops 273940480 | bytes 5779456 | tf_op jit(solution)/shard_map/brn,bnd->brd/dot_general | solution.py:23
  75.6 5.5 %collective-permute-done.8 = bf16[2,32,2048]{2,1,0:T(8,128)(2,1)S(1)} collective-permute-done((bf16[2,32,2048]{2,1,0:T(8,128)(2,1)S(1)}, bf16[2,32,2048]{2,1,0:T(8,128)(2,1)S(1)}, u32[]{:S(2)}, u32[]{:S(2)}) %collective-permute-start.8) | collective-permute-done | bytes 262176 | tf_op jit(solution)/shard_map/ppermute | solution.py:80
  81.9 4.8 %fusion = f32[4,32,2048]{2,1,0:T(8,128)S(1)} fusion(bf16[4,32,2048]{2,1,0:T(8,128)(2,1)S(1)} %bitcast.289, bf16[2048,2048]{1,0:T(8,128)(2,1)} %param.27), kind=kOutput, calls=%fused_computation.1 | convolution fusion | flops 1073741824 | bytes 9961472 | tf_op jit(solution)/shard_map/dot_general | solution.py:248
  91.9 4.6 %collective-permute-start.12 = (bf16[96,2048]{1,0:T(8,128)(2,1)S(1)}, bf16[96,2048]{1,0:T(8,128)(2,1)S(1)}, u32[]{:S(2)}, u32[]{:S(2)}) collective-permute-start(bf16[96,2048]{1,0:T(8,128)(2,1)S(1)} %pad_maximum_fusion.7), channel_id=1, source_target_pairs={{0,1},{1,2},{2,3},{4,5},{5,6},{6,7},{8,9},{9,10},{10,11},{12,13},{... | collective-permute-start | bytes 1179656 | tf_op jit(solution)/shard_map/ppermute | solution.py:119
  96.8 7.2 %collective-permute-done.15 = bf16[96,2048]{1,0:T(8,128)(2,1)S(1)} collective-permute-done((bf16[96,2048]{1,0:T(8,128)(2,1)S(1)}, bf16[96,2048]{1,0:T(8,128)(2,1)S(1)}, u32[]{:S(2)}, u32[]{:S(2)}) %collective-permute-start.15) | collective-permute-done | bytes 393248 | tf_op jit(solution)/shard_map/ppermute | solution.py:120
  105.4 4.6 %collective-permute-start.13 = (bf16[96,2048]{1,0:T(8,128)(2,1)S(1)}, bf16[96,2048]{1,0:T(8,128)(2,1)S(1)}, u32[]{:S(2)}, u32[]{:S(2)}) collective-permute-start(bf16[96,2048]{1,0:T(8,128)(2,1)S(1)} %fusion.75), channel_id=1, source_target_pairs={{0,1},{1,2},{2,3},{4,5},{5,6},{6,7},{8,9},{9,10},{10,11},{12,13},{... | collective-permute-start | bytes 1179656 | tf_op jit(solution)/shard_map/ppermute | solution.py:119
  110.0 6.6 %collective-permute-done.16 = bf16[96,2048]{1,0:T(8,128)(2,1)S(1)} collective-permute-done((bf16[96,2048]{1,0:T(8,128)(2,1)S(1)}, bf16[96,2048]{1,0:T(8,128)(2,1)S(1)}, u32[]{:S(2)}, u32[]{:S(2)}) %collective-permute-start.16) | collective-permute-done | bytes 393248 | tf_op jit(solution)/shard_map/ppermute | solution.py:120
  118.1 4.6 %collective-permute-start.14 = (bf16[96,2048]{1,0:T(8,128)(2,1)S(1)}, bf16[96,2048]{1,0:T(8,128)(2,1)S(1)}, u32[]{:S(2)}, u32[]{:S(2)}) collective-permute-start(bf16[96,2048]{1,0:T(8,128)(2,1)S(1)} %fusion.74), channel_id=1, source_target_pairs={{0,1},{1,2},{2,3},{4,5},{5,6},{6,7},{8,9},{9,10},{10,11},{12,13},{... | collective-permute-start | bytes 1179656 | tf_op jit(solution)/shard_map/ppermute | solution.py:119
  122.7 5.7 %collective-permute-done.17 = bf16[96,2048]{1,0:T(8,128)(2,1)S(1)} collective-permute-done((bf16[96,2048]{1,0:T(8,128)(2,1)S(1)}, bf16[96,2048]{1,0:T(8,128)(2,1)S(1)}, u32[]{:S(2)}, u32[]{:S(2)}) %collective-permute-start.17) | collective-permute-done | bytes 393248 | tf_op jit(solution)/shard_map/ppermute | solution.py:120
  130.6 4.4 %collective-permute-start.18 = (bf16[96,2048]{1,0:T(8,128)(2,1)S(1)}, bf16[96,2048]{1,0:T(8,128)(2,1)S(1)}, u32[]{:S(2)}, u32[]{:S(2)}) collective-permute-start(bf16[96,2048]{1,0:T(8,128)(2,1)S(1)} %get-tuple-element.33), channel_id=1, source_target_pairs={{0,1},{1,2},{2,3},{4,5},{5,6},{6,7},{8,9},{9,10},{10,11},{12,13},{... | collective-permute-start | bytes 1179656 | tf_op jit(solution)/shard_map/ppermute | solution.py:126
  136.3 4.7 %collective-permute-done.18 = bf16[96,2048]{1,0:T(8,128)(2,1)S(1)} collective-permute-done((bf16[96,2048]{1,0:T(8,128)(2,1)S(1)}, bf16[96,2048]{1,0:T(8,128)(2,1)S(1)}, u32[]{:S(2)}, u32[]{:S(2)}) %collective-permute-start.18) | collective-permute-done | bytes 393248 | tf_op jit(solution)/shard_map/ppermute | solution.py:126
  141.1 4.4 %collective-permute-start.19 = (bf16[96,2048]{1,0:T(8,128)(2,1)S(1)}, bf16[96,2048]{1,0:T(8,128)(2,1)S(1)}, u32[]{:S(2)}, u32[]{:S(2)}) collective-permute-start(bf16[96,2048]{1,0:T(8,128)(2,1)S(1)} %collective-permute-done.18), channel_id=1, source_target_pairs={{0,1},{1,2},{2,3},{4,5},{5,6},{6,7},{8,9},{9,10},{10,11},{12,13},{... | collective-permute-start | bytes 1179656 | tf_op jit(solution)/shard_map/ppermute | solution.py:126
  147.6 3.2 %collective-permute-done.19 = bf16[96,2048]{1,0:T(8,128)(2,1)S(1)} collective-permute-done((bf16[96,2048]{1,0:T(8,128)(2,1)S(1)}, bf16[96,2048]{1,0:T(8,128)(2,1)S(1)}, u32[]{:S(2)}, u32[]{:S(2)}) %collective-permute-start.19) | collective-permute-done | bytes 393248 | tf_op jit(solution)/shard_map/ppermute | solution.py:126
  150.8 4.4 %collective-permute-start.20 = (bf16[96,2048]{1,0:T(8,128)(2,1)S(1)}, bf16[96,2048]{1,0:T(8,128)(2,1)S(1)}, u32[]{:S(2)}, u32[]{:S(2)}) collective-permute-start(bf16[96,2048]{1,0:T(8,128)(2,1)S(1)} %collective-permute-done.19), channel_id=1, source_target_pairs={{0,1},{1,2},{2,3},{4,5},{5,6},{6,7},{8,9},{9,10},{10,11},{12,13},{... | collective-permute-start | bytes 1179656 | tf_op jit(solution)/shard_map/ppermute | solution.py:126
  157.4 3.0 %collective-permute-done.20 = bf16[96,2048]{1,0:T(8,128)(2,1)S(1)} collective-permute-done((bf16[96,2048]{1,0:T(8,128)(2,1)S(1)}, bf16[96,2048]{1,0:T(8,128)(2,1)S(1)}, u32[]{:S(2)}, u32[]{:S(2)}) %collective-permute-start.20) | collective-permute-done | bytes 393248 | tf_op jit(solution)/shard_map/ppermute | solution.py:126
  165.7 2.4 %gather_fusion = bf16[4,96,2048]{2,1,0:T(8,128)(2,1)S(1)} fusion(bf16[7,96,2048]{2,1,0:T(8,128)(2,1)} %bitcast_dynamic-update-slice_fusion, s32[1024]{0:T(1024)S(1)} %pad_clamp_fusion), kind=kCustom, calls=%fused_computation | custom fusion | bytes 3145744 | tf_op jit(solution)/shard_map/jit(_take)/gather | solution.py:137
  (200 shorter events, 65.6 us)
Async XLA Ops:
  2.4 20.3 %collective-permute-start.2 = (bf16[2,2,512,128]{3,2,1,0:T(8,128)(2,1)S(1)}, bf16[2,2,512,128]{3,2,1,0:T(8,128)(2,1)}, u32[]{:S(2)}, u32[]{:S(2)}) collective-permute-start(bf16[2,2,512,128]{3,2,1,0:T(8,128)(2,1)S(1)} %bitcast.285), channel_id=1, source_target_pairs={{0,8},{4,12},{8,0},{12,4},{1,9},{5,13},{9,1},{13,5},{2,10},{6,14},... | collective-permute-start | bytes 1572872 | tf_op jit(solution)/shard_map/ppermute | solution.py:197
  5.4 22.1 %collective-permute-start = (bf16[2,2,512,128]{3,2,1,0:T(8,128)(2,1)S(1)}, bf16[2,2,512,128]{3,2,1,0:T(8,128)(2,1)S(1)}, u32[]{:S(2)}, u32[]{:S(2)}) collective-permute-start(bf16[2,2,512,128]{3,2,1,0:T(8,128)(2,1)S(1)} %bitcast.286), channel_id=1, source_target_pairs={{0,4},{4,0},{8,12},{12,8},{1,5},{5,1},{9,13},{13,9},{2,6},{6,2},{1... | collective-permute-start | bytes 1572872 | tf_op jit(solution)/shard_map/ppermute | solution.py:201
  5.5 13.3 %collective-permute-start.6 = (bf16[2,2,32,2,128]{4,2,3,1,0:T(8,128)(2,1)S(1)}, bf16[2,2,32,2,128]{4,2,3,1,0:T(8,128)(2,1)S(1)}, u32[]{:S(2)}, u32[]{:S(2)}) collective-permute-start(bf16[2,2,32,2,128]{4,2,3,1,0:T(8,128)(2,1)S(1)} %get-tuple-element.70), channel_id=1, source_target_pairs={{0,8},{4,12},{8,0},{12,4},{1,9},{5,13},{9,1},{13,5},{2,10},{6,14},... | collective-permute-start | bytes 196616 | tf_op jit(solution)/shard_map/ppermute | solution.py:80
  7.0 49.0 %collective-permute-start.1 = (bf16[2,2,512,128]{3,2,1,0:T(8,128)(2,1)}, bf16[2,2,512,128]{3,2,1,0:T(8,128)(2,1)}, u32[]{:S(2)}, u32[]{:S(2)}) collective-permute-start(bf16[2,2,512,128]{3,2,1,0:T(8,128)(2,1)} %bitcast.15), channel_id=1, source_target_pairs={{0,4},{4,0},{8,12},{12,8},{1,5},{5,1},{9,13},{13,9},{2,6},{6,2},{1... | collective-permute-start | bytes 1572872 | tf_op jit(solution)/shard_map/ppermute | solution.py:201
  18.8 1.4 collective-permute-start.7
  22.7 13.2 %collective-permute-start.4 = (bf16[2,2,512,128]{3,2,1,0:T(8,128)(2,1)}, bf16[2,2,512,128]{3,2,1,0:T(8,128)(2,1)}, u32[]{:S(2)}, u32[]{:S(2)}) collective-permute-start(bf16[2,2,512,128]{3,2,1,0:T(8,128)(2,1)} %collective-permute-done.2), channel_id=1, source_target_pairs={{0,4},{4,0},{8,12},{12,8},{1,5},{5,1},{9,13},{13,9},{2,6},{6,2},{1... | collective-permute-start | bytes 1572872 | tf_op jit(solution)/shard_map/ppermute | solution.py:202
  22.8 40.4 %collective-permute-start.3 = (bf16[2,2,512,128]{3,2,1,0:T(8,128)(2,1)}, bf16[2,2,512,128]{3,2,1,0:T(8,128)(2,1)}, u32[]{:S(2)}, u32[]{:S(2)}) collective-permute-start(bf16[2,2,512,128]{3,2,1,0:T(8,128)(2,1)} %bitcast.15), channel_id=1, source_target_pairs={{0,8},{4,12},{8,0},{12,4},{1,9},{5,13},{9,1},{13,5},{2,10},{6,14},... | collective-permute-start | bytes 1572872 | tf_op jit(solution)/shard_map/ppermute | solution.py:199
  64.9 3.0 %collective-permute-start.5 = (bf16[2,2,512,128]{3,2,1,0:T(8,128)(2,1)}, bf16[2,2,512,128]{3,2,1,0:T(8,128)(2,1)S(1)}, u32[]{:S(2)}, u32[]{:S(2)}) collective-permute-start(bf16[2,2,512,128]{3,2,1,0:T(8,128)(2,1)} %collective-permute-done.3), channel_id=1, source_target_pairs={{0,4},{4,0},{8,12},{12,8},{1,5},{5,1},{9,13},{13,9},{2,6},{6,2},{1... | collective-permute-start | bytes 1572872 | tf_op jit(solution)/shard_map/ppermute | solution.py:202
  69.5 5.9 %collective-permute-start.10 = (bf16[4,8,2048]{2,1,0:T(8,128)(2,1)S(1)}, bf16[4,8,2048]{2,1,0:T(8,128)(2,1)S(1)}, u32[]{:S(2)}, u32[]{:S(2)}) collective-permute-start(bf16[4,8,2048]{2,1,0:T(8,128)(2,1)S(1)} %reshape.384), channel_id=1, source_target_pairs={{0,8},{4,12},{8,0},{12,4},{1,9},{5,13},{9,1},{13,5},{2,10},{6,14},... | collective-permute-start | bytes 393224 | tf_op jit(solution)/shard_map/ppermute | solution.py:80
  72.4 8.7 %collective-permute-start.8 = (bf16[2,32,2048]{2,1,0:T(8,128)(2,1)S(1)}, bf16[2,32,2048]{2,1,0:T(8,128)(2,1)S(1)}, u32[]{:S(2)}, u32[]{:S(2)}) collective-permute-start(bf16[2,32,2048]{2,1,0:T(8,128)(2,1)S(1)} %reshape.380), channel_id=1, source_target_pairs={{0,8},{4,12},{8,0},{12,4},{1,9},{5,13},{9,1},{13,5},{2,10},{6,14},... | collective-permute-start | bytes 786440 | tf_op jit(solution)/shard_map/ppermute | solution.py:80
  75.4 5.9 %collective-permute-start.11 = (bf16[2,4,8,2048]{3,2,1,0:T(8,128)(2,1)S(1)}, bf16[2,4,8,2048]{3,2,1,0:T(8,128)(2,1)S(1)}, u32[]{:S(2)}, u32[]{:S(2)}) collective-permute-start(bf16[2,4,8,2048]{3,2,1,0:T(8,128)(2,1)S(1)} %pad_maximum_fusion.9), channel_id=1, source_target_pairs={{0,4},{4,0},{8,12},{12,8},{1,5},{5,1},{9,13},{13,9},{2,6},{6,2},{1... | collective-permute-start | bytes 786440 | tf_op jit(solution)/shard_map/ppermute | solution.py:82
  81.2 5.7 %collective-permute-start.9 = (bf16[2,2,32,2048]{3,2,1,0:T(8,128)(2,1)S(1)}, bf16[2,2,32,2048]{3,2,1,0:T(8,128)(2,1)S(1)}, u32[]{:S(2)}, u32[]{:S(2)}) collective-permute-start(bf16[2,2,32,2048]{3,2,1,0:T(8,128)(2,1)S(1)} %pad_maximum_fusion.6), channel_id=1, source_target_pairs={{0,4},{4,0},{8,12},{12,8},{1,5},{5,1},{9,13},{13,9},{2,6},{6,2},{1... | collective-permute-start | bytes 1572872 | tf_op jit(solution)/shard_map/ppermute | solution.py:82
  90.5 13.4 %collective-permute-start.15 = (bf16[96,2048]{1,0:T(8,128)(2,1)S(1)}, bf16[96,2048]{1,0:T(8,128)(2,1)S(1)}, u32[]{:S(2)}, u32[]{:S(2)}) collective-permute-start(bf16[96,2048]{1,0:T(8,128)(2,1)S(1)} %pad_maximum_fusion.8), channel_id=1, source_target_pairs={{1,0},{2,1},{3,2},{5,4},{6,5},{7,6},{9,8},{10,9},{11,10},{13,12},{... | collective-permute-start | bytes 1179656 | tf_op jit(solution)/shard_map/ppermute | solution.py:120
  91.9 13.4 %collective-permute-start.12 = (bf16[96,2048]{1,0:T(8,128)(2,1)S(1)}, bf16[96,2048]{1,0:T(8,128)(2,1)S(1)}, u32[]{:S(2)}, u32[]{:S(2)}) collective-permute-start(bf16[96,2048]{1,0:T(8,128)(2,1)S(1)} %pad_maximum_fusion.7), channel_id=1, source_target_pairs={{0,1},{1,2},{2,3},{4,5},{5,6},{6,7},{8,9},{9,10},{10,11},{12,13},{... | collective-permute-start | bytes 1179656 | tf_op jit(solution)/shard_map/ppermute | solution.py:119
  104.0 12.6 %collective-permute-start.16 = (bf16[96,2048]{1,0:T(8,128)(2,1)S(1)}, bf16[96,2048]{1,0:T(8,128)(2,1)S(1)}, u32[]{:S(2)}, u32[]{:S(2)}) collective-permute-start(bf16[96,2048]{1,0:T(8,128)(2,1)S(1)} %fusion.77), channel_id=1, source_target_pairs={{1,0},{2,1},{3,2},{5,4},{6,5},{7,6},{9,8},{10,9},{11,10},{13,12},{... | collective-permute-start | bytes 1179656 | tf_op jit(solution)/shard_map/ppermute | solution.py:120
  105.4 12.6 %collective-permute-start.13 = (bf16[96,2048]{1,0:T(8,128)(2,1)S(1)}, bf16[96,2048]{1,0:T(8,128)(2,1)S(1)}, u32[]{:S(2)}, u32[]{:S(2)}) collective-permute-start(bf16[96,2048]{1,0:T(8,128)(2,1)S(1)} %fusion.75), channel_id=1, source_target_pairs={{0,1},{1,2},{2,3},{4,5},{5,6},{6,7},{8,9},{9,10},{10,11},{12,13},{... | collective-permute-start | bytes 1179656 | tf_op jit(solution)/shard_map/ppermute | solution.py:119
  116.7 11.7 %collective-permute-start.17 = (bf16[96,2048]{1,0:T(8,128)(2,1)S(1)}, bf16[96,2048]{1,0:T(8,128)(2,1)S(1)}, u32[]{:S(2)}, u32[]{:S(2)}) collective-permute-start(bf16[96,2048]{1,0:T(8,128)(2,1)S(1)} %fusion.76), channel_id=1, source_target_pairs={{1,0},{2,1},{3,2},{5,4},{6,5},{7,6},{9,8},{10,9},{11,10},{13,12},{... | collective-permute-start | bytes 1179656 | tf_op jit(solution)/shard_map/ppermute | solution.py:120
  118.1 11.6 %collective-permute-start.14 = (bf16[96,2048]{1,0:T(8,128)(2,1)S(1)}, bf16[96,2048]{1,0:T(8,128)(2,1)S(1)}, u32[]{:S(2)}, u32[]{:S(2)}) collective-permute-start(bf16[96,2048]{1,0:T(8,128)(2,1)S(1)} %fusion.74), channel_id=1, source_target_pairs={{0,1},{1,2},{2,3},{4,5},{5,6},{6,7},{8,9},{9,10},{10,11},{12,13},{... | collective-permute-start | bytes 1179656 | tf_op jit(solution)/shard_map/ppermute | solution.py:119
  130.6 10.5 %collective-permute-start.18 = (bf16[96,2048]{1,0:T(8,128)(2,1)S(1)}, bf16[96,2048]{1,0:T(8,128)(2,1)S(1)}, u32[]{:S(2)}, u32[]{:S(2)}) collective-permute-start(bf16[96,2048]{1,0:T(8,128)(2,1)S(1)} %get-tuple-element.33), channel_id=1, source_target_pairs={{0,1},{1,2},{2,3},{4,5},{5,6},{6,7},{8,9},{9,10},{10,11},{12,13},{... | collective-permute-start | bytes 1179656 | tf_op jit(solution)/shard_map/ppermute | solution.py:126
  135.0 10.5 %collective-permute-start.21 = (bf16[96,2048]{1,0:T(8,128)(2,1)S(1)}, bf16[96,2048]{1,0:T(8,128)(2,1)S(1)}, u32[]{:S(2)}, u32[]{:S(2)}) collective-permute-start(bf16[96,2048]{1,0:T(8,128)(2,1)S(1)} %get-tuple-element.33), channel_id=1, source_target_pairs={{1,0},{2,1},{3,2},{5,4},{6,5},{7,6},{9,8},{10,9},{11,10},{13,12},{... | collective-permute-start | bytes 1179656 | tf_op jit(solution)/shard_map/ppermute | solution.py:127
  141.1 9.7 %collective-permute-start.19 = (bf16[96,2048]{1,0:T(8,128)(2,1)S(1)}, bf16[96,2048]{1,0:T(8,128)(2,1)S(1)}, u32[]{:S(2)}, u32[]{:S(2)}) collective-permute-start(bf16[96,2048]{1,0:T(8,128)(2,1)S(1)} %collective-permute-done.18), channel_id=1, source_target_pairs={{0,1},{1,2},{2,3},{4,5},{5,6},{6,7},{8,9},{9,10},{10,11},{12,13},{... | collective-permute-start | bytes 1179656 | tf_op jit(solution)/shard_map/ppermute | solution.py:126
  145.5 9.8 %collective-permute-start.22 = (bf16[96,2048]{1,0:T(8,128)(2,1)S(1)}, bf16[96,2048]{1,0:T(8,128)(2,1)S(1)}, u32[]{:S(2)}, u32[]{:S(2)}) collective-permute-start(bf16[96,2048]{1,0:T(8,128)(2,1)S(1)} %collective-permute-done.21), channel_id=1, source_target_pairs={{1,0},{2,1},{3,2},{5,4},{6,5},{7,6},{9,8},{10,9},{11,10},{13,12},{... | collective-permute-start | bytes 1179656 | tf_op jit(solution)/shard_map/ppermute | solution.py:127
  150.8 9.7 %collective-permute-start.20 = (bf16[96,2048]{1,0:T(8,128)(2,1)S(1)}, bf16[96,2048]{1,0:T(8,128)(2,1)S(1)}, u32[]{:S(2)}, u32[]{:S(2)}) collective-permute-start(bf16[96,2048]{1,0:T(8,128)(2,1)S(1)} %collective-permute-done.19), channel_id=1, source_target_pairs={{0,1},{1,2},{2,3},{4,5},{5,6},{6,7},{8,9},{9,10},{10,11},{12,13},{... | collective-permute-start | bytes 1179656 | tf_op jit(solution)/shard_map/ppermute | solution.py:126
  155.3 9.7 %collective-permute-start.23 = (bf16[96,2048]{1,0:T(8,128)(2,1)S(1)}, bf16[96,2048]{1,0:T(8,128)(2,1)S(1)}, u32[]{:S(2)}, u32[]{:S(2)}) collective-permute-start(bf16[96,2048]{1,0:T(8,128)(2,1)S(1)} %collective-permute-done.22), channel_id=1, source_target_pairs={{1,0},{2,1},{3,2},{5,4},{6,5},{7,6},{9,8},{10,9},{11,10},{13,12},{... | collective-permute-start | bytes 1179656 | tf_op jit(solution)/shard_map/ppermute | solution.py:127
  (34 other events, 183.8 us)
